TPU v7x, 256 devices: a whole 4x4x8 slice. The times are simulated.
256 devices in a mesh: dp: 8 (over x, core), ctx: 32 (over z, y).
Axes of the slice: x: 4, y: 4, z: 8, core: 2. Of those that a mesh axis runs over, the one named last changes fastest.
Arguments:
- query_proj: bfloat16 [8, 4096, 4096], P('dp', 'ctx'), may hold values from -6 to 6
- key_proj: bfloat16 [8, 4096, 4096], P('dp', 'ctx'), may hold values from -6 to 6
- value_proj: bfloat16 [8, 4096, 4096], P('dp', 'ctx'), may hold values from -6 to 6
- doc_offset: int32 [8, 4096], P('dp', 'ctx'), may hold values from 0 to 4095, as said below
- short_taps: float32 [3, 7, 4096], replicated, may hold values from -2.5 to 2.5
- rate_scale: float32 [16, 4096], replicated, may hold values from 0.1 to 120
- residue: float32 [16, 4096], replicated, may hold values from -2.5 to 2.5
- skip_gain: float32 [4096], replicated, may hold values from 0.5 to 1.5
- out_grad: bfloat16 [8, 4096, 4096], P('dp', 'ctx'), may hold values from -6 to 6
Outputs:
- mixed_out: bfloat16 [8, 4096, 4096], P('dp', 'ctx')
- query_grad: bfloat16 [8, 4096, 4096], P('dp', 'ctx')
- key_grad: bfloat16 [8, 4096, 4096], P('dp', 'ctx')
- value_grad: bfloat16 [8, 4096, 4096], P('dp', 'ctx')
- taps_grad: float32 [3, 7, 4096], replicated
- skip_grad: float32 [4096], replicated
- residue_grad: float32 [16, 4096], replicated
Inputs may be any that keep to these rules, and one draw needn't show every extreme that they name: `doc_offset`: each row is a run of whole documents: the value is a token's index inside its document, 0 at a document's first position and rising by one along it. The first row holds a single document.
All inputs are finite; a program needn't handle non-finite values.
Results may differ from a plain program's by a relative error of at most 0.0013.
Values may be sent and summed in bfloat16 or wider, within the bound.
No kernel may reach another device: no remote copies, remote signals or barrier semaphores. Data moves between devices by JAX's collectives and lax.ppermute only.
A program may use at most 192 MiB of HBM per device.

v0:
```python
import math

import jax
import jax.numpy as jnp
from jax import lax
from jax.sharding import PartitionSpec as P


def from_behind(block, axis, distance):
    devices = range(lax.axis_size(axis))
    route = [(i - distance, i) for i in devices if i - distance in devices]
    return lax.ppermute(block, axis, route)


def shards(
    query_proj,
    key_proj,
    value_proj,
    doc_offset,
    short_taps,
    rate_scale,
    residue,
    skip_gain,
    out_grad,
):
    row_count, tok_len, channels = query_proj.shape
    ctx_count = lax.axis_size("ctx")
    seq_len = tok_len * ctx_count
    total_tokens = row_count * lax.axis_size("dp") * seq_len
    ctx_index = lax.axis_index("ctx")
    tap_count = short_taps.shape[1]
    rim_len = tap_count - 1
    block_len = math.gcd(tok_len, 16)
    sub_count = tok_len // block_len
    rims = from_behind(
        (
            query_proj[:, tok_len - rim_len :, :],
            key_proj[:, tok_len - rim_len :, :],
            value_proj[:, tok_len - rim_len :, :],
        ),
        "ctx",
        1,
    )
    sources = (query_proj, key_proj, value_proj)
    extended = jnp.stack(
        [
            jnp.concatenate([rims[branch_index], sources[branch_index]], axis=1)
            for branch_index in range(3)
        ],
        axis=0,
    )
    tap_masks = [(doc_offset >= tap_index)[None, :, :, None] for tap_index in range(tap_count)]

    def window(tap_index):
        piece = extended[:, :, rim_len - tap_index : rim_len - tap_index + tok_len, :].astype(
            jnp.float32
        )
        return jnp.where(tap_masks[tap_index], piece, 0.0)

    shorts = jnp.zeros((3, row_count, tok_len, channels), jnp.float32)
    for tap_index in range(tap_count):
        shorts = shorts + short_taps[:, tap_index][:, None, None, :] * window(tap_index)
    query_short = shorts[0]
    key_short = shorts[1]
    value_short = shorts[2]
    lam_log = -rate_scale / seq_len
    decay_step = jnp.exp(lam_log)
    norm_factor = jnp.sqrt(-jnp.expm1(2.0 * lam_log))
    mode_coef = residue * norm_factor
    slot_index = jnp.arange(block_len, dtype=jnp.int32)
    slot_float = slot_index.astype(jnp.float32)
    pow_zero = jnp.exp(slot_float[:, None, None] * lam_log[None, :, :])
    pow_one = pow_zero * decay_step[None]
    pow_end = pow_zero[::-1]
    pow_back = pow_one[::-1]
    filter_taps = jnp.sum(mode_coef[None] * pow_zero, axis=1)
    decay_block = jnp.exp(block_len * lam_log)
    offsets = doc_offset.reshape(row_count, sub_count, block_len)
    valid_in = (offsets > slot_index[None, None, :]).astype(jnp.float32)[..., None]
    last_doc = (slot_index[None, None, :] >= block_len - 1 - offsets[:, :, -1:]).astype(
        jnp.float32
    )[..., None]
    pass_sub = (offsets[:, :, -1] >= block_len).astype(jnp.float32)
    pass_dev = (doc_offset[:, -1] >= tok_len).astype(jnp.float32)
    zero_state = jnp.zeros((row_count,) + rate_scale.shape, jnp.float32)
    lag_masks = [(offsets >= lag)[..., None] for lag in range(block_len)]

    def intra_backward(grads):
        total = jnp.zeros_like(grads)
        for lag in range(block_len):
            masked = jnp.where(lag_masks[lag], grads, 0.0)
            padded = jnp.pad(masked, ((0, 0), (0, 0), (0, block_len), (0, 0)))
            total = total + filter_taps[lag] * padded[:, :, lag : lag + block_len, :]
        return total

    def sweep(initial, terms, reverse_flag):

        def advance(carried, inputs):
            passed, term = inputs
            return (term + decay_block * passed[:, None, None] * carried, carried)

        return lax.scan(advance, initial, (pass_sub.T, terms), reverse=reverse_flag)

    mixed = key_short * value_short
    mixed_blocks = mixed.reshape(row_count, sub_count, block_len, channels)
    intra_padded = jnp.pad(mixed_blocks, ((0, 0), (0, 0), (block_len, 0), (0, 0)))
    total = jnp.zeros_like(mixed_blocks)
    for intra_lag in range(block_len):
        shifted = intra_padded[:, :, block_len - intra_lag : 2 * block_len - intra_lag, :]
        total = total + filter_taps[intra_lag] * jnp.where(lag_masks[intra_lag], shifted, 0.0)
    sigma = jnp.swapaxes(
        jnp.sum(pow_end[None, None] * (mixed_blocks * last_doc)[:, :, :, None, :], axis=2), 0, 1
    )
    block_sum, _ = sweep(zero_state, sigma, False)
    first_source = (ctx_index * tok_len - doc_offset[:, 0]) // tok_len
    sums = lax.all_gather(block_sum[None], "ctx", axis=0, tiled=True)
    marks = lax.all_gather(pass_dev[None], "ctx", axis=0, tiled=True)
    source = jnp.arange(sums.shape[0], dtype=jnp.int32)
    weight = jnp.logical_and(
        source[:, None] < ctx_index, source[:, None] >= first_source[None, :]
    ).astype(jnp.float32)
    distance = jnp.maximum(ctx_index - 1 - source, 0).astype(jnp.float32)
    decay_span = jnp.exp((tok_len * distance)[:, None, None] * lam_log[None])
    states = jnp.sum(weight[:, :, None, None] * decay_span[:, None] * sums, axis=0)
    _, enters = sweep(states, sigma, False)
    cross = valid_in * jnp.sum(
        (mode_coef[None] * pow_one)[None, None] * jnp.swapaxes(enters, 0, 1)[:, :, None], axis=3
    )
    long_out = (total + cross).reshape(row_count, tok_len, channels)
    z_full = long_out + skip_gain * mixed
    mixed_out = (query_short * z_full).astype(jnp.bfloat16)
    grad_in = out_grad.astype(jnp.float32)
    z_grad = grad_in * query_short
    query_short_grad = grad_in * z_full
    grad_blocks = z_grad.reshape(row_count, sub_count, block_len, channels)
    inner_back = intra_backward(grad_blocks)
    gamma = jnp.swapaxes(
        jnp.sum(pow_zero[None, None] * (grad_blocks * valid_in)[:, :, :, None, :], axis=2), 0, 1
    )
    block_adj, _ = sweep(zero_state, gamma, True)
    device_ids = jnp.arange(ctx_count, dtype=jnp.int32)
    blocked = jnp.logical_and(device_ids[:, None] > ctx_index, marks < 0.5)
    last_source = jnp.min(jnp.where(blocked, device_ids[:, None], ctx_count - 1), axis=0)
    piece = lax.all_gather(block_adj[None], "ctx", axis=0, tiled=True)
    source = jnp.arange(piece.shape[0], dtype=jnp.int32)
    weight = jnp.logical_and(
        source[:, None] > ctx_index, source[:, None] <= last_source[None, :]
    ).astype(jnp.float32)
    distance = jnp.maximum(source - ctx_index - 1, 0).astype(jnp.float32)
    decay_span = jnp.exp((tok_len * distance)[:, None, None] * lam_log[None])
    adj_in = jnp.sum(weight[:, :, None, None] * decay_span[:, None] * piece, axis=0)
    _, exits = sweep(adj_in, gamma, True)
    cross_back = last_doc * jnp.sum(
        (mode_coef[None] * pow_back)[None, None] * jnp.swapaxes(exits, 0, 1)[:, :, None], axis=3
    )
    mixed_grad = (inner_back + cross_back).reshape(
        row_count, tok_len, channels
    ) + skip_gain * z_grad
    key_short_grad = mixed_grad * value_short
    value_short_grad = mixed_grad * key_short
    padded_mixed = jnp.pad(mixed_blocks, ((0, 0), (0, 0), (block_len, 0), (0, 0)))
    lag_sums = jnp.stack(
        [
            jnp.sum(
                grad_blocks
                * jnp.where(
                    lag_masks[lag],
                    padded_mixed[:, :, block_len - lag : 2 * block_len - lag, :],
                    0.0,
                ),
                axis=(0, 1, 2),
            )
            for lag in range(block_len)
        ],
        axis=0,
    )
    residue_term = norm_factor * (
        jnp.sum(lag_sums[:, None, :] * pow_zero, axis=0)
        + jnp.sum(decay_step[None, None] * gamma * enters, axis=(0, 1))
    )
    skip_term = jnp.sum(z_grad * mixed, axis=(0, 1))
    short_grads = jnp.stack([query_short_grad, key_short_grad, value_short_grad], axis=0)
    spread = jnp.zeros((3, row_count, tok_len + rim_len, channels), jnp.float32)
    tap_terms = []
    for tap_index in range(tap_count):
        masked = jnp.where(tap_masks[tap_index], short_grads, 0.0)
        padded = jnp.pad(masked, ((0, 0), (0, 0), (rim_len, rim_len), (0, 0)))
        spread = (
            spread
            + short_taps[:, tap_index][:, None, None, :]
            * padded[:, :, tap_index : tap_index + tok_len + rim_len, :]
        )
        tap_terms.append(jnp.sum(window(tap_index) * short_grads, axis=(1, 2)))
    heads = spread[:, :, :rim_len, :]
    owns = spread[:, :, rim_len:, :]
    incoming = from_behind((heads[0], heads[1], heads[2]), "ctx", -1)
    input_grads = [
        (
            owns[branch_index]
            + jnp.pad(incoming[branch_index], ((0, 0), (tok_len - rim_len, 0), (0, 0)))
        ).astype(jnp.bfloat16)
        for branch_index in range(3)
    ]
    taps_sum, skip_sum, residue_sum = lax.psum(
        (jnp.stack(tap_terms, axis=1), skip_term, residue_term), ("dp", "ctx")
    )
    scale = 1.0 / math.sqrt(total_tokens)
    return (
        mixed_out,
        input_grads[0],
        input_grads[1],
        input_grads[2],
        taps_sum * scale,
        skip_sum * scale,
        residue_sum * scale,
    )


def solution(mesh):
    in_specs = (
        P("dp", "ctx", None),
        P("dp", "ctx", None),
        P("dp", "ctx", None),
        P("dp", "ctx"),
        P(),
        P(),
        P(),
        P(),
        P("dp", "ctx", None),
    )
    out_specs = (
        P("dp", "ctx", None),
        P("dp", "ctx", None),
        P("dp", "ctx", None),
        P("dp", "ctx", None),
        P(),
        P(),
        P(),
    )
    return jax.shard_map(shards, mesh=mesh, in_specs=in_specs, out_specs=out_specs, check_vma=False)
```

profile of v0, /device:TPU:2, one launch (start us, length us, event | category | flops | bytes accessed | tf_op | source)
XLA Modules:
  0.0 801.4 jit_solution(16420344117029963431)
XLA Ops:
  8.8 3.5 collective-permute-start
  13.8 3.5 collective-permute-start.1
  18.7 3.2 collective-permute-start.2
  24.8 2.6 fusion.83
  36.6 9.8 %multiply_add_fusion = f32[3,1,128,4096]{3,2,1,0:T(8,128)S(1)} fusion(f32[3,4096]{1,0:T(4,128)S(1)} %copy-done.28, f32[3,4096]{1,0:T(4,128)S(1)} %copy-done.30, f32[3,4096]{1,0:T(4,128)S(1)} %get-tuple-element.545, f32[3,4096]{1,0:T(4,128)S(1)} %copy-done.26, f32[3,4096]{1,0:T(4,128)S(1)} %get-tuple-element.547, f32[3,4096]{1,0:T(4,128)S(1)} %get-tuple-element.548, ...), kind=kLoop, calls=%fused_computation.65 | loop fusion | flops 42467328 | bytes 28656512 | tf_op jit(solution)/shard_map/add | solution.py:62
  50.4 2.6 multiply_reduce_fusion.28
  53.1 4.1 multiply_reduce_fusion.22
  57.3 4.5 multiply_reduce_fusion.13
  61.8 3.3 stack.131
  65.2 7.9 fusion.19
  73.1 4.6 rev.6
  80.5 4.0 multiply_reduce_fusion.3
  84.5 24.5 %while.56 = (s32[]{:T(128)}, f32[1,16,4096]{2,1,0:T(8,128)}, f32[8,1,16,4096]{3,2,1,0:T(8,128)}, f32[8,1]{0,1:T(1,128)S(1)}, f32[16,4096]{1,0:T(8,128)}, /*index=5*/s32[]{:T(128)}, s32[]{:T(128)}) while((s32[]{:T(128)}, f32[1,16,4096]{2,1,0:T(8,128)}, f32[8,1,16,4096]{3,2,1,0:T(8,128)}, f32[8,1]{0,1:T(1,128)S(1)}, ...), condition=%wide.region_3.4_spmd.clone, body=%wide.region_2.3_spmd.clone.sunk | while | flops 262147 | bytes 1048683 | solution.py:102
  88.1 2.5 fusion.92
  91.2 2.5 fusion.92
  94.3 2.5 fusion.92
  97.3 2.5 fusion.92
  100.4 2.5 fusion.92
  103.5 2.5 fusion.92
  106.6 2.5 fusion.92
  112.0 4.0 multiply_reduce_fusion.1
  116.0 29.6 %while.57 = (s32[]{:T(128)}, f32[1,16,4096]{2,1,0:T(8,128)}, f32[8,1,16,4096]{3,2,1,0:T(8,128)}, f32[8,1]{0,1:T(1,128)}, f32[16,4096]{1,0:T(8,128)}, /*index=5*/s32[]{:T(128)}, s32[]{:T(128)}, s32[]{:T(128)}) while((s32[]{:T(128)}, f32[1,16,4096]{2,1,0:T(8,128)}, f32[8,1,16,4096]{3,2,1,0:T(8,128)}, f32[8,1]{0,1:T(1,128)}, ...), condition=%wide.region_11.12_spmd.clone, body=%wide.region_10.11_spmd.clone.sunk | while | flops 262148 | bytes 1048703 | solution.py:102
  120.9 2.5 fusion.93
  124.6 2.5 fusion.93
  128.3 2.5 fusion.93
  135.7 2.5 fusion.93
  152.0 74.3 %all-reduce.26 = f32[32]{0:T(128)} all-reduce(f32[32]{0:T(128)} %bitcast_dynamic-update-slice_fusion.9), channel_id=1, replica_groups=mesh['dp'=8,'ctx'=32] {'ctx'}, use_global_device_ids=true, to_apply=%add.26 | all-reduce | flops 32 | bytes 256
  229.8 79.4 %psum.22 = f32[4096]{0:T(1024)} all-reduce(f32[4096]{0:T(1024)S(1)} %copy-done.49), channel_id=1, replica_groups=mesh['dp'=8,'ctx'=32] {'dp','ctx'}, use_global_device_ids=true, to_apply=%region_25.26 | all-reduce | flops 4096 | bytes 32768 | tf_op jit(solution)/shard_map/psum | solution.py:204
  310.6 3.0 fusion.84
  313.7 4.7 reverse_multiply_fusion
  318.6 10.0 %broadcast_select_fusion.8 = (f32[1,8,16,4096]{3,2,1,0:T(8,128)}, f32[1,8,16,4096]{3,2,1,0:T(8,128)}, f32[1,8,16,4096]{3,2,1,0:T(8,128)}, f32[1,8,16,4096]{3,2,1...) fusion(pred[8,16]{1,0:T(8,128)(4,1)S(1)} %copy-done.54, ...), kind=kLoop, calls=%fused_computation.199 | loop fusion | flops 7340032 | bytes 31459072 | tf_op jit(solution)/shard_map/jit(_where)/select_n | solution.py:91
  328.6 8.7 %fusion.4 = (f32[16,4096]{1,0:T(8,128)}, f32[16,4096]{1,0:T(8,128)}) fusion(f32[32,16,4096]{2,1,0:T(8,128)} %all-gather.7.cloned.1.call-done, f32[32]{0:T(128)} %get-tuple-element.549, f32[32]{0:T(128)} %and_convert_fusion, f32[16,4096]{1,0:T(8,128)} %get-tuple-element.514, f32[32,16,4096]{2,1,0:T(8,128)} %all-gather.5.cloned.1.call-done, ...), kind=kLoop, calls=%fused_computation.34 | loop fusion | flops 16646144 | bytes 17564160 | tf_op jit(solution)/shard_map/reduce_sum | solution.py:151
  338.9 42.8 %while.54 = (s32[]{:T(128)}, f32[1,16,4096]{2,1,0:T(8,128)}, f32[8,1,16,4096]{3,2,1,0:T(8,128)}, f32[8,1,16,4096]{3,2,1,0:T(8,128)}, f32[8,1]{0,1:T(1,128)}, /*index=5*/f32[16,4096]{1,0:T(8,128)}, s32[]{:T(128)}) while((s32[]{:T(128)}, f32[1,16,4096]{2,1,0:T(8,128)}, f32[8,1,16,4096]{3,2,1,0:T(8,128)}, f32[8,1,16,4096]{3,2,1,0:T(8,128)}, ...), condition=%wide.region_6.7_spmd, body=%wide.region_5.6_spmd.sunk | while | flops 196610 | bytes 1573473 | solution.py:102
  341.7 2.5 fusion.90
  347.1 2.5 fusion.90
  352.4 2.5 fusion.90
  357.7 2.5 fusion.90
  363.1 2.5 fusion.90
  368.5 2.5 fusion.90
  373.8 2.5 fusion.90
  379.2 2.5 fusion.90
  381.7 3.3 fusion.73
  386.5 42.8 %while.55 = (s32[]{:T(128)}, f32[1,16,4096]{2,1,0:T(8,128)}, f32[8,1,16,4096]{3,2,1,0:T(8,128)}, f32[8,1,16,4096]{3,2,1,0:T(8,128)}, f32[8,1]{0,1:T(1,128)}, /*index=5*/f32[16,4096]{1,0:T(8,128)}, s32[]{:T(128)}, s32[]{:T(128)}) while((s32[]{:T(128)}, f32[1,16,4096]{2,1,0:T(8,128)}, f32[8,1,16,4096]{3,2,1,0:T(8,128)}, ...), condition=%wide.region_14.15_spmd, body=%wide.region_13.14_spmd.sunk | while | flops 196611 | bytes 1572985 | solution.py:102
  389.3 2.5 fusion.91
  394.6 2.5 fusion.91
  400.0 2.5 fusion.91
  405.3 2.5 fusion.91
  410.7 2.5 fusion.91
  416.1 2.5 fusion.91
  421.4 2.5 fusion.91
  426.8 2.5 fusion.91
  429.3 9.9 %multiply_reduce_fusion.2 = f32[8,16,4096]{2,1,0:T(8,128)S(1)} fusion(f32[8,16,4096]{2,1,0:T(8,128)} %bitcast.280, f32[16,16,4096]{2,1,0:T(8,128)} %get-tuple-element.486), kind=kLoop, calls=%fused_computation.16 | loop fusion | flops 16252928 | bytes 8388608 | tf_op jit(solution)/shard_map/reduce_sum | solution.py:126
  439.2 9.7 %multiply_reduce_fusion = f32[8,16,4096]{2,1,0:T(8,128)S(1)} fusion(f32[8,16,4096]{2,1,0:T(8,128)} %bitcast.282, f32[16,16,4096]{2,1,0:T(8,128)S(1)} %copy-done.9), kind=kLoop, calls=%fused_computation.14 | loop fusion | flops 16252928 | bytes 8388608 | tf_op jit(solution)/shard_map/reduce_sum | solution.py:153
  449.2 8.4 %fusion.76 = f32[1,8,16,4096]{3,2,1,0:T(8,128)} fusion(f32[8,16,4096]{2,1,0:T(8,128)S(1)} %multiply_reduce_fusion.2, f32[1,8,16,4096]{3,2,1,0:T(8,128)S(1)} %bitcast.275, f32[8,16]{1,0:T(8,128)} %get-tuple-element.518, f32[4096]{0:T(1024)S(1)} %bitcast.287, f32[4096]{0:T(1024)S(1)} %bitcast.289, f32[4096]{0:T(1024)S(1)} %bitcast.291, ...), kind=kLoop, calls=%fused_computation.172 | loop fusion | flops 25690112 | bytes 6556160 | tf_op jit(solution)/shard_map/add | solution.py:129
  457.8 8.1 %fusion.37 = f32[1,8,16,4096]{3,2,1,0:T(8,128)} fusion(f32[1,8,16,4096]{3,2,1,0:T(8,128)} %get-tuple-element.484, f32[1,8,16,4096]{3,2,1,0:T(8,128)S(1)} %copy-done.12, f32[1,8,16,4096]{3,2,1,0:T(8,128)S(1)} %copy-done.13, f32[1,8,16,4096]{3,2,1,0:T(8,128)S(1)} %copy-done.14, f32[1,8,16,4096]{3,2,1,0:T(8,128)S(1)} %copy-done.15, ...), kind=kLoop, calls=%fused_computation.120 | loop fusion | flops 17825792 | bytes 38011520 | tf_op jit(solution)/shard_map/add | solution.py:156
  466.0 8.3 %fusion.74 = (f32[1,1,128,4096]{3,2,1,0:T(8,128)S(1)}, f32[1,1,128,4096]{3,2,1,0:T(8,128)S(1)}, bf16[1,128,4096]{2,1,0:T(8,128)(2,1)}, f32[1,1,128,4096]{3,2,1,0:T(8,128)}) fusion(f32[3,1,128,4096]{3,2,1,0:T(8,128)} %copy-done.3, f32[1,128,4096]{2,1,0:T(8,128)S(1)} %copy-done.2, f32[4096]{0:T(1024)} %param.24, f32[1,8,16,4096]{3,2,1,0:T(8,128)} %fusion.37, ...), kind=kLoop, calls=%fused_computation.167 | loop fusion | flops 5242880 | bytes 23085056 | tf_op jit(solution)/shard_map/stack | solution.py:182
  474.3 11.1 %multiply_reduce_fusion.4 = (f32[3,4096]{1,0:T(4,128)S(1)}, f32[3,4096]{1,0:T(4,128)S(1)}, f32[3,4096]{1,0:T(4,128)S(1)}, f32[3,4096]{1,0:T(4,128)S(1)}, f32[3,4096]{1,0:T(4,128)S(1)}, /*index=5*/f32[3,4096]{1,0:T(4,128)S(1)}) fusion(pred[128]{0:T(512)(128)(4,1)S(1)} %copy-done.90, bf16[3,1,134,4096]{3,2,1,0:T(8,128)(2,1)S(1)} %pad_maximum_fusion.1, ...), kind=kLoop, calls=%fused_computation.58 | loop fusion | flops 40820736 | bytes 25461504 | tf_op jit(solution)/shard_map/reduce_sum | solution.py:193
  485.5 8.0 multiply_reduce_fusion.10
  493.6 9.9 %broadcast_select_fusion.2 = (f32[3,1,128,4096]{3,2,1,0:T(8,128)}, f32[3,1,128,4096]{3,2,1,0:T(8,128)}, f32[3,1,128,4096]{3,2,1,0:T(8,128)}, f32[3,1,128,4096]{3,2,1,0:T(8,128)}) fusion(pred[128]{0:T(512)(128)(4,1)S(1)} %copy-done.94, f32[1,1,128,4096]{3,2,1,0:T(8,128)S(1)} %get-tuple-element.451, f32[1,1,128,4096]{3,2,1,0:T(8,128)S(1)} %get-tuple-element.450, ...), kind=kLoop, calls=%fused_computation.96 | loop fusion | flops 9437184 | bytes 31457792 | tf_op jit(solution)/shard_map/jit(_where)/select_n | solution.py:186
  503.6 15.8 %fusion.12 = f32[3,1,134,4096]{3,2,1,0:T(8,128)S(1)} fusion(f32[3,1,128,4096]{3,2,1,0:T(8,128)} %get-tuple-element.463, f32[3,1,128,4096]{3,2,1,0:T(8,128)} %get-tuple-element.469, f32[3,1,128,4096]{3,2,1,0:T(8,128)} %get-tuple-element.468, f32[3,1,128,4096]{3,2,1,0:T(8,128)} %get-tuple-element.467, f32[3,1,128,4096]{3,2,1,0:T(8,128)} %get-tuple-element.466, ...), kind=kLoop, calls=%fused_computation.50 | loop fusion | flops 21405696 | bytes 50970624 | tf_op jit(solution)/shard_map/add | solution.py:189
  519.4 2.8 copy-done.8
  530.0 2.8 collective-permute-done.4
  534.7 5.0 fusion.68
  539.7 251.2 %all-reduce.30.cloned.1.call-done = (f32[3,7,4096]{2,0,1:T(4,128)}, f32[16,4096]{1,0:T(8,128)}) async-done(((f32[3,7,4096]{2,0,1:T(4,128)}, f32[16,4096]{1,0:T(8,128)}), (f32[3,7,4096]{2,0,1:T(4,128)}, f32[16,4096]{1,0:T(8,128)})) %all-reduce.30.cloned.1.call-update) | async-done | bytes 606224 | tf_op jit(solution)/shard_map/psum | solution.py:204
  (322 shorter events, 125.1 us)
Async XLA Ops:
  7.2 26.9 %copy-start.19 = (bf16[1,128,4096]{2,1,0:T(8,128)(2,1)S(1)}, bf16[1,128,4096]{2,1,0:T(8,128)(2,1)}, u32[]{:S(2)}) copy-start(bf16[1,128,4096]{2,1,0:T(8,128)(2,1)} %param.17) | copy-start | bytes 3145732
  7.2 321.4 %all-gather.5.cloned.1.call-start = ((), (), s32[]{:S(2)}) async-start(), calls=%async_computation | async-start | bytes 8650752 | tf_op jit(solution)/shard_map/all_gather | solution.py:116
  8.8 25.3 %collective-permute-start = (bf16[1,6,4096]{2,1,0:T(8,128)(2,1)}, bf16[1,6,4096]{2,1,0:T(8,128)(2,1)S(1)}, u32[]{:S(2)}, u32[]{:S(2)}) collective-permute-start(bf16[1,6,4096]{2,1,0:T(8,128)(2,1)} %slice.304), channel_id=1, source_target_pairs={{0,1},{1,2},{2,3},{3,4},{4,5},{5,6},{6,7},{7,8},{8,9},{9,10},{10,1... | collective-permute-start | bytes 147464 | tf_op jit(solution)/shard_map/ppermute | solution.py:12
  13.8 20.7 %collective-permute-start.1 = (bf16[1,6,4096]{2,1,0:T(8,128)(2,1)}, bf16[1,6,4096]{2,1,0:T(8,128)(2,1)S(1)}, u32[]{:S(2)}, u32[]{:S(2)}) collective-permute-start(bf16[1,6,4096]{2,1,0:T(8,128)(2,1)} %slice.305), channel_id=1, source_target_pairs={{0,1},{1,2},{2,3},{3,4},{4,5},{5,6},{6,7},{7,8},{8,9},{9,10},{10,1... | collective-permute-start | bytes 147464 | tf_op jit(solution)/shard_map/ppermute | solution.py:12
  18.7 16.0 %collective-permute-start.2 = (bf16[1,6,4096]{2,1,0:T(8,128)(2,1)}, bf16[1,6,4096]{2,1,0:T(8,128)(2,1)S(1)}, u32[]{:S(2)}, u32[]{:S(2)}) collective-permute-start(bf16[1,6,4096]{2,1,0:T(8,128)(2,1)} %slice.306), channel_id=1, source_target_pairs={{0,1},{1,2},{2,3},{3,4},{4,5},{5,6},{6,7},{7,8},{8,9},{9,10},{10,1... | collective-permute-start | bytes 147464 | tf_op jit(solution)/shard_map/ppermute | solution.py:12
  23.1 13.0 %copy-start.86 = (pred[128]{0:T(512)(128)(4,1)}, pred[128]{0:T(512)(128)(4,1)S(1)}, u32[]{:S(2)}) copy-start(pred[128]{0:T(512)(128)(4,1)S(1)} %get-tuple-element.536) | copy-start | bytes 388
  23.1 13.0 %copy-start.89 = (pred[128]{0:T(512)(128)(4,1)}, pred[128]{0:T(512)(128)(4,1)S(1)}, u32[]{:S(2)}) copy-start(pred[128]{0:T(512)(128)(4,1)S(1)} %get-tuple-element.537) | copy-start | bytes 388
  23.1 13.0 %copy-start.91 = (pred[128]{0:T(512)(128)(4,1)}, pred[128]{0:T(512)(128)(4,1)S(1)}, u32[]{:S(2)}) copy-start(pred[128]{0:T(512)(128)(4,1)S(1)} %get-tuple-element.538) | copy-start | bytes 388
  31.4 15.2 %copy-start.83 = (pred[8,16]{1,0:T(8,128)(4,1)}, pred[8,16]{1,0:T(8,128)(4,1)S(1)}, u32[]{:S(2)}) copy-start(pred[8,16]{1,0:T(8,128)(4,1)S(1)} %get-tuple-element.519) | copy-start | bytes 388
  46.7 10.6 %copy-start.4 = (f32[1,1,128,4096]{3,2,1,0:T(8,128)}, f32[1,1,128,4096]{3,2,1,0:T(8,128)S(1)}, u32[]{:S(2)}) copy-start(f32[1,1,128,4096]{3,2,1,0:T(8,128)S(1)} %slice_multiply_fusion) | copy-start | bytes 6291460
  50.3 6.9 copy-start
  84.5 24.6 %copy-start.52 = (f32[8,16]{1,0:T(8,128)S(1)}, f32[8,16]{1,0:T(8,128)}, u32[]{:S(2)}) copy-start(f32[8,16]{1,0:T(8,128)} %get-tuple-element.518) | copy-start | bytes 1540
  109.1 219.5 %all-gather.7.cloned.1.call-start = ((), (), s32[]{:S(2)}) async-start(), calls=%async_computation.1 | async-start | bytes 8650752 | tf_op jit(solution)/shard_map/all_gather | solution.py:144
  116.0 113.8 %copy-start.49 = (f32[4096]{0:T(1024)S(1)}, f32[4096]{0:T(1024)}, u32[]{:S(2)}) copy-start(f32[4096]{0:T(1024)} %get-tuple-element.396) | copy-start | bytes 49156
  145.6 645.3 %all-reduce.30.cloned.1.call-start = ((), (), s32[]{:S(2)}) async-start(), calls=%async_computation.2 | async-start | bytes 1441792 | tf_op jit(solution)/shard_map/psum | solution.py:204
  313.6 4.9 copy-start.1
  313.6 4.9 copy-start.54
  429.3 9.9 %copy-start.9 = (f32[16,16,4096]{2,1,0:T(8,128)S(1)}, f32[16,16,4096]{2,1,0:T(8,128)}, u32[]{:S(2)}) copy-start(f32[16,16,4096]{2,1,0:T(8,128)} %reverse_multiply_fusion) | copy-start | bytes 12582916
  429.3 19.7 %copy-start.37 = (f32[1,4096]{1,0:T(1,128)S(1)}, f32[1,4096]{1,0:T(1,128)}, u32[]{:S(2)}) copy-start(f32[1,4096]{1,0:T(1,128)} %get-tuple-element.501) | copy-start | bytes 49156
  429.3 28.3 %copy-start.16 = (f32[1,8,16,4096]{3,2,1,0:T(8,128)S(1)}, f32[1,8,16,4096]{3,2,1,0:T(8,128)}, u32[]{:S(2)}) copy-start(f32[1,8,16,4096]{3,2,1,0:T(8,128)} %get-tuple-element.476) | copy-start | bytes 6291460
  429.3 28.3 %copy-start.17 = (f32[1,8,16,4096]{3,2,1,0:T(8,128)S(1)}, f32[1,8,16,4096]{3,2,1,0:T(8,128)}, u32[]{:S(2)}) copy-start(f32[1,8,16,4096]{3,2,1,0:T(8,128)} %get-tuple-element.477) | copy-start | bytes 6291460
  439.1 9.9 %copy-start.5 = (f32[1,1,128,4096]{3,2,1,0:T(8,128)S(1)}, f32[1,1,128,4096]{3,2,1,0:T(8,128)}, u32[]{:S(2)}) copy-start(f32[1,1,128,4096]{3,2,1,0:T(8,128)} %copy-done.4) | copy-start | bytes 6291460
  439.1 9.9 %copy-start.34 = (f32[1,4096]{1,0:T(1,128)S(1)}, f32[1,4096]{1,0:T(1,128)}, u32[]{:S(2)}) copy-start(f32[1,4096]{1,0:T(1,128)} %get-tuple-element.498) | copy-start | bytes 49156
  439.2 9.9 %copy-start.35 = (f32[1,4096]{1,0:T(1,128)S(1)}, f32[1,4096]{1,0:T(1,128)}, u32[]{:S(2)}) copy-start(f32[1,4096]{1,0:T(1,128)} %get-tuple-element.499) | copy-start | bytes 49156
  439.2 9.9 %copy-start.36 = (f32[1,4096]{1,0:T(1,128)S(1)}, f32[1,4096]{1,0:T(1,128)}, u32[]{:S(2)}) copy-start(f32[1,4096]{1,0:T(1,128)} %get-tuple-element.500) | copy-start | bytes 49156
  439.2 9.9 %copy-start.55 = (pred[8,16]{1,0:T(8,128)(4,1)S(1)}, pred[8,16]{1,0:T(8,128)(4,1)}, u32[]{:S(2)}) copy-start(pred[8,16]{1,0:T(8,128)(4,1)} %get-tuple-element.520) | copy-start | bytes 388
  439.2 9.9 %copy-start.58 = (pred[8,16]{1,0:T(8,128)(4,1)S(1)}, pred[8,16]{1,0:T(8,128)(4,1)}, u32[]{:S(2)}) copy-start(pred[8,16]{1,0:T(8,128)(4,1)} %get-tuple-element.521) | copy-start | bytes 388
  439.2 18.4 %copy-start.13 = (f32[1,8,16,4096]{3,2,1,0:T(8,128)S(1)}, f32[1,8,16,4096]{3,2,1,0:T(8,128)}, u32[]{:S(2)}) copy-start(f32[1,8,16,4096]{3,2,1,0:T(8,128)} %get-tuple-element.473) | copy-start | bytes 6291460
  439.2 18.4 %copy-start.14 = (f32[1,8,16,4096]{3,2,1,0:T(8,128)S(1)}, f32[1,8,16,4096]{3,2,1,0:T(8,128)}, u32[]{:S(2)}) copy-start(f32[1,8,16,4096]{3,2,1,0:T(8,128)} %get-tuple-element.474) | copy-start | bytes 6291460
  439.2 18.4 %copy-start.15 = (f32[1,8,16,4096]{3,2,1,0:T(8,128)S(1)}, f32[1,8,16,4096]{3,2,1,0:T(8,128)}, u32[]{:S(2)}) copy-start(f32[1,8,16,4096]{3,2,1,0:T(8,128)} %get-tuple-element.475) | copy-start | bytes 6291460
  449.0 8.6 %copy-start.2 = (f32[1,128,4096]{2,1,0:T(8,128)S(1)}, f32[1,128,4096]{2,1,0:T(8,128)}, u32[]{:S(2)}) copy-start(f32[1,128,4096]{2,1,0:T(8,128)} %copy-done) | copy-start | bytes 6291460
  449.1 8.6 %copy-start.11 = (f32[1,8,16,4096]{3,2,1,0:T(8,128)S(1)}, f32[1,8,16,4096]{3,2,1,0:T(8,128)}, u32[]{:S(2)}) copy-start(f32[1,8,16,4096]{3,2,1,0:T(8,128)} %get-tuple-element.471) | copy-start | bytes 6291460
  449.1 8.6 %copy-start.12 = (f32[1,8,16,4096]{3,2,1,0:T(8,128)S(1)}, f32[1,8,16,4096]{3,2,1,0:T(8,128)}, u32[]{:S(2)}) copy-start(f32[1,8,16,4096]{3,2,1,0:T(8,128)} %get-tuple-element.472) | copy-start | bytes 6291460
  449.1 8.6 %copy-start.38 = (f32[1,4096]{1,0:T(1,128)S(1)}, f32[1,4096]{1,0:T(1,128)}, u32[]{:S(2)}) copy-start(f32[1,4096]{1,0:T(1,128)} %get-tuple-element.502) | copy-start | bytes 49156
  449.1 8.6 %copy-start.39 = (f32[1,4096]{1,0:T(1,128)S(1)}, f32[1,4096]{1,0:T(1,128)}, u32[]{:S(2)}) copy-start(f32[1,4096]{1,0:T(1,128)} %get-tuple-element.503) | copy-start | bytes 49156
  449.1 8.6 %copy-start.40 = (f32[1,4096]{1,0:T(1,128)S(1)}, f32[1,4096]{1,0:T(1,128)}, u32[]{:S(2)}) copy-start(f32[1,4096]{1,0:T(1,128)} %get-tuple-element.504) | copy-start | bytes 49156
  449.1 8.6 %copy-start.41 = (f32[1,4096]{1,0:T(1,128)S(1)}, f32[1,4096]{1,0:T(1,128)}, u32[]{:S(2)}) copy-start(f32[1,4096]{1,0:T(1,128)} %get-tuple-element.505) | copy-start | bytes 49156
  449.1 8.6 %copy-start.42 = (f32[1,4096]{1,0:T(1,128)S(1)}, f32[1,4096]{1,0:T(1,128)}, u32[]{:S(2)}) copy-start(f32[1,4096]{1,0:T(1,128)} %get-tuple-element.506) | copy-start | bytes 49156
  449.1 8.6 %copy-start.43 = (f32[1,4096]{1,0:T(1,128)S(1)}, f32[1,4096]{1,0:T(1,128)}, u32[]{:S(2)}) copy-start(f32[1,4096]{1,0:T(1,128)} %get-tuple-element.507) | copy-start | bytes 49156
  449.1 8.6 %copy-start.44 = (f32[1,4096]{1,0:T(1,128)S(1)}, f32[1,4096]{1,0:T(1,128)}, u32[]{:S(2)}) copy-start(f32[1,4096]{1,0:T(1,128)} %get-tuple-element.508) | copy-start | bytes 49156
  449.1 8.6 %copy-start.45 = (f32[1,4096]{1,0:T(1,128)S(1)}, f32[1,4096]{1,0:T(1,128)}, u32[]{:S(2)}) copy-start(f32[1,4096]{1,0:T(1,128)} %get-tuple-element.509) | copy-start | bytes 49156
  449.2 8.6 %copy-start.46 = (f32[1,4096]{1,0:T(1,128)S(1)}, f32[1,4096]{1,0:T(1,128)}, u32[]{:S(2)}) copy-start(f32[1,4096]{1,0:T(1,128)} %get-tuple-element.510) | copy-start | bytes 49156
  449.2 8.6 %copy-start.47 = (f32[1,4096]{1,0:T(1,128)S(1)}, f32[1,4096]{1,0:T(1,128)}, u32[]{:S(2)}) copy-start(f32[1,4096]{1,0:T(1,128)} %get-tuple-element.511) | copy-start | bytes 49156
  449.2 8.6 %copy-start.48 = (f32[1,4096]{1,0:T(1,128)S(1)}, f32[1,4096]{1,0:T(1,128)}, u32[]{:S(2)}) copy-start(f32[1,4096]{1,0:T(1,128)} %get-tuple-element.512) | copy-start | bytes 49156
  449.2 8.6 %copy-start.51 = (f32[8,16]{1,0:T(8,128)S(1)}, f32[8,16]{1,0:T(8,128)}, u32[]{:S(2)}) copy-start(f32[8,16]{1,0:T(8,128)} %get-tuple-element.551) | copy-start | bytes 1540
  449.2 8.6 %copy-start.85 = (pred[8,16]{1,0:T(8,128)(4,1)S(1)}, pred[8,16]{1,0:T(8,128)(4,1)}, u32[]{:S(2)}) copy-start(pred[8,16]{1,0:T(8,128)(4,1)} %get-tuple-element.517) | copy-start | bytes 388
  465.9 8.4 %copy-start.90 = (pred[128]{0:T(512)(128)(4,1)S(1)}, pred[128]{0:T(512)(128)(4,1)}, u32[]{:S(2)}) copy-start(pred[128]{0:T(512)(128)(4,1)} %copy-done.89) | copy-start | bytes 388
  465.9 8.4 %copy-start.92 = (pred[128]{0:T(512)(128)(4,1)S(1)}, pred[128]{0:T(512)(128)(4,1)}, u32[]{:S(2)}) copy-start(pred[128]{0:T(512)(128)(4,1)} %copy-done.91) | copy-start | bytes 388
  465.9 8.4 %copy-start.94 = (pred[128]{0:T(512)(128)(4,1)S(1)}, pred[128]{0:T(512)(128)(4,1)}, u32[]{:S(2)}) copy-start(pred[128]{0:T(512)(128)(4,1)} %get-tuple-element.539) | copy-start | bytes 388
  465.9 8.4 %copy-start.96 = (pred[128]{0:T(512)(128)(4,1)S(1)}, pred[128]{0:T(512)(128)(4,1)}, u32[]{:S(2)}) copy-start(pred[128]{0:T(512)(128)(4,1)} %get-tuple-element.540) | copy-start | bytes 388
  465.9 8.4 %copy-start.98 = (pred[128]{0:T(512)(128)(4,1)S(1)}, pred[128]{0:T(512)(128)(4,1)}, u32[]{:S(2)}) copy-start(pred[128]{0:T(512)(128)(4,1)} %get-tuple-element.541) | copy-start | bytes 388
  465.9 8.4 %copy-start.100 = (pred[128]{0:T(512)(128)(4,1)S(1)}, pred[128]{0:T(512)(128)(4,1)}, u32[]{:S(2)}) copy-start(pred[128]{0:T(512)(128)(4,1)} %get-tuple-element.542) | copy-start | bytes 388
  474.3 11.2 %copy-start.7 = (f32[1,1,128,4096]{3,2,1,0:T(8,128)S(1)}, f32[1,1,128,4096]{3,2,1,0:T(8,128)}, u32[]{:S(2)}) copy-start(f32[1,1,128,4096]{3,2,1,0:T(8,128)} %get-tuple-element.470) | copy-start | bytes 6291460
  474.3 11.2 %copy-start.88 = (pred[128]{0:T(512)(128)(4,1)S(1)}, pred[128]{0:T(512)(128)(4,1)}, u32[]{:S(2)}) copy-start(pred[128]{0:T(512)(128)(4,1)} %copy-done.86) | copy-start | bytes 388
  493.5 10.0 %copy-start.27 = (f32[3,4096]{1,0:T(4,128)S(1)}, f32[3,4096]{1,0:T(4,128)}, u32[]{:S(2)}) copy-start(f32[3,4096]{1,0:T(4,128)} %get-tuple-element.546) | copy-start | bytes 147460
  493.5 10.0 %copy-start.29 = (f32[3,4096]{1,0:T(4,128)S(1)}, f32[3,4096]{1,0:T(4,128)}, u32[]{:S(2)}) copy-start(f32[3,4096]{1,0:T(4,128)} %get-tuple-element.543) | copy-start | bytes 147460
  493.5 10.0 %copy-start.31 = (f32[3,4096]{1,0:T(4,128)S(1)}, f32[3,4096]{1,0:T(4,128)}, u32[]{:S(2)}) copy-start(f32[3,4096]{1,0:T(4,128)} %get-tuple-element.544) | copy-start | bytes 147460
  493.5 10.0 %copy-start.33 = (f32[3,1,4096]{2,0,1:T(4,128)S(1)}, f32[3,1,4096]{2,0,1:T(4,128)}, u32[]{:S(2)}) copy-start(f32[3,1,4096]{2,0,1:T(4,128)} %copy-done.32) | copy-start | bytes 147460
  503.5 22.6 %copy-start.22 = (f32[16,4096]{1,0:T(8,128)S(1)}, f32[16,4096]{1,0:T(8,128)}, u32[]{:S(2)}) copy-start(f32[16,4096]{1,0:T(8,128)} %get-tuple-element.488) | copy-start | bytes 786436
  503.5 22.6 %copy-start.23 = (f32[16,4096]{1,0:T(8,128)S(1)}, f32[16,4096]{1,0:T(8,128)}, u32[]{:S(2)}) copy-start(f32[16,4096]{1,0:T(8,128)} %fusion.73) | copy-start | bytes 786436
  503.6 22.6 %copy-start.24 = (f32[16,4096]{1,0:T(8,128)S(1)}, f32[16,4096]{1,0:T(8,128)}, u32[]{:S(2)}) copy-start(f32[16,4096]{1,0:T(8,128)} %param.22) | copy-start | bytes 786436
  522.2 7.8 collective-permute-start.3
  523.5 9.3 %collective-permute-start.4 = (f32[1,6,4096]{2,1,0:T(8,128)S(1)}, f32[1,6,4096]{2,1,0:T(8,128)S(1)}, u32[]{:S(2)}, u32[]{:S(2)}) collective-permute-start(f32[1,6,4096]{2,1,0:T(8,128)S(1)} %get-tuple-element.459), channel_id=1, source_target_pairs={{1,0},{2,1},{3,2},{4,3},{5,4},{6,5},{7,6},{8,7},{9,8},{10,9},{11,1... | collective-permute-start | bytes 294920 | tf_op jit(solution)/shard_map/ppermute | solution.py:12
  524.8 9.9 %collective-permute-start.5 = (f32[1,6,4096]{2,1,0:T(8,128)S(1)}, f32[1,6,4096]{2,1,0:T(8,128)S(1)}, u32[]{:S(2)}, u32[]{:S(2)}) collective-permute-start(f32[1,6,4096]{2,1,0:T(8,128)S(1)} %get-tuple-element.458), channel_id=1, source_target_pairs={{1,0},{2,1},{3,2},{4,3},{5,4},{6,5},{7,6},{8,7},{9,8},{10,9},{11,1... | collective-permute-start | bytes 294920 | tf_op jit(solution)/shard_map/ppermute | solution.py:12
  (47 other events, 156.6 us)
Sparse Core Ops, SparseCore 0:
  109.2 100.9 all-gather.4
  213.4 95.3 all-gather.6
  528.1 262.7 all-reduce.29
where the time goes:
time: 807 us; the launch traced here: 801 us
  other arithmetic  260 us (32%)
  waiting for transfers between devices  258 us (32%)
  blocking collectives  154 us (19%)
  local copies, waits for them, and re-layouts  98.6 us (12%)
  between operations  16.8 us (2%)
  starting transfers between devices  14.1 us (2%)
    psum x1, waiting for transfers between devices, shards(): lax.psum((jnp.stack(tap_terms, axis=1), skip_term, residue_term), ('dp',...  251 us
    add x32, other arithmetic, advance(): return (term + decay_block * passed[:, None, None] * carried, carried)  79.6 us
    psum x1, blocking collectives, shards(): lax.psum((jnp.stack(tap_terms, axis=1), skip_term, residue_term), ('dp',...  79.4 us
    unnamed x1, blocking collectives  74.3 us
    dynamic_slice x32, local copies, waits for them, and re-layouts, sweep(): return lax.scan(advance, initial, (pass_sub.T, terms), reverse=reverse_flag)  33.3 us
    dynamic_update_slice x16, local copies, waits for them, and re-layouts, sweep(): return lax.scan(advance, initial, (pass_sub.T, terms), reverse=reverse_flag)  26.7 us
    reduce_sum x2, other arithmetic, shards(): tap_terms.append(jnp.sum(window(tap_index) * short_grads, axis=(1, 2)))  19.1 us
  transfers between devices with their start and end apart: 9, of which 4 were waited for; matrix products, arithmetic and copies ran while one was open for 11% of the time, Pallas kernels for 0%

commit v1 on v0

--- a/solution.py
+++ b/solution.py
@@ -10,6 +10,34 @@
     devices = range(lax.axis_size(axis))
     route = [(i - distance, i) for i in devices if i - distance in devices]
     return lax.ppermute(block, axis, route)
+
+
+def device_scan(flags, values, step_log, direction):
+    count = lax.axis_size("ctx")
+    gates = flags[:, None, None]
+    sums = values
+    distance = 1
+    while distance < count:
+        route = [(i, i + distance * direction) for i in range(count) if 0 <= i + distance * direction < count]
+        got_gates, got_sums = lax.ppermute((gates, sums), "ctx", route)
+        sums = sums + gates * jnp.exp(distance * step_log) * got_sums
+        gates = gates * got_gates
+        distance *= 2
+    route = [(i, i + direction) for i in range(count) if 0 <= i + direction < count]
+    return lax.ppermute(sums, "ctx", route)
+
+
+def butterfly_sum(value, axes):
+    for axis in axes:
+        count = lax.axis_size(axis)
+        if count & (count - 1):
+            value = lax.psum(value, axis)
+            continue
+        step = 1
+        while step < count:
+            value = value + lax.ppermute(value, axis, [(i, i ^ step) for i in range(count)])
+            step *= 2
+    return value
 
 
 def shards(
@@ -94,12 +122,14 @@
         return total
 
     def sweep(initial, terms, reverse_flag):
-
-        def advance(carried, inputs):
-            passed, term = inputs
-            return (term + decay_block * passed[:, None, None] * carried, carried)
-
-        return lax.scan(advance, initial, (pass_sub.T, terms), reverse=reverse_flag)
+        carried = initial
+        visited = [None] * sub_count
+        order = range(sub_count - 1, -1, -1) if reverse_flag else range(sub_count)
+        for sub_index in order:
+            visited[sub_index] = carried
+            passed = pass_sub[:, sub_index][:, None, None]
+            carried = terms[sub_index] + decay_block * passed * carried
+        return carried, jnp.stack(visited)
 
     mixed = key_short * value_short
     mixed_blocks = mixed.reshape(row_count, sub_count, block_len, channels)
@@ -112,16 +142,7 @@
         jnp.sum(pow_end[None, None] * (mixed_blocks * last_doc)[:, :, :, None, :], axis=2), 0, 1
     )
     block_sum, _ = sweep(zero_state, sigma, False)
-    first_source = (ctx_index * tok_len - doc_offset[:, 0]) // tok_len
-    sums = lax.all_gather(block_sum[None], "ctx", axis=0, tiled=True)
-    marks = lax.all_gather(pass_dev[None], "ctx", axis=0, tiled=True)
-    source = jnp.arange(sums.shape[0], dtype=jnp.int32)
-    weight = jnp.logical_and(
-        source[:, None] < ctx_index, source[:, None] >= first_source[None, :]
-    ).astype(jnp.float32)
-    distance = jnp.maximum(ctx_index - 1 - source, 0).astype(jnp.float32)
-    decay_span = jnp.exp((tok_len * distance)[:, None, None] * lam_log[None])
-    states = jnp.sum(weight[:, :, None, None] * decay_span[:, None] * sums, axis=0)
+    states = device_scan(pass_dev, block_sum, tok_len * lam_log, 1)
     _, enters = sweep(states, sigma, False)
     cross = valid_in * jnp.sum(
         (mode_coef[None] * pow_one)[None, None] * jnp.swapaxes(enters, 0, 1)[:, :, None], axis=3
@@ -138,17 +159,7 @@
         jnp.sum(pow_zero[None, None] * (grad_blocks * valid_in)[:, :, :, None, :], axis=2), 0, 1
     )
     block_adj, _ = sweep(zero_state, gamma, True)
-    device_ids = jnp.arange(ctx_count, dtype=jnp.int32)
-    blocked = jnp.logical_and(device_ids[:, None] > ctx_index, marks < 0.5)
-    last_source = jnp.min(jnp.where(blocked, device_ids[:, None], ctx_count - 1), axis=0)
-    piece = lax.all_gather(block_adj[None], "ctx", axis=0, tiled=True)
-    source = jnp.arange(piece.shape[0], dtype=jnp.int32)
-    weight = jnp.logical_and(
-        source[:, None] > ctx_index, source[:, None] <= last_source[None, :]
-    ).astype(jnp.float32)
-    distance = jnp.maximum(source - ctx_index - 1, 0).astype(jnp.float32)
-    decay_span = jnp.exp((tok_len * distance)[:, None, None] * lam_log[None])
-    adj_in = jnp.sum(weight[:, :, None, None] * decay_span[:, None] * piece, axis=0)
+    adj_in = device_scan(pass_dev, block_adj, tok_len * lam_log, -1)
     _, exits = sweep(adj_in, gamma, True)
     cross_back = last_doc * jnp.sum(
         (mode_coef[None] * pow_back)[None, None] * jnp.swapaxes(exits, 0, 1)[:, :, None], axis=3
@@ -201,9 +212,12 @@
         ).astype(jnp.bfloat16)
         for branch_index in range(3)
     ]
-    taps_sum, skip_sum, residue_sum = lax.psum(
-        (jnp.stack(tap_terms, axis=1), skip_term, residue_term), ("dp", "ctx")
-    )
+    tap_stack = jnp.stack(tap_terms, axis=1)
+    flat = jnp.concatenate([tap_stack.reshape(-1), skip_term, residue_term.reshape(-1)])
+    flat = butterfly_sum(flat, ("ctx", "dp"))
+    taps_sum = flat[: tap_stack.size].reshape(tap_stack.shape)
+    skip_sum = flat[tap_stack.size : tap_stack.size + skip_term.size]
+    residue_sum = flat[tap_stack.size + skip_term.size :].reshape(residue_term.shape)
     scale = 1.0 / math.sqrt(total_tokens)
     return (
         mixed_out,

time: 807 us -> 476 us (0.59)
  blocking collectives: 154 us -> 0 us
  waiting for transfers between devices: 258 us -> 134 us
  starting transfers between devices: 14.1 us -> 138 us
  other arithmetic: 260 us -> 166 us
  local copies, waits for them, and re-layouts: 98.6 us -> 24.7 us
    psum x1 -> x0, waiting for transfers between devices: 251 us -> none  [shards(): lax.psum((jnp.stack(tap_terms, axis=1), skip_term, residue_term), ('dp',...]
    ppermute x0 -> x28, waiting for transfers between devices: none -> 134 us  [the longest x8 80 us: butterfly_sum(): lax.ppermute(value, axis, [(i, i ^ step) for i in range(count)])]
    ppermute x0 -> x28, starting transfers between devices: none -> 124 us  [the longest x18 84.4 us: device_scan(): got_gates, got_sums = lax.ppermute((gates, sums), 'ctx', route)]
    psum x1 -> x0, blocking collectives: 79.4 us -> none  [shards(): lax.psum((jnp.stack(tap_terms, axis=1), skip_term, residue_term), ('dp',...]
    unnamed x1 -> x0, blocking collectives: 74.3 us -> none
    add x32 -> x19, other arithmetic: 79.6 us -> 8.66 us  [the longest x1 5.4 us: sweep(): carried = terms[sub_index] + decay_block * passed * carried]
    dynamic_slice x32 -> x0, local copies, waits for them, and re-layouts: 33.3 us -> none  [sweep(): return lax.scan(advance, initial, (pass_sub.T, terms), reverse=reverse_flag)]
    dynamic_update_slice x16 -> x0, local copies, waits for them, and re-layouts: 26.7 us -> none  [sweep(): return lax.scan(advance, initial, (pass_sub.T, terms), reverse=reverse_flag)]
  transfers between devices with their start and end apart: 9 -> 34, of which waited for: 4 -> 16; matrix products, arithmetic and copies ran while one was open for 11% -> 14% of each run, Pallas kernels for 0% -> 0%
where the time goes in v1:
time: 476 us; the launch traced here: 472 us
  other arithmetic  166 us (35%)
  starting transfers between devices  138 us (29%)
  waiting for transfers between devices  134 us (28%)
  local copies, waits for them, and re-layouts  24.7 us (5%)
  between operations  8.8 us (2%)
    ppermute x18, starting transfers between devices, device_scan(): got_gates, got_sums = lax.ppermute((gates, sums), 'ctx', route)  84.4 us
    ppermute x8, waiting for transfers between devices, butterfly_sum(): lax.ppermute(value, axis, [(i, i ^ step) for i in range(count)])  80 us
    ppermute x18, waiting for transfers between devices, device_scan(): got_gates, got_sums = lax.ppermute((gates, sums), 'ctx', route)  52.9 us
    ppermute x8, starting transfers between devices, butterfly_sum(): lax.ppermute(value, axis, [(i, i ^ step) for i in range(count)])  32.2 us
    reduce_sum x2, other arithmetic, shards(): tap_terms.append(jnp.sum(window(tap_index) * short_grads, axis=(1, 2)))  19.7 us
    unnamed x14, other arithmetic  18.6 us
    ppermute x6, starting transfers between devices, from_behind(): return lax.ppermute(block, axis, route)  14 us
    add x1, other arithmetic, shards(): spread + short_taps[:, tap_index][:, None, None, :] * padded[:, :, tap_in...  12.3 us
  transfers between devices with their start and end apart: 34, of which 16 were waited for; matrix products, arithmetic and copies ran while one was open for 14% of the time, Pallas kernels for 0%

profile of v1, /device:TPU:2, one launch (start us, length us, event | category | flops | bytes accessed | tf_op | source)
XLA Modules:
  0.0 471.6 jit_solution(17733566232858467229)
XLA Ops:
  1.6 3.5 collective-permute-start.2
  5.9 3.5 collective-permute-start.1
  10.3 3.2 collective-permute-start
  17.9 2.7 fusion.131
  21.6 2.2 fusion.121
  26.4 9.9 %multiply_add_fusion = f32[3,1,128,4096]{3,2,1,0:T(8,128)S(1)} fusion(f32[3,4096]{1,0:T(4,128)S(1)} %get-tuple-element.153, f32[3,4096]{1,0:T(4,128)S(1)} %get-tuple-element.154, f32[3,4096]{1,0:T(4,128)S(1)} %get-tuple-element.155, f32[3,4096]{1,0:T(4,128)S(1)} %get-tuple-element.156, f32[3,4096]{1,0:T(4,128)S(1)} %get-tuple-element.157, ...), kind=kLoop, calls=%fused_computation.47 | loop fusion | flops 42467328 | bytes 28656512 | tf_op jit(solution)/shard_map/add | solution.py:90
  36.6 1.7 copy-done.24
  38.3 1.9 broadcast_select_fusion.7
  40.2 2.1 multiply_reduce_fusion.30
  42.3 4.1 multiply_reduce_fusion.23
  46.5 4.5 multiply_reduce_fusion.14
  51.0 3.3 stack.205
  54.3 8.0 %fusion.13 = (f32[16,16,4096]{2,1,0:T(8,128)}, f32[16,16,4096]{2,1,0:T(8,128)}, f32[16,4096]{1,0:T(8,128)}, f32[16,4096]{1,0:T(8,128)}, f32[16,16,4096]{2,1,0:T(8,128)}) fusion(f32[16,4096]{1,0:T(8,128)} %get-tuple-element.118, f32[16,4096]{1,0:T(8,128)} %get-tuple-element.119, f32[16]{0:T(128)} %iota_convert_fusion, f32[16,4096]{1,0:T(8,128)} %get-tuple-element.120, ...), kind=kLoop, calls=%fused_computation.74 | loop fusion | flops 7208960 | bytes 14155840 | tf_op jit(solution)/shard_map/mul | solution.py:101
  62.3 4.7 rev.6
  67.0 2.0 broadcast_multiply_fusion.2
  69.8 2.7 multiply_reduce_fusion.3
  72.7 5.4 %fusion.73 = f32[1,16,4096]{2,1,0:T(8,128)S(1)} fusion(f32[1,8,16,4096]{3,2,1,0:T(8,128)S(1)} %bitcast.498, f32[]{:T(128)} %bitcast.45, f32[]{:T(128)} %bitcast.43, f32[]{:T(128)} %bitcast.41, f32[]{:T(128)} %bitcast.39, f32[]{:T(128)} %bitcast.37, f32[]{:T(128)} %bitcast.35, f32[]{:T(128)} %bitcast.33, f32[]{:T(128)} %bitcast.31, f32[16,4096]{1,0:T(8,128)S(1)} %copy-done), kind=kLoop, calls=%fused_computation.201 | loop fusion | flops 1703936 | bytes 2621472 | tf_op jit(solution)/shard_map/add | solution.py:131
  78.1 3.5 collective-permute-start.3
  84.1 7.1 %collective-permute-start.4 = (f32[1,1,1]{2,1,0:T(1,128)}, f32[1,1,1]{2,1,0:T(1,128)}, u32[]{:S(2)}, u32[]{:S(2)}) collective-permute-start(f32[1,1,1]{2,1,0:T(1,128)} %bitcast.49), channel_id=1, source_target_pairs={{0,1},{1,2},{2,3},{3,4},{4,5},{5,6},{6,7},{7,8},{8,9},{9,10},{10,1... | collective-permute-start | bytes 20 | tf_op jit(solution)/shard_map/ppermute | solution.py:22
  93.8 8.6 %collective-permute-start.6 = (f32[1,1,1]{2,1,0:T(1,128)}, f32[1,1,1]{2,1,0:T(1,128)}, u32[]{:S(2)}, u32[]{:S(2)}) collective-permute-start(f32[1,1,1]{2,1,0:T(1,128)} %mul.1479), channel_id=1, source_target_pairs={{0,2},{1,3},{2,4},{3,5},{4,6},{5,7},{6,8},{7,9},{8,10},{9,11},{10,... | collective-permute-start | bytes 20 | tf_op jit(solution)/shard_map/ppermute | solution.py:22
  105.1 7.5 %collective-permute-start.8 = (f32[1,1,1]{2,1,0:T(1,128)}, f32[1,1,1]{2,1,0:T(1,128)}, u32[]{:S(2)}, u32[]{:S(2)}) collective-permute-start(f32[1,1,1]{2,1,0:T(1,128)} %mul.1487), channel_id=1, source_target_pairs={{0,4},{1,5},{2,6},{3,7},{4,8},{5,9},{6,10},{7,11},{8,12},{9,13},{1... | collective-permute-start | bytes 20 | tf_op jit(solution)/shard_map/ppermute | solution.py:22
  115.2 9.0 %collective-permute-start.10 = (f32[1,1,1]{2,1,0:T(1,128)}, f32[1,1,1]{2,1,0:T(1,128)}, u32[]{:S(2)}, u32[]{:S(2)}) collective-permute-start(f32[1,1,1]{2,1,0:T(1,128)} %mul.1495), channel_id=1, source_target_pairs={{0,8},{1,9},{2,10},{3,11},{4,12},{5,13},{6,14},{7,15},{8,16},{9,17... | collective-permute-start | bytes 20 | tf_op jit(solution)/shard_map/ppermute | solution.py:22
  125.7 7.4 %collective-permute-start.5 = (f32[1,16,4096]{2,1,0:T(8,128)S(1)}, f32[1,16,4096]{2,1,0:T(8,128)S(1)}, u32[]{:S(2)}, u32[]{:S(2)}) collective-permute-start(f32[1,16,4096]{2,1,0:T(8,128)S(1)} %fusion.103), channel_id=1, source_target_pairs={{0,2},{1,3},{2,4},{3,5},{4,6},{5,7},{6,8},{7,9},{8,10},{9,11},{10,... | collective-permute-start | bytes 786440 | tf_op jit(solution)/shard_map/ppermute | solution.py:22
  133.2 9.1 %broadcast_select_fusion.8 = (f32[1,8,16,4096]{3,2,1,0:T(8,128)S(1)}, f32[1,8,16,4096]{3,2,1,0:T(8,128)S(1)}, f32[1,8,16,4096]{3,2,1,0:T(8,128)}, f32[1,8,16,409...) fusion(pred[8,16]{1,0:T(8,128)(4,1)S(1)} %get-tuple-element.124, ...), kind=kLoop, calls=%fused_computation.179 | loop fusion | flops 7340032 | bytes 31459072 | tf_op jit(solution)/shard_map/jit(_where)/select_n | solution.py:119
  142.4 5.1 %collective-permute-start.7 = (f32[1,16,4096]{2,1,0:T(8,128)S(1)}, f32[1,16,4096]{2,1,0:T(8,128)S(1)}, u32[]{:S(2)}, u32[]{:S(2)}) collective-permute-start(f32[1,16,4096]{2,1,0:T(8,128)S(1)} %fusion.102), channel_id=1, source_target_pairs={{0,4},{1,5},{2,6},{3,7},{4,8},{5,9},{6,10},{7,11},{8,12},{9,13},{1... | collective-permute-start | bytes 786440 | tf_op jit(solution)/shard_map/ppermute | solution.py:22
  148.0 6.2 %collective-permute-done.7 = f32[1,16,4096]{2,1,0:T(8,128)S(1)} collective-permute-done((f32[1,16,4096]{2,1,0:T(8,128)S(1)}, f32[1,16,4096]{2,1,0:T(8,128)S(1)}, u32[]{:S(2)}, u32[]{:S(2)}) %collective-permute-start.7) | collective-permute-done | bytes 262176 | tf_op jit(solution)/shard_map/ppermute | solution.py:22
  154.2 8.3 %collective-permute-start.9 = (f32[1,16,4096]{2,1,0:T(8,128)S(1)}, f32[1,16,4096]{2,1,0:T(8,128)S(1)}, u32[]{:S(2)}, u32[]{:S(2)}) collective-permute-start(f32[1,16,4096]{2,1,0:T(8,128)S(1)} %fusion.101), channel_id=1, source_target_pairs={{0,8},{1,9},{2,10},{3,11},{4,12},{5,13},{6,14},{7,15},{8,16},{9,17... | collective-permute-start | bytes 786440 | tf_op jit(solution)/shard_map/ppermute | solution.py:22
  162.8 3.8 collective-permute-done.9
  166.7 15.9 %collective-permute-start.11 = (f32[1,16,4096]{2,1,0:T(8,128)S(1)}, f32[1,16,4096]{2,1,0:T(8,128)S(1)}, u32[]{:S(2)}, u32[]{:S(2)}) collective-permute-start(f32[1,16,4096]{2,1,0:T(8,128)S(1)} %fusion.100), channel_id=1, source_target_pairs={{0,16},{1,17},{2,18},{3,19},{4,20},{5,21},{6,22},{7,23},{8,24},{9,... | collective-permute-start | bytes 786440 | tf_op jit(solution)/shard_map/ppermute | solution.py:22
  183.4 3.0 collective-permute-done.11
  186.6 5.8 %collective-permute-start.12 = (f32[1,16,4096]{2,1,0:T(8,128)S(1)}, f32[1,16,4096]{2,1,0:T(8,128)S(1)}, u32[]{:S(2)}, u32[]{:S(2)}) collective-permute-start(f32[1,16,4096]{2,1,0:T(8,128)S(1)} %fusion.99), channel_id=1, source_target_pairs={{0,1},{1,2},{2,3},{3,4},{4,5},{5,6},{6,7},{7,8},{8,9},{9,10},{10,1... | collective-permute-start | bytes 786440 | tf_op jit(solution)/shard_map/ppermute | solution.py:27
  192.4 2.8 multiply_reduce_fusion.1
  202.2 5.4 %multiply_bitcast_fusion = (f32[2,32,8,128]{3,2,1,0:T(8,128)S(1)}, f32[1,16,4096]{2,1,0:T(8,128)S(1)}) fusion(f32[16,4096]{1,0:T(8,128)S(1)} %copy-done.32, f32[16,4096]{1,0:T(8,128)S(1)} %multiply_reduce_fusion.13, f32[16,4096]{1,0:T(8,128)S(1)} %copy-done, f32[]{:T(128)} %bitcast.31, f32[1,8,16,4096]{3,2,1,0:T(8,128)S(1)} %bitcast.489, f32[]{:T(128)} %bitcast.33, ...), kind=kLoop, calls=%fused_computation.294 | loop fusion | flops 1966080 | bytes 3407904
  209.0 7.3 %collective-permute-done.13 = f32[1,16,4096]{2,1,0:T(8,128)S(1)} collective-permute-done((f32[1,16,4096]{2,1,0:T(8,128)S(1)}, f32[1,16,4096]{2,1,0:T(8,128)S(1)}, u32[]{:S(2)}, u32[]{:S(2)}) %collective-permute-start.13) | collective-permute-done | bytes 262176 | tf_op jit(solution)/shard_map/ppermute | solution.py:22
  217.7 8.4 %collective-permute-done.15 = f32[1,16,4096]{2,1,0:T(8,128)S(1)} collective-permute-done((f32[1,16,4096]{2,1,0:T(8,128)S(1)}, f32[1,16,4096]{2,1,0:T(8,128)S(1)}, u32[]{:S(2)}, u32[]{:S(2)}) %collective-permute-start.15) | collective-permute-done | bytes 262176 | tf_op jit(solution)/shard_map/ppermute | solution.py:22
  226.3 1.6 collective-permute-start.17
  227.9 7.3 %collective-permute-done.17 = f32[1,16,4096]{2,1,0:T(8,128)S(1)} collective-permute-done((f32[1,16,4096]{2,1,0:T(8,128)S(1)}, f32[1,16,4096]{2,1,0:T(8,128)S(1)}, u32[]{:S(2)}, u32[]{:S(2)}) %collective-permute-start.17) | collective-permute-done | bytes 262176 | tf_op jit(solution)/shard_map/ppermute | solution.py:22
  236.5 13.9 %collective-permute-done.19 = f32[1,16,4096]{2,1,0:T(8,128)S(1)} collective-permute-done((f32[1,16,4096]{2,1,0:T(8,128)S(1)}, f32[1,16,4096]{2,1,0:T(8,128)S(1)}, u32[]{:S(2)}, u32[]{:S(2)}) %collective-permute-start.19) | collective-permute-done | bytes 262176 | tf_op jit(solution)/shard_map/ppermute | solution.py:22
  251.9 8.5 %multiply_reduce_fusion.2 = f32[8,16,4096]{2,1,0:T(8,128)S(1)} fusion(f32[8,16,4096]{2,1,0:T(8,128)S(1)} %bitcast.507, f32[16,16,4096]{2,1,0:T(8,128)S(1)} %copy-done.14), kind=kLoop, calls=%fused_computation.2 | loop fusion | flops 16252928 | bytes 8388608 | tf_op jit(solution)/shard_map/reduce_sum | solution.py:147
  260.5 3.0 collective-permute-done.21
  265.0 7.2 %fusion.69 = f32[1,8,16,4096]{3,2,1,0:T(8,128)} fusion(f32[8,16,4096]{2,1,0:T(8,128)S(1)} %multiply_reduce_fusion.2, f32[1,8,16,4096]{3,2,1,0:T(8,128)S(1)} %bitcast.488, f32[8,16]{1,0:T(8,128)S(1)} %get-tuple-element.122, f32[4096]{0:T(1024)S(1)} %bitcast.514, f32[4096]{0:T(1024)S(1)} %bitcast.516, f32[4096]{0:T(1024)S(1)} %bitcast.518, ...), kind=kLoop, calls=%fused_computation.151 | loop fusion | flops 25690112 | bytes 6556160 | tf_op jit(solution)/shard_map/add | solution.py:150
  273.0 5.2 %bitcast_dynamic-update-slice_fusion.7 = (f32[8,1,16,4096]{3,2,1,0:T(8,128)S(1)}, f32[1,16,4096]{2,1,0:T(8,128)S(1)}, f32[1,16,4096]{2,1,0:T(8,128)S(1)}, f32[1,16,4096]{2,1,0:T(8,128)S(1)}) fusion(f32[1,8,16,4096]{3,2,1,0:T(8,128)S(1)} %bitcast.490, f32[]{:T(128)} %bitcast.43, f32[]{:T(128)} %bitcast.41, f32[16,4096]{1,0:T(8,128)S(1)} %copy-done, ...), kind=kLoop, calls=%fused_computation.209 | loop fusion | flops 1507327 | bytes 3407900
  280.9 8.4 %multiply_reduce_fusion = f32[8,16,4096]{2,1,0:T(8,128)S(1)} fusion(f32[8,16,4096]{2,1,0:T(8,128)S(1)} %bitcast.506, f32[16,16,4096]{2,1,0:T(8,128)S(1)} %reverse_multiply_fusion), kind=kLoop, calls=%fused_computation | loop fusion | flops 16252928 | bytes 8388608 | tf_op jit(solution)/shard_map/reduce_sum | solution.py:164
  289.3 7.5 %fusion.31 = f32[1,8,16,4096]{3,2,1,0:T(8,128)} fusion(f32[1,8,16,4096]{3,2,1,0:T(8,128)} %get-tuple-element.87, f32[1,8,16,4096]{3,2,1,0:T(8,128)S(1)} %get-tuple-element.75, f32[1,8,16,4096]{3,2,1,0:T(8,128)S(1)} %copy-done.16, f32[1,8,16,4096]{3,2,1,0:T(8,128)S(1)} %copy-done.17, f32[1,8,16,4096]{3,2,1,0:T(8,128)S(1)} %copy-done.18, ...), kind=kLoop, calls=%fused_computation.102 | loop fusion | flops 17825792 | bytes 38011520 | tf_op jit(solution)/shard_map/add | solution.py:167
  296.8 8.2 %fusion.67 = (f32[1,1,128,4096]{3,2,1,0:T(8,128)S(1)}, f32[1,1,128,4096]{3,2,1,0:T(8,128)S(1)}, bf16[1,128,4096]{2,1,0:T(8,128)(2,1)}, f32[1,1,128,4096]{3,2,1,0:T(8,128)}) fusion(f32[3,1,128,4096]{3,2,1,0:T(8,128)} %copy-done.3, f32[1,128,4096]{2,1,0:T(8,128)S(1)} %copy-done.2, f32[4096]{0:T(1024)} %param.16, f32[1,8,16,4096]{3,2,1,0:T(8,128)} %fusion.31, ...), kind=kLoop, calls=%fused_computation.146 | loop fusion | flops 5242880 | bytes 23085056 | tf_op jit(solution)/shard_map/stack | solution.py:193
  305.1 11.8 %multiply_reduce_fusion.4 = (f32[3,4096]{1,0:T(4,128)S(1)}, f32[3,4096]{1,0:T(4,128)S(1)}, f32[3,4096]{1,0:T(4,128)S(1)}, f32[3,4096]{1,0:T(4,128)S(1)}, f32[3,4096]{1,0:T(4,128)S(1)}, /*index=5*/f32[3,4096]{1,0:T(4,128)S(1)}) fusion(pred[128]{0:T(512)(128)(4,1)S(1)} %copy-done.80, bf16[3,1,134,4096]{3,2,1,0:T(8,128)(2,1)S(1)} %pad_maximum_fusion.1, ...), kind=kLoop, calls=%fused_computation.40 | loop fusion | flops 40820736 | bytes 25461504 | tf_op jit(solution)/shard_map/reduce_sum | solution.py:204
  316.9 8.0 %multiply_reduce_fusion.10 = (f32[3,4096]{1,0:T(4,128)S(1)}, f32[3,1,128,4096]{3,2,1,0:T(8,128)}, f32[3,1,128,4096]{3,2,1,0:T(8,128)}, f32[3,1,128,4096]{3,2,1,0:T(8,128)}) fusion(pred[128]{0:T(512)(128)(4,1)S(1)} %copy-done.78, bf16[3,1,134,4096]{3,2,1,0:T(8,128)(2,1)S(1)} %pad_maximum_fusion.1, f32[1,1,128,4096]{3,2,1,0:T(8,128)S(1)} %get-tuple-element.54, ...), kind=kLoop, calls=%fused_computation.46 | loop fusion | flops 14143488 | bytes 28361088 | tf_op jit(solution)/shard_map/reduce_sum | solution.py:204
  326.0 3.5 collective-permute-start.26
  329.5 8.2 %collective-permute-done.26 = f32[155648]{0:T(1024)S(1)} collective-permute-done((f32[155648]{0:T(1024)S(1)}, f32[155648]{0:T(1024)S(1)}, u32[]{:S(2)}, u32[]{:S(2)}) %collective-permute-start.26) | collective-permute-done | bytes 622624 | tf_op jit(solution)/shard_map/ppermute | solution.py:38
  337.8 7.7 %collective-permute-start.27 = (f32[155648]{0:T(1024)S(1)}, f32[155648]{0:T(1024)S(1)}, u32[]{:S(2)}, u32[]{:S(2)}) collective-permute-start(f32[155648]{0:T(1024)S(1)} %fusion.122), channel_id=1, source_target_pairs={{0,2},{1,3},{2,0},{3,1},{4,6},{5,7},{6,4},{7,5},{8,10},{9,11},{10,... | collective-permute-start | bytes 1867784 | tf_op jit(solution)/shard_map/ppermute | solution.py:38
  345.5 8.2 %collective-permute-done.27 = f32[155648]{0:T(1024)S(1)} collective-permute-done((f32[155648]{0:T(1024)S(1)}, f32[155648]{0:T(1024)S(1)}, u32[]{:S(2)}, u32[]{:S(2)}) %collective-permute-start.27) | collective-permute-done | bytes 622624 | tf_op jit(solution)/shard_map/ppermute | solution.py:38
  353.8 5.3 %collective-permute-start.28 = (f32[155648]{0:T(1024)S(1)}, f32[155648]{0:T(1024)S(1)}, u32[]{:S(2)}, u32[]{:S(2)}) collective-permute-start(f32[155648]{0:T(1024)S(1)} %add.471), channel_id=1, source_target_pairs={{0,4},{1,5},{2,6},{3,7},{4,0},{5,1},{6,2},{7,3},{8,12},{9,13},{10,... | collective-permute-start | bytes 1867784 | tf_op jit(solution)/shard_map/ppermute | solution.py:38
  359.1 18.3 %collective-permute-done.28 = f32[155648]{0:T(1024)S(1)} collective-permute-done((f32[155648]{0:T(1024)S(1)}, f32[155648]{0:T(1024)S(1)}, u32[]{:S(2)}, u32[]{:S(2)}) %collective-permute-start.28) | collective-permute-done | bytes 622624 | tf_op jit(solution)/shard_map/ppermute | solution.py:38
  377.5 8.4 %collective-permute-start.29 = (f32[155648]{0:T(1024)S(1)}, f32[155648]{0:T(1024)S(1)}, u32[]{:S(2)}, u32[]{:S(2)}) collective-permute-start(f32[155648]{0:T(1024)S(1)} %add.472), channel_id=1, source_target_pairs={{0,8},{1,9},{2,10},{3,11},{4,12},{5,13},{6,14},{7,15},{8,0},{9,1},... | collective-permute-start | bytes 1867784 | tf_op jit(solution)/shard_map/ppermute | solution.py:38
  385.8 13.9 %collective-permute-done.29 = f32[155648]{0:T(1024)S(1)} collective-permute-done((f32[155648]{0:T(1024)S(1)}, f32[155648]{0:T(1024)S(1)}, u32[]{:S(2)}, u32[]{:S(2)}) %collective-permute-start.29) | collective-permute-done | bytes 622624 | tf_op jit(solution)/shard_map/ppermute | solution.py:38
  399.8 4.5 collective-permute-start.30
  404.3 9.8 %broadcast_select_fusion.2 = (f32[3,1,128,4096]{3,2,1,0:T(8,128)}, f32[3,1,128,4096]{3,2,1,0:T(8,128)}, f32[3,1,128,4096]{3,2,1,0:T(8,128)}, f32[3,1,128,4096]{3,2,1,0:T(8,128)}) fusion(pred[128]{0:T(512)(128)(4,1)S(1)} %copy-done.84, f32[1,1,128,4096]{3,2,1,0:T(8,128)S(1)} %copy-done.10, f32[1,1,128,4096]{3,2,1,0:T(8,128)S(1)} %copy-done.8, ...), kind=kLoop, calls=%fused_computation.78 | loop fusion | flops 9437184 | bytes 31457792 | tf_op jit(solution)/shard_map/jit(_where)/select_n | solution.py:197
  414.2 6.6 %collective-permute-done.30 = f32[155648]{0:T(1024)S(1)} collective-permute-done((f32[155648]{0:T(1024)S(1)}, f32[155648]{0:T(1024)S(1)}, u32[]{:S(2)}, u32[]{:S(2)}) %collective-permute-start.30) | collective-permute-done | bytes 622624 | tf_op jit(solution)/shard_map/ppermute | solution.py:38
  421.7 12.3 %fusion.6 = f32[3,1,134,4096]{3,2,1,0:T(8,128)S(1)} fusion(f32[3,1,128,4096]{3,2,1,0:T(8,128)S(1)} %bitcast.495, f32[3,1,128,4096]{3,2,1,0:T(8,128)} %get-tuple-element.72, f32[3,1,128,4096]{3,2,1,0:T(8,128)} %get-tuple-element.71, f32[3,1,128,4096]{3,2,1,0:T(8,128)} %get-tuple-element.70, f32[3,1,128,4096]{3,2,1,0:T(8,128)} %get-tuple-element.69, ...), kind=kLoop, calls=%fused_computation.32 | loop fusion | flops 21405696 | bytes 50970624 | tf_op jit(solution)/shard_map/add | solution.py:200
  434.0 1.3 add.475
  439.9 12.0 %collective-permute-done.32 = f32[155648]{0:T(1024)S(1)} collective-permute-done((f32[155648]{0:T(1024)S(1)}, f32[155648]{0:T(1024)S(1)}, u32[]{:S(2)}, u32[]{:S(2)}) %collective-permute-start.32) | collective-permute-done | bytes 622624 | tf_op jit(solution)/shard_map/ppermute | solution.py:38
  451.9 2.2 collective-permute-start.33
  454.1 2.0 fusion.62
  456.2 12.9 %collective-permute-done.33 = f32[155648]{0:T(1024)S(1)} collective-permute-done((f32[155648]{0:T(1024)S(1)}, f32[155648]{0:T(1024)S(1)}, u32[]{:S(2)}, u32[]{:S(2)}) %collective-permute-start.33) | collective-permute-done | bytes 622624 | tf_op jit(solution)/shard_map/ppermute | solution.py:38
  (310 shorter events, 45.5 us)
Async XLA Ops:
  0.6 23.8 %copy-start.28 = (bf16[1,128,4096]{2,1,0:T(8,128)(2,1)S(1)}, bf16[1,128,4096]{2,1,0:T(8,128)(2,1)}, u32[]{:S(2)}) copy-start(bf16[1,128,4096]{2,1,0:T(8,128)(2,1)} %param.9) | copy-start | bytes 3145732
  1.6 23.4 %collective-permute-start.2 = (bf16[1,6,4096]{2,1,0:T(8,128)(2,1)S(1)}, bf16[1,6,4096]{2,1,0:T(8,128)(2,1)S(1)}, u32[]{:S(2)}, u32[]{:S(2)}) collective-permute-start(bf16[1,6,4096]{2,1,0:T(8,128)(2,1)S(1)} %slice.444), channel_id=1, source_target_pairs={{0,1},{1,2},{2,3},{3,4},{4,5},{5,6},{6,7},{7,8},{8,9},{9,10},{10,1... | collective-permute-start | bytes 147464 | tf_op jit(solution)/shard_map/ppermute | solution.py:12
  5.9 18.8 %collective-permute-start.1 = (bf16[1,6,4096]{2,1,0:T(8,128)(2,1)S(1)}, bf16[1,6,4096]{2,1,0:T(8,128)(2,1)S(1)}, u32[]{:S(2)}, u32[]{:S(2)}) collective-permute-start(bf16[1,6,4096]{2,1,0:T(8,128)(2,1)S(1)} %slice.443), channel_id=1, source_target_pairs={{0,1},{1,2},{2,3},{3,4},{4,5},{5,6},{6,7},{7,8},{8,9},{9,10},{10,1... | collective-permute-start | bytes 147464 | tf_op jit(solution)/shard_map/ppermute | solution.py:12
  10.3 14.1 %collective-permute-start = (bf16[1,6,4096]{2,1,0:T(8,128)(2,1)S(1)}, bf16[1,6,4096]{2,1,0:T(8,128)(2,1)S(1)}, u32[]{:S(2)}, u32[]{:S(2)}) collective-permute-start(bf16[1,6,4096]{2,1,0:T(8,128)(2,1)S(1)} %slice.442), channel_id=1, source_target_pairs={{0,1},{1,2},{2,3},{3,4},{4,5},{5,6},{6,7},{7,8},{8,9},{9,10},{10,1... | collective-permute-start | bytes 147464 | tf_op jit(solution)/shard_map/ppermute | solution.py:12
  14.2 26.0 %copy-start.77 = (pred[128]{0:T(512)(128)(4,1)}, pred[128]{0:T(512)(128)(4,1)S(1)}, u32[]{:S(2)}) copy-start(pred[128]{0:T(512)(128)(4,1)S(1)} %get-tuple-element.146) | copy-start | bytes 388
  21.2 25.2 %copy-start.39 = (pred[8,16]{1,0:T(8,128)(4,1)}, pred[8,16]{1,0:T(8,128)(4,1)S(1)}, u32[]{:S(2)}) copy-start(pred[8,16]{1,0:T(8,128)(4,1)S(1)} %get-tuple-element.126) | copy-start | bytes 388
  21.3 25.2 %copy-start.41 = (pred[8,16]{1,0:T(8,128)(4,1)}, pred[8,16]{1,0:T(8,128)(4,1)S(1)}, u32[]{:S(2)}) copy-start(pred[8,16]{1,0:T(8,128)(4,1)S(1)} %get-tuple-element.127) | copy-start | bytes 388
  21.3 25.2 %copy-start.44 = (pred[8,16]{1,0:T(8,128)(4,1)}, pred[8,16]{1,0:T(8,128)(4,1)S(1)}, u32[]{:S(2)}) copy-start(pred[8,16]{1,0:T(8,128)(4,1)S(1)} %get-tuple-element.128) | copy-start | bytes 388
  21.3 25.2 %copy-start.47 = (pred[8,16]{1,0:T(8,128)(4,1)}, pred[8,16]{1,0:T(8,128)(4,1)S(1)}, u32[]{:S(2)}) copy-start(pred[8,16]{1,0:T(8,128)(4,1)S(1)} %get-tuple-element.129) | copy-start | bytes 388
  21.3 25.2 %copy-start.50 = (pred[8,16]{1,0:T(8,128)(4,1)}, pred[8,16]{1,0:T(8,128)(4,1)S(1)}, u32[]{:S(2)}) copy-start(pred[8,16]{1,0:T(8,128)(4,1)S(1)} %get-tuple-element.130) | copy-start | bytes 388
  21.3 25.2 %copy-start.53 = (pred[8,16]{1,0:T(8,128)(4,1)}, pred[8,16]{1,0:T(8,128)(4,1)S(1)}, u32[]{:S(2)}) copy-start(pred[8,16]{1,0:T(8,128)(4,1)S(1)} %get-tuple-element.131) | copy-start | bytes 388
  21.3 25.2 %copy-start.74 = (pred[8,16]{1,0:T(8,128)(4,1)}, pred[8,16]{1,0:T(8,128)(4,1)S(1)}, u32[]{:S(2)}) copy-start(pred[8,16]{1,0:T(8,128)(4,1)S(1)} %get-tuple-element.123) | copy-start | bytes 388
  72.5 60.5 %copy-start.2 = (f32[1,128,4096]{2,1,0:T(8,128)S(1)}, f32[1,128,4096]{2,1,0:T(8,128)}, u32[]{:S(2)}) copy-start(f32[1,128,4096]{2,1,0:T(8,128)} %copy-done.1) | copy-start | bytes 6291460
  72.5 60.5 %copy-start.40 = (pred[8,16]{1,0:T(8,128)(4,1)S(1)}, pred[8,16]{1,0:T(8,128)(4,1)}, u32[]{:S(2)}) copy-start(pred[8,16]{1,0:T(8,128)(4,1)} %copy-done.39) | copy-start | bytes 388
  72.5 60.5 %copy-start.42 = (pred[8,16]{1,0:T(8,128)(4,1)S(1)}, pred[8,16]{1,0:T(8,128)(4,1)}, u32[]{:S(2)}) copy-start(pred[8,16]{1,0:T(8,128)(4,1)} %copy-done.41) | copy-start | bytes 388
  72.5 60.5 %copy-start.45 = (pred[8,16]{1,0:T(8,128)(4,1)S(1)}, pred[8,16]{1,0:T(8,128)(4,1)}, u32[]{:S(2)}) copy-start(pred[8,16]{1,0:T(8,128)(4,1)} %copy-done.44) | copy-start | bytes 388
  72.6 60.5 %copy-start.48 = (pred[8,16]{1,0:T(8,128)(4,1)S(1)}, pred[8,16]{1,0:T(8,128)(4,1)}, u32[]{:S(2)}) copy-start(pred[8,16]{1,0:T(8,128)(4,1)} %copy-done.47) | copy-start | bytes 388
  72.6 60.5 %copy-start.51 = (pred[8,16]{1,0:T(8,128)(4,1)S(1)}, pred[8,16]{1,0:T(8,128)(4,1)}, u32[]{:S(2)}) copy-start(pred[8,16]{1,0:T(8,128)(4,1)} %copy-done.50) | copy-start | bytes 388
  72.6 60.5 %copy-start.54 = (pred[8,16]{1,0:T(8,128)(4,1)S(1)}, pred[8,16]{1,0:T(8,128)(4,1)}, u32[]{:S(2)}) copy-start(pred[8,16]{1,0:T(8,128)(4,1)} %copy-done.53) | copy-start | bytes 388
  72.6 60.5 %copy-start.57 = (pred[8,16]{1,0:T(8,128)(4,1)S(1)}, pred[8,16]{1,0:T(8,128)(4,1)}, u32[]{:S(2)}) copy-start(pred[8,16]{1,0:T(8,128)(4,1)} %copy-done.56) | copy-start | bytes 388
  72.6 60.5 %copy-start.60 = (pred[8,16]{1,0:T(8,128)(4,1)S(1)}, pred[8,16]{1,0:T(8,128)(4,1)}, u32[]{:S(2)}) copy-start(pred[8,16]{1,0:T(8,128)(4,1)} %copy-done.59) | copy-start | bytes 388
  72.6 60.5 %copy-start.63 = (pred[8,16]{1,0:T(8,128)(4,1)S(1)}, pred[8,16]{1,0:T(8,128)(4,1)}, u32[]{:S(2)}) copy-start(pred[8,16]{1,0:T(8,128)(4,1)} %copy-done.62) | copy-start | bytes 388
  72.6 60.5 %copy-start.66 = (pred[8,16]{1,0:T(8,128)(4,1)S(1)}, pred[8,16]{1,0:T(8,128)(4,1)}, u32[]{:S(2)}) copy-start(pred[8,16]{1,0:T(8,128)(4,1)} %copy-done.65) | copy-start | bytes 388
  72.6 60.5 %copy-start.69 = (pred[8,16]{1,0:T(8,128)(4,1)S(1)}, pred[8,16]{1,0:T(8,128)(4,1)}, u32[]{:S(2)}) copy-start(pred[8,16]{1,0:T(8,128)(4,1)} %copy-done.68) | copy-start | bytes 388
  72.6 60.5 %copy-start.72 = (pred[8,16]{1,0:T(8,128)(4,1)S(1)}, pred[8,16]{1,0:T(8,128)(4,1)}, u32[]{:S(2)}) copy-start(pred[8,16]{1,0:T(8,128)(4,1)} %copy-done.71) | copy-start | bytes 388
  78.1 47.5 %collective-permute-start.3 = (f32[1,16,4096]{2,1,0:T(8,128)S(1)}, f32[1,16,4096]{2,1,0:T(8,128)S(1)}, u32[]{:S(2)}, u32[]{:S(2)}) collective-permute-start(f32[1,16,4096]{2,1,0:T(8,128)S(1)} %fusion.73), channel_id=1, source_target_pairs={{0,1},{1,2},{2,3},{3,4},{4,5},{5,6},{6,7},{7,8},{8,9},{9,10},{10,1... | collective-permute-start | bytes 786440 | tf_op jit(solution)/shard_map/ppermute | solution.py:22
  82.8 8.4 %collective-permute-start.14 = (f32[1,1,1]{2,1,0:T(1,128)}, f32[1,1,1]{2,1,0:T(1,128)}, u32[]{:S(2)}, u32[]{:S(2)}) collective-permute-start(f32[1,1,1]{2,1,0:T(1,128)} %bitcast.49), channel_id=1, source_target_pairs={{1,0},{2,1},{3,2},{4,3},{5,4},{6,5},{7,6},{8,7},{9,8},{10,9},{11,1... | collective-permute-start | bytes 20 | tf_op jit(solution)/shard_map/ppermute | solution.py:22
  84.1 9.0 %collective-permute-start.4 = (f32[1,1,1]{2,1,0:T(1,128)}, f32[1,1,1]{2,1,0:T(1,128)}, u32[]{:S(2)}, u32[]{:S(2)}) collective-permute-start(f32[1,1,1]{2,1,0:T(1,128)} %bitcast.49), channel_id=1, source_target_pairs={{0,1},{1,2},{2,3},{3,4},{4,5},{5,6},{6,7},{7,8},{8,9},{9,10},{10,1... | collective-permute-start | bytes 20 | tf_op jit(solution)/shard_map/ppermute | solution.py:22
  91.8 10.6 %collective-permute-start.16 = (f32[1,1,1]{2,1,0:T(1,128)}, f32[1,1,1]{2,1,0:T(1,128)}, u32[]{:S(2)}, u32[]{:S(2)}) collective-permute-start(f32[1,1,1]{2,1,0:T(1,128)} %mul.1570), channel_id=1, source_target_pairs={{2,0},{3,1},{4,2},{5,3},{6,4},{7,5},{8,6},{9,7},{10,8},{11,9},{12,... | collective-permute-start | bytes 20 | tf_op jit(solution)/shard_map/ppermute | solution.py:22
  93.8 10.5 %collective-permute-start.6 = (f32[1,1,1]{2,1,0:T(1,128)}, f32[1,1,1]{2,1,0:T(1,128)}, u32[]{:S(2)}, u32[]{:S(2)}) collective-permute-start(f32[1,1,1]{2,1,0:T(1,128)} %mul.1479), channel_id=1, source_target_pairs={{0,2},{1,3},{2,4},{3,5},{4,6},{5,7},{6,8},{7,9},{8,10},{9,11},{10,... | collective-permute-start | bytes 20 | tf_op jit(solution)/shard_map/ppermute | solution.py:22
  103.1 9.5 %collective-permute-start.18 = (f32[1,1,1]{2,1,0:T(1,128)}, f32[1,1,1]{2,1,0:T(1,128)}, u32[]{:S(2)}, u32[]{:S(2)}) collective-permute-start(f32[1,1,1]{2,1,0:T(1,128)} %mul.1576), channel_id=1, source_target_pairs={{4,0},{5,1},{6,2},{7,3},{8,4},{9,5},{10,6},{11,7},{12,8},{13,9},{1... | collective-permute-start | bytes 20 | tf_op jit(solution)/shard_map/ppermute | solution.py:22
  105.1 9.5 %collective-permute-start.8 = (f32[1,1,1]{2,1,0:T(1,128)}, f32[1,1,1]{2,1,0:T(1,128)}, u32[]{:S(2)}, u32[]{:S(2)}) collective-permute-start(f32[1,1,1]{2,1,0:T(1,128)} %mul.1487), channel_id=1, source_target_pairs={{0,4},{1,5},{2,6},{3,7},{4,8},{5,9},{6,10},{7,11},{8,12},{9,13},{1... | collective-permute-start | bytes 20 | tf_op jit(solution)/shard_map/ppermute | solution.py:22
  113.2 11.0 %collective-permute-start.20 = (f32[1,1,1]{2,1,0:T(1,128)}, f32[1,1,1]{2,1,0:T(1,128)}, u32[]{:S(2)}, u32[]{:S(2)}) collective-permute-start(f32[1,1,1]{2,1,0:T(1,128)} %mul.1582), channel_id=1, source_target_pairs={{8,0},{9,1},{10,2},{11,3},{12,4},{13,5},{14,6},{15,7},{16,8},{17,9... | collective-permute-start | bytes 20 | tf_op jit(solution)/shard_map/ppermute | solution.py:22
  115.2 9.7 %collective-permute-start.10 = (f32[1,1,1]{2,1,0:T(1,128)}, f32[1,1,1]{2,1,0:T(1,128)}, u32[]{:S(2)}, u32[]{:S(2)}) collective-permute-start(f32[1,1,1]{2,1,0:T(1,128)} %mul.1495), channel_id=1, source_target_pairs={{0,8},{1,9},{2,10},{3,11},{4,12},{5,13},{6,14},{7,15},{8,16},{9,17... | collective-permute-start | bytes 20 | tf_op jit(solution)/shard_map/ppermute | solution.py:22
  125.7 16.6 %collective-permute-start.5 = (f32[1,16,4096]{2,1,0:T(8,128)S(1)}, f32[1,16,4096]{2,1,0:T(8,128)S(1)}, u32[]{:S(2)}, u32[]{:S(2)}) collective-permute-start(f32[1,16,4096]{2,1,0:T(8,128)S(1)} %fusion.103), channel_id=1, source_target_pairs={{0,2},{1,3},{2,4},{3,5},{4,6},{5,7},{6,8},{7,9},{8,10},{9,11},{10,... | collective-permute-start | bytes 786440 | tf_op jit(solution)/shard_map/ppermute | solution.py:22
  142.4 11.8 %collective-permute-start.7 = (f32[1,16,4096]{2,1,0:T(8,128)S(1)}, f32[1,16,4096]{2,1,0:T(8,128)S(1)}, u32[]{:S(2)}, u32[]{:S(2)}) collective-permute-start(f32[1,16,4096]{2,1,0:T(8,128)S(1)} %fusion.102), channel_id=1, source_target_pairs={{0,4},{1,5},{2,6},{3,7},{4,8},{5,9},{6,10},{7,11},{8,12},{9,13},{1... | collective-permute-start | bytes 786440 | tf_op jit(solution)/shard_map/ppermute | solution.py:22
  154.2 12.4 %collective-permute-start.9 = (f32[1,16,4096]{2,1,0:T(8,128)S(1)}, f32[1,16,4096]{2,1,0:T(8,128)S(1)}, u32[]{:S(2)}, u32[]{:S(2)}) collective-permute-start(f32[1,16,4096]{2,1,0:T(8,128)S(1)} %fusion.101), channel_id=1, source_target_pairs={{0,8},{1,9},{2,10},{3,11},{4,12},{5,13},{6,14},{7,15},{8,16},{9,17... | collective-permute-start | bytes 786440 | tf_op jit(solution)/shard_map/ppermute | solution.py:22
  162.6 29.8 %copy-start.6 = (f32[16,16,4096]{2,1,0:T(8,128)S(1)}, f32[16,16,4096]{2,1,0:T(8,128)}, u32[]{:S(2)}) copy-start(f32[16,16,4096]{2,1,0:T(8,128)} %get-tuple-element.99) | copy-start | bytes 12582916
  166.7 19.8 %collective-permute-start.11 = (f32[1,16,4096]{2,1,0:T(8,128)S(1)}, f32[1,16,4096]{2,1,0:T(8,128)S(1)}, u32[]{:S(2)}, u32[]{:S(2)}) collective-permute-start(f32[1,16,4096]{2,1,0:T(8,128)S(1)} %fusion.100), channel_id=1, source_target_pairs={{0,16},{1,17},{2,18},{3,19},{4,20},{5,21},{6,22},{7,23},{8,24},{9,... | collective-permute-start | bytes 786440 | tf_op jit(solution)/shard_map/ppermute | solution.py:22
  186.6 9.7 %collective-permute-start.12 = (f32[1,16,4096]{2,1,0:T(8,128)S(1)}, f32[1,16,4096]{2,1,0:T(8,128)S(1)}, u32[]{:S(2)}, u32[]{:S(2)}) collective-permute-start(f32[1,16,4096]{2,1,0:T(8,128)S(1)} %fusion.99), channel_id=1, source_target_pairs={{0,1},{1,2},{2,3},{3,4},{4,5},{5,6},{6,7},{7,8},{8,9},{9,10},{10,1... | collective-permute-start | bytes 786440 | tf_op jit(solution)/shard_map/ppermute | solution.py:27
  207.6 8.7 %collective-permute-start.13 = (f32[1,16,4096]{2,1,0:T(8,128)S(1)}, f32[1,16,4096]{2,1,0:T(8,128)S(1)}, u32[]{:S(2)}, u32[]{:S(2)}) collective-permute-start(f32[1,16,4096]{2,1,0:T(8,128)S(1)} %get-tuple-element.101), channel_id=1, source_target_pairs={{1,0},{2,1},{3,2},{4,3},{5,4},{6,5},{7,6},{8,7},{9,8},{10,9},{11,1... | collective-permute-start | bytes 786440 | tf_op jit(solution)/shard_map/ppermute | solution.py:22
  216.4 9.8 %collective-permute-start.15 = (f32[1,16,4096]{2,1,0:T(8,128)S(1)}, f32[1,16,4096]{2,1,0:T(8,128)S(1)}, u32[]{:S(2)}, u32[]{:S(2)}) collective-permute-start(f32[1,16,4096]{2,1,0:T(8,128)S(1)} %fusion.104), channel_id=1, source_target_pairs={{2,0},{3,1},{4,2},{5,3},{6,4},{7,5},{8,6},{9,7},{10,8},{11,9},{12,... | collective-permute-start | bytes 786440 | tf_op jit(solution)/shard_map/ppermute | solution.py:22
  226.2 25.6 %copy-start.14 = (f32[16,16,4096]{2,1,0:T(8,128)S(1)}, f32[16,16,4096]{2,1,0:T(8,128)}, u32[]{:S(2)}) copy-start(f32[16,16,4096]{2,1,0:T(8,128)} %get-tuple-element.89) | copy-start | bytes 12582916
  226.3 8.9 %collective-permute-start.17 = (f32[1,16,4096]{2,1,0:T(8,128)S(1)}, f32[1,16,4096]{2,1,0:T(8,128)S(1)}, u32[]{:S(2)}, u32[]{:S(2)}) collective-permute-start(f32[1,16,4096]{2,1,0:T(8,128)S(1)} %fusion.77), channel_id=1, source_target_pairs={{4,0},{5,1},{6,2},{7,3},{8,4},{9,5},{10,6},{11,7},{12,8},{13,9},{1... | collective-permute-start | bytes 786440 | tf_op jit(solution)/shard_map/ppermute | solution.py:22
  235.2 15.2 %collective-permute-start.19 = (f32[1,16,4096]{2,1,0:T(8,128)S(1)}, f32[1,16,4096]{2,1,0:T(8,128)S(1)}, u32[]{:S(2)}, u32[]{:S(2)}) collective-permute-start(f32[1,16,4096]{2,1,0:T(8,128)S(1)} %fusion.76), channel_id=1, source_target_pairs={{8,0},{9,1},{10,2},{11,3},{12,4},{13,5},{14,6},{15,7},{16,8},{17,9... | collective-permute-start | bytes 786440 | tf_op jit(solution)/shard_map/ppermute | solution.py:22
  250.5 13.0 %collective-permute-start.21 = (f32[1,16,4096]{2,1,0:T(8,128)S(1)}, f32[1,16,4096]{2,1,0:T(8,128)S(1)}, u32[]{:S(2)}, u32[]{:S(2)}) collective-permute-start(f32[1,16,4096]{2,1,0:T(8,128)S(1)} %fusion.75), channel_id=1, source_target_pairs={{16,0},{17,1},{18,2},{19,3},{20,4},{21,5},{22,6},{23,7},{24,8},{25... | collective-permute-start | bytes 786440 | tf_op jit(solution)/shard_map/ppermute | solution.py:22
  263.6 9.4 %collective-permute-start.22 = (f32[1,16,4096]{2,1,0:T(8,128)S(1)}, f32[1,16,4096]{2,1,0:T(8,128)S(1)}, u32[]{:S(2)}, u32[]{:S(2)}) collective-permute-start(f32[1,16,4096]{2,1,0:T(8,128)S(1)} %fusion.74), channel_id=1, source_target_pairs={{1,0},{2,1},{3,2},{4,3},{5,4},{6,5},{7,6},{8,7},{9,8},{10,9},{11,1... | collective-permute-start | bytes 786440 | tf_op jit(solution)/shard_map/ppermute | solution.py:27
  326.0 11.7 %collective-permute-start.26 = (f32[155648]{0:T(1024)S(1)}, f32[155648]{0:T(1024)S(1)}, u32[]{:S(2)}, u32[]{:S(2)}) collective-permute-start(f32[155648]{0:T(1024)S(1)} %pad_maximum_fusion.2), channel_id=1, source_target_pairs={{0,1},{1,0},{2,3},{3,2},{4,5},{5,4},{6,7},{7,6},{8,9},{9,8},{10,11... | collective-permute-start | bytes 1867784 | tf_op jit(solution)/shard_map/ppermute | solution.py:38
  337.7 66.6 %copy-start.12 = (f32[1,1,128,4096]{3,2,1,0:T(8,128)S(1)}, f32[1,1,128,4096]{3,2,1,0:T(8,128)}, u32[]{:S(2)}) copy-start(f32[1,1,128,4096]{3,2,1,0:T(8,128)} %get-tuple-element.73) | copy-start | bytes 6291460
  337.8 15.9 %collective-permute-start.27 = (f32[155648]{0:T(1024)S(1)}, f32[155648]{0:T(1024)S(1)}, u32[]{:S(2)}, u32[]{:S(2)}) collective-permute-start(f32[155648]{0:T(1024)S(1)} %fusion.122), channel_id=1, source_target_pairs={{0,2},{1,3},{2,0},{3,1},{4,6},{5,7},{6,4},{7,5},{8,10},{9,11},{10,... | collective-permute-start | bytes 1867784 | tf_op jit(solution)/shard_map/ppermute | solution.py:38
  353.7 50.6 %copy-start.10 = (f32[1,1,128,4096]{3,2,1,0:T(8,128)S(1)}, f32[1,1,128,4096]{3,2,1,0:T(8,128)}, u32[]{:S(2)}) copy-start(f32[1,1,128,4096]{3,2,1,0:T(8,128)} %copy-done.9) | copy-start | bytes 6291460
  353.8 50.6 %copy-start.8 = (f32[1,1,128,4096]{3,2,1,0:T(8,128)S(1)}, f32[1,1,128,4096]{3,2,1,0:T(8,128)}, u32[]{:S(2)}) copy-start(f32[1,1,128,4096]{3,2,1,0:T(8,128)} %copy-done.7) | copy-start | bytes 6291460
  353.8 23.6 %collective-permute-start.28 = (f32[155648]{0:T(1024)S(1)}, f32[155648]{0:T(1024)S(1)}, u32[]{:S(2)}, u32[]{:S(2)}) collective-permute-start(f32[155648]{0:T(1024)S(1)} %add.471), channel_id=1, source_target_pairs={{0,4},{1,5},{2,6},{3,7},{4,0},{5,1},{6,2},{7,3},{8,12},{9,13},{10,... | collective-permute-start | bytes 1867784 | tf_op jit(solution)/shard_map/ppermute | solution.py:38
  377.5 22.2 %collective-permute-start.29 = (f32[155648]{0:T(1024)S(1)}, f32[155648]{0:T(1024)S(1)}, u32[]{:S(2)}, u32[]{:S(2)}) collective-permute-start(f32[155648]{0:T(1024)S(1)} %add.472), channel_id=1, source_target_pairs={{0,8},{1,9},{2,10},{3,11},{4,12},{5,13},{6,14},{7,15},{8,0},{9,1},... | collective-permute-start | bytes 1867784 | tf_op jit(solution)/shard_map/ppermute | solution.py:38
  399.7 21.9 %slice-start = ((s8[6291456]{0:T(1024)(128)(4,1)}), s8[4194304]{0:T(1024)(128)(4,1)S(1)}, s32[]{:S(2)}) async-start(s8[6291456]{0:T(1024)(128)(4,1)} %bitcast.494), calls=%async_computation | async-start | bytes 8388608
  399.7 21.9 %slice-start.2 = ((s8[6291456]{0:T(1024)(128)(4,1)}), s8[4194304]{0:T(1024)(128)(4,1)S(1)}, s32[]{:S(2)}) async-start(s8[6291456]{0:T(1024)(128)(4,1)} %bitcast.496), calls=%async_computation.2 | async-start | bytes 8388608
  399.8 21.9 %slice-start.1 = ((s8[6291456]{0:T(1024)(128)(4,1)}), s8[2097152]{0:T(1024)(128)(4,1)S(1)}, s32[]{:S(2)}) async-start(s8[6291456]{0:T(1024)(128)(4,1)} %bitcast.494), calls=%async_computation.1 | async-start | bytes 4194304
  399.8 20.9 %collective-permute-start.30 = (f32[155648]{0:T(1024)S(1)}, f32[155648]{0:T(1024)S(1)}, u32[]{:S(2)}, u32[]{:S(2)}) collective-permute-start(f32[155648]{0:T(1024)S(1)} %add.473), channel_id=1, source_target_pairs={{0,16},{1,17},{2,18},{3,19},{4,20},{5,21},{6,22},{7,23},{8,24},{9,... | collective-permute-start | bytes 1867784 | tf_op jit(solution)/shard_map/ppermute | solution.py:38
  421.6 12.4 %collective-permute-start.31 = (f32[155648]{0:T(1024)}, f32[155648]{0:T(1024)}, u32[]{:S(2)}, u32[]{:S(2)}) collective-permute-start(f32[155648]{0:T(1024)} %add.474), channel_id=1, source_target_pairs={{0,32},{32,0},{64,96},{96,64},{128,160},{160,128},{192,224},{224,1... | collective-permute-start | bytes 1867784 | tf_op jit(solution)/shard_map/ppermute | solution.py:38
  435.3 16.5 %collective-permute-start.32 = (f32[155648]{0:T(1024)S(1)}, f32[155648]{0:T(1024)S(1)}, u32[]{:S(2)}, u32[]{:S(2)}) collective-permute-start(f32[155648]{0:T(1024)S(1)} %add.475), channel_id=1, source_target_pairs={{0,64},{32,96},{64,0},{96,32},{128,192},{160,224},{192,128},{224,1... | collective-permute-start | bytes 1867784 | tf_op jit(solution)/shard_map/ppermute | solution.py:38
  436.0 18.1 %collective-permute-start.25 = (f32[1,6,4096]{2,1,0:T(8,128)S(1)}, f32[1,6,4096]{2,1,0:T(8,128)S(1)}, u32[]{:S(2)}, u32[]{:S(2)}) collective-permute-start(f32[1,6,4096]{2,1,0:T(8,128)S(1)} %get-tuple-element.61), channel_id=1, source_target_pairs={{1,0},{2,1},{3,2},{4,3},{5,4},{6,5},{7,6},{8,7},{9,8},{10,9},{11,1... | collective-permute-start | bytes 294920 | tf_op jit(solution)/shard_map/ppermute | solution.py:12
  437.3 16.8 %collective-permute-start.24 = (f32[1,6,4096]{2,1,0:T(8,128)S(1)}, f32[1,6,4096]{2,1,0:T(8,128)S(1)}, u32[]{:S(2)}, u32[]{:S(2)}) collective-permute-start(f32[1,6,4096]{2,1,0:T(8,128)S(1)} %get-tuple-element.62), channel_id=1, source_target_pairs={{1,0},{2,1},{3,2},{4,3},{5,4},{6,5},{7,6},{8,7},{9,8},{10,9},{11,1... | collective-permute-start | bytes 294920 | tf_op jit(solution)/shard_map/ppermute | solution.py:12
  438.6 15.6 %collective-permute-start.23 = (f32[1,6,4096]{2,1,0:T(8,128)S(1)}, f32[1,6,4096]{2,1,0:T(8,128)S(1)}, u32[]{:S(2)}, u32[]{:S(2)}) collective-permute-start(f32[1,6,4096]{2,1,0:T(8,128)S(1)} %get-tuple-element.63), channel_id=1, source_target_pairs={{1,0},{2,1},{3,2},{4,3},{5,4},{6,5},{7,6},{8,7},{9,8},{10,9},{11,1... | collective-permute-start | bytes 294920 | tf_op jit(solution)/shard_map/ppermute | solution.py:12
  451.9 17.2 %collective-permute-start.33 = (f32[155648]{0:T(1024)S(1)}, f32[155648]{0:T(1024)S(1)}, u32[]{:S(2)}, u32[]{:S(2)}) collective-permute-start(f32[155648]{0:T(1024)S(1)} %add.476), channel_id=1, source_target_pairs={{0,128},{32,160},{64,192},{96,224},{128,0},{160,32},{192,64},{224,... | collective-permute-start | bytes 1867784 | tf_op jit(solution)/shard_map/ppermute | solution.py:38
  (66 other events, 724.7 us)

commit v2 on v1

--- a/solution.py
+++ b/solution.py
@@ -12,16 +12,18 @@
     return lax.ppermute(block, axis, route)
 
 
-def device_scan(flags, values, step_log, direction):
+def device_scan(ends, values, step_log, direction, tok_len):
     count = lax.axis_size("ctx")
-    gates = flags[:, None, None]
     sums = values
     distance = 1
     while distance < count:
         route = [(i, i + distance * direction) for i in range(count) if 0 <= i + distance * direction < count]
-        got_gates, got_sums = lax.ppermute((gates, sums), "ctx", route)
-        sums = sums + gates * jnp.exp(distance * step_log) * got_sums
-        gates = gates * got_gates
+        gate = (ends >= distance * tok_len) if direction > 0 else (ends > distance * tok_len)
+        gate = gate.astype(jnp.float32)[:, None, None]
+        if direction > 0:
+            sums = sums + gate * jnp.exp(distance * step_log) * lax.ppermute(sums, "ctx", route)
+        else:
+            sums = sums + jnp.exp(distance * step_log) * lax.ppermute(gate * sums, "ctx", route)
         distance *= 2
     route = [(i, i + direction) for i in range(count) if 0 <= i + direction < count]
     return lax.ppermute(sums, "ctx", route)
@@ -38,6 +40,31 @@
             value = value + lax.ppermute(value, axis, [(i, i ^ step) for i in range(count)])
             step *= 2
     return value
+
+
+def spread_sum(value, scatter_axis, other_axes):
+    count = lax.axis_size(scatter_axis)
+    if count & (count - 1) or value.shape[0] % count:
+        return butterfly_sum(value, (scatter_axis,) + tuple(other_axes))
+    index = lax.axis_index(scatter_axis)
+    lanes = 128 if (value.shape[0] // count) % 128 == 0 else 1
+    blocks = value.reshape(count, -1, lanes)
+    step = count // 2
+    while step >= 1:
+        half = blocks.shape[0] // 2
+        low = (index // step) % 2 == 0
+        keep = jnp.where(low, blocks[:half], blocks[half:])
+        send = jnp.where(low, blocks[half:], blocks[:half])
+        blocks = keep + lax.ppermute(send, scatter_axis, [(i, i ^ step) for i in range(count)])
+        step //= 2
+    blocks = butterfly_sum(blocks, other_axes)
+    step = 1
+    while step < count:
+        got = lax.ppermute(blocks, scatter_axis, [(i, i ^ step) for i in range(count)])
+        low = (index // step) % 2 == 0
+        blocks = jnp.where(low, jnp.concatenate([blocks, got]), jnp.concatenate([got, blocks]))
+        step *= 2
+    return blocks.reshape(-1)
 
 
 def shards(
@@ -142,7 +169,7 @@
         jnp.sum(pow_end[None, None] * (mixed_blocks * last_doc)[:, :, :, None, :], axis=2), 0, 1
     )
     block_sum, _ = sweep(zero_state, sigma, False)
-    states = device_scan(pass_dev, block_sum, tok_len * lam_log, 1)
+    states = device_scan(doc_offset[:, -1], block_sum, tok_len * lam_log, 1, tok_len)
     _, enters = sweep(states, sigma, False)
     cross = valid_in * jnp.sum(
         (mode_coef[None] * pow_one)[None, None] * jnp.swapaxes(enters, 0, 1)[:, :, None], axis=3
@@ -159,7 +186,7 @@
         jnp.sum(pow_zero[None, None] * (grad_blocks * valid_in)[:, :, :, None, :], axis=2), 0, 1
     )
     block_adj, _ = sweep(zero_state, gamma, True)
-    adj_in = device_scan(pass_dev, block_adj, tok_len * lam_log, -1)
+    adj_in = device_scan(doc_offset[:, 0], block_adj, tok_len * lam_log, -1, tok_len)
     _, exits = sweep(adj_in, gamma, True)
     cross_back = last_doc * jnp.sum(
         (mode_coef[None] * pow_back)[None, None] * jnp.swapaxes(exits, 0, 1)[:, :, None], axis=3
@@ -214,7 +241,7 @@
     ]
     tap_stack = jnp.stack(tap_terms, axis=1)
     flat = jnp.concatenate([tap_stack.reshape(-1), skip_term, residue_term.reshape(-1)])
-    flat = butterfly_sum(flat, ("ctx", "dp"))
+    flat = spread_sum(flat, "ctx", ("dp",))
     taps_sum = flat[: tap_stack.size].reshape(tap_stack.shape)
     skip_sum = flat[tap_stack.size : tap_stack.size + skip_term.size]
     residue_sum = flat[tap_stack.size + skip_term.size :].reshape(residue_term.shape)

time: 476 us -> 418 us (0.88)
  the two profiles are of different devices: /device:TPU:2 before, /device:TPU:58 now
where the time goes in v2:
time: 418 us; the launch traced here: 414 us
  other arithmetic  173 us (41%)
  waiting for transfers between devices  106 us (25%)
  starting transfers between devices  96 us (23%)
  local copies, waits for them, and re-layouts  28.7 us (7%)
  between operations  9.29 us (2%)
    ppermute x5, waiting for transfers between devices, device_scan(): lax.ppermute(gate * sums, 'ctx', route)  36.9 us
    ppermute x5, starting transfers between devices, device_scan(): lax.ppermute(sums, 'ctx', route)  25.2 us
    ppermute x5, waiting for transfers between devices, spread_sum(): lax.ppermute(send, scatter_axis, [(i, i ^ step) for i in range(count)])  22.9 us
    ppermute x6, waiting for transfers between devices, from_behind(): return lax.ppermute(block, axis, route)  20 us
    reduce_sum x2, other arithmetic, shards(): tap_terms.append(jnp.sum(window(tap_index) * short_grads, axis=(1, 2)))  20 us
    ppermute x5, starting transfers between devices, spread_sum(): lax.ppermute(send, scatter_axis, [(i, i ^ step) for i in range(count)])  17.4 us
    ppermute x6, starting transfers between devices, from_behind(): return lax.ppermute(block, axis, route)  16.7 us
    ppermute x5, waiting for transfers between devices, device_scan(): lax.ppermute(sums, 'ctx', route)  15.5 us
  transfers between devices with their start and end apart: 31, of which 21 were waited for; matrix products, arithmetic and copies ran while one was open for 20% of the time, Pallas kernels for 0%

profile of v2, /device:TPU:58, one launch (start us, length us, event | category | flops | bytes accessed | tf_op | source)
XLA Modules:
  0.0 413.6 jit_solution(2638823652301202013)
XLA Ops:
  2.2 3.5 collective-permute-start.2
  7.2 3.5 collective-permute-start.1
  12.2 3.5 collective-permute-start
  21.9 2.6 fusion.131
  25.6 2.1 fusion.120
  31.1 9.5 %multiply_add_fusion = f32[3,1,128,4096]{3,2,1,0:T(8,128)S(1)} fusion(f32[3,4096]{1,0:T(4,128)S(1)} %get-tuple-element.166, f32[3,4096]{1,0:T(4,128)S(1)} %get-tuple-element.167, f32[3,4096]{1,0:T(4,128)S(1)} %get-tuple-element.168, f32[3,4096]{1,0:T(4,128)S(1)} %get-tuple-element.169, f32[3,4096]{1,0:T(4,128)S(1)} %get-tuple-element.170, ...), kind=kLoop, calls=%fused_computation.47 | loop fusion | flops 42467328 | bytes 28656512 | tf_op jit(solution)/shard_map/add | solution.py:117
  44.5 2.7 multiply_reduce_fusion.30
  47.2 4.1 multiply_reduce_fusion.23
  51.4 4.5 %multiply_reduce_fusion.14 = (f32[4096]{0:T(1024)}, f32[4096]{0:T(1024)}, f32[4096]{0:T(1024)}, f32[4096]{0:T(1024)}, f32[4096]{0:T(1024)}, /*index=5*/f32[4096]...) fusion(f32[1,8,16,4096]{3,2,1,0:T(8,128)S(1)} %bitcast.515, f32[1,8,16,4096]{3,2,1,0:T(8,128)S(1)} %bitcast.518, ...), kind=kLoop, calls=%fused_computation.153 | loop fusion | flops 14118912 | bytes 4342912 | tf_op jit(solution)/shard_map/reduce_sum | solution.py:202
  55.9 3.3 stack.205
  59.2 7.9 %fusion.13 = (f32[16,16,4096]{2,1,0:T(8,128)}, f32[16,16,4096]{2,1,0:T(8,128)}, f32[16,4096]{1,0:T(8,128)}, f32[16,4096]{1,0:T(8,128)}, f32[16,16,4096]{2,1,0:T(8,128)}) fusion(f32[16,4096]{1,0:T(8,128)} %get-tuple-element.129, f32[16,4096]{1,0:T(8,128)} %get-tuple-element.130, f32[16]{0:T(128)} %iota_convert_fusion, f32[16,4096]{1,0:T(8,128)} %get-tuple-element.131, ...), kind=kLoop, calls=%fused_computation.74 | loop fusion | flops 7208960 | bytes 14155840 | tf_op jit(solution)/shard_map/mul | solution.py:128
  67.1 4.6 %rev.6 = f32[16,16,4096]{2,1,0:T(8,128)} reverse(f32[16,16,4096]{2,1,0:T(8,128)} %get-tuple-element.105), dimensions={0} | reverse | bytes 8388608 | tf_op jit(solution)/shard_map/rev | solution.py:129
  71.8 2.0 broadcast_multiply_fusion.1
  74.6 2.7 multiply_reduce_fusion.1
  77.3 6.2 %multiply_bitcast_fusion.1 = (f32[1,16,4096]{2,1,0:T(8,128)S(1)}, f32[16,4096]{1,0:T(8,128)S(1)}) fusion(f32[]{:T(128)} %bitcast.106, f32[]{:T(128)} %bitcast.31, f32[1,8,16,4096]{3,2,1,0:T(8,128)S(1)} %bitcast.521, f32[]{:T(128)} %bitcast.33, f32[]{:T(128)} %bitcast.35, f32[]{:T(128)} %bitcast.37, f32[]{:T(128)} %bitcast.39, f32[]{:T(128)} %bitcast.41, ...), kind=kLoop, calls=%fused_computation.299 | loop fusion | flops 1769472 | bytes 2883620 | tf_op jit(solution)/shard_map/mul | solution.py:26
  83.5 2.4 collective-permute-start.9
  88.1 2.7 multiply_reduce_fusion.3
  90.8 5.4 %fusion.72 = f32[1,16,4096]{2,1,0:T(8,128)S(1)} fusion(f32[1,8,16,4096]{3,2,1,0:T(8,128)S(1)} %bitcast.528, f32[]{:T(128)} %bitcast.45, f32[]{:T(128)} %bitcast.43, f32[]{:T(128)} %bitcast.41, f32[]{:T(128)} %bitcast.39, f32[]{:T(128)} %bitcast.37, f32[]{:T(128)} %bitcast.35, f32[]{:T(128)} %bitcast.33, f32[]{:T(128)} %bitcast.31, f32[16,4096]{1,0:T(8,128)S(1)} %copy-done.2), kind=kLoop, calls=%fused_computation.205 | loop fusion | flops 1703936 | bytes 2621472 | tf_op jit(solution)/shard_map/add | solution.py:158
  96.2 5.6 %collective-permute-start.3 = (f32[1,16,4096]{2,1,0:T(8,128)S(1)}, f32[1,16,4096]{2,1,0:T(8,128)S(1)}, u32[]{:S(2)}, u32[]{:S(2)}) collective-permute-start(f32[1,16,4096]{2,1,0:T(8,128)S(1)} %fusion.72), channel_id=1, source_target_pairs={{0,1},{1,2},{2,3},{3,4},{4,5},{5,6},{6,7},{7,8},{8,9},{9,10},{10,1... | collective-permute-start | bytes 786440 | tf_op jit(solution)/shard_map/ppermute | solution.py:24
  103.0 3.2 collective-permute-done.3
  107.1 4.5 %collective-permute-start.4 = (f32[1,16,4096]{2,1,0:T(8,128)S(1)}, f32[1,16,4096]{2,1,0:T(8,128)S(1)}, u32[]{:S(2)}, u32[]{:S(2)}) collective-permute-start(f32[1,16,4096]{2,1,0:T(8,128)S(1)} %get-tuple-element.112), channel_id=1, source_target_pairs={{0,2},{1,3},{2,4},{3,5},{4,6},{5,7},{6,8},{7,9},{8,10},{9,11},{10,... | collective-permute-start | bytes 786440 | tf_op jit(solution)/shard_map/ppermute | solution.py:24
  112.2 5.0 %collective-permute-done.4 = f32[1,16,4096]{2,1,0:T(8,128)S(1)} collective-permute-done((f32[1,16,4096]{2,1,0:T(8,128)S(1)}, f32[1,16,4096]{2,1,0:T(8,128)S(1)}, u32[]{:S(2)}, u32[]{:S(2)}) %collective-permute-start.4) | collective-permute-done | bytes 262176 | tf_op jit(solution)/shard_map/ppermute | solution.py:24
  118.0 3.8 collective-permute-start.5
  127.7 7.7 %collective-permute-start.6 = (f32[1,16,4096]{2,1,0:T(8,128)S(1)}, f32[1,16,4096]{2,1,0:T(8,128)S(1)}, u32[]{:S(2)}, u32[]{:S(2)}) collective-permute-start(f32[1,16,4096]{2,1,0:T(8,128)S(1)} %fusion.101), channel_id=1, source_target_pairs={{0,8},{1,9},{2,10},{3,11},{4,12},{5,13},{6,14},{7,15},{8,16},{9,17... | collective-permute-start | bytes 786440 | tf_op jit(solution)/shard_map/ppermute | solution.py:24
  135.5 9.3 %broadcast_select_fusion.8 = (f32[1,8,16,4096]{3,2,1,0:T(8,128)S(1)}, f32[1,8,16,4096]{3,2,1,0:T(8,128)S(1)}, f32[1,8,16,4096]{3,2,1,0:T(8,128)S(1)}, f32[1,8,16...) fusion(pred[8,16]{1,0:T(8,128)(4,1)S(1)} %copy-done.81, ...), kind=kLoop, calls=%fused_computation.179 | loop fusion | flops 7340032 | bytes 31459072 | tf_op jit(solution)/shard_map/jit(_where)/select_n | solution.py:146
  144.9 3.5 collective-permute-start.7
  149.0 6.1 %collective-permute-done.7 = f32[1,16,4096]{2,1,0:T(8,128)S(1)} collective-permute-done((f32[1,16,4096]{2,1,0:T(8,128)S(1)}, f32[1,16,4096]{2,1,0:T(8,128)S(1)}, u32[]{:S(2)}, u32[]{:S(2)}) %collective-permute-start.7) | collective-permute-done | bytes 262176 | tf_op jit(solution)/shard_map/ppermute | solution.py:24
  155.2 12.9 %collective-permute-start.8 = (f32[1,16,4096]{2,1,0:T(8,128)S(1)}, f32[1,16,4096]{2,1,0:T(8,128)S(1)}, u32[]{:S(2)}, u32[]{:S(2)}) collective-permute-start(f32[1,16,4096]{2,1,0:T(8,128)S(1)} %fusion.99), channel_id=1, source_target_pairs={{0,1},{1,2},{2,3},{3,4},{4,5},{5,6},{6,7},{7,8},{8,9},{9,10},{10,1... | collective-permute-start | bytes 786440 | tf_op jit(solution)/shard_map/ppermute | solution.py:29
  168.4 1.9 collective-permute-start.10
  172.1 7.0 %collective-permute-done.10 = f32[1,16,4096]{2,1,0:T(8,128)S(1)} collective-permute-done((f32[1,16,4096]{2,1,0:T(8,128)S(1)}, f32[1,16,4096]{2,1,0:T(8,128)S(1)}, u32[]{:S(2)}, u32[]{:S(2)}) %collective-permute-start.10) | collective-permute-done | bytes 262176 | tf_op jit(solution)/shard_map/ppermute | solution.py:26
  179.9 1.9 collective-permute-start.11
  181.9 6.3 %collective-permute-done.11 = f32[1,16,4096]{2,1,0:T(8,128)S(1)} collective-permute-done((f32[1,16,4096]{2,1,0:T(8,128)S(1)}, f32[1,16,4096]{2,1,0:T(8,128)S(1)}, u32[]{:S(2)}, u32[]{:S(2)}) %collective-permute-start.11) | collective-permute-done | bytes 262176 | tf_op jit(solution)/shard_map/ppermute | solution.py:26
  190.4 12.7 %collective-permute-done.12 = f32[1,16,4096]{2,1,0:T(8,128)S(1)} collective-permute-done((f32[1,16,4096]{2,1,0:T(8,128)S(1)}, f32[1,16,4096]{2,1,0:T(8,128)S(1)}, u32[]{:S(2)}, u32[]{:S(2)}) %collective-permute-start.12) | collective-permute-done | bytes 262176 | tf_op jit(solution)/shard_map/ppermute | solution.py:26
  205.2 10.8 %collective-permute-done.13 = f32[1,16,4096]{2,1,0:T(8,128)S(1)} collective-permute-done((f32[1,16,4096]{2,1,0:T(8,128)S(1)}, f32[1,16,4096]{2,1,0:T(8,128)S(1)}, u32[]{:S(2)}, u32[]{:S(2)}) %collective-permute-start.13) | collective-permute-done | bytes 262176 | tf_op jit(solution)/shard_map/ppermute | solution.py:26
  221.9 8.6 %multiply_reduce_fusion.2 = f32[8,16,4096]{2,1,0:T(8,128)S(1)} fusion(f32[8,16,4096]{2,1,0:T(8,128)S(1)} %bitcast.537, f32[16,16,4096]{2,1,0:T(8,128)S(1)} %copy-done.18), kind=kLoop, calls=%fused_computation.2 | loop fusion | flops 16252928 | bytes 8388608 | tf_op jit(solution)/shard_map/reduce_sum | solution.py:174
  230.8 6.9 %fusion.69 = f32[1,8,16,4096]{3,2,1,0:T(8,128)} fusion(f32[8,16,4096]{2,1,0:T(8,128)S(1)} %multiply_reduce_fusion.2, f32[1,8,16,4096]{3,2,1,0:T(8,128)S(1)} %bitcast.520, f32[8,16]{1,0:T(8,128)S(1)} %copy-done.79, f32[4096]{0:T(1024)S(1)} %bitcast.543, f32[4096]{0:T(1024)S(1)} %bitcast.545, f32[4096]{0:T(1024)S(1)} %bitcast.547, f32[4096]{0:T(1024)S(1)} %bitcast.549, ...), kind=kLoop, calls=%fused_computation.151 | loop fusion | flops 25690112 | bytes 6556160 | tf_op jit(solution)/shard_map/add | solution.py:177
  239.6 5.3 %bitcast_dynamic-update-slice_fusion.7 = (f32[8,1,16,4096]{3,2,1,0:T(8,128)S(1)}, f32[1,16,4096]{2,1,0:T(8,128)S(1)}, f32[1,16,4096]{2,1,0:T(8,128)S(1)}, f32[1,16,4096]{2,1,0:T(8,128)S(1)}) fusion(f32[1,8,16,4096]{3,2,1,0:T(8,128)S(1)} %bitcast.522, f32[]{:T(128)} %bitcast.43, f32[]{:T(128)} %bitcast.41, f32[16,4096]{1,0:T(8,128)S(1)} %copy-done.3, ...), kind=kLoop, calls=%fused_computation.213 | loop fusion | flops 1507327 | bytes 3407900
  247.6 8.4 %multiply_reduce_fusion = f32[8,16,4096]{2,1,0:T(8,128)S(1)} fusion(f32[8,16,4096]{2,1,0:T(8,128)S(1)} %bitcast.536, f32[16,16,4096]{2,1,0:T(8,128)S(1)} %reverse_multiply_fusion), kind=kLoop, calls=%fused_computation | loop fusion | flops 16252928 | bytes 8388608 | tf_op jit(solution)/shard_map/reduce_sum | solution.py:191
  256.2 7.0 %fusion.31 = f32[1,8,16,4096]{3,2,1,0:T(8,128)} fusion(f32[1,8,16,4096]{3,2,1,0:T(8,128)} %get-tuple-element.91, f32[1,8,16,4096]{3,2,1,0:T(8,128)S(1)} %get-tuple-element.79, f32[1,8,16,4096]{3,2,1,0:T(8,128)S(1)} %get-tuple-element.80, f32[1,8,16,4096]{3,2,1,0:T(8,128)S(1)} %copy-done.20, f32[1,8,16,4096]{3,2,1,0:T(8,128)S(1)} %copy-done.21, ...), kind=kLoop, calls=%fused_computation.102 | loop fusion | flops 17825792 | bytes 38011520 | tf_op jit(solution)/shard_map/add | solution.py:194
  263.3 8.2 %fusion.67 = (f32[1,1,128,4096]{3,2,1,0:T(8,128)S(1)}, f32[1,1,128,4096]{3,2,1,0:T(8,128)S(1)}, bf16[1,128,4096]{2,1,0:T(8,128)(2,1)}, f32[1,1,128,4096]{3,2,1,0:T(8,128)}) fusion(f32[3,1,128,4096]{3,2,1,0:T(8,128)} %copy-done.4, f32[1,128,4096]{2,1,0:T(8,128)S(1)} %copy-done.1, f32[4096]{0:T(1024)} %param.16, f32[1,8,16,4096]{3,2,1,0:T(8,128)} %fusion.31, ...), kind=kLoop, calls=%fused_computation.146 | loop fusion | flops 5242880 | bytes 23085056 | tf_op jit(solution)/shard_map/stack | solution.py:220
  271.6 11.8 %multiply_reduce_fusion.4 = (f32[3,4096]{1,0:T(4,128)S(1)}, f32[3,4096]{1,0:T(4,128)S(1)}, f32[3,4096]{1,0:T(4,128)S(1)}, f32[3,4096]{1,0:T(4,128)S(1)}, f32[3,4096]{1,0:T(4,128)S(1)}, /*index=5*/f32[3,4096]{1,0:T(4,128)S(1)}) fusion(pred[128]{0:T(512)(128)(4,1)S(1)} %copy-done.120, bf16[3,1,134,4096]{3,2,1,0:T(8,128)(2,1)S(1)} %pad_maximum_fusion.1, ...), kind=kLoop, calls=%fused_computation.40 | loop fusion | flops 40820736 | bytes 25461504 | tf_op jit(solution)/shard_map/reduce_sum | solution.py:231
  283.4 8.2 %multiply_reduce_fusion.10 = (f32[3,4096]{1,0:T(4,128)S(1)}, f32[3,1,128,4096]{3,2,1,0:T(8,128)}, f32[3,1,128,4096]{3,2,1,0:T(8,128)}, f32[3,1,128,4096]{3,2,1,0:T(8,128)}) fusion(pred[128]{0:T(512)(128)(4,1)S(1)} %copy-done.118, bf16[3,1,134,4096]{3,2,1,0:T(8,128)(2,1)S(1)} %pad_maximum_fusion.1, f32[1,1,128,4096]{3,2,1,0:T(8,128)S(1)} %get-tuple-element.58, ...), kind=kLoop, calls=%fused_computation.46 | loop fusion | flops 14143488 | bytes 28361088 | tf_op jit(solution)/shard_map/reduce_sum | solution.py:231
  293.0 12.8 %collective-permute-done.18 = f32[16,38,128]{2,1,0:T(8,128)} collective-permute-done((f32[16,38,128]{2,1,0:T(8,128)S(1)}, f32[16,38,128]{2,1,0:T(8,128)}, u32[]{:S(2)}, u32[]{:S(2)}) %collective-permute-start.18) | collective-permute-done | bytes 311328 | tf_op jit(solution)/shard_map/ppermute | solution.py:58
  306.8 4.7 %collective-permute-start.19 = (f32[8,38,128]{2,1,0:T(8,128)S(1)}, f32[8,38,128]{2,1,0:T(8,128)S(1)}, u32[]{:S(2)}, u32[]{:S(2)}) collective-permute-start(f32[8,38,128]{2,1,0:T(8,128)S(1)} %slice_select_fusion.2), channel_id=1, source_target_pairs={{0,8},{1,9},{2,10},{3,11},{4,12},{5,13},{6,14},{7,15},{8,0},{9,1},... | collective-permute-start | bytes 466952 | tf_op jit(solution)/shard_map/ppermute | solution.py:58
  311.5 3.9 collective-permute-done.19
  315.5 2.8 collective-permute-start.20
  318.3 2.4 collective-permute-done.20
  320.7 7.3 %collective-permute-start.21 = (f32[2,38,128]{2,1,0:T(8,128)S(1)}, f32[2,38,128]{2,1,0:T(8,128)S(1)}, u32[]{:S(2)}, u32[]{:S(2)}) collective-permute-start(f32[2,38,128]{2,1,0:T(8,128)S(1)} %slice_select_fusion.4), channel_id=1, source_target_pairs={{0,2},{1,3},{2,0},{3,1},{4,6},{5,7},{6,4},{7,5},{8,10},{9,11},{10,... | collective-permute-start | bytes 116744 | tf_op jit(solution)/shard_map/ppermute | solution.py:58
  328.0 2.0 collective-permute-done.21
  330.0 2.5 collective-permute-start.22
  336.1 3.2 collective-permute-done.24
  339.3 2.1 collective-permute-start.25
  341.5 3.2 collective-permute-done.25
  344.6 2.0 collective-permute-start.26
  348.5 3.2 collective-permute-start.27
  351.7 11.5 %broadcast_select_fusion.2 = (f32[3,1,128,4096]{3,2,1,0:T(8,128)}, f32[3,1,128,4096]{3,2,1,0:T(8,128)}, f32[3,1,128,4096]{3,2,1,0:T(8,128)}, f32[3,1,128,4096]{3,2,1,0:T(8,128)}) fusion(pred[128]{0:T(512)(128)(4,1)S(1)} %copy-done.124, f32[1,1,128,4096]{3,2,1,0:T(8,128)} %copy-done.13, f32[1,1,128,4096]{3,2,1,0:T(8,128)S(1)} %copy-done.12, ...), kind=kLoop, calls=%fused_computation.78 | loop fusion | flops 9437184 | bytes 31457792 | tf_op jit(solution)/shard_map/jit(_where)/select_n | solution.py:224
  363.4 14.0 %fusion.6 = f32[3,1,134,4096]{3,2,1,0:T(8,128)S(1)} fusion(f32[3,1,128,4096]{3,2,1,0:T(8,128)S(1)} %bitcast.527, f32[3,1,128,4096]{3,2,1,0:T(8,128)} %get-tuple-element.76, f32[3,1,128,4096]{3,2,1,0:T(8,128)} %get-tuple-element.75, f32[3,1,128,4096]{3,2,1,0:T(8,128)} %get-tuple-element.74, f32[3,1,128,4096]{3,2,1,0:T(8,128)} %get-tuple-element.73, ...), kind=kLoop, calls=%fused_computation.32 | loop fusion | flops 21405696 | bytes 50970624 | tf_op jit(solution)/shard_map/add | solution.py:227
  377.4 3.3 collective-permute-start.29
  382.7 2.0 collective-permute-start.16
  384.7 2.3 collective-permute-start.15
  389.0 3.5 collective-permute-done.17
  392.5 10.0 %collective-permute-done.16 = f32[1,6,4096]{2,1,0:T(8,128)S(1)} collective-permute-done((f32[1,6,4096]{2,1,0:T(8,128)S(1)}, f32[1,6,4096]{2,1,0:T(8,128)S(1)}, u32[]{:S(2)}, u32[]{:S(2)}) %collective-permute-start.16) | collective-permute-done | bytes 98336 | tf_op jit(solution)/shard_map/ppermute | solution.py:12
  402.5 6.4 %collective-permute-done.15 = f32[1,6,4096]{2,1,0:T(8,128)S(1)} collective-permute-done((f32[1,6,4096]{2,1,0:T(8,128)S(1)}, f32[1,6,4096]{2,1,0:T(8,128)S(1)}, u32[]{:S(2)}, u32[]{:S(2)}) %collective-permute-start.15) | collective-permute-done | bytes 98336 | tf_op jit(solution)/shard_map/ppermute | solution.py:12
  409.0 2.0 fusion.62
  (385 shorter events, 57.0 us)
Async XLA Ops:
  0.6 28.3 %copy-start.34 = (bf16[1,128,4096]{2,1,0:T(8,128)(2,1)S(1)}, bf16[1,128,4096]{2,1,0:T(8,128)(2,1)}, u32[]{:S(2)}) copy-start(bf16[1,128,4096]{2,1,0:T(8,128)(2,1)} %param.9) | copy-start | bytes 3145732
  2.2 27.3 %collective-permute-start.2 = (bf16[1,6,4096]{2,1,0:T(8,128)(2,1)}, bf16[1,6,4096]{2,1,0:T(8,128)(2,1)S(1)}, u32[]{:S(2)}, u32[]{:S(2)}) collective-permute-start(bf16[1,6,4096]{2,1,0:T(8,128)(2,1)} %slice.491), channel_id=1, source_target_pairs={{0,1},{1,2},{2,3},{3,4},{4,5},{5,6},{6,7},{7,8},{8,9},{9,10},{10,1... | collective-permute-start | bytes 147464 | tf_op jit(solution)/shard_map/ppermute | solution.py:12
  7.2 22.0 %collective-permute-start.1 = (bf16[1,6,4096]{2,1,0:T(8,128)(2,1)}, bf16[1,6,4096]{2,1,0:T(8,128)(2,1)S(1)}, u32[]{:S(2)}, u32[]{:S(2)}) collective-permute-start(bf16[1,6,4096]{2,1,0:T(8,128)(2,1)} %slice.490), channel_id=1, source_target_pairs={{0,1},{1,2},{2,3},{3,4},{4,5},{5,6},{6,7},{7,8},{8,9},{9,10},{10,1... | collective-permute-start | bytes 147464 | tf_op jit(solution)/shard_map/ppermute | solution.py:12
  12.2 16.8 %collective-permute-start = (bf16[1,6,4096]{2,1,0:T(8,128)(2,1)}, bf16[1,6,4096]{2,1,0:T(8,128)(2,1)S(1)}, u32[]{:S(2)}, u32[]{:S(2)}) collective-permute-start(bf16[1,6,4096]{2,1,0:T(8,128)(2,1)} %slice.489), channel_id=1, source_target_pairs={{0,1},{1,2},{2,3},{3,4},{4,5},{5,6},{6,7},{7,8},{8,9},{9,10},{10,1... | collective-permute-start | bytes 147464 | tf_op jit(solution)/shard_map/ppermute | solution.py:12
  25.2 21.9 %copy-start.108 = (pred[8,16]{1,0:T(8,128)(4,1)}, pred[8,16]{1,0:T(8,128)(4,1)S(1)}, u32[]{:S(2)}) copy-start(pred[8,16]{1,0:T(8,128)(4,1)S(1)} %get-tuple-element.147) | copy-start | bytes 388
  25.3 21.9 %copy-start.110 = (pred[8,16]{1,0:T(8,128)(4,1)}, pred[8,16]{1,0:T(8,128)(4,1)S(1)}, u32[]{:S(2)}) copy-start(pred[8,16]{1,0:T(8,128)(4,1)S(1)} %get-tuple-element.148) | copy-start | bytes 388
  25.3 26.0 %copy-start.80 = (pred[8,16]{1,0:T(8,128)(4,1)}, pred[8,16]{1,0:T(8,128)(4,1)S(1)}, u32[]{:S(2)}) copy-start(pred[8,16]{1,0:T(8,128)(4,1)S(1)} %get-tuple-element.135) | copy-start | bytes 388
  25.3 26.0 %copy-start.83 = (pred[8,16]{1,0:T(8,128)(4,1)}, pred[8,16]{1,0:T(8,128)(4,1)S(1)}, u32[]{:S(2)}) copy-start(pred[8,16]{1,0:T(8,128)(4,1)S(1)} %get-tuple-element.136) | copy-start | bytes 388
  25.3 26.0 %copy-start.86 = (pred[8,16]{1,0:T(8,128)(4,1)}, pred[8,16]{1,0:T(8,128)(4,1)S(1)}, u32[]{:S(2)}) copy-start(pred[8,16]{1,0:T(8,128)(4,1)S(1)} %get-tuple-element.137) | copy-start | bytes 388
  25.3 26.0 %copy-start.89 = (pred[8,16]{1,0:T(8,128)(4,1)}, pred[8,16]{1,0:T(8,128)(4,1)S(1)}, u32[]{:S(2)}) copy-start(pred[8,16]{1,0:T(8,128)(4,1)S(1)} %get-tuple-element.138) | copy-start | bytes 388
  25.3 26.0 %copy-start.92 = (pred[8,16]{1,0:T(8,128)(4,1)}, pred[8,16]{1,0:T(8,128)(4,1)S(1)}, u32[]{:S(2)}) copy-start(pred[8,16]{1,0:T(8,128)(4,1)S(1)} %get-tuple-element.139) | copy-start | bytes 388
  25.3 26.0 %copy-start.94 = (pred[8,16]{1,0:T(8,128)(4,1)}, pred[8,16]{1,0:T(8,128)(4,1)S(1)}, u32[]{:S(2)}) copy-start(pred[8,16]{1,0:T(8,128)(4,1)S(1)} %get-tuple-element.140) | copy-start | bytes 388
  25.3 26.0 %copy-start.96 = (pred[8,16]{1,0:T(8,128)(4,1)}, pred[8,16]{1,0:T(8,128)(4,1)S(1)}, u32[]{:S(2)}) copy-start(pred[8,16]{1,0:T(8,128)(4,1)S(1)} %get-tuple-element.141) | copy-start | bytes 388
  25.3 26.0 %copy-start.98 = (pred[8,16]{1,0:T(8,128)(4,1)}, pred[8,16]{1,0:T(8,128)(4,1)S(1)}, u32[]{:S(2)}) copy-start(pred[8,16]{1,0:T(8,128)(4,1)S(1)} %get-tuple-element.142) | copy-start | bytes 388
  25.3 26.0 %copy-start.112 = (pred[8,16]{1,0:T(8,128)(4,1)}, pred[8,16]{1,0:T(8,128)(4,1)S(1)}, u32[]{:S(2)}) copy-start(pred[8,16]{1,0:T(8,128)(4,1)S(1)} %get-tuple-element.134) | copy-start | bytes 388
  83.5 22.8 %copy-start.32 = (f32[16,4096]{1,0:T(8,128)}, f32[16,4096]{1,0:T(8,128)S(1)}, u32[]{:S(2)}) copy-start(f32[16,4096]{1,0:T(8,128)S(1)} %get-tuple-element.53) | copy-start | bytes 786436
  83.5 19.5 %collective-permute-start.9 = (f32[1,16,4096]{2,1,0:T(8,128)S(1)}, f32[1,16,4096]{2,1,0:T(8,128)S(1)}, u32[]{:S(2)}, u32[]{:S(2)}) collective-permute-start(f32[1,16,4096]{2,1,0:T(8,128)S(1)} %get-tuple-element.52), channel_id=1, source_target_pairs={{1,0},{2,1},{3,2},{4,3},{5,4},{6,5},{7,6},{8,7},{9,8},{10,9},{11,1... | collective-permute-start | bytes 786440 | tf_op jit(solution)/shard_map/ppermute | solution.py:26
  96.2 39.3 %copy-start.81 = (pred[8,16]{1,0:T(8,128)(4,1)S(1)}, pred[8,16]{1,0:T(8,128)(4,1)}, u32[]{:S(2)}) copy-start(pred[8,16]{1,0:T(8,128)(4,1)} %copy-done.80) | copy-start | bytes 388
  96.2 39.3 %copy-start.84 = (pred[8,16]{1,0:T(8,128)(4,1)S(1)}, pred[8,16]{1,0:T(8,128)(4,1)}, u32[]{:S(2)}) copy-start(pred[8,16]{1,0:T(8,128)(4,1)} %copy-done.83) | copy-start | bytes 388
  96.2 39.3 %copy-start.87 = (pred[8,16]{1,0:T(8,128)(4,1)S(1)}, pred[8,16]{1,0:T(8,128)(4,1)}, u32[]{:S(2)}) copy-start(pred[8,16]{1,0:T(8,128)(4,1)} %copy-done.86) | copy-start | bytes 388
  96.2 39.3 %copy-start.90 = (pred[8,16]{1,0:T(8,128)(4,1)S(1)}, pred[8,16]{1,0:T(8,128)(4,1)}, u32[]{:S(2)}) copy-start(pred[8,16]{1,0:T(8,128)(4,1)} %copy-done.89) | copy-start | bytes 388
  96.2 10.0 %collective-permute-start.3 = (f32[1,16,4096]{2,1,0:T(8,128)S(1)}, f32[1,16,4096]{2,1,0:T(8,128)S(1)}, u32[]{:S(2)}, u32[]{:S(2)}) collective-permute-start(f32[1,16,4096]{2,1,0:T(8,128)S(1)} %fusion.72), channel_id=1, source_target_pairs={{0,1},{1,2},{2,3},{3,4},{4,5},{5,6},{6,7},{7,8},{8,9},{9,10},{10,1... | collective-permute-start | bytes 786440 | tf_op jit(solution)/shard_map/ppermute | solution.py:24
  107.1 10.1 %collective-permute-start.4 = (f32[1,16,4096]{2,1,0:T(8,128)S(1)}, f32[1,16,4096]{2,1,0:T(8,128)S(1)}, u32[]{:S(2)}, u32[]{:S(2)}) collective-permute-start(f32[1,16,4096]{2,1,0:T(8,128)S(1)} %get-tuple-element.112), channel_id=1, source_target_pairs={{0,2},{1,3},{2,4},{3,5},{4,6},{5,7},{6,8},{7,9},{8,10},{9,11},{10,... | collective-permute-start | bytes 786440 | tf_op jit(solution)/shard_map/ppermute | solution.py:24
  118.0 8.6 %collective-permute-start.5 = (f32[1,16,4096]{2,1,0:T(8,128)}, f32[1,16,4096]{2,1,0:T(8,128)}, u32[]{:S(2)}, u32[]{:S(2)}) collective-permute-start(f32[1,16,4096]{2,1,0:T(8,128)} %fusion.102), channel_id=1, source_target_pairs={{0,4},{1,5},{2,6},{3,7},{4,8},{5,9},{6,10},{7,11},{8,12},{9,13},{1... | collective-permute-start | bytes 786440 | tf_op jit(solution)/shard_map/ppermute | solution.py:24
  127.7 17.1 %collective-permute-start.6 = (f32[1,16,4096]{2,1,0:T(8,128)S(1)}, f32[1,16,4096]{2,1,0:T(8,128)S(1)}, u32[]{:S(2)}, u32[]{:S(2)}) collective-permute-start(f32[1,16,4096]{2,1,0:T(8,128)S(1)} %fusion.101), channel_id=1, source_target_pairs={{0,8},{1,9},{2,10},{3,11},{4,12},{5,13},{6,14},{7,15},{8,16},{9,17... | collective-permute-start | bytes 786440 | tf_op jit(solution)/shard_map/ppermute | solution.py:24
  144.9 10.2 %collective-permute-start.7 = (f32[1,16,4096]{2,1,0:T(8,128)S(1)}, f32[1,16,4096]{2,1,0:T(8,128)S(1)}, u32[]{:S(2)}, u32[]{:S(2)}) collective-permute-start(f32[1,16,4096]{2,1,0:T(8,128)S(1)} %fusion.100), channel_id=1, source_target_pairs={{0,16},{1,17},{2,18},{3,19},{4,20},{5,21},{6,22},{7,23},{8,24},{9,... | collective-permute-start | bytes 786440 | tf_op jit(solution)/shard_map/ppermute | solution.py:24
  148.5 30.6 %copy-start.33 = (f32[16,4096]{1,0:T(8,128)S(1)}, f32[16,4096]{1,0:T(8,128)}, u32[]{:S(2)}) copy-start(f32[16,4096]{1,0:T(8,128)} %copy-done.32) | copy-start | bytes 786436
  148.5 30.6 %copy-start.38 = (f32[1,16,4096]{2,1,0:T(8,128)S(1)}, f32[1,16,4096]{2,1,0:T(8,128)}, u32[]{:S(2)}) copy-start(f32[1,16,4096]{2,1,0:T(8,128)} %copy-done.37) | copy-start | bytes 786436
  149.0 30.2 %copy-start.16 = (f32[8,16,4096]{2,1,0:T(8,128)S(1)}, f32[8,16,4096]{2,1,0:T(8,128)}, u32[]{:S(2)}) copy-start(f32[8,16,4096]{2,1,0:T(8,128)} %copy-done.15) | copy-start | bytes 6291460
  155.2 16.9 %collective-permute-start.8 = (f32[1,16,4096]{2,1,0:T(8,128)S(1)}, f32[1,16,4096]{2,1,0:T(8,128)S(1)}, u32[]{:S(2)}, u32[]{:S(2)}) collective-permute-start(f32[1,16,4096]{2,1,0:T(8,128)S(1)} %fusion.99), channel_id=1, source_target_pairs={{0,1},{1,2},{2,3},{3,4},{4,5},{5,6},{6,7},{7,8},{8,9},{9,10},{10,1... | collective-permute-start | bytes 786440 | tf_op jit(solution)/shard_map/ppermute | solution.py:29
  168.3 62.2 %copy-start.51 = (f32[1,4096]{1,0:T(1,128)}, f32[1,4096]{1,0:T(1,128)S(1)}, u32[]{:S(2)}) copy-start(f32[1,4096]{1,0:T(1,128)S(1)} %get-tuple-element.117) | copy-start | bytes 49156
  168.3 62.2 %copy-start.53 = (f32[1,4096]{1,0:T(1,128)}, f32[1,4096]{1,0:T(1,128)S(1)}, u32[]{:S(2)}) copy-start(f32[1,4096]{1,0:T(1,128)S(1)} %get-tuple-element.118) | copy-start | bytes 49156
  168.3 62.2 %copy-start.55 = (f32[1,4096]{1,0:T(1,128)}, f32[1,4096]{1,0:T(1,128)S(1)}, u32[]{:S(2)}) copy-start(f32[1,4096]{1,0:T(1,128)S(1)} %get-tuple-element.119) | copy-start | bytes 49156
  168.3 62.2 %copy-start.57 = (f32[1,4096]{1,0:T(1,128)}, f32[1,4096]{1,0:T(1,128)S(1)}, u32[]{:S(2)}) copy-start(f32[1,4096]{1,0:T(1,128)S(1)} %get-tuple-element.120) | copy-start | bytes 49156
  168.4 62.2 %copy-start.59 = (f32[1,4096]{1,0:T(1,128)}, f32[1,4096]{1,0:T(1,128)S(1)}, u32[]{:S(2)}) copy-start(f32[1,4096]{1,0:T(1,128)S(1)} %get-tuple-element.121) | copy-start | bytes 49156
  168.4 62.2 %copy-start.61 = (f32[1,4096]{1,0:T(1,128)}, f32[1,4096]{1,0:T(1,128)S(1)}, u32[]{:S(2)}) copy-start(f32[1,4096]{1,0:T(1,128)S(1)} %get-tuple-element.122) | copy-start | bytes 49156
  168.4 62.2 %copy-start.63 = (f32[1,4096]{1,0:T(1,128)}, f32[1,4096]{1,0:T(1,128)S(1)}, u32[]{:S(2)}) copy-start(f32[1,4096]{1,0:T(1,128)S(1)} %get-tuple-element.123) | copy-start | bytes 49156
  168.4 62.2 %copy-start.65 = (f32[1,4096]{1,0:T(1,128)}, f32[1,4096]{1,0:T(1,128)S(1)}, u32[]{:S(2)}) copy-start(f32[1,4096]{1,0:T(1,128)S(1)} %get-tuple-element.124) | copy-start | bytes 49156
  168.4 62.2 %copy-start.67 = (f32[1,4096]{1,0:T(1,128)}, f32[1,4096]{1,0:T(1,128)S(1)}, u32[]{:S(2)}) copy-start(f32[1,4096]{1,0:T(1,128)S(1)} %get-tuple-element.125) | copy-start | bytes 49156
  168.4 62.2 %copy-start.69 = (f32[1,4096]{1,0:T(1,128)}, f32[1,4096]{1,0:T(1,128)S(1)}, u32[]{:S(2)}) copy-start(f32[1,4096]{1,0:T(1,128)S(1)} %get-tuple-element.126) | copy-start | bytes 49156
  168.4 62.2 %copy-start.71 = (f32[1,4096]{1,0:T(1,128)}, f32[1,4096]{1,0:T(1,128)S(1)}, u32[]{:S(2)}) copy-start(f32[1,4096]{1,0:T(1,128)S(1)} %get-tuple-element.127) | copy-start | bytes 49156
  168.4 62.2 %copy-start.73 = (f32[1,4096]{1,0:T(1,128)}, f32[1,4096]{1,0:T(1,128)S(1)}, u32[]{:S(2)}) copy-start(f32[1,4096]{1,0:T(1,128)S(1)} %get-tuple-element.128) | copy-start | bytes 49156
  168.4 10.7 %collective-permute-start.10 = (f32[1,16,4096]{2,1,0:T(8,128)S(1)}, f32[1,16,4096]{2,1,0:T(8,128)S(1)}, u32[]{:S(2)}, u32[]{:S(2)}) collective-permute-start(f32[1,16,4096]{2,1,0:T(8,128)S(1)} %copy-done.50), channel_id=1, source_target_pairs={{2,0},{3,1},{4,2},{5,3},{6,4},{7,5},{8,6},{9,7},{10,8},{11,9},{12,... | collective-permute-start | bytes 786440 | tf_op jit(solution)/shard_map/ppermute | solution.py:26
  179.9 8.3 %collective-permute-start.11 = (f32[1,16,4096]{2,1,0:T(8,128)S(1)}, f32[1,16,4096]{2,1,0:T(8,128)S(1)}, u32[]{:S(2)}, u32[]{:S(2)}) collective-permute-start(f32[1,16,4096]{2,1,0:T(8,128)S(1)} %get-tuple-element.50), channel_id=1, source_target_pairs={{4,0},{5,1},{6,2},{7,3},{8,4},{9,5},{10,6},{11,7},{12,8},{13,9},{1... | collective-permute-start | bytes 786440 | tf_op jit(solution)/shard_map/ppermute | solution.py:26
  189.0 14.0 %collective-permute-start.12 = (f32[1,16,4096]{2,1,0:T(8,128)S(1)}, f32[1,16,4096]{2,1,0:T(8,128)S(1)}, u32[]{:S(2)}, u32[]{:S(2)}) collective-permute-start(f32[1,16,4096]{2,1,0:T(8,128)S(1)} %get-tuple-element.108), channel_id=1, source_target_pairs={{8,0},{9,1},{10,2},{11,3},{12,4},{13,5},{14,6},{15,7},{16,8},{17,9... | collective-permute-start | bytes 786440 | tf_op jit(solution)/shard_map/ppermute | solution.py:26
  203.9 12.2 %collective-permute-start.13 = (f32[1,16,4096]{2,1,0:T(8,128)S(1)}, f32[1,16,4096]{2,1,0:T(8,128)S(1)}, u32[]{:S(2)}, u32[]{:S(2)}) collective-permute-start(f32[1,16,4096]{2,1,0:T(8,128)S(1)} %get-tuple-element.107), channel_id=1, source_target_pairs={{16,0},{17,1},{18,2},{19,3},{20,4},{21,5},{22,6},{23,7},{24,8},{25... | collective-permute-start | bytes 786440 | tf_op jit(solution)/shard_map/ppermute | solution.py:26
  216.9 22.7 %collective-permute-start.14 = (f32[1,16,4096]{2,1,0:T(8,128)S(1)}, f32[1,16,4096]{2,1,0:T(8,128)S(1)}, u32[]{:S(2)}, u32[]{:S(2)}) collective-permute-start(f32[1,16,4096]{2,1,0:T(8,128)S(1)} %get-tuple-element.106), channel_id=1, source_target_pairs={{1,0},{2,1},{3,2},{4,3},{5,4},{6,5},{7,6},{8,7},{9,8},{10,9},{11,1... | collective-permute-start | bytes 786440 | tf_op jit(solution)/shard_map/ppermute | solution.py:29
  292.8 58.9 %copy-start.12 = (f32[1,1,128,4096]{3,2,1,0:T(8,128)S(1)}, f32[1,1,128,4096]{3,2,1,0:T(8,128)}, u32[]{:S(2)}) copy-start(f32[1,1,128,4096]{3,2,1,0:T(8,128)} %copy-done.11) | copy-start | bytes 6291460
  292.8 13.0 %collective-permute-start.18 = (f32[16,38,128]{2,1,0:T(8,128)S(1)}, f32[16,38,128]{2,1,0:T(8,128)}, u32[]{:S(2)}, u32[]{:S(2)}) collective-permute-start(f32[16,38,128]{2,1,0:T(8,128)S(1)} %select_n.592), channel_id=1, source_target_pairs={{0,16},{1,17},{2,18},{3,19},{4,20},{5,21},{6,22},{7,23},{8,24},{9,... | collective-permute-start | bytes 933896 | tf_op jit(solution)/shard_map/ppermute | solution.py:58
  306.8 8.6 %collective-permute-start.19 = (f32[8,38,128]{2,1,0:T(8,128)S(1)}, f32[8,38,128]{2,1,0:T(8,128)S(1)}, u32[]{:S(2)}, u32[]{:S(2)}) collective-permute-start(f32[8,38,128]{2,1,0:T(8,128)S(1)} %slice_select_fusion.2), channel_id=1, source_target_pairs={{0,8},{1,9},{2,10},{3,11},{4,12},{5,13},{6,14},{7,15},{8,0},{9,1},... | collective-permute-start | bytes 466952 | tf_op jit(solution)/shard_map/ppermute | solution.py:58
  315.5 5.2 %collective-permute-start.20 = (f32[4,38,128]{2,1,0:T(8,128)S(1)}, f32[4,38,128]{2,1,0:T(8,128)S(1)}, u32[]{:S(2)}, u32[]{:S(2)}) collective-permute-start(f32[4,38,128]{2,1,0:T(8,128)S(1)} %slice_select_fusion.3), channel_id=1, source_target_pairs={{0,4},{1,5},{2,6},{3,7},{4,0},{5,1},{6,2},{7,3},{8,12},{9,13},{10,... | collective-permute-start | bytes 233480 | tf_op jit(solution)/shard_map/ppermute | solution.py:58
  320.7 9.3 %collective-permute-start.21 = (f32[2,38,128]{2,1,0:T(8,128)S(1)}, f32[2,38,128]{2,1,0:T(8,128)S(1)}, u32[]{:S(2)}, u32[]{:S(2)}) collective-permute-start(f32[2,38,128]{2,1,0:T(8,128)S(1)} %slice_select_fusion.4), channel_id=1, source_target_pairs={{0,2},{1,3},{2,0},{3,1},{4,6},{5,7},{6,4},{7,5},{8,10},{9,11},{10,... | collective-permute-start | bytes 116744 | tf_op jit(solution)/shard_map/ppermute | solution.py:58
  330.0 4.3 %collective-permute-start.22 = (f32[1,38,128]{2,1,0:T(8,128)S(1)}, f32[1,38,128]{2,1,0:T(8,128)S(1)}, u32[]{:S(2)}, u32[]{:S(2)}) collective-permute-start(f32[1,38,128]{2,1,0:T(8,128)S(1)} %slice_select_fusion.5), channel_id=1, source_target_pairs={{0,1},{1,0},{2,3},{3,2},{4,5},{5,4},{6,7},{7,6},{8,9},{9,8},{10,11... | collective-permute-start | bytes 58376 | tf_op jit(solution)/shard_map/ppermute | solution.py:58
  334.4 1.2 collective-permute-start.23
  335.6 3.8 collective-permute-start.24
  339.3 5.3 %collective-permute-start.25 = (f32[1,38,128]{2,1,0:T(8,128)S(1)}, f32[1,38,128]{2,1,0:T(8,128)S(1)}, u32[]{:S(2)}, u32[]{:S(2)}) collective-permute-start(f32[1,38,128]{2,1,0:T(8,128)S(1)} %add.507), channel_id=1, source_target_pairs={{0,128},{32,160},{64,192},{96,224},{128,0},{160,32},{192,64},{224,... | collective-permute-start | bytes 58376 | tf_op jit(solution)/shard_map/ppermute | solution.py:40
  344.6 3.8 collective-permute-start.26
  348.5 14.7 %collective-permute-start.27 = (f32[2,38,128]{2,1,0:T(8,128)S(1)}, f32[2,38,128]{2,1,0:T(8,128)S(1)}, u32[]{:S(2)}, u32[]{:S(2)}) collective-permute-start(f32[2,38,128]{2,1,0:T(8,128)S(1)} %maximum_select_fusion.4), channel_id=1, source_target_pairs={{0,2},{1,3},{2,0},{3,1},{4,6},{5,7},{6,4},{7,5},{8,10},{9,11},{10,... | collective-permute-start | bytes 116744 | tf_op jit(solution)/shard_map/ppermute | solution.py:63
  363.2 14.1 %collective-permute-start.28 = (f32[4,38,128]{2,1,0:T(8,128)S(1)}, f32[4,38,128]{2,1,0:T(8,128)S(1)}, u32[]{:S(2)}, u32[]{:S(2)}) collective-permute-start(f32[4,38,128]{2,1,0:T(8,128)S(1)} %maximum_select_fusion.3), channel_id=1, source_target_pairs={{0,4},{1,5},{2,6},{3,7},{4,0},{5,1},{6,2},{7,3},{8,12},{9,13},{10,... | collective-permute-start | bytes 233480 | tf_op jit(solution)/shard_map/ppermute | solution.py:63
  377.4 9.7 %collective-permute-start.29 = (f32[8,38,128]{2,1,0:T(8,128)S(1)}, f32[8,38,128]{2,1,0:T(8,128)S(1)}, u32[]{:S(2)}, u32[]{:S(2)}) collective-permute-start(f32[8,38,128]{2,1,0:T(8,128)S(1)} %maximum_select_fusion.2), channel_id=1, source_target_pairs={{0,8},{1,9},{2,10},{3,11},{4,12},{5,13},{6,14},{7,15},{8,0},{9,1},... | collective-permute-start | bytes 466952 | tf_op jit(solution)/shard_map/ppermute | solution.py:63
  380.8 11.7 %collective-permute-start.17 = (f32[1,6,4096]{2,1,0:T(8,128)S(1)}, f32[1,6,4096]{2,1,0:T(8,128)S(1)}, u32[]{:S(2)}, u32[]{:S(2)}) collective-permute-start(f32[1,6,4096]{2,1,0:T(8,128)S(1)} %get-tuple-element.65), channel_id=1, source_target_pairs={{1,0},{2,1},{3,2},{4,3},{5,4},{6,5},{7,6},{8,7},{9,8},{10,9},{11,1... | collective-permute-start | bytes 294920 | tf_op jit(solution)/shard_map/ppermute | solution.py:12
  382.7 19.8 %collective-permute-start.16 = (f32[1,6,4096]{2,1,0:T(8,128)S(1)}, f32[1,6,4096]{2,1,0:T(8,128)S(1)}, u32[]{:S(2)}, u32[]{:S(2)}) collective-permute-start(f32[1,6,4096]{2,1,0:T(8,128)S(1)} %get-tuple-element.66), channel_id=1, source_target_pairs={{1,0},{2,1},{3,2},{4,3},{5,4},{6,5},{7,6},{8,7},{9,8},{10,9},{11,1... | collective-permute-start | bytes 294920 | tf_op jit(solution)/shard_map/ppermute | solution.py:12
  384.7 24.2 %collective-permute-start.15 = (f32[1,6,4096]{2,1,0:T(8,128)S(1)}, f32[1,6,4096]{2,1,0:T(8,128)S(1)}, u32[]{:S(2)}, u32[]{:S(2)}) collective-permute-start(f32[1,6,4096]{2,1,0:T(8,128)S(1)} %get-tuple-element.67), channel_id=1, source_target_pairs={{1,0},{2,1},{3,2},{4,3},{5,4},{6,5},{7,6},{8,7},{9,8},{10,9},{11,1... | collective-permute-start | bytes 294920 | tf_op jit(solution)/shard_map/ppermute | solution.py:12
  387.1 23.9 %collective-permute-start.30 = (f32[16,38,128]{2,1,0:T(8,128)S(1)}, f32[16,38,128]{2,1,0:T(8,128)S(1)}, u32[]{:S(2)}, u32[]{:S(2)}) collective-permute-start(f32[16,38,128]{2,1,0:T(8,128)S(1)} %maximum_select_fusion.1), channel_id=1, source_target_pairs={{0,16},{1,17},{2,18},{3,19},{4,20},{5,21},{6,22},{7,23},{8,24},{9,... | collective-permute-start | bytes 933896 | tf_op jit(solution)/shard_map/ppermute | solution.py:63
  (100 other events, 969.7 us)

commit v3 on v2

--- a/solution.py
+++ b/solution.py
@@ -49,21 +49,19 @@
     index = lax.axis_index(scatter_axis)
     lanes = 128 if (value.shape[0] // count) % 128 == 0 else 1
     blocks = value.reshape(count, -1, lanes)
-    step = count // 2
-    while step >= 1:
+    steps = [1 << bit for bit in range(count.bit_length() - 1)]
+    steps = [s for s in steps if s in (1, 4)] + [s for s in steps if s not in (1, 4)]
+    for step in steps:
         half = blocks.shape[0] // 2
         low = (index // step) % 2 == 0
         keep = jnp.where(low, blocks[:half], blocks[half:])
         send = jnp.where(low, blocks[half:], blocks[:half])
         blocks = keep + lax.ppermute(send, scatter_axis, [(i, i ^ step) for i in range(count)])
-        step //= 2
     blocks = butterfly_sum(blocks, other_axes)
-    step = 1
-    while step < count:
+    for step in reversed(steps):
         got = lax.ppermute(blocks, scatter_axis, [(i, i ^ step) for i in range(count)])
         low = (index // step) % 2 == 0
         blocks = jnp.where(low, jnp.concatenate([blocks, got]), jnp.concatenate([got, blocks]))
-        step *= 2
     return blocks.reshape(-1)
 
 

time: 418 us -> 407 us (0.974)
  the two profiles are of different devices: /device:TPU:58 before, /device:TPU:2 now
where the time goes in v3:
time: 407 us; the launch traced here: 402 us
  other arithmetic  173 us (43%)
  waiting for transfers between devices  96.9 us (24%)
  starting transfers between devices  94.1 us (23%)
  local copies, waits for them, and re-layouts  28.7 us (7%)
  between operations  9.23 us (2%)
    ppermute x5, starting transfers between devices, device_scan(): lax.ppermute(sums, 'ctx', route)  39.8 us
    ppermute x5, waiting for transfers between devices, device_scan(): lax.ppermute(gate * sums, 'ctx', route)  36.6 us
    ppermute x5, waiting for transfers between devices, spread_sum(): lax.ppermute(send, scatter_axis, [(i, i ^ step) for i in range(count)])  22.2 us
    reduce_sum x2, other arithmetic, shards(): tap_terms.append(jnp.sum(window(tap_index) * short_grads, axis=(1, 2)))  20 us
    ppermute x5, starting transfers between devices, spread_sum(): lax.ppermute(send, scatter_axis, [(i, i ^ step) for i in range(count)])  17.6 us
    ppermute x6, starting transfers between devices, from_behind(): return lax.ppermute(block, axis, route)  14 us
    add x1, other arithmetic, shards(): spread + short_taps[:, tap_index][:, None, None, :] * padded[:, :, tap_in...  14 us
    unnamed x12, other arithmetic  13.2 us
  transfers between devices with their start and end apart: 31, of which 22 were waited for; matrix products, arithmetic and copies ran while one was open for 20% of the time, Pallas kernels for 0%

profile of v3, /device:TPU:2, one launch (start us, length us, event | category | flops | bytes accessed | tf_op | source)
XLA Modules:
  0.0 402.3 jit_solution(5409235043125709644)
XLA Ops:
  0.6 1.6 slice.491
  2.2 3.5 collective-permute-start.2
  7.2 3.5 collective-permute-start.1
  12.2 3.2 collective-permute-start
  21.6 2.6 fusion.131
  25.3 2.1 fusion.120
  30.8 9.5 %multiply_add_fusion = f32[3,1,128,4096]{3,2,1,0:T(8,128)S(1)} fusion(f32[3,4096]{1,0:T(4,128)S(1)} %get-tuple-element.166, f32[3,4096]{1,0:T(4,128)S(1)} %get-tuple-element.167, f32[3,4096]{1,0:T(4,128)S(1)} %get-tuple-element.168, f32[3,4096]{1,0:T(4,128)S(1)} %get-tuple-element.169, f32[3,4096]{1,0:T(4,128)S(1)} %get-tuple-element.170, ...), kind=kLoop, calls=%fused_computation.47 | loop fusion | flops 42467328 | bytes 28656512 | tf_op jit(solution)/shard_map/add | solution.py:115
  40.6 1.7 copy-done.29
  42.4 1.8 broadcast_select_fusion.7
  44.2 2.7 multiply_reduce_fusion.30
  46.9 4.1 %multiply_reduce_fusion.23 = (f32[4096]{0:T(1024)}, f32[4096]{0:T(1024)}, f32[4096]{0:T(1024)}, f32[4096]{0:T(1024)}, f32[4096]{0:T(1024)}, /*index=5*/f32[4096]{0:T(1024)}) fusion(f32[1,8,16,4096]{3,2,1,0:T(8,128)S(1)} %bitcast.514, f32[1,8,16,4096]{3,2,1,0:T(8,128)S(1)} %bitcast.517, pred[8,16]{1,0:T(8,128)(4,1)S(1)} %get-tuple-element.143, ...), kind=kLoop, calls=%fused_computation.162 | loop fusion | flops 9412608 | bytes 4293376 | tf_op jit(solution)/shard_map/reduce_sum | solution.py:200
  51.1 4.5 %multiply_reduce_fusion.14 = (f32[4096]{0:T(1024)}, f32[4096]{0:T(1024)}, f32[4096]{0:T(1024)}, f32[4096]{0:T(1024)}, f32[4096]{0:T(1024)}, /*index=5*/f32[4096]...) fusion(f32[1,8,16,4096]{3,2,1,0:T(8,128)S(1)} %bitcast.515, f32[1,8,16,4096]{3,2,1,0:T(8,128)S(1)} %bitcast.518, ...), kind=kLoop, calls=%fused_computation.153 | loop fusion | flops 14118912 | bytes 4342912 | tf_op jit(solution)/shard_map/reduce_sum | solution.py:200
  55.6 3.3 stack.205
  58.9 7.9 %fusion.13 = (f32[16,16,4096]{2,1,0:T(8,128)}, f32[16,16,4096]{2,1,0:T(8,128)}, f32[16,4096]{1,0:T(8,128)}, f32[16,4096]{1,0:T(8,128)}, f32[16,16,4096]{2,1,0:T(8,128)}) fusion(f32[16,4096]{1,0:T(8,128)} %get-tuple-element.129, f32[16,4096]{1,0:T(8,128)} %get-tuple-element.130, f32[16]{0:T(128)} %iota_convert_fusion, f32[16,4096]{1,0:T(8,128)} %get-tuple-element.131, ...), kind=kLoop, calls=%fused_computation.74 | loop fusion | flops 7208960 | bytes 14155840 | tf_op jit(solution)/shard_map/mul | solution.py:126
  66.8 4.6 %rev.6 = f32[16,16,4096]{2,1,0:T(8,128)} reverse(f32[16,16,4096]{2,1,0:T(8,128)} %get-tuple-element.105), dimensions={0} | reverse | bytes 8388608 | tf_op jit(solution)/shard_map/rev | solution.py:127
  71.5 2.0 broadcast_multiply_fusion.1
  74.3 2.7 multiply_reduce_fusion.1
  77.0 6.2 %multiply_bitcast_fusion.1 = (f32[1,16,4096]{2,1,0:T(8,128)S(1)}, f32[16,4096]{1,0:T(8,128)S(1)}) fusion(f32[]{:T(128)} %bitcast.106, f32[]{:T(128)} %bitcast.31, f32[1,8,16,4096]{3,2,1,0:T(8,128)S(1)} %bitcast.521, f32[]{:T(128)} %bitcast.33, f32[]{:T(128)} %bitcast.35, f32[]{:T(128)} %bitcast.37, f32[]{:T(128)} %bitcast.39, f32[]{:T(128)} %bitcast.41, ...), kind=kLoop, calls=%fused_computation.299 | loop fusion | flops 1769472 | bytes 2883620 | tf_op jit(solution)/shard_map/mul | solution.py:26
  84.8 1.9 copy-done.17
  86.7 2.7 multiply_reduce_fusion.3
  89.5 5.4 %fusion.72 = f32[1,16,4096]{2,1,0:T(8,128)S(1)} fusion(f32[1,8,16,4096]{3,2,1,0:T(8,128)S(1)} %bitcast.528, f32[]{:T(128)} %bitcast.45, f32[]{:T(128)} %bitcast.43, f32[]{:T(128)} %bitcast.41, f32[]{:T(128)} %bitcast.39, f32[]{:T(128)} %bitcast.37, f32[]{:T(128)} %bitcast.35, f32[]{:T(128)} %bitcast.33, f32[]{:T(128)} %bitcast.31, f32[16,4096]{1,0:T(8,128)S(1)} %copy-done.2), kind=kLoop, calls=%fused_computation.205 | loop fusion | flops 1703936 | bytes 2621472 | tf_op jit(solution)/shard_map/add | solution.py:156
  94.9 4.6 %collective-permute-start.3 = (f32[1,16,4096]{2,1,0:T(8,128)S(1)}, f32[1,16,4096]{2,1,0:T(8,128)S(1)}, u32[]{:S(2)}, u32[]{:S(2)}) collective-permute-start(f32[1,16,4096]{2,1,0:T(8,128)S(1)} %fusion.72), channel_id=1, source_target_pairs={{0,1},{1,2},{2,3},{3,4},{4,5},{5,6},{6,7},{7,8},{8,9},{9,10},{10,1... | collective-permute-start | bytes 786440 | tf_op jit(solution)/shard_map/ppermute | solution.py:24
  100.7 3.2 collective-permute-done.3
  104.7 6.4 %collective-permute-start.4 = (f32[1,16,4096]{2,1,0:T(8,128)S(1)}, f32[1,16,4096]{2,1,0:T(8,128)S(1)}, u32[]{:S(2)}, u32[]{:S(2)}) collective-permute-start(f32[1,16,4096]{2,1,0:T(8,128)S(1)} %get-tuple-element.112), channel_id=1, source_target_pairs={{0,2},{1,3},{2,4},{3,5},{4,6},{5,7},{6,8},{7,9},{8,10},{9,11},{10,... | collective-permute-start | bytes 786440 | tf_op jit(solution)/shard_map/ppermute | solution.py:24
  111.7 3.2 collective-permute-done.4
  115.7 10.7 %collective-permute-start.5 = (f32[1,16,4096]{2,1,0:T(8,128)}, f32[1,16,4096]{2,1,0:T(8,128)}, u32[]{:S(2)}, u32[]{:S(2)}) collective-permute-start(f32[1,16,4096]{2,1,0:T(8,128)} %fusion.102), channel_id=1, source_target_pairs={{0,4},{1,5},{2,6},{3,7},{4,8},{5,9},{6,10},{7,11},{8,12},{9,13},{1... | collective-permute-start | bytes 786440 | tf_op jit(solution)/shard_map/ppermute | solution.py:24
  131.2 5.8 %collective-permute-start.6 = (f32[1,16,4096]{2,1,0:T(8,128)S(1)}, f32[1,16,4096]{2,1,0:T(8,128)S(1)}, u32[]{:S(2)}, u32[]{:S(2)}) collective-permute-start(f32[1,16,4096]{2,1,0:T(8,128)S(1)} %fusion.101), channel_id=1, source_target_pairs={{0,8},{1,9},{2,10},{3,11},{4,12},{5,13},{6,14},{7,15},{8,16},{9,17... | collective-permute-start | bytes 786440 | tf_op jit(solution)/shard_map/ppermute | solution.py:24
  137.0 9.3 %broadcast_select_fusion.8 = (f32[1,8,16,4096]{3,2,1,0:T(8,128)S(1)}, f32[1,8,16,4096]{3,2,1,0:T(8,128)S(1)}, f32[1,8,16,4096]{3,2,1,0:T(8,128)S(1)}, f32[1,8,16...) fusion(pred[8,16]{1,0:T(8,128)(4,1)S(1)} %copy-done.81, ...), kind=kLoop, calls=%fused_computation.179 | loop fusion | flops 7340032 | bytes 31459072 | tf_op jit(solution)/shard_map/jit(_where)/select_n | solution.py:144
  146.4 12.3 %collective-permute-start.7 = (f32[1,16,4096]{2,1,0:T(8,128)S(1)}, f32[1,16,4096]{2,1,0:T(8,128)S(1)}, u32[]{:S(2)}, u32[]{:S(2)}) collective-permute-start(f32[1,16,4096]{2,1,0:T(8,128)S(1)} %fusion.100), channel_id=1, source_target_pairs={{0,16},{1,17},{2,18},{3,19},{4,20},{5,21},{6,22},{7,23},{8,24},{9,... | collective-permute-start | bytes 786440 | tf_op jit(solution)/shard_map/ppermute | solution.py:24
  159.3 3.8 collective-permute-done.7
  166.2 6.9 %collective-permute-done.8 = f32[1,16,4096]{2,1,0:T(8,128)S(1)} collective-permute-done((f32[1,16,4096]{2,1,0:T(8,128)S(1)}, f32[1,16,4096]{2,1,0:T(8,128)S(1)}, u32[]{:S(2)}, u32[]{:S(2)}) %collective-permute-start.8) | collective-permute-done | bytes 262176 | tf_op jit(solution)/shard_map/ppermute | solution.py:29
  176.8 6.9 %collective-permute-done.11 = f32[1,16,4096]{2,1,0:T(8,128)S(1)} collective-permute-done((f32[1,16,4096]{2,1,0:T(8,128)S(1)}, f32[1,16,4096]{2,1,0:T(8,128)S(1)}, u32[]{:S(2)}, u32[]{:S(2)}) %collective-permute-start.11) | collective-permute-done | bytes 262176 | tf_op jit(solution)/shard_map/ppermute | solution.py:26
  185.9 14.5 %collective-permute-done.12 = f32[1,16,4096]{2,1,0:T(8,128)S(1)} collective-permute-done((f32[1,16,4096]{2,1,0:T(8,128)S(1)}, f32[1,16,4096]{2,1,0:T(8,128)S(1)}, u32[]{:S(2)}, u32[]{:S(2)}) %collective-permute-start.12) | collective-permute-done | bytes 262176 | tf_op jit(solution)/shard_map/ppermute | solution.py:26
  202.6 13.6 %collective-permute-done.13 = f32[1,16,4096]{2,1,0:T(8,128)S(1)} collective-permute-done((f32[1,16,4096]{2,1,0:T(8,128)S(1)}, f32[1,16,4096]{2,1,0:T(8,128)S(1)}, u32[]{:S(2)}, u32[]{:S(2)}) %collective-permute-start.13) | collective-permute-done | bytes 262176 | tf_op jit(solution)/shard_map/ppermute | solution.py:26
  221.4 8.6 %multiply_reduce_fusion.2 = f32[8,16,4096]{2,1,0:T(8,128)S(1)} fusion(f32[8,16,4096]{2,1,0:T(8,128)S(1)} %bitcast.537, f32[16,16,4096]{2,1,0:T(8,128)S(1)} %copy-done.18), kind=kLoop, calls=%fused_computation.2 | loop fusion | flops 16252928 | bytes 8388608 | tf_op jit(solution)/shard_map/reduce_sum | solution.py:172
  230.3 6.9 %fusion.69 = f32[1,8,16,4096]{3,2,1,0:T(8,128)} fusion(f32[8,16,4096]{2,1,0:T(8,128)S(1)} %multiply_reduce_fusion.2, f32[1,8,16,4096]{3,2,1,0:T(8,128)S(1)} %bitcast.520, f32[8,16]{1,0:T(8,128)S(1)} %copy-done.79, f32[4096]{0:T(1024)S(1)} %bitcast.543, f32[4096]{0:T(1024)S(1)} %bitcast.545, f32[4096]{0:T(1024)S(1)} %bitcast.547, f32[4096]{0:T(1024)S(1)} %bitcast.549, ...), kind=kLoop, calls=%fused_computation.151 | loop fusion | flops 25690112 | bytes 6556160 | tf_op jit(solution)/shard_map/add | solution.py:175
  239.1 5.3 %bitcast_dynamic-update-slice_fusion.7 = (f32[8,1,16,4096]{3,2,1,0:T(8,128)S(1)}, f32[1,16,4096]{2,1,0:T(8,128)S(1)}, f32[1,16,4096]{2,1,0:T(8,128)S(1)}, f32[1,16,4096]{2,1,0:T(8,128)S(1)}) fusion(f32[1,8,16,4096]{3,2,1,0:T(8,128)S(1)} %bitcast.522, f32[]{:T(128)} %bitcast.43, f32[]{:T(128)} %bitcast.41, f32[16,4096]{1,0:T(8,128)S(1)} %copy-done.3, ...), kind=kLoop, calls=%fused_computation.213 | loop fusion | flops 1507327 | bytes 3407900
  247.1 8.4 %multiply_reduce_fusion = f32[8,16,4096]{2,1,0:T(8,128)S(1)} fusion(f32[8,16,4096]{2,1,0:T(8,128)S(1)} %bitcast.536, f32[16,16,4096]{2,1,0:T(8,128)S(1)} %reverse_multiply_fusion), kind=kLoop, calls=%fused_computation | loop fusion | flops 16252928 | bytes 8388608 | tf_op jit(solution)/shard_map/reduce_sum | solution.py:189
  255.7 7.0 %fusion.31 = f32[1,8,16,4096]{3,2,1,0:T(8,128)} fusion(f32[1,8,16,4096]{3,2,1,0:T(8,128)} %get-tuple-element.91, f32[1,8,16,4096]{3,2,1,0:T(8,128)S(1)} %get-tuple-element.79, f32[1,8,16,4096]{3,2,1,0:T(8,128)S(1)} %get-tuple-element.80, f32[1,8,16,4096]{3,2,1,0:T(8,128)S(1)} %copy-done.20, f32[1,8,16,4096]{3,2,1,0:T(8,128)S(1)} %copy-done.21, ...), kind=kLoop, calls=%fused_computation.102 | loop fusion | flops 17825792 | bytes 38011520 | tf_op jit(solution)/shard_map/add | solution.py:192
  262.8 8.2 %fusion.67 = (f32[1,1,128,4096]{3,2,1,0:T(8,128)S(1)}, f32[1,1,128,4096]{3,2,1,0:T(8,128)S(1)}, bf16[1,128,4096]{2,1,0:T(8,128)(2,1)}, f32[1,1,128,4096]{3,2,1,0:T(8,128)}) fusion(f32[3,1,128,4096]{3,2,1,0:T(8,128)} %copy-done.4, f32[1,128,4096]{2,1,0:T(8,128)S(1)} %copy-done.1, f32[4096]{0:T(1024)} %param.16, f32[1,8,16,4096]{3,2,1,0:T(8,128)} %fusion.31, ...), kind=kLoop, calls=%fused_computation.146 | loop fusion | flops 5242880 | bytes 23085056 | tf_op jit(solution)/shard_map/stack | solution.py:218
  271.1 11.8 %multiply_reduce_fusion.4 = (f32[3,4096]{1,0:T(4,128)S(1)}, f32[3,4096]{1,0:T(4,128)S(1)}, f32[3,4096]{1,0:T(4,128)S(1)}, f32[3,4096]{1,0:T(4,128)S(1)}, f32[3,4096]{1,0:T(4,128)S(1)}, /*index=5*/f32[3,4096]{1,0:T(4,128)S(1)}) fusion(pred[128]{0:T(512)(128)(4,1)S(1)} %copy-done.120, bf16[3,1,134,4096]{3,2,1,0:T(8,128)(2,1)S(1)} %pad_maximum_fusion.1, ...), kind=kLoop, calls=%fused_computation.40 | loop fusion | flops 40820736 | bytes 25461504 | tf_op jit(solution)/shard_map/reduce_sum | solution.py:229
  282.9 8.2 %multiply_reduce_fusion.10 = (f32[3,4096]{1,0:T(4,128)S(1)}, f32[3,1,128,4096]{3,2,1,0:T(8,128)}, f32[3,1,128,4096]{3,2,1,0:T(8,128)}, f32[3,1,128,4096]{3,2,1,0:T(8,128)}) fusion(pred[128]{0:T(512)(128)(4,1)S(1)} %copy-done.118, bf16[3,1,134,4096]{3,2,1,0:T(8,128)(2,1)S(1)} %pad_maximum_fusion.1, f32[1,1,128,4096]{3,2,1,0:T(8,128)S(1)} %get-tuple-element.58, ...), kind=kLoop, calls=%fused_computation.46 | loop fusion | flops 14143488 | bytes 28361088 | tf_op jit(solution)/shard_map/reduce_sum | solution.py:229
  292.3 2.7 collective-permute-start.18
  295.1 5.6 %collective-permute-done.18 = f32[16,38,128]{2,1,0:T(8,128)} collective-permute-done((f32[16,38,128]{2,1,0:T(8,128)S(1)}, f32[16,38,128]{2,1,0:T(8,128)}, u32[]{:S(2)}, u32[]{:S(2)}) %collective-permute-start.18) | collective-permute-done | bytes 311328 | tf_op jit(solution)/shard_map/ppermute | solution.py:59
  301.7 8.7 %collective-permute-start.19 = (f32[8,38,128]{2,1,0:T(8,128)S(1)}, f32[8,38,128]{2,1,0:T(8,128)S(1)}, u32[]{:S(2)}, u32[]{:S(2)}) collective-permute-start(f32[8,38,128]{2,1,0:T(8,128)S(1)} %slice_select_fusion.2), channel_id=1, source_target_pairs={{0,4},{1,5},{2,6},{3,7},{4,0},{5,1},{6,2},{7,3},{8,12},{9,13},{10,... | collective-permute-start | bytes 466952 | tf_op jit(solution)/shard_map/ppermute | solution.py:59
  310.5 3.8 collective-permute-done.19
  314.3 3.1 collective-permute-start.20
  317.4 2.9 collective-permute-done.20
  320.5 4.9 %collective-permute-done.21 = f32[2,38,128]{2,1,0:T(8,128)S(1)} collective-permute-done((f32[2,38,128]{2,1,0:T(8,128)S(1)}, f32[2,38,128]{2,1,0:T(8,128)S(1)}, u32[]{:S(2)}, u32[]{:S(2)}) %collective-permute-start.21) | collective-permute-done | bytes 38944 | tf_op jit(solution)/shard_map/ppermute | solution.py:59
  325.4 2.9 collective-permute-start.22
  328.3 5.0 %collective-permute-done.22 = f32[1,38,128]{2,1,0:T(8,128)S(1)} collective-permute-done((f32[1,38,128]{2,1,0:T(8,128)S(1)}, f32[1,38,128]{2,1,0:T(8,128)S(1)}, u32[]{:S(2)}, u32[]{:S(2)}) %collective-permute-start.22) | collective-permute-done | bytes 19488 | tf_op jit(solution)/shard_map/ppermute | solution.py:59
  335.0 3.2 collective-permute-done.24
  338.3 2.1 collective-permute-start.25
  340.4 3.2 collective-permute-done.25
  343.6 2.7 collective-permute-start.26
  346.3 5.0 %collective-permute-done.26 = f32[1,38,128]{2,1,0:T(8,128)S(1)} collective-permute-done((f32[1,38,128]{2,1,0:T(8,128)S(1)}, f32[1,38,128]{2,1,0:T(8,128)S(1)}, u32[]{:S(2)}, u32[]{:S(2)}) %collective-permute-start.26) | collective-permute-done | bytes 19488 | tf_op jit(solution)/shard_map/ppermute | solution.py:62
  351.5 11.6 %broadcast_select_fusion.2 = (f32[3,1,128,4096]{3,2,1,0:T(8,128)}, f32[3,1,128,4096]{3,2,1,0:T(8,128)}, f32[3,1,128,4096]{3,2,1,0:T(8,128)}, f32[3,1,128,4096]{3,2,1,0:T(8,128)}) fusion(pred[128]{0:T(512)(128)(4,1)S(1)} %copy-done.124, f32[1,1,128,4096]{3,2,1,0:T(8,128)} %copy-done.13, f32[1,1,128,4096]{3,2,1,0:T(8,128)S(1)} %copy-done.12, ...), kind=kLoop, calls=%fused_computation.78 | loop fusion | flops 9437184 | bytes 31457792 | tf_op jit(solution)/shard_map/jit(_where)/select_n | solution.py:222
  363.1 3.2 collective-permute-start.28
  366.4 14.0 %fusion.6 = f32[3,1,134,4096]{3,2,1,0:T(8,128)S(1)} fusion(f32[3,1,128,4096]{3,2,1,0:T(8,128)S(1)} %bitcast.527, f32[3,1,128,4096]{3,2,1,0:T(8,128)} %get-tuple-element.76, f32[3,1,128,4096]{3,2,1,0:T(8,128)} %get-tuple-element.75, f32[3,1,128,4096]{3,2,1,0:T(8,128)} %get-tuple-element.74, f32[3,1,128,4096]{3,2,1,0:T(8,128)} %get-tuple-element.73, ...), kind=kLoop, calls=%fused_computation.32 | loop fusion | flops 21405696 | bytes 50970624 | tf_op jit(solution)/shard_map/add | solution.py:225
  380.4 2.1 collective-permute-start.29
  387.6 2.9 collective-permute-start.30
  390.8 2.8 collective-permute-done.16
  393.6 2.6 collective-permute-done.15
  396.2 2.0 fusion.62
  (385 shorter events, 52.8 us)
Async XLA Ops:
  0.6 28.0 %copy-start.34 = (bf16[1,128,4096]{2,1,0:T(8,128)(2,1)S(1)}, bf16[1,128,4096]{2,1,0:T(8,128)(2,1)}, u32[]{:S(2)}) copy-start(bf16[1,128,4096]{2,1,0:T(8,128)(2,1)} %param.9) | copy-start | bytes 3145732
  2.2 27.0 %collective-permute-start.2 = (bf16[1,6,4096]{2,1,0:T(8,128)(2,1)}, bf16[1,6,4096]{2,1,0:T(8,128)(2,1)S(1)}, u32[]{:S(2)}, u32[]{:S(2)}) collective-permute-start(bf16[1,6,4096]{2,1,0:T(8,128)(2,1)} %slice.491), channel_id=1, source_target_pairs={{0,1},{1,2},{2,3},{3,4},{4,5},{5,6},{6,7},{7,8},{8,9},{9,10},{10,1... | collective-permute-start | bytes 147464 | tf_op jit(solution)/shard_map/ppermute | solution.py:12
  7.2 21.7 %collective-permute-start.1 = (bf16[1,6,4096]{2,1,0:T(8,128)(2,1)}, bf16[1,6,4096]{2,1,0:T(8,128)(2,1)S(1)}, u32[]{:S(2)}, u32[]{:S(2)}) collective-permute-start(bf16[1,6,4096]{2,1,0:T(8,128)(2,1)} %slice.490), channel_id=1, source_target_pairs={{0,1},{1,2},{2,3},{3,4},{4,5},{5,6},{6,7},{7,8},{8,9},{9,10},{10,1... | collective-permute-start | bytes 147464 | tf_op jit(solution)/shard_map/ppermute | solution.py:12
  12.2 16.5 %collective-permute-start = (bf16[1,6,4096]{2,1,0:T(8,128)(2,1)}, bf16[1,6,4096]{2,1,0:T(8,128)(2,1)S(1)}, u32[]{:S(2)}, u32[]{:S(2)}) collective-permute-start(bf16[1,6,4096]{2,1,0:T(8,128)(2,1)} %slice.489), channel_id=1, source_target_pairs={{0,1},{1,2},{2,3},{3,4},{4,5},{5,6},{6,7},{7,8},{8,9},{9,10},{10,1... | collective-permute-start | bytes 147464 | tf_op jit(solution)/shard_map/ppermute | solution.py:12
  24.9 21.9 %copy-start.102 = (pred[8,16]{1,0:T(8,128)(4,1)}, pred[8,16]{1,0:T(8,128)(4,1)S(1)}, u32[]{:S(2)}) copy-start(pred[8,16]{1,0:T(8,128)(4,1)S(1)} %get-tuple-element.144) | copy-start | bytes 388
  24.9 21.9 %copy-start.104 = (pred[8,16]{1,0:T(8,128)(4,1)}, pred[8,16]{1,0:T(8,128)(4,1)S(1)}, u32[]{:S(2)}) copy-start(pred[8,16]{1,0:T(8,128)(4,1)S(1)} %get-tuple-element.145) | copy-start | bytes 388
  24.9 21.9 %copy-start.106 = (pred[8,16]{1,0:T(8,128)(4,1)}, pred[8,16]{1,0:T(8,128)(4,1)S(1)}, u32[]{:S(2)}) copy-start(pred[8,16]{1,0:T(8,128)(4,1)S(1)} %get-tuple-element.146) | copy-start | bytes 388
  24.9 21.9 %copy-start.108 = (pred[8,16]{1,0:T(8,128)(4,1)}, pred[8,16]{1,0:T(8,128)(4,1)S(1)}, u32[]{:S(2)}) copy-start(pred[8,16]{1,0:T(8,128)(4,1)S(1)} %get-tuple-element.147) | copy-start | bytes 388
  25.0 21.9 %copy-start.110 = (pred[8,16]{1,0:T(8,128)(4,1)}, pred[8,16]{1,0:T(8,128)(4,1)S(1)}, u32[]{:S(2)}) copy-start(pred[8,16]{1,0:T(8,128)(4,1)S(1)} %get-tuple-element.148) | copy-start | bytes 388
  25.0 26.0 %copy-start.80 = (pred[8,16]{1,0:T(8,128)(4,1)}, pred[8,16]{1,0:T(8,128)(4,1)S(1)}, u32[]{:S(2)}) copy-start(pred[8,16]{1,0:T(8,128)(4,1)S(1)} %get-tuple-element.135) | copy-start | bytes 388
  25.0 26.0 %copy-start.83 = (pred[8,16]{1,0:T(8,128)(4,1)}, pred[8,16]{1,0:T(8,128)(4,1)S(1)}, u32[]{:S(2)}) copy-start(pred[8,16]{1,0:T(8,128)(4,1)S(1)} %get-tuple-element.136) | copy-start | bytes 388
  25.0 26.0 %copy-start.86 = (pred[8,16]{1,0:T(8,128)(4,1)}, pred[8,16]{1,0:T(8,128)(4,1)S(1)}, u32[]{:S(2)}) copy-start(pred[8,16]{1,0:T(8,128)(4,1)S(1)} %get-tuple-element.137) | copy-start | bytes 388
  25.0 26.0 %copy-start.89 = (pred[8,16]{1,0:T(8,128)(4,1)}, pred[8,16]{1,0:T(8,128)(4,1)S(1)}, u32[]{:S(2)}) copy-start(pred[8,16]{1,0:T(8,128)(4,1)S(1)} %get-tuple-element.138) | copy-start | bytes 388
  25.0 26.0 %copy-start.92 = (pred[8,16]{1,0:T(8,128)(4,1)}, pred[8,16]{1,0:T(8,128)(4,1)S(1)}, u32[]{:S(2)}) copy-start(pred[8,16]{1,0:T(8,128)(4,1)S(1)} %get-tuple-element.139) | copy-start | bytes 388
  25.0 26.0 %copy-start.94 = (pred[8,16]{1,0:T(8,128)(4,1)}, pred[8,16]{1,0:T(8,128)(4,1)S(1)}, u32[]{:S(2)}) copy-start(pred[8,16]{1,0:T(8,128)(4,1)S(1)} %get-tuple-element.140) | copy-start | bytes 388
  25.0 26.0 %copy-start.96 = (pred[8,16]{1,0:T(8,128)(4,1)}, pred[8,16]{1,0:T(8,128)(4,1)S(1)}, u32[]{:S(2)}) copy-start(pred[8,16]{1,0:T(8,128)(4,1)S(1)} %get-tuple-element.141) | copy-start | bytes 388
  25.0 26.0 %copy-start.98 = (pred[8,16]{1,0:T(8,128)(4,1)}, pred[8,16]{1,0:T(8,128)(4,1)S(1)}, u32[]{:S(2)}) copy-start(pred[8,16]{1,0:T(8,128)(4,1)S(1)} %get-tuple-element.142) | copy-start | bytes 388
  25.0 26.0 %copy-start.112 = (pred[8,16]{1,0:T(8,128)(4,1)}, pred[8,16]{1,0:T(8,128)(4,1)S(1)}, u32[]{:S(2)}) copy-start(pred[8,16]{1,0:T(8,128)(4,1)S(1)} %get-tuple-element.134) | copy-start | bytes 388
  83.2 17.4 %collective-permute-start.9 = (f32[1,16,4096]{2,1,0:T(8,128)S(1)}, f32[1,16,4096]{2,1,0:T(8,128)S(1)}, u32[]{:S(2)}, u32[]{:S(2)}) collective-permute-start(f32[1,16,4096]{2,1,0:T(8,128)S(1)} %get-tuple-element.52), channel_id=1, source_target_pairs={{1,0},{2,1},{3,2},{4,3},{5,4},{6,5},{7,6},{8,7},{9,8},{10,9},{11,1... | collective-permute-start | bytes 786440 | tf_op jit(solution)/shard_map/ppermute | solution.py:26
  94.8 42.1 %copy-start.81 = (pred[8,16]{1,0:T(8,128)(4,1)S(1)}, pred[8,16]{1,0:T(8,128)(4,1)}, u32[]{:S(2)}) copy-start(pred[8,16]{1,0:T(8,128)(4,1)} %copy-done.80) | copy-start | bytes 388
  94.8 42.1 %copy-start.84 = (pred[8,16]{1,0:T(8,128)(4,1)S(1)}, pred[8,16]{1,0:T(8,128)(4,1)}, u32[]{:S(2)}) copy-start(pred[8,16]{1,0:T(8,128)(4,1)} %copy-done.83) | copy-start | bytes 388
  94.9 42.1 %copy-start.87 = (pred[8,16]{1,0:T(8,128)(4,1)S(1)}, pred[8,16]{1,0:T(8,128)(4,1)}, u32[]{:S(2)}) copy-start(pred[8,16]{1,0:T(8,128)(4,1)} %copy-done.86) | copy-start | bytes 388
  94.9 42.1 %copy-start.90 = (pred[8,16]{1,0:T(8,128)(4,1)S(1)}, pred[8,16]{1,0:T(8,128)(4,1)}, u32[]{:S(2)}) copy-start(pred[8,16]{1,0:T(8,128)(4,1)} %copy-done.89) | copy-start | bytes 388
  94.9 9.0 %collective-permute-start.3 = (f32[1,16,4096]{2,1,0:T(8,128)S(1)}, f32[1,16,4096]{2,1,0:T(8,128)S(1)}, u32[]{:S(2)}, u32[]{:S(2)}) collective-permute-start(f32[1,16,4096]{2,1,0:T(8,128)S(1)} %fusion.72), channel_id=1, source_target_pairs={{0,1},{1,2},{2,3},{3,4},{4,5},{5,6},{6,7},{7,8},{8,9},{9,10},{10,1... | collective-permute-start | bytes 786440 | tf_op jit(solution)/shard_map/ppermute | solution.py:24
  104.7 10.3 %collective-permute-start.4 = (f32[1,16,4096]{2,1,0:T(8,128)S(1)}, f32[1,16,4096]{2,1,0:T(8,128)S(1)}, u32[]{:S(2)}, u32[]{:S(2)}) collective-permute-start(f32[1,16,4096]{2,1,0:T(8,128)S(1)} %get-tuple-element.112), channel_id=1, source_target_pairs={{0,2},{1,3},{2,4},{3,5},{4,6},{5,7},{6,8},{7,9},{8,10},{9,11},{10,... | collective-permute-start | bytes 786440 | tf_op jit(solution)/shard_map/ppermute | solution.py:24
  115.7 14.3 %collective-permute-start.5 = (f32[1,16,4096]{2,1,0:T(8,128)}, f32[1,16,4096]{2,1,0:T(8,128)}, u32[]{:S(2)}, u32[]{:S(2)}) collective-permute-start(f32[1,16,4096]{2,1,0:T(8,128)} %fusion.102), channel_id=1, source_target_pairs={{0,4},{1,5},{2,6},{3,7},{4,8},{5,9},{6,10},{7,11},{8,12},{9,13},{1... | collective-permute-start | bytes 786440 | tf_op jit(solution)/shard_map/ppermute | solution.py:24
  131.2 27.6 %copy-start.31 = (f32[16,4096]{1,0:T(8,128)S(1)}, f32[16,4096]{1,0:T(8,128)}, u32[]{:S(2)}) copy-start(f32[16,4096]{1,0:T(8,128)} %get-tuple-element.131) | copy-start | bytes 786436
  131.2 15.1 %collective-permute-start.6 = (f32[1,16,4096]{2,1,0:T(8,128)S(1)}, f32[1,16,4096]{2,1,0:T(8,128)S(1)}, u32[]{:S(2)}, u32[]{:S(2)}) collective-permute-start(f32[1,16,4096]{2,1,0:T(8,128)S(1)} %fusion.101), channel_id=1, source_target_pairs={{0,8},{1,9},{2,10},{3,11},{4,12},{5,13},{6,14},{7,15},{8,16},{9,17... | collective-permute-start | bytes 786440 | tf_op jit(solution)/shard_map/ppermute | solution.py:24
  146.4 16.7 %collective-permute-start.7 = (f32[1,16,4096]{2,1,0:T(8,128)S(1)}, f32[1,16,4096]{2,1,0:T(8,128)S(1)}, u32[]{:S(2)}, u32[]{:S(2)}) collective-permute-start(f32[1,16,4096]{2,1,0:T(8,128)S(1)} %fusion.100), channel_id=1, source_target_pairs={{0,16},{1,17},{2,18},{3,19},{4,20},{5,21},{6,22},{7,23},{8,24},{9,... | collective-permute-start | bytes 786440 | tf_op jit(solution)/shard_map/ppermute | solution.py:24
  163.2 9.9 %collective-permute-start.8 = (f32[1,16,4096]{2,1,0:T(8,128)S(1)}, f32[1,16,4096]{2,1,0:T(8,128)S(1)}, u32[]{:S(2)}, u32[]{:S(2)}) collective-permute-start(f32[1,16,4096]{2,1,0:T(8,128)S(1)} %fusion.99), channel_id=1, source_target_pairs={{0,1},{1,2},{2,3},{3,4},{4,5},{5,6},{6,7},{7,8},{8,9},{9,10},{10,1... | collective-permute-start | bytes 786440 | tf_op jit(solution)/shard_map/ppermute | solution.py:29
  164.8 65.2 %copy-start.51 = (f32[1,4096]{1,0:T(1,128)}, f32[1,4096]{1,0:T(1,128)S(1)}, u32[]{:S(2)}) copy-start(f32[1,4096]{1,0:T(1,128)S(1)} %get-tuple-element.117) | copy-start | bytes 49156
  164.8 65.2 %copy-start.53 = (f32[1,4096]{1,0:T(1,128)}, f32[1,4096]{1,0:T(1,128)S(1)}, u32[]{:S(2)}) copy-start(f32[1,4096]{1,0:T(1,128)S(1)} %get-tuple-element.118) | copy-start | bytes 49156
  164.8 65.2 %copy-start.55 = (f32[1,4096]{1,0:T(1,128)}, f32[1,4096]{1,0:T(1,128)S(1)}, u32[]{:S(2)}) copy-start(f32[1,4096]{1,0:T(1,128)S(1)} %get-tuple-element.119) | copy-start | bytes 49156
  164.8 65.2 %copy-start.57 = (f32[1,4096]{1,0:T(1,128)}, f32[1,4096]{1,0:T(1,128)S(1)}, u32[]{:S(2)}) copy-start(f32[1,4096]{1,0:T(1,128)S(1)} %get-tuple-element.120) | copy-start | bytes 49156
  164.8 65.2 %copy-start.59 = (f32[1,4096]{1,0:T(1,128)}, f32[1,4096]{1,0:T(1,128)S(1)}, u32[]{:S(2)}) copy-start(f32[1,4096]{1,0:T(1,128)S(1)} %get-tuple-element.121) | copy-start | bytes 49156
  164.8 65.2 %copy-start.61 = (f32[1,4096]{1,0:T(1,128)}, f32[1,4096]{1,0:T(1,128)S(1)}, u32[]{:S(2)}) copy-start(f32[1,4096]{1,0:T(1,128)S(1)} %get-tuple-element.122) | copy-start | bytes 49156
  164.8 65.2 %copy-start.63 = (f32[1,4096]{1,0:T(1,128)}, f32[1,4096]{1,0:T(1,128)S(1)}, u32[]{:S(2)}) copy-start(f32[1,4096]{1,0:T(1,128)S(1)} %get-tuple-element.123) | copy-start | bytes 49156
  164.8 65.2 %copy-start.65 = (f32[1,4096]{1,0:T(1,128)}, f32[1,4096]{1,0:T(1,128)S(1)}, u32[]{:S(2)}) copy-start(f32[1,4096]{1,0:T(1,128)S(1)} %get-tuple-element.124) | copy-start | bytes 49156
  164.8 65.2 %copy-start.67 = (f32[1,4096]{1,0:T(1,128)}, f32[1,4096]{1,0:T(1,128)S(1)}, u32[]{:S(2)}) copy-start(f32[1,4096]{1,0:T(1,128)S(1)} %get-tuple-element.125) | copy-start | bytes 49156
  164.8 65.2 %copy-start.69 = (f32[1,4096]{1,0:T(1,128)}, f32[1,4096]{1,0:T(1,128)S(1)}, u32[]{:S(2)}) copy-start(f32[1,4096]{1,0:T(1,128)S(1)} %get-tuple-element.126) | copy-start | bytes 49156
  164.9 65.2 %copy-start.71 = (f32[1,4096]{1,0:T(1,128)}, f32[1,4096]{1,0:T(1,128)S(1)}, u32[]{:S(2)}) copy-start(f32[1,4096]{1,0:T(1,128)S(1)} %get-tuple-element.127) | copy-start | bytes 49156
  164.9 65.2 %copy-start.73 = (f32[1,4096]{1,0:T(1,128)}, f32[1,4096]{1,0:T(1,128)S(1)}, u32[]{:S(2)}) copy-start(f32[1,4096]{1,0:T(1,128)S(1)} %get-tuple-element.128) | copy-start | bytes 49156
  164.9 9.8 %collective-permute-start.10 = (f32[1,16,4096]{2,1,0:T(8,128)S(1)}, f32[1,16,4096]{2,1,0:T(8,128)S(1)}, u32[]{:S(2)}, u32[]{:S(2)}) collective-permute-start(f32[1,16,4096]{2,1,0:T(8,128)S(1)} %copy-done.50), channel_id=1, source_target_pairs={{2,0},{3,1},{4,2},{5,3},{6,4},{7,5},{8,6},{9,7},{10,8},{11,9},{12,... | collective-permute-start | bytes 786440 | tf_op jit(solution)/shard_map/ppermute | solution.py:26
  175.5 8.3 %collective-permute-start.11 = (f32[1,16,4096]{2,1,0:T(8,128)S(1)}, f32[1,16,4096]{2,1,0:T(8,128)S(1)}, u32[]{:S(2)}, u32[]{:S(2)}) collective-permute-start(f32[1,16,4096]{2,1,0:T(8,128)S(1)} %get-tuple-element.50), channel_id=1, source_target_pairs={{4,0},{5,1},{6,2},{7,3},{8,4},{9,5},{10,6},{11,7},{12,8},{13,9},{1... | collective-permute-start | bytes 786440 | tf_op jit(solution)/shard_map/ppermute | solution.py:26
  184.6 15.9 %collective-permute-start.12 = (f32[1,16,4096]{2,1,0:T(8,128)S(1)}, f32[1,16,4096]{2,1,0:T(8,128)S(1)}, u32[]{:S(2)}, u32[]{:S(2)}) collective-permute-start(f32[1,16,4096]{2,1,0:T(8,128)S(1)} %get-tuple-element.108), channel_id=1, source_target_pairs={{8,0},{9,1},{10,2},{11,3},{12,4},{13,5},{14,6},{15,7},{16,8},{17,9... | collective-permute-start | bytes 786440 | tf_op jit(solution)/shard_map/ppermute | solution.py:26
  201.3 14.9 %collective-permute-start.13 = (f32[1,16,4096]{2,1,0:T(8,128)S(1)}, f32[1,16,4096]{2,1,0:T(8,128)S(1)}, u32[]{:S(2)}, u32[]{:S(2)}) collective-permute-start(f32[1,16,4096]{2,1,0:T(8,128)S(1)} %get-tuple-element.107), channel_id=1, source_target_pairs={{16,0},{17,1},{18,2},{19,3},{20,4},{21,5},{22,6},{23,7},{24,8},{25... | collective-permute-start | bytes 786440 | tf_op jit(solution)/shard_map/ppermute | solution.py:26
  217.0 22.0 %collective-permute-start.14 = (f32[1,16,4096]{2,1,0:T(8,128)S(1)}, f32[1,16,4096]{2,1,0:T(8,128)S(1)}, u32[]{:S(2)}, u32[]{:S(2)}) collective-permute-start(f32[1,16,4096]{2,1,0:T(8,128)S(1)} %get-tuple-element.106), channel_id=1, source_target_pairs={{1,0},{2,1},{3,2},{4,3},{5,4},{6,5},{7,6},{8,7},{9,8},{10,9},{11,1... | collective-permute-start | bytes 786440 | tf_op jit(solution)/shard_map/ppermute | solution.py:29
  292.3 8.4 %collective-permute-start.18 = (f32[16,38,128]{2,1,0:T(8,128)S(1)}, f32[16,38,128]{2,1,0:T(8,128)}, u32[]{:S(2)}, u32[]{:S(2)}) collective-permute-start(f32[16,38,128]{2,1,0:T(8,128)S(1)} %select_n.592), channel_id=1, source_target_pairs={{0,1},{1,0},{2,3},{3,2},{4,5},{5,4},{6,7},{7,6},{8,9},{9,8},{10,11... | collective-permute-start | bytes 933896 | tf_op jit(solution)/shard_map/ppermute | solution.py:59
  295.1 56.4 %copy-start.12 = (f32[1,1,128,4096]{3,2,1,0:T(8,128)S(1)}, f32[1,1,128,4096]{3,2,1,0:T(8,128)}, u32[]{:S(2)}) copy-start(f32[1,1,128,4096]{3,2,1,0:T(8,128)} %copy-done.11) | copy-start | bytes 6291460
  301.7 12.5 %collective-permute-start.19 = (f32[8,38,128]{2,1,0:T(8,128)S(1)}, f32[8,38,128]{2,1,0:T(8,128)S(1)}, u32[]{:S(2)}, u32[]{:S(2)}) collective-permute-start(f32[8,38,128]{2,1,0:T(8,128)S(1)} %slice_select_fusion.2), channel_id=1, source_target_pairs={{0,4},{1,5},{2,6},{3,7},{4,0},{5,1},{6,2},{7,3},{8,12},{9,13},{10,... | collective-permute-start | bytes 466952 | tf_op jit(solution)/shard_map/ppermute | solution.py:59
  314.3 6.0 %collective-permute-start.20 = (f32[4,38,128]{2,1,0:T(8,128)S(1)}, f32[4,38,128]{2,1,0:T(8,128)S(1)}, u32[]{:S(2)}, u32[]{:S(2)}) collective-permute-start(f32[4,38,128]{2,1,0:T(8,128)S(1)} %slice_select_fusion.3), channel_id=1, source_target_pairs={{0,2},{1,3},{2,0},{3,1},{4,6},{5,7},{6,4},{7,5},{8,10},{9,11},{10,... | collective-permute-start | bytes 233480 | tf_op jit(solution)/shard_map/ppermute | solution.py:59
  320.4 5.0 %collective-permute-start.21 = (f32[2,38,128]{2,1,0:T(8,128)S(1)}, f32[2,38,128]{2,1,0:T(8,128)S(1)}, u32[]{:S(2)}, u32[]{:S(2)}) collective-permute-start(f32[2,38,128]{2,1,0:T(8,128)S(1)} %slice_select_fusion.4), channel_id=1, source_target_pairs={{0,8},{1,9},{2,10},{3,11},{4,12},{5,13},{6,14},{7,15},{8,0},{9,1},... | collective-permute-start | bytes 116744 | tf_op jit(solution)/shard_map/ppermute | solution.py:59
  325.4 7.9 %collective-permute-start.22 = (f32[1,38,128]{2,1,0:T(8,128)S(1)}, f32[1,38,128]{2,1,0:T(8,128)S(1)}, u32[]{:S(2)}, u32[]{:S(2)}) collective-permute-start(f32[1,38,128]{2,1,0:T(8,128)S(1)} %slice_select_fusion.5), channel_id=1, source_target_pairs={{0,16},{1,17},{2,18},{3,19},{4,20},{5,21},{6,22},{7,23},{8,24},{9,... | collective-permute-start | bytes 58376 | tf_op jit(solution)/shard_map/ppermute | solution.py:59
  333.3 1.2 collective-permute-start.23
  334.5 3.8 collective-permute-start.24
  338.3 5.3 %collective-permute-start.25 = (f32[1,38,128]{2,1,0:T(8,128)S(1)}, f32[1,38,128]{2,1,0:T(8,128)S(1)}, u32[]{:S(2)}, u32[]{:S(2)}) collective-permute-start(f32[1,38,128]{2,1,0:T(8,128)S(1)} %add.507), channel_id=1, source_target_pairs={{0,128},{32,160},{64,192},{96,224},{128,0},{160,32},{192,64},{224,... | collective-permute-start | bytes 58376 | tf_op jit(solution)/shard_map/ppermute | solution.py:40
  343.6 7.7 %collective-permute-start.26 = (f32[1,38,128]{2,1,0:T(8,128)S(1)}, f32[1,38,128]{2,1,0:T(8,128)S(1)}, u32[]{:S(2)}, u32[]{:S(2)}) collective-permute-start(f32[1,38,128]{2,1,0:T(8,128)S(1)} %add.508), channel_id=1, source_target_pairs={{0,16},{1,17},{2,18},{3,19},{4,20},{5,21},{6,22},{7,23},{8,24},{9,... | collective-permute-start | bytes 58376 | tf_op jit(solution)/shard_map/ppermute | solution.py:62
  351.4 11.8 %collective-permute-start.27 = (f32[2,38,128]{2,1,0:T(8,128)S(1)}, f32[2,38,128]{2,1,0:T(8,128)S(1)}, u32[]{:S(2)}, u32[]{:S(2)}) collective-permute-start(f32[2,38,128]{2,1,0:T(8,128)S(1)} %maximum_select_fusion.4), channel_id=1, source_target_pairs={{0,8},{1,9},{2,10},{3,11},{4,12},{5,13},{6,14},{7,15},{8,0},{9,1},... | collective-permute-start | bytes 116744 | tf_op jit(solution)/shard_map/ppermute | solution.py:62
  363.1 17.2 %collective-permute-start.28 = (f32[4,38,128]{2,1,0:T(8,128)S(1)}, f32[4,38,128]{2,1,0:T(8,128)S(1)}, u32[]{:S(2)}, u32[]{:S(2)}) collective-permute-start(f32[4,38,128]{2,1,0:T(8,128)S(1)} %maximum_select_fusion.3), channel_id=1, source_target_pairs={{0,2},{1,3},{2,0},{3,1},{4,6},{5,7},{6,4},{7,5},{8,10},{9,11},{10,... | collective-permute-start | bytes 233480 | tf_op jit(solution)/shard_map/ppermute | solution.py:62
  380.4 7.2 %collective-permute-start.29 = (f32[8,38,128]{2,1,0:T(8,128)S(1)}, f32[8,38,128]{2,1,0:T(8,128)S(1)}, u32[]{:S(2)}, u32[]{:S(2)}) collective-permute-start(f32[8,38,128]{2,1,0:T(8,128)S(1)} %maximum_select_fusion.2), channel_id=1, source_target_pairs={{0,4},{1,5},{2,6},{3,7},{4,0},{5,1},{6,2},{7,3},{8,12},{9,13},{10,... | collective-permute-start | bytes 466952 | tf_op jit(solution)/shard_map/ppermute | solution.py:62
  382.5 8.3 %collective-permute-start.17 = (f32[1,6,4096]{2,1,0:T(8,128)S(1)}, f32[1,6,4096]{2,1,0:T(8,128)S(1)}, u32[]{:S(2)}, u32[]{:S(2)}) collective-permute-start(f32[1,6,4096]{2,1,0:T(8,128)S(1)} %get-tuple-element.65), channel_id=1, source_target_pairs={{1,0},{2,1},{3,2},{4,3},{5,4},{6,5},{7,6},{8,7},{9,8},{10,9},{11,1... | collective-permute-start | bytes 294920 | tf_op jit(solution)/shard_map/ppermute | solution.py:12
  383.8 9.8 %collective-permute-start.16 = (f32[1,6,4096]{2,1,0:T(8,128)S(1)}, f32[1,6,4096]{2,1,0:T(8,128)S(1)}, u32[]{:S(2)}, u32[]{:S(2)}) collective-permute-start(f32[1,6,4096]{2,1,0:T(8,128)S(1)} %get-tuple-element.66), channel_id=1, source_target_pairs={{1,0},{2,1},{3,2},{4,3},{5,4},{6,5},{7,6},{8,7},{9,8},{10,9},{11,1... | collective-permute-start | bytes 294920 | tf_op jit(solution)/shard_map/ppermute | solution.py:12
  385.1 11.0 %collective-permute-start.15 = (f32[1,6,4096]{2,1,0:T(8,128)S(1)}, f32[1,6,4096]{2,1,0:T(8,128)S(1)}, u32[]{:S(2)}, u32[]{:S(2)}) collective-permute-start(f32[1,6,4096]{2,1,0:T(8,128)S(1)} %get-tuple-element.67), channel_id=1, source_target_pairs={{1,0},{2,1},{3,2},{4,3},{5,4},{6,5},{7,6},{8,7},{9,8},{10,9},{11,1... | collective-permute-start | bytes 294920 | tf_op jit(solution)/shard_map/ppermute | solution.py:12
  387.6 12.1 %collective-permute-start.30 = (f32[16,38,128]{2,1,0:T(8,128)S(1)}, f32[16,38,128]{2,1,0:T(8,128)S(1)}, u32[]{:S(2)}, u32[]{:S(2)}) collective-permute-start(f32[16,38,128]{2,1,0:T(8,128)S(1)} %maximum_select_fusion.1), channel_id=1, source_target_pairs={{0,1},{1,0},{2,3},{3,2},{4,5},{5,4},{6,7},{7,6},{8,9},{9,8},{10,11... | collective-permute-start | bytes 933896 | tf_op jit(solution)/shard_map/ppermute | solution.py:62
  (100 other events, 926.6 us)

commit v4 on v3

--- a/solution.py
+++ b/solution.py
@@ -226,7 +226,6 @@
             + short_taps[:, tap_index][:, None, None, :]
             * padded[:, :, tap_index : tap_index + tok_len + rim_len, :]
         )
-        tap_terms.append(jnp.sum(window(tap_index) * short_grads, axis=(1, 2)))
     heads = spread[:, :, :rim_len, :]
     owns = spread[:, :, rim_len:, :]
     incoming = from_behind((heads[0], heads[1], heads[2]), "ctx", -1)
@@ -237,12 +236,24 @@
         ).astype(jnp.bfloat16)
         for branch_index in range(3)
     ]
-    tap_stack = jnp.stack(tap_terms, axis=1)
-    flat = jnp.concatenate([tap_stack.reshape(-1), skip_term, residue_term.reshape(-1)])
-    flat = spread_sum(flat, "ctx", ("dp",))
-    taps_sum = flat[: tap_stack.size].reshape(tap_stack.shape)
-    skip_sum = flat[tap_stack.size : tap_stack.size + skip_term.size]
-    residue_sum = flat[tap_stack.size + skip_term.size :].reshape(residue_term.shape)
+    query_taps = jnp.stack(
+        [jnp.sum(window(tap_index)[0] * query_short_grad, axis=(0, 1)) for tap_index in range(tap_count)]
+    )
+    early = jnp.concatenate([query_taps.reshape(-1), skip_term, residue_term.reshape(-1)])
+    early = spread_sum(early, "ctx", ("dp",))
+    late_taps = jnp.stack(
+        [
+            jnp.sum(window(tap_index)[1:] * short_grads[1:], axis=(1, 2))
+            for tap_index in range(tap_count)
+        ],
+        axis=1,
+    )
+    late = spread_sum(late_taps.reshape(-1), "ctx", ("dp",))
+    taps_sum = jnp.concatenate(
+        [early[: query_taps.size].reshape((1,) + query_taps.shape), late.reshape(late_taps.shape)]
+    )
+    skip_sum = early[query_taps.size : query_taps.size + skip_term.size]
+    residue_sum = early[query_taps.size + skip_term.size :].reshape(residue_term.shape)
     scale = 1.0 / math.sqrt(total_tokens)
     return (
         mixed_out,

time: 407 us -> 429 us (1.054)
  starting transfers between devices: 94.1 us -> 118 us
  other arithmetic: 173 us -> 194 us
  waiting for transfers between devices: 96.9 us -> 75.9 us
    select_n x0 -> x1, other arithmetic: none -> 15.1 us  [window(): return jnp.where(tap_masks[tap_index], piece, 0.0)]
    ppermute x5 -> x10, starting transfers between devices: 11 us -> 25.1 us  [spread_sum(): lax.ppermute(blocks, scatter_axis, [(i, i ^ step) for i in range(count)])]
    ppermute x5 -> x10, starting transfers between devices: 17.6 us -> 28.4 us  [spread_sum(): lax.ppermute(send, scatter_axis, [(i, i ^ step) for i in range(count)])]
    reduce_sum x2 -> x1, other arithmetic: 20 us -> 12.5 us  [shards(): jnp.sum(window(tap_index)[1:] * short_grads[1:], axis=(1, 2))]
    ppermute x3 -> x6, waiting for transfers between devices: 7.59 us -> 1.09 us  [butterfly_sum(): lax.ppermute(value, axis, [(i, i ^ step) for i in range(count)])]
    ppermute x5 -> x10, waiting for transfers between devices: 22.2 us -> 15.8 us  [spread_sum(): lax.ppermute(send, scatter_axis, [(i, i ^ step) for i in range(count)])]
    ppermute x5, waiting for transfers between devices: 10.3 us -> 4.45 us  [device_scan(): lax.ppermute(sums, 'ctx', route)]
    ppermute x6, waiting for transfers between devices: 5.72 us -> 0.02 us  [from_behind(): return lax.ppermute(block, axis, route)]
  transfers between devices with their start and end apart: 31 -> 44, of which waited for: 22 -> 23; matrix products, arithmetic and copies ran while one was open for 20% -> 24% of each run, Pallas kernels for 0% -> 0%
where the time goes in v4:
time: 429 us; the launch traced here: 423 us
  other arithmetic  194 us (45%)
  starting transfers between devices  118 us (28%)
  waiting for transfers between devices  75.9 us (18%)
  local copies, waits for them, and re-layouts  25.2 us (6%)
  between operations  10.2 us (2%)
    ppermute x5, waiting for transfers between devices, device_scan(): lax.ppermute(gate * sums, 'ctx', route)  39.8 us
    ppermute x5, starting transfers between devices, device_scan(): lax.ppermute(sums, 'ctx', route)  35.6 us
    ppermute x10, starting transfers between devices, spread_sum(): lax.ppermute(send, scatter_axis, [(i, i ^ step) for i in range(count)])  28.4 us
    ppermute x10, starting transfers between devices, spread_sum(): lax.ppermute(blocks, scatter_axis, [(i, i ^ step) for i in range(count)])  25.1 us
    select_n x2, other arithmetic, shards(): masked = jnp.where(tap_masks[tap_index], short_grads, 0.0)  16.6 us
    ppermute x10, waiting for transfers between devices, spread_sum(): lax.ppermute(send, scatter_axis, [(i, i ^ step) for i in range(count)])  15.8 us
    select_n x1, other arithmetic, window(): return jnp.where(tap_masks[tap_index], piece, 0.0)  15.1 us
    ppermute x6, starting transfers between devices, from_behind(): return lax.ppermute(block, axis, route)  14 us
  transfers between devices with their start and end apart: 44, of which 23 were waited for; matrix products, arithmetic and copies ran while one was open for 24% of the time, Pallas kernels for 0%

profile of v4, /device:TPU:2, one launch (start us, length us, event | category | flops | bytes accessed | tf_op | source)
XLA Modules:
  0.0 423.2 jit_solution(3210889540823457727)
XLA Ops:
  1.6 3.5 collective-permute-start.2
  5.9 3.5 collective-permute-start.1
  10.3 3.2 collective-permute-start
  19.8 2.6 fusion.151
  23.4 2.1 fusion.140
  29.1 9.6 %multiply_add_fusion = f32[3,1,128,4096]{3,2,1,0:T(8,128)S(1)} fusion(f32[3,4096]{1,0:T(4,128)S(1)} %get-tuple-element.185, f32[3,4096]{1,0:T(4,128)S(1)} %get-tuple-element.186, f32[3,4096]{1,0:T(4,128)S(1)} %get-tuple-element.187, f32[3,4096]{1,0:T(4,128)S(1)} %get-tuple-element.188, f32[3,4096]{1,0:T(4,128)S(1)} %get-tuple-element.189, ...), kind=kLoop, calls=%fused_computation.40 | loop fusion | flops 42467328 | bytes 28656512 | tf_op jit(solution)/shard_map/add | solution.py:115
  39.0 1.7 copy-done.27
  40.8 1.9 broadcast_select_fusion.7
  42.7 2.5 multiply_reduce_fusion.23
  45.3 4.1 multiply_reduce_fusion.16
  49.5 4.5 %multiply_reduce_fusion.7 = (f32[4096]{0:T(1024)}, f32[4096]{0:T(1024)}, f32[4096]{0:T(1024)}, f32[4096]{0:T(1024)}, f32[4096]{0:T(1024)}, /*index=5*/f32[4096]{...) fusion(f32[1,8,16,4096]{3,2,1,0:T(8,128)S(1)} %bitcast.565, f32[1,8,16,4096]{3,2,1,0:T(8,128)S(1)} %bitcast.570, ...), kind=kLoop, calls=%fused_computation.181 | loop fusion | flops 14118912 | bytes 4342912 | tf_op jit(solution)/shard_map/reduce_sum | solution.py:200
  54.0 3.3 stack.231
  57.3 7.9 %fusion.20 = (f32[16,16,4096]{2,1,0:T(8,128)}, f32[16,16,4096]{2,1,0:T(8,128)}, f32[16,4096]{1,0:T(8,128)}, f32[16,4096]{1,0:T(8,128)}, f32[16,16,4096]{2,1,0:T(8,128)}) fusion(f32[16,4096]{1,0:T(8,128)} %get-tuple-element.148, f32[16,4096]{1,0:T(8,128)} %get-tuple-element.149, f32[16]{0:T(128)} %iota_convert_fusion, f32[16,4096]{1,0:T(8,128)} %get-tuple-element.150, ...), kind=kLoop, calls=%fused_computation.82 | loop fusion | flops 7208960 | bytes 14155840 | tf_op jit(solution)/shard_map/mul | solution.py:126
  65.3 4.6 %rev.6 = f32[16,16,4096]{2,1,0:T(8,128)} reverse(f32[16,16,4096]{2,1,0:T(8,128)} %get-tuple-element.122), dimensions={0} | reverse | bytes 8388608 | tf_op jit(solution)/shard_map/rev | solution.py:127
  69.9 2.0 broadcast_multiply_fusion.1
  72.7 2.7 multiply_reduce_fusion.1
  75.4 5.9 %multiply_bitcast_fusion = (f32[1,16,4096]{2,1,0:T(8,128)S(1)}, f32[16,4096]{1,0:T(8,128)S(1)}) fusion(f32[]{:T(128)} %bitcast.106, f32[]{:T(128)} %bitcast.31, f32[1,8,16,4096]{3,2,1,0:T(8,128)S(1)} %bitcast.573, f32[]{:T(128)} %bitcast.33, f32[]{:T(128)} %bitcast.35, f32[]{:T(128)} %bitcast.37, f32[]{:T(128)} %bitcast.39, f32[]{:T(128)} %bitcast.41, ...), kind=kLoop, calls=%fused_computation.323 | loop fusion | flops 1769472 | bytes 2883620 | tf_op jit(solution)/shard_map/mul | solution.py:26
  83.0 1.9 copy-done.19
  84.9 2.7 multiply_reduce_fusion.3
  87.6 5.2 %fusion.92 = f32[1,16,4096]{2,1,0:T(8,128)S(1)} fusion(f32[1,8,16,4096]{3,2,1,0:T(8,128)S(1)} %bitcast.580, f32[]{:T(128)} %bitcast.45, f32[]{:T(128)} %bitcast.43, f32[]{:T(128)} %bitcast.41, f32[]{:T(128)} %bitcast.39, f32[]{:T(128)} %bitcast.37, f32[]{:T(128)} %bitcast.35, f32[]{:T(128)} %bitcast.33, f32[]{:T(128)} %bitcast.31, f32[16,4096]{1,0:T(8,128)S(1)} %copy-done.3), kind=kLoop, calls=%fused_computation.228 | loop fusion | flops 1703936 | bytes 2621472 | tf_op jit(solution)/shard_map/add | solution.py:156
  92.9 4.6 %collective-permute-start.3 = (f32[1,16,4096]{2,1,0:T(8,128)S(1)}, f32[1,16,4096]{2,1,0:T(8,128)S(1)}, u32[]{:S(2)}, u32[]{:S(2)}) collective-permute-start(f32[1,16,4096]{2,1,0:T(8,128)S(1)} %fusion.92), channel_id=1, source_target_pairs={{0,1},{1,2},{2,3},{3,4},{4,5},{5,6},{6,7},{7,8},{8,9},{9,10},{10,1... | collective-permute-start | bytes 786440 | tf_op jit(solution)/shard_map/ppermute | solution.py:24
  98.7 3.1 collective-permute-done.3
  102.7 6.7 %collective-permute-start.4 = (f32[1,16,4096]{2,1,0:T(8,128)}, f32[1,16,4096]{2,1,0:T(8,128)}, u32[]{:S(2)}, u32[]{:S(2)}) collective-permute-start(f32[1,16,4096]{2,1,0:T(8,128)} %get-tuple-element.131), channel_id=1, source_target_pairs={{0,2},{1,3},{2,4},{3,5},{4,6},{5,7},{6,8},{7,9},{8,10},{9,11},{10,... | collective-permute-start | bytes 786440 | tf_op jit(solution)/shard_map/ppermute | solution.py:24
  115.3 9.0 %collective-permute-start.5 = (f32[1,16,4096]{2,1,0:T(8,128)S(1)}, f32[1,16,4096]{2,1,0:T(8,128)S(1)}, u32[]{:S(2)}, u32[]{:S(2)}) collective-permute-start(f32[1,16,4096]{2,1,0:T(8,128)S(1)} %fusion.122), channel_id=1, source_target_pairs={{0,4},{1,5},{2,6},{3,7},{4,8},{5,9},{6,10},{7,11},{8,12},{9,13},{1... | collective-permute-start | bytes 786440 | tf_op jit(solution)/shard_map/ppermute | solution.py:24
  124.3 15.1 %convert_select_fusion.6 = (f32[3,1,128,4096]{3,2,1,0:T(8,128)}, f32[3,1,128,4096]{3,2,1,0:T(8,128)}, f32[3,1,128,4096]{3,2,1,0:T(8,128)}, f32[3,1,128,4096]{3,2...) fusion(bf16[3,1,134,4096]{3,2,1,0:T(8,128)(2,1)S(1)} %pad_maximum_fusion.2, ...), kind=kLoop, calls=%fused_computation.47 | loop fusion | flops 22020096 | bytes 66061184 | tf_op jit(solution)/shard_map/jit(_where)/select_n | solution.py:111
  139.5 5.3 %collective-permute-start.6 = (f32[1,16,4096]{2,1,0:T(8,128)S(1)}, f32[1,16,4096]{2,1,0:T(8,128)S(1)}, u32[]{:S(2)}, u32[]{:S(2)}) collective-permute-start(f32[1,16,4096]{2,1,0:T(8,128)S(1)} %fusion.121), channel_id=1, source_target_pairs={{0,8},{1,9},{2,10},{3,11},{4,12},{5,13},{6,14},{7,15},{8,16},{9,17... | collective-permute-start | bytes 786440 | tf_op jit(solution)/shard_map/ppermute | solution.py:24
  145.0 10.4 %broadcast_select_fusion.8 = (f32[1,8,16,4096]{3,2,1,0:T(8,128)}, f32[1,8,16,4096]{3,2,1,0:T(8,128)}, f32[1,8,16,4096]{3,2,1,0:T(8,128)}, f32[1,8,16,4096]{3,2,1...) fusion(pred[8,16]{1,0:T(8,128)(4,1)S(1)} %copy-done.85, ...), kind=kLoop, calls=%fused_computation.207 | loop fusion | flops 7340032 | bytes 31459072 | tf_op jit(solution)/shard_map/jit(_where)/select_n | solution.py:144
  155.5 10.0 %collective-permute-start.7 = (f32[1,16,4096]{2,1,0:T(8,128)S(1)}, f32[1,16,4096]{2,1,0:T(8,128)S(1)}, u32[]{:S(2)}, u32[]{:S(2)}) collective-permute-start(f32[1,16,4096]{2,1,0:T(8,128)S(1)} %fusion.120), channel_id=1, source_target_pairs={{0,16},{1,17},{2,18},{3,19},{4,20},{5,21},{6,22},{7,23},{8,24},{9,... | collective-permute-start | bytes 786440 | tf_op jit(solution)/shard_map/ppermute | solution.py:24
  165.6 2.5 reverse_multiply_fusion
  172.5 7.8 %collective-permute-done.8 = f32[1,16,4096]{2,1,0:T(8,128)S(1)} collective-permute-done((f32[1,16,4096]{2,1,0:T(8,128)S(1)}, f32[1,16,4096]{2,1,0:T(8,128)S(1)}, u32[]{:S(2)}, u32[]{:S(2)}) %collective-permute-start.8) | collective-permute-done | bytes 262176 | tf_op jit(solution)/shard_map/ppermute | solution.py:29
  183.1 13.0 %collective-permute-done.11 = f32[1,16,4096]{2,1,0:T(8,128)S(1)} collective-permute-done((f32[1,16,4096]{2,1,0:T(8,128)S(1)}, f32[1,16,4096]{2,1,0:T(8,128)S(1)}, u32[]{:S(2)}, u32[]{:S(2)}) %collective-permute-start.11) | collective-permute-done | bytes 262176 | tf_op jit(solution)/shard_map/ppermute | solution.py:26
  198.1 14.1 %collective-permute-done.12 = f32[1,16,4096]{2,1,0:T(8,128)S(1)} collective-permute-done((f32[1,16,4096]{2,1,0:T(8,128)S(1)}, f32[1,16,4096]{2,1,0:T(8,128)S(1)}, u32[]{:S(2)}, u32[]{:S(2)}) %collective-permute-start.12) | collective-permute-done | bytes 262176 | tf_op jit(solution)/shard_map/ppermute | solution.py:26
  214.4 12.0 %collective-permute-done.13 = f32[1,16,4096]{2,1,0:T(8,128)S(1)} collective-permute-done((f32[1,16,4096]{2,1,0:T(8,128)S(1)}, f32[1,16,4096]{2,1,0:T(8,128)S(1)}, u32[]{:S(2)}, u32[]{:S(2)}) %collective-permute-start.13) | collective-permute-done | bytes 262176 | tf_op jit(solution)/shard_map/ppermute | solution.py:26
  232.5 8.5 %multiply_reduce_fusion.2 = f32[8,16,4096]{2,1,0:T(8,128)S(1)} fusion(f32[8,16,4096]{2,1,0:T(8,128)S(1)} %bitcast.589, f32[16,16,4096]{2,1,0:T(8,128)S(1)} %copy-done.20), kind=kLoop, calls=%fused_computation.2 | loop fusion | flops 16252928 | bytes 8388608 | tf_op jit(solution)/shard_map/reduce_sum | solution.py:172
  241.4 7.1 %fusion.89 = f32[1,8,16,4096]{3,2,1,0:T(8,128)} fusion(f32[8,16,4096]{2,1,0:T(8,128)S(1)} %multiply_reduce_fusion.2, f32[1,8,16,4096]{3,2,1,0:T(8,128)S(1)} %bitcast.572, f32[8,16]{1,0:T(8,128)S(1)} %copy-done.83, f32[4096]{0:T(1024)S(1)} %bitcast.600, f32[4096]{0:T(1024)S(1)} %bitcast.602, f32[4096]{0:T(1024)S(1)} %bitcast.604, f32[4096]{0:T(1024)S(1)} %bitcast.606, ...), kind=kLoop, calls=%fused_computation.179 | loop fusion | flops 25690112 | bytes 6556160 | tf_op jit(solution)/shard_map/add | solution.py:175
  249.4 5.1 %bitcast_dynamic-update-slice_fusion.7 = (f32[8,1,16,4096]{3,2,1,0:T(8,128)S(1)}, f32[1,16,4096]{2,1,0:T(8,128)S(1)}, f32[1,16,4096]{2,1,0:T(8,128)S(1)}, f32[1,16,4096]{2,1,0:T(8,128)S(1)}) fusion(f32[1,8,16,4096]{3,2,1,0:T(8,128)S(1)} %bitcast.574, f32[]{:T(128)} %bitcast.43, f32[]{:T(128)} %bitcast.41, f32[16,4096]{1,0:T(8,128)S(1)} %copy-done.5, ...), kind=kLoop, calls=%fused_computation.237 | loop fusion | flops 1507327 | bytes 3407900
  257.6 8.4 %multiply_reduce_fusion = f32[8,16,4096]{2,1,0:T(8,128)S(1)} fusion(f32[8,16,4096]{2,1,0:T(8,128)S(1)} %bitcast.588, f32[16,16,4096]{2,1,0:T(8,128)S(1)} %copy-done.18), kind=kLoop, calls=%fused_computation | loop fusion | flops 16252928 | bytes 8388608 | tf_op jit(solution)/shard_map/reduce_sum | solution.py:189
  266.3 9.3 %fusion.37 = f32[1,8,16,4096]{3,2,1,0:T(8,128)} fusion(f32[1,8,16,4096]{3,2,1,0:T(8,128)} %get-tuple-element.110, f32[1,8,16,4096]{3,2,1,0:T(8,128)S(1)} %copy-done.23, f32[1,8,16,4096]{3,2,1,0:T(8,128)S(1)} %copy-done.24, f32[1,8,16,4096]{3,2,1,0:T(8,128)S(1)} %copy-done.25, f32[1,8,16,4096]{3,2,1,0:T(8,128)S(1)} %copy-done.26, ...), kind=kLoop, calls=%fused_computation.109 | loop fusion | flops 17825792 | bytes 38011520 | tf_op jit(solution)/shard_map/add | solution.py:192
  275.7 10.4 %fusion.87 = (f32[1,1,128,4096]{3,2,1,0:T(8,128)S(1)}, f32[1,1,128,4096]{3,2,1,0:T(8,128)S(1)}, bf16[1,128,4096]{2,1,0:T(8,128)(2,1)}, f32[4096]{0:T(1024)S(1)},...) fusion(f32[3,1,128,4096]{3,2,1,0:T(8,128)S(1)} %bitcast.568, ...), kind=kLoop, calls=%fused_computation.174 | loop fusion | flops 12554240 | bytes 37879808 | tf_op jit(solution)/shard_map/stack | solution.py:218
  286.1 12.5 %fusion.13 = (f32[2,4096]{1,0:T(2,128)S(1)}, f32[2,4096]{1,0:T(2,128)S(1)}, f32[2,4096]{1,0:T(2,128)S(1)}, f32[2,4096]{1,0:T(2,128)S(1)}, f32[2,4096]{1,0:T(2,12...) fusion(f32[3,1,128,4096]{3,2,1,0:T(8,128)} %get-tuple-element.91, f32[1,1,128,4096]{3,2,1,0:T(8,128)S(1)} %get-tuple-element.66, ...), kind=kLoop, calls=%fused_computation.49 | loop fusion | flops 15671296 | bytes 33783808 | tf_op jit(solution)/shard_map/reduce_sum | solution.py:246
  299.5 2.8 collective-permute-start.31
  302.4 2.9 collective-permute-done.31
  306.3 3.6 collective-permute-start.32
  309.9 2.1 collective-permute-start.18
  312.5 3.1 collective-permute-done.18
  315.7 2.0 collective-permute-done.33
  317.7 7.0 %collective-permute-start.34 = (f32[2,14,128]{2,1,0:T(8,128)S(1)}, f32[2,14,128]{2,1,0:T(8,128)S(1)}, u32[]{:S(2)}, u32[]{:S(2)}) collective-permute-start(f32[2,14,128]{2,1,0:T(8,128)S(1)} %slice_select_fusion.7), channel_id=1, source_target_pairs={{0,8},{1,9},{2,10},{3,11},{4,12},{5,13},{6,14},{7,15},{8,0},{9,1},... | collective-permute-start | bytes 43016 | tf_op jit(solution)/shard_map/ppermute | solution.py:59
  326.4 3.0 collective-permute-done.19
  330.1 4.4 %collective-permute-start.35 = (f32[1,14,128]{2,1,0:T(8,128)S(1)}, f32[1,14,128]{2,1,0:T(8,128)S(1)}, u32[]{:S(2)}, u32[]{:S(2)}) collective-permute-start(f32[1,14,128]{2,1,0:T(8,128)S(1)} %slice_select_fusion.9), channel_id=1, source_target_pairs={{0,16},{1,17},{2,18},{3,19},{4,20},{5,21},{6,22},{7,23},{8,24},{9,... | collective-permute-start | bytes 21512 | tf_op jit(solution)/shard_map/ppermute | solution.py:59
  335.1 2.4 collective-permute-start.21
  337.7 2.2 collective-permute-done.21
  339.9 5.0 %collective-permute-start.22 = (f32[1,24,128]{2,1,0:T(8,128)S(1)}, f32[1,24,128]{2,1,0:T(8,128)S(1)}, u32[]{:S(2)}, u32[]{:S(2)}) collective-permute-start(f32[1,24,128]{2,1,0:T(8,128)S(1)} %slice_select_fusion.8), channel_id=1, source_target_pairs={{0,16},{1,17},{2,18},{3,19},{4,20},{5,21},{6,22},{7,23},{8,24},{9,... | collective-permute-start | bytes 36872 | tf_op jit(solution)/shard_map/ppermute | solution.py:59
  345.0 11.2 %broadcast_select_fusion = (f32[3,1,128,4096]{3,2,1,0:T(8,128)}, f32[3,1,128,4096]{3,2,1,0:T(8,128)}, f32[3,1,128,4096]{3,2,1,0:T(8,128)}, f32[3,1,128,4096]{3,2,1,0:T(8,128)}) fusion(pred[128]{0:T(512)(128)(4,1)S(1)} %copy-done.143, f32[1,1,128,4096]{3,2,1,0:T(8,128)S(1)} %copy-done.14, f32[1,1,128,4096]{3,2,1,0:T(8,128)S(1)} %get-tuple-element.65, ...), kind=kLoop, calls=%fused_computation.84 | loop fusion | flops 9437184 | bytes 31457792 | tf_op jit(solution)/shard_map/jit(_where)/select_n | solution.py:222
  357.0 5.4 %broadcast_select_fusion.1 = (f32[3,1,128,4096]{3,2,1,0:T(8,128)S(1)}, f32[3,1,128,4096]{3,2,1,0:T(8,128)}, f32[3,1,128,4096]{3,2,1,0:T(8,128)}) fusion(pred[128]{0:T(512)(128)(4,1)S(1)} %copy-done.137, f32[1,1,128,4096]{3,2,1,0:T(8,128)S(1)} %copy-done.14, f32[1,1,128,4096]{3,2,1,0:T(8,128)S(1)} %get-tuple-element.65, f32[1,1,128,4096]{3,2,1,0:T(8,128)S(1)} %bitcast.579, ...), kind=kLoop, calls=%fused_computation.85 | loop fusion | flops 7864320 | bytes 25166208 | tf_op jit(solution)/shard_map/jit(_where)/select_n | solution.py:222
  362.5 2.5 collective-permute-start.38
  365.0 2.0 collective-permute-start.24
  367.1 14.0 %fusion.6 = f32[3,1,134,4096]{3,2,1,0:T(8,128)S(1)} fusion(f32[3,1,128,4096]{3,2,1,0:T(8,128)} %get-tuple-element.80, f32[3,1,128,4096]{3,2,1,0:T(8,128)} %get-tuple-element.75, f32[3,1,128,4096]{3,2,1,0:T(8,128)} %get-tuple-element.76, f32[3,1,128,4096]{3,2,1,0:T(8,128)} %get-tuple-element.77, f32[3,1,128,4096]{3,2,1,0:T(8,128)} %get-tuple-element.79, ...), kind=kLoop, calls=%fused_computation.32 | loop fusion | flops 21405696 | bytes 50970624 | tf_op jit(solution)/shard_map/add | solution.py:225
  387.4 9.0 %collective-permute-start.26 = (f32[1,24,128]{2,1,0:T(8,128)S(1)}, f32[1,24,128]{2,1,0:T(8,128)S(1)}, u32[]{:S(2)}, u32[]{:S(2)}) collective-permute-start(f32[1,24,128]{2,1,0:T(8,128)S(1)} %add.542), channel_id=1, source_target_pairs={{0,16},{1,17},{2,18},{3,19},{4,20},{5,21},{6,22},{7,23},{8,24},{9,... | collective-permute-start | bytes 36872 | tf_op jit(solution)/shard_map/ppermute | solution.py:62
  398.1 3.1 collective-permute-start.27
  401.6 2.5 collective-permute-start.41
  407.0 2.2 collective-permute-start.42
  409.8 2.5 collective-permute-start.29
  416.2 2.0 fusion.82
  418.3 2.3 collective-permute-done.30
  (473 shorter events, 63.2 us)
Async XLA Ops:
  1.6 25.9 %collective-permute-start.2 = (bf16[1,6,4096]{2,1,0:T(8,128)(2,1)S(1)}, bf16[1,6,4096]{2,1,0:T(8,128)(2,1)S(1)}, u32[]{:S(2)}, u32[]{:S(2)}) collective-permute-start(bf16[1,6,4096]{2,1,0:T(8,128)(2,1)S(1)} %slice.595), channel_id=1, source_target_pairs={{0,1},{1,2},{2,3},{3,4},{4,5},{5,6},{6,7},{7,8},{8,9},{9,10},{10,1... | collective-permute-start | bytes 147464 | tf_op jit(solution)/shard_map/ppermute | solution.py:12
  5.9 21.3 %collective-permute-start.1 = (bf16[1,6,4096]{2,1,0:T(8,128)(2,1)S(1)}, bf16[1,6,4096]{2,1,0:T(8,128)(2,1)S(1)}, u32[]{:S(2)}, u32[]{:S(2)}) collective-permute-start(bf16[1,6,4096]{2,1,0:T(8,128)(2,1)S(1)} %slice.594), channel_id=1, source_target_pairs={{0,1},{1,2},{2,3},{3,4},{4,5},{5,6},{6,7},{7,8},{8,9},{9,10},{10,1... | collective-permute-start | bytes 147464 | tf_op jit(solution)/shard_map/ppermute | solution.py:12
  10.3 16.6 %collective-permute-start = (bf16[1,6,4096]{2,1,0:T(8,128)(2,1)S(1)}, bf16[1,6,4096]{2,1,0:T(8,128)(2,1)S(1)}, u32[]{:S(2)}, u32[]{:S(2)}) collective-permute-start(bf16[1,6,4096]{2,1,0:T(8,128)(2,1)S(1)} %slice.593), channel_id=1, source_target_pairs={{0,1},{1,2},{2,3},{3,4},{4,5},{5,6},{6,7},{7,8},{8,9},{9,10},{10,1... | collective-permute-start | bytes 147464 | tf_op jit(solution)/shard_map/ppermute | solution.py:12
  81.4 17.3 %collective-permute-start.9 = (f32[1,16,4096]{2,1,0:T(8,128)S(1)}, f32[1,16,4096]{2,1,0:T(8,128)S(1)}, u32[]{:S(2)}, u32[]{:S(2)}) collective-permute-start(f32[1,16,4096]{2,1,0:T(8,128)S(1)} %get-tuple-element.60), channel_id=1, source_target_pairs={{1,0},{2,1},{3,2},{4,3},{5,4},{6,5},{7,6},{8,7},{9,8},{10,9},{11,1... | collective-permute-start | bytes 786440 | tf_op jit(solution)/shard_map/ppermute | solution.py:26
  92.9 9.0 %collective-permute-start.3 = (f32[1,16,4096]{2,1,0:T(8,128)S(1)}, f32[1,16,4096]{2,1,0:T(8,128)S(1)}, u32[]{:S(2)}, u32[]{:S(2)}) collective-permute-start(f32[1,16,4096]{2,1,0:T(8,128)S(1)} %fusion.92), channel_id=1, source_target_pairs={{0,1},{1,2},{2,3},{3,4},{4,5},{5,6},{6,7},{7,8},{8,9},{9,10},{10,1... | collective-permute-start | bytes 786440 | tf_op jit(solution)/shard_map/ppermute | solution.py:24
  102.7 11.2 %collective-permute-start.4 = (f32[1,16,4096]{2,1,0:T(8,128)}, f32[1,16,4096]{2,1,0:T(8,128)}, u32[]{:S(2)}, u32[]{:S(2)}) collective-permute-start(f32[1,16,4096]{2,1,0:T(8,128)} %get-tuple-element.131), channel_id=1, source_target_pairs={{0,2},{1,3},{2,4},{3,5},{4,6},{5,7},{6,8},{7,9},{8,10},{9,11},{10,... | collective-permute-start | bytes 786440 | tf_op jit(solution)/shard_map/ppermute | solution.py:24
  115.3 24.2 %collective-permute-start.5 = (f32[1,16,4096]{2,1,0:T(8,128)S(1)}, f32[1,16,4096]{2,1,0:T(8,128)S(1)}, u32[]{:S(2)}, u32[]{:S(2)}) collective-permute-start(f32[1,16,4096]{2,1,0:T(8,128)S(1)} %fusion.122), channel_id=1, source_target_pairs={{0,4},{1,5},{2,6},{3,7},{4,8},{5,9},{6,10},{7,11},{8,12},{9,13},{1... | collective-permute-start | bytes 786440 | tf_op jit(solution)/shard_map/ppermute | solution.py:24
  139.5 15.9 %collective-permute-start.6 = (f32[1,16,4096]{2,1,0:T(8,128)S(1)}, f32[1,16,4096]{2,1,0:T(8,128)S(1)}, u32[]{:S(2)}, u32[]{:S(2)}) collective-permute-start(f32[1,16,4096]{2,1,0:T(8,128)S(1)} %fusion.121), channel_id=1, source_target_pairs={{0,8},{1,9},{2,10},{3,11},{4,12},{5,13},{6,14},{7,15},{8,16},{9,17... | collective-permute-start | bytes 786440 | tf_op jit(solution)/shard_map/ppermute | solution.py:24
  155.5 13.9 %collective-permute-start.7 = (f32[1,16,4096]{2,1,0:T(8,128)S(1)}, f32[1,16,4096]{2,1,0:T(8,128)S(1)}, u32[]{:S(2)}, u32[]{:S(2)}) collective-permute-start(f32[1,16,4096]{2,1,0:T(8,128)S(1)} %fusion.120), channel_id=1, source_target_pairs={{0,16},{1,17},{2,18},{3,19},{4,20},{5,21},{6,22},{7,23},{8,24},{9,... | collective-permute-start | bytes 786440 | tf_op jit(solution)/shard_map/ppermute | solution.py:24
  169.4 10.8 %collective-permute-start.8 = (f32[1,16,4096]{2,1,0:T(8,128)S(1)}, f32[1,16,4096]{2,1,0:T(8,128)S(1)}, u32[]{:S(2)}, u32[]{:S(2)}) collective-permute-start(f32[1,16,4096]{2,1,0:T(8,128)S(1)} %fusion.119), channel_id=1, source_target_pairs={{0,1},{1,2},{2,3},{3,4},{4,5},{5,6},{6,7},{7,8},{8,9},{9,10},{10,1... | collective-permute-start | bytes 786440 | tf_op jit(solution)/shard_map/ppermute | solution.py:29
  171.0 70.0 %copy-start.49 = (f32[1,4096]{1,0:T(1,128)}, f32[1,4096]{1,0:T(1,128)S(1)}, u32[]{:S(2)}) copy-start(f32[1,4096]{1,0:T(1,128)S(1)} %get-tuple-element.133) | copy-start | bytes 49156
  171.0 70.0 %copy-start.51 = (f32[1,4096]{1,0:T(1,128)}, f32[1,4096]{1,0:T(1,128)S(1)}, u32[]{:S(2)}) copy-start(f32[1,4096]{1,0:T(1,128)S(1)} %get-tuple-element.134) | copy-start | bytes 49156
  171.0 70.0 %copy-start.53 = (f32[1,4096]{1,0:T(1,128)}, f32[1,4096]{1,0:T(1,128)S(1)}, u32[]{:S(2)}) copy-start(f32[1,4096]{1,0:T(1,128)S(1)} %get-tuple-element.135) | copy-start | bytes 49156
  171.0 70.0 %copy-start.55 = (f32[1,4096]{1,0:T(1,128)}, f32[1,4096]{1,0:T(1,128)S(1)}, u32[]{:S(2)}) copy-start(f32[1,4096]{1,0:T(1,128)S(1)} %get-tuple-element.136) | copy-start | bytes 49156
  171.0 70.0 %copy-start.57 = (f32[1,4096]{1,0:T(1,128)}, f32[1,4096]{1,0:T(1,128)S(1)}, u32[]{:S(2)}) copy-start(f32[1,4096]{1,0:T(1,128)S(1)} %get-tuple-element.137) | copy-start | bytes 49156
  171.1 70.0 %copy-start.59 = (f32[1,4096]{1,0:T(1,128)}, f32[1,4096]{1,0:T(1,128)S(1)}, u32[]{:S(2)}) copy-start(f32[1,4096]{1,0:T(1,128)S(1)} %get-tuple-element.138) | copy-start | bytes 49156
  171.1 70.0 %copy-start.61 = (f32[1,4096]{1,0:T(1,128)}, f32[1,4096]{1,0:T(1,128)S(1)}, u32[]{:S(2)}) copy-start(f32[1,4096]{1,0:T(1,128)S(1)} %get-tuple-element.139) | copy-start | bytes 49156
  171.1 70.0 %copy-start.63 = (f32[1,4096]{1,0:T(1,128)}, f32[1,4096]{1,0:T(1,128)S(1)}, u32[]{:S(2)}) copy-start(f32[1,4096]{1,0:T(1,128)S(1)} %get-tuple-element.140) | copy-start | bytes 49156
  171.1 70.0 %copy-start.65 = (f32[1,4096]{1,0:T(1,128)}, f32[1,4096]{1,0:T(1,128)S(1)}, u32[]{:S(2)}) copy-start(f32[1,4096]{1,0:T(1,128)S(1)} %get-tuple-element.141) | copy-start | bytes 49156
  171.1 70.0 %copy-start.67 = (f32[1,4096]{1,0:T(1,128)}, f32[1,4096]{1,0:T(1,128)S(1)}, u32[]{:S(2)}) copy-start(f32[1,4096]{1,0:T(1,128)S(1)} %get-tuple-element.142) | copy-start | bytes 49156
  171.1 70.0 %copy-start.69 = (f32[1,4096]{1,0:T(1,128)}, f32[1,4096]{1,0:T(1,128)S(1)}, u32[]{:S(2)}) copy-start(f32[1,4096]{1,0:T(1,128)S(1)} %get-tuple-element.143) | copy-start | bytes 49156
  171.1 70.0 %copy-start.71 = (f32[1,4096]{1,0:T(1,128)}, f32[1,4096]{1,0:T(1,128)S(1)}, u32[]{:S(2)}) copy-start(f32[1,4096]{1,0:T(1,128)S(1)} %get-tuple-element.144) | copy-start | bytes 49156
  171.1 70.0 %copy-start.73 = (f32[1,4096]{1,0:T(1,128)}, f32[1,4096]{1,0:T(1,128)S(1)}, u32[]{:S(2)}) copy-start(f32[1,4096]{1,0:T(1,128)S(1)} %get-tuple-element.145) | copy-start | bytes 49156
  171.1 70.0 %copy-start.75 = (f32[1,4096]{1,0:T(1,128)}, f32[1,4096]{1,0:T(1,128)S(1)}, u32[]{:S(2)}) copy-start(f32[1,4096]{1,0:T(1,128)S(1)} %get-tuple-element.146) | copy-start | bytes 49156
  171.1 70.0 %copy-start.77 = (f32[1,4096]{1,0:T(1,128)}, f32[1,4096]{1,0:T(1,128)S(1)}, u32[]{:S(2)}) copy-start(f32[1,4096]{1,0:T(1,128)S(1)} %get-tuple-element.147) | copy-start | bytes 49156
  171.2 9.8 %collective-permute-start.10 = (f32[1,16,4096]{2,1,0:T(8,128)S(1)}, f32[1,16,4096]{2,1,0:T(8,128)S(1)}, u32[]{:S(2)}, u32[]{:S(2)}) collective-permute-start(f32[1,16,4096]{2,1,0:T(8,128)S(1)} %copy-done.48), channel_id=1, source_target_pairs={{2,0},{3,1},{4,2},{5,3},{6,4},{7,5},{8,6},{9,7},{10,8},{11,9},{12,... | collective-permute-start | bytes 786440 | tf_op jit(solution)/shard_map/ppermute | solution.py:26
  181.8 14.3 %collective-permute-start.11 = (f32[1,16,4096]{2,1,0:T(8,128)S(1)}, f32[1,16,4096]{2,1,0:T(8,128)S(1)}, u32[]{:S(2)}, u32[]{:S(2)}) collective-permute-start(f32[1,16,4096]{2,1,0:T(8,128)S(1)} %get-tuple-element.58), channel_id=1, source_target_pairs={{4,0},{5,1},{6,2},{7,3},{8,4},{9,5},{10,6},{11,7},{12,8},{13,9},{1... | collective-permute-start | bytes 786440 | tf_op jit(solution)/shard_map/ppermute | solution.py:26
  196.8 15.4 %collective-permute-start.12 = (f32[1,16,4096]{2,1,0:T(8,128)S(1)}, f32[1,16,4096]{2,1,0:T(8,128)S(1)}, u32[]{:S(2)}, u32[]{:S(2)}) collective-permute-start(f32[1,16,4096]{2,1,0:T(8,128)S(1)} %get-tuple-element.127), channel_id=1, source_target_pairs={{8,0},{9,1},{10,2},{11,3},{12,4},{13,5},{14,6},{15,7},{16,8},{17,9... | collective-permute-start | bytes 786440 | tf_op jit(solution)/shard_map/ppermute | solution.py:26
  213.0 13.4 %collective-permute-start.13 = (f32[1,16,4096]{2,1,0:T(8,128)S(1)}, f32[1,16,4096]{2,1,0:T(8,128)S(1)}, u32[]{:S(2)}, u32[]{:S(2)}) collective-permute-start(f32[1,16,4096]{2,1,0:T(8,128)S(1)} %get-tuple-element.126), channel_id=1, source_target_pairs={{16,0},{17,1},{18,2},{19,3},{20,4},{21,5},{22,6},{23,7},{24,8},{25... | collective-permute-start | bytes 786440 | tf_op jit(solution)/shard_map/ppermute | solution.py:26
  230.5 18.3 %collective-permute-start.14 = (f32[1,16,4096]{2,1,0:T(8,128)}, f32[1,16,4096]{2,1,0:T(8,128)S(1)}, u32[]{:S(2)}, u32[]{:S(2)}) collective-permute-start(f32[1,16,4096]{2,1,0:T(8,128)} %get-tuple-element.125), channel_id=1, source_target_pairs={{1,0},{2,1},{3,2},{4,3},{5,4},{6,5},{7,6},{8,7},{9,8},{10,9},{11,1... | collective-permute-start | bytes 786440 | tf_op jit(solution)/shard_map/ppermute | solution.py:29
  299.5 5.9 %collective-permute-start.31 = (f32[16,14,128]{2,1,0:T(8,128)S(1)}, f32[16,14,128]{2,1,0:T(8,128)}, u32[]{:S(2)}, u32[]{:S(2)}) collective-permute-start(f32[16,14,128]{2,1,0:T(8,128)S(1)} %select_n.751), channel_id=1, source_target_pairs={{0,1},{1,0},{2,3},{3,2},{4,5},{5,4},{6,7},{7,6},{8,9},{9,8},{10,11... | collective-permute-start | bytes 344072 | tf_op jit(solution)/shard_map/ppermute | solution.py:59
  302.3 42.6 %copy-start.143 = (pred[128]{0:T(512)(128)(4,1)S(1)}, pred[128]{0:T(512)(128)(4,1)}, u32[]{:S(2)}) copy-start(pred[128]{0:T(512)(128)(4,1)} %copy-done.141) | copy-start | bytes 388
  302.3 42.6 %copy-start.145 = (pred[128]{0:T(512)(128)(4,1)S(1)}, pred[128]{0:T(512)(128)(4,1)}, u32[]{:S(2)}) copy-start(pred[128]{0:T(512)(128)(4,1)} %get-tuple-element.181) | copy-start | bytes 388
  302.4 42.6 %copy-start.147 = (pred[128]{0:T(512)(128)(4,1)S(1)}, pred[128]{0:T(512)(128)(4,1)}, u32[]{:S(2)}) copy-start(pred[128]{0:T(512)(128)(4,1)} %get-tuple-element.182) | copy-start | bytes 388
  302.4 42.6 %copy-start.149 = (pred[128]{0:T(512)(128)(4,1)S(1)}, pred[128]{0:T(512)(128)(4,1)}, u32[]{:S(2)}) copy-start(pred[128]{0:T(512)(128)(4,1)} %get-tuple-element.183) | copy-start | bytes 388
  302.4 42.6 %copy-start.14 = (f32[1,1,128,4096]{3,2,1,0:T(8,128)S(1)}, f32[1,1,128,4096]{3,2,1,0:T(8,128)}, u32[]{:S(2)}) copy-start(f32[1,1,128,4096]{3,2,1,0:T(8,128)} %copy-done.13) | copy-start | bytes 6291460
  306.3 5.8 %collective-permute-start.32 = (f32[8,14,128]{2,1,0:T(8,128)S(1)}, f32[8,14,128]{2,1,0:T(8,128)S(1)}, u32[]{:S(2)}, u32[]{:S(2)}) collective-permute-start(f32[8,14,128]{2,1,0:T(8,128)S(1)} %slice_select_fusion.3), channel_id=1, source_target_pairs={{0,4},{1,5},{2,6},{3,7},{4,0},{5,1},{6,2},{7,3},{8,12},{9,13},{10,... | collective-permute-start | bytes 172040 | tf_op jit(solution)/shard_map/ppermute | solution.py:59
  309.9 5.8 %collective-permute-start.18 = (f32[16,24,128]{2,1,0:T(8,128)S(1)}, f32[16,24,128]{2,1,0:T(8,128)S(1)}, u32[]{:S(2)}, u32[]{:S(2)}) collective-permute-start(f32[16,24,128]{2,1,0:T(8,128)S(1)} %broadcast_select_fusion.22), channel_id=1, source_target_pairs={{0,1},{1,0},{2,3},{3,2},{4,5},{5,4},{6,7},{7,6},{8,9},{9,8},{10,11... | collective-permute-start | bytes 589832 | tf_op jit(solution)/shard_map/ppermute | solution.py:59
  312.1 5.5 %collective-permute-start.33 = (f32[4,14,128]{2,1,0:T(8,128)S(1)}, f32[4,14,128]{2,1,0:T(8,128)S(1)}, u32[]{:S(2)}, u32[]{:S(2)}) collective-permute-start(f32[4,14,128]{2,1,0:T(8,128)S(1)} %slice_select_fusion.5), channel_id=1, source_target_pairs={{0,2},{1,3},{2,0},{3,1},{4,6},{5,7},{6,4},{7,5},{8,10},{9,11},{10,... | collective-permute-start | bytes 86024 | tf_op jit(solution)/shard_map/ppermute | solution.py:59
  317.7 8.7 %collective-permute-start.34 = (f32[2,14,128]{2,1,0:T(8,128)S(1)}, f32[2,14,128]{2,1,0:T(8,128)S(1)}, u32[]{:S(2)}, u32[]{:S(2)}) collective-permute-start(f32[2,14,128]{2,1,0:T(8,128)S(1)} %slice_select_fusion.7), channel_id=1, source_target_pairs={{0,8},{1,9},{2,10},{3,11},{4,12},{5,13},{6,14},{7,15},{8,0},{9,1},... | collective-permute-start | bytes 43016 | tf_op jit(solution)/shard_map/ppermute | solution.py:59
  324.7 4.7 %collective-permute-start.19 = (f32[8,24,128]{2,1,0:T(8,128)S(1)}, f32[8,24,128]{2,1,0:T(8,128)S(1)}, u32[]{:S(2)}, u32[]{:S(2)}) collective-permute-start(f32[8,24,128]{2,1,0:T(8,128)S(1)} %slice_select_fusion.2), channel_id=1, source_target_pairs={{0,4},{1,5},{2,6},{3,7},{4,0},{5,1},{6,2},{7,3},{8,12},{9,13},{10,... | collective-permute-start | bytes 294920 | tf_op jit(solution)/shard_map/ppermute | solution.py:59
  329.4 5.7 %collective-permute-start.20 = (f32[4,24,128]{2,1,0:T(8,128)S(1)}, f32[4,24,128]{2,1,0:T(8,128)S(1)}, u32[]{:S(2)}, u32[]{:S(2)}) collective-permute-start(f32[4,24,128]{2,1,0:T(8,128)S(1)} %slice_select_fusion.4), channel_id=1, source_target_pairs={{0,2},{1,3},{2,0},{3,1},{4,6},{5,7},{6,4},{7,5},{8,10},{9,11},{10,... | collective-permute-start | bytes 147464 | tf_op jit(solution)/shard_map/ppermute | solution.py:59
  330.1 7.6 %collective-permute-start.35 = (f32[1,14,128]{2,1,0:T(8,128)S(1)}, f32[1,14,128]{2,1,0:T(8,128)S(1)}, u32[]{:S(2)}, u32[]{:S(2)}) collective-permute-start(f32[1,14,128]{2,1,0:T(8,128)S(1)} %slice_select_fusion.9), channel_id=1, source_target_pairs={{0,16},{1,17},{2,18},{3,19},{4,20},{5,21},{6,22},{7,23},{8,24},{9,... | collective-permute-start | bytes 21512 | tf_op jit(solution)/shard_map/ppermute | solution.py:59
  335.1 4.8 %collective-permute-start.21 = (f32[2,24,128]{2,1,0:T(8,128)S(1)}, f32[2,24,128]{2,1,0:T(8,128)S(1)}, u32[]{:S(2)}, u32[]{:S(2)}) collective-permute-start(f32[2,24,128]{2,1,0:T(8,128)S(1)} %slice_select_fusion.6), channel_id=1, source_target_pairs={{0,8},{1,9},{2,10},{3,11},{4,12},{5,13},{6,14},{7,15},{8,0},{9,1},... | collective-permute-start | bytes 73736 | tf_op jit(solution)/shard_map/ppermute | solution.py:59
  337.7 18.5 %collective-permute-start.36 = (f32[1,14,128]{2,1,0:T(8,128)S(1)}, f32[1,14,128]{2,1,0:T(8,128)S(1)}, u32[]{:S(2)}, u32[]{:S(2)}) collective-permute-start(f32[1,14,128]{2,1,0:T(8,128)S(1)} %select_add_fusion.8), channel_id=1, source_target_pairs={{0,32},{32,0},{64,96},{96,64},{128,160},{160,128},{192,224},{224,1... | collective-permute-start | bytes 21512 | tf_op jit(solution)/shard_map/ppermute | solution.py:40
  339.9 16.9 %collective-permute-start.22 = (f32[1,24,128]{2,1,0:T(8,128)S(1)}, f32[1,24,128]{2,1,0:T(8,128)S(1)}, u32[]{:S(2)}, u32[]{:S(2)}) collective-permute-start(f32[1,24,128]{2,1,0:T(8,128)S(1)} %slice_select_fusion.8), channel_id=1, source_target_pairs={{0,16},{1,17},{2,18},{3,19},{4,20},{5,21},{6,22},{7,23},{8,24},{9,... | collective-permute-start | bytes 36872 | tf_op jit(solution)/shard_map/ppermute | solution.py:59
  356.2 6.3 %collective-permute-start.37 = (f32[1,14,128]{2,1,0:T(8,128)S(1)}, f32[1,14,128]{2,1,0:T(8,128)S(1)}, u32[]{:S(2)}, u32[]{:S(2)}) collective-permute-start(f32[1,14,128]{2,1,0:T(8,128)S(1)} %add.548), channel_id=1, source_target_pairs={{0,64},{32,96},{64,0},{96,32},{128,192},{160,224},{192,128},{224,1... | collective-permute-start | bytes 21512 | tf_op jit(solution)/shard_map/ppermute | solution.py:40
  356.9 8.1 %collective-permute-start.23 = (f32[1,24,128]{2,1,0:T(8,128)S(1)}, f32[1,24,128]{2,1,0:T(8,128)S(1)}, u32[]{:S(2)}, u32[]{:S(2)}) collective-permute-start(f32[1,24,128]{2,1,0:T(8,128)S(1)} %select_add_fusion.7), channel_id=1, source_target_pairs={{0,32},{32,0},{64,96},{96,64},{128,160},{160,128},{192,224},{224,1... | collective-permute-start | bytes 36872 | tf_op jit(solution)/shard_map/ppermute | solution.py:40
  362.5 18.6 %collective-permute-start.38 = (f32[1,14,128]{2,1,0:T(8,128)S(1)}, f32[1,14,128]{2,1,0:T(8,128)S(1)}, u32[]{:S(2)}, u32[]{:S(2)}) collective-permute-start(f32[1,14,128]{2,1,0:T(8,128)S(1)} %add.549), channel_id=1, source_target_pairs={{0,128},{32,160},{64,192},{96,224},{128,0},{160,32},{192,64},{224,... | collective-permute-start | bytes 21512 | tf_op jit(solution)/shard_map/ppermute | solution.py:40
  365.0 17.2 %collective-permute-start.24 = (f32[1,24,128]{2,1,0:T(8,128)S(1)}, f32[1,24,128]{2,1,0:T(8,128)S(1)}, u32[]{:S(2)}, u32[]{:S(2)}) collective-permute-start(f32[1,24,128]{2,1,0:T(8,128)S(1)} %add.540), channel_id=1, source_target_pairs={{0,64},{32,96},{64,0},{96,32},{128,192},{160,224},{192,128},{224,1... | collective-permute-start | bytes 36872 | tf_op jit(solution)/shard_map/ppermute | solution.py:40
  381.1 15.3 %collective-permute-start.39 = (f32[1,14,128]{2,1,0:T(8,128)S(1)}, f32[1,14,128]{2,1,0:T(8,128)S(1)}, u32[]{:S(2)}, u32[]{:S(2)}) collective-permute-start(f32[1,14,128]{2,1,0:T(8,128)S(1)} %add.550), channel_id=1, source_target_pairs={{0,16},{1,17},{2,18},{3,19},{4,20},{5,21},{6,22},{7,23},{8,24},{9,... | collective-permute-start | bytes 21512 | tf_op jit(solution)/shard_map/ppermute | solution.py:62
  382.2 5.2 %collective-permute-start.25 = (f32[1,24,128]{2,1,0:T(8,128)S(1)}, f32[1,24,128]{2,1,0:T(8,128)S(1)}, u32[]{:S(2)}, u32[]{:S(2)}) collective-permute-start(f32[1,24,128]{2,1,0:T(8,128)S(1)} %add.541), channel_id=1, source_target_pairs={{0,128},{32,160},{64,192},{96,224},{128,0},{160,32},{192,64},{224,... | collective-permute-start | bytes 36872 | tf_op jit(solution)/shard_map/ppermute | solution.py:40
  382.4 33.8 %collective-permute-start.17 = (f32[1,6,4096]{2,1,0:T(8,128)S(1)}, f32[1,6,4096]{2,1,0:T(8,128)S(1)}, u32[]{:S(2)}, u32[]{:S(2)}) collective-permute-start(f32[1,6,4096]{2,1,0:T(8,128)S(1)} %get-tuple-element.70), channel_id=1, source_target_pairs={{1,0},{2,1},{3,2},{4,3},{5,4},{6,5},{7,6},{8,7},{9,8},{10,9},{11,1... | collective-permute-start | bytes 294920 | tf_op jit(solution)/shard_map/ppermute | solution.py:12
  383.7 32.5 %collective-permute-start.16 = (f32[1,6,4096]{2,1,0:T(8,128)S(1)}, f32[1,6,4096]{2,1,0:T(8,128)S(1)}, u32[]{:S(2)}, u32[]{:S(2)}) collective-permute-start(f32[1,6,4096]{2,1,0:T(8,128)S(1)} %get-tuple-element.71), channel_id=1, source_target_pairs={{1,0},{2,1},{3,2},{4,3},{5,4},{6,5},{7,6},{8,7},{9,8},{10,9},{11,1... | collective-permute-start | bytes 294920 | tf_op jit(solution)/shard_map/ppermute | solution.py:12
  385.0 31.2 %collective-permute-start.15 = (f32[1,6,4096]{2,1,0:T(8,128)S(1)}, f32[1,6,4096]{2,1,0:T(8,128)S(1)}, u32[]{:S(2)}, u32[]{:S(2)}) collective-permute-start(f32[1,6,4096]{2,1,0:T(8,128)S(1)} %get-tuple-element.72), channel_id=1, source_target_pairs={{1,0},{2,1},{3,2},{4,3},{5,4},{6,5},{7,6},{8,7},{9,8},{10,9},{11,1... | collective-permute-start | bytes 294920 | tf_op jit(solution)/shard_map/ppermute | solution.py:12
  387.4 10.7 %collective-permute-start.26 = (f32[1,24,128]{2,1,0:T(8,128)S(1)}, f32[1,24,128]{2,1,0:T(8,128)S(1)}, u32[]{:S(2)}, u32[]{:S(2)}) collective-permute-start(f32[1,24,128]{2,1,0:T(8,128)S(1)} %add.542), channel_id=1, source_target_pairs={{0,16},{1,17},{2,18},{3,19},{4,20},{5,21},{6,22},{7,23},{8,24},{9,... | collective-permute-start | bytes 36872 | tf_op jit(solution)/shard_map/ppermute | solution.py:62
  396.4 5.2 %collective-permute-start.40 = (f32[2,14,128]{2,1,0:T(8,128)S(1)}, f32[2,14,128]{2,1,0:T(8,128)S(1)}, u32[]{:S(2)}, u32[]{:S(2)}) collective-permute-start(f32[2,14,128]{2,1,0:T(8,128)S(1)} %maximum_select_fusion.9), channel_id=1, source_target_pairs={{0,8},{1,9},{2,10},{3,11},{4,12},{5,13},{6,14},{7,15},{8,0},{9,1},... | collective-permute-start | bytes 43016 | tf_op jit(solution)/shard_map/ppermute | solution.py:62
  398.1 6.0 %collective-permute-start.27 = (f32[2,24,128]{2,1,0:T(8,128)S(1)}, f32[2,24,128]{2,1,0:T(8,128)S(1)}, u32[]{:S(2)}, u32[]{:S(2)}) collective-permute-start(f32[2,24,128]{2,1,0:T(8,128)S(1)} %maximum_select_fusion.8), channel_id=1, source_target_pairs={{0,8},{1,9},{2,10},{3,11},{4,12},{5,13},{6,14},{7,15},{8,0},{9,1},... | collective-permute-start | bytes 73736 | tf_op jit(solution)/shard_map/ppermute | solution.py:62
  401.6 5.4 %collective-permute-start.41 = (f32[4,14,128]{2,1,0:T(8,128)S(1)}, f32[4,14,128]{2,1,0:T(8,128)S(1)}, u32[]{:S(2)}, u32[]{:S(2)}) collective-permute-start(f32[4,14,128]{2,1,0:T(8,128)S(1)} %maximum_select_fusion.7), channel_id=1, source_target_pairs={{0,2},{1,3},{2,0},{3,1},{4,6},{5,7},{6,4},{7,5},{8,10},{9,11},{10,... | collective-permute-start | bytes 86024 | tf_op jit(solution)/shard_map/ppermute | solution.py:62
  404.1 5.7 %collective-permute-start.28 = (f32[4,24,128]{2,1,0:T(8,128)S(1)}, f32[4,24,128]{2,1,0:T(8,128)S(1)}, u32[]{:S(2)}, u32[]{:S(2)}) collective-permute-start(f32[4,24,128]{2,1,0:T(8,128)S(1)} %maximum_select_fusion.6), channel_id=1, source_target_pairs={{0,2},{1,3},{2,0},{3,1},{4,6},{5,7},{6,4},{7,5},{8,10},{9,11},{10,... | collective-permute-start | bytes 147464 | tf_op jit(solution)/shard_map/ppermute | solution.py:62
  407.0 5.2 %collective-permute-start.42 = (f32[8,14,128]{2,1,0:T(8,128)S(1)}, f32[8,14,128]{2,1,0:T(8,128)S(1)}, u32[]{:S(2)}, u32[]{:S(2)}) collective-permute-start(f32[8,14,128]{2,1,0:T(8,128)S(1)} %maximum_select_fusion.5), channel_id=1, source_target_pairs={{0,4},{1,5},{2,6},{3,7},{4,0},{5,1},{6,2},{7,3},{8,12},{9,13},{10,... | collective-permute-start | bytes 172040 | tf_op jit(solution)/shard_map/ppermute | solution.py:62
  409.8 5.1 %collective-permute-start.29 = (f32[8,24,128]{2,1,0:T(8,128)S(1)}, f32[8,24,128]{2,1,0:T(8,128)S(1)}, u32[]{:S(2)}, u32[]{:S(2)}) collective-permute-start(f32[8,24,128]{2,1,0:T(8,128)S(1)} %maximum_select_fusion.4), channel_id=1, source_target_pairs={{0,4},{1,5},{2,6},{3,7},{4,0},{5,1},{6,2},{7,3},{8,12},{9,13},{10,... | collective-permute-start | bytes 294920 | tf_op jit(solution)/shard_map/ppermute | solution.py:62
  412.3 6.0 %collective-permute-start.43 = (f32[16,14,128]{2,1,0:T(8,128)S(1)}, f32[16,14,128]{2,1,0:T(8,128)S(1)}, u32[]{:S(2)}, u32[]{:S(2)}) collective-permute-start(f32[16,14,128]{2,1,0:T(8,128)S(1)} %maximum_select_fusion.3), channel_id=1, source_target_pairs={{0,1},{1,0},{2,3},{3,2},{4,5},{5,4},{6,7},{7,6},{8,9},{9,8},{10,11... | collective-permute-start | bytes 344072 | tf_op jit(solution)/shard_map/ppermute | solution.py:62
  414.9 5.8 %collective-permute-start.30 = (f32[16,24,128]{2,1,0:T(8,128)S(1)}, f32[16,24,128]{2,1,0:T(8,128)S(1)}, u32[]{:S(2)}, u32[]{:S(2)}) collective-permute-start(f32[16,24,128]{2,1,0:T(8,128)S(1)} %maximum_select_fusion.2), channel_id=1, source_target_pairs={{0,1},{1,0},{2,3},{3,2},{4,5},{5,4},{6,7},{7,6},{8,9},{9,8},{10,11... | collective-permute-start | bytes 589832 | tf_op jit(solution)/shard_map/ppermute | solution.py:62
  (132 other events, 1835.4 us)

commit v5 on v3

--- a/solution.py
+++ b/solution.py
@@ -12,21 +12,31 @@
     return lax.ppermute(block, axis, route)
 
 
-def device_scan(ends, values, step_log, direction, tok_len):
+def device_scan(firsts, lasts, values, step_log, direction, tok_len):
     count = lax.axis_size("ctx")
-    sums = values
-    distance = 1
+
+    def moved(block, distance):
+        route = [(i, i + distance * direction) for i in range(count) if 0 <= i + distance * direction < count]
+        return lax.ppermute(block, "ctx", route)
+
+    def gate(condition):
+        return condition.astype(jnp.float32)[:, None, None]
+
+    sums = moved(values, 1)
+    if count <= 2:
+        return sums
+    if direction > 0:
+        sums = sums + gate(firsts > tok_len) * jnp.exp(step_log) * moved(values, 2)
+    else:
+        sums = sums + jnp.exp(step_log) * moved(gate(firsts > tok_len) * values, 2)
+    distance = 2
     while distance < count:
-        route = [(i, i + distance * direction) for i in range(count) if 0 <= i + distance * direction < count]
-        gate = (ends >= distance * tok_len) if direction > 0 else (ends > distance * tok_len)
-        gate = gate.astype(jnp.float32)[:, None, None]
         if direction > 0:
-            sums = sums + gate * jnp.exp(distance * step_log) * lax.ppermute(sums, "ctx", route)
+            sums = sums + gate(firsts > distance * tok_len) * jnp.exp(distance * step_log) * moved(sums, distance)
         else:
-            sums = sums + jnp.exp(distance * step_log) * lax.ppermute(gate * sums, "ctx", route)
+            sums = sums + jnp.exp(distance * step_log) * moved(gate(lasts >= distance * tok_len) * sums, distance)
         distance *= 2
-    route = [(i, i + direction) for i in range(count) if 0 <= i + direction < count]
-    return lax.ppermute(sums, "ctx", route)
+    return sums
 
 
 def butterfly_sum(value, axes):
@@ -167,7 +177,7 @@
         jnp.sum(pow_end[None, None] * (mixed_blocks * last_doc)[:, :, :, None, :], axis=2), 0, 1
     )
     block_sum, _ = sweep(zero_state, sigma, False)
-    states = device_scan(doc_offset[:, -1], block_sum, tok_len * lam_log, 1, tok_len)
+    states = device_scan(doc_offset[:, 0], doc_offset[:, -1], block_sum, tok_len * lam_log, 1, tok_len)
     _, enters = sweep(states, sigma, False)
     cross = valid_in * jnp.sum(
         (mode_coef[None] * pow_one)[None, None] * jnp.swapaxes(enters, 0, 1)[:, :, None], axis=3
@@ -184,7 +194,7 @@
         jnp.sum(pow_zero[None, None] * (grad_blocks * valid_in)[:, :, :, None, :], axis=2), 0, 1
     )
     block_adj, _ = sweep(zero_state, gamma, True)
-    adj_in = device_scan(doc_offset[:, 0], block_adj, tok_len * lam_log, -1, tok_len)
+    adj_in = device_scan(doc_offset[:, 0], doc_offset[:, -1], block_adj, tok_len * lam_log, -1, tok_len)
     _, exits = sweep(adj_in, gamma, True)
     cross_back = last_doc * jnp.sum(
         (mode_coef[None] * pow_back)[None, None] * jnp.swapaxes(exits, 0, 1)[:, :, None], axis=3

time: 407 us -> 390 us (0.958)
  waiting for transfers between devices: 96.9 us -> 70.4 us
  starting transfers between devices: 94.1 us -> 106 us
    ppermute x12, waiting for transfers between devices: 53.8 us -> 34.1 us  [moved(): return lax.ppermute(block, 'ctx', route)]
    ppermute x12, starting transfers between devices: 48.9 us -> 56.7 us  [moved(): return lax.ppermute(block, 'ctx', route)]
    ppermute x5, waiting for transfers between devices: 22.2 us -> 16.5 us  [spread_sum(): lax.ppermute(send, scatter_axis, [(i, i ^ step) for i in range(count)])]
    mul x3 -> x4, other arithmetic: 7.76 us -> 8.88 us  [the longest x1 5.85 us: device_scan(): sums = sums + jnp.exp(step_log) * moved(gate(firsts > tok_len) * values, 2)]
    unnamed x283 -> x286, local copies, waits for them, and re-layouts: 8.42 us -> 9.43 us
  transfers between devices with their start and end apart: 31 -> 31, of which waited for: 22 -> 21; matrix products, arithmetic and copies ran while one was open for 20% -> 21% of each run, Pallas kernels for 0% -> 0%
where the time goes in v5:
time: 390 us; the launch traced here: 385 us
  other arithmetic  172 us (44%)
  starting transfers between devices  106 us (27%)
  waiting for transfers between devices  70.4 us (18%)
  local copies, waits for them, and re-layouts  27.8 us (7%)
  between operations  9.12 us (2%)
    ppermute x12, starting transfers between devices, moved(): return lax.ppermute(block, 'ctx', route)  56.7 us
    ppermute x12, waiting for transfers between devices, moved(): return lax.ppermute(block, 'ctx', route)  34.1 us
    reduce_sum x2, other arithmetic, shards(): tap_terms.append(jnp.sum(window(tap_index) * short_grads, axis=(1, 2)))  19.9 us
    ppermute x5, starting transfers between devices, spread_sum(): lax.ppermute(send, scatter_axis, [(i, i ^ step) for i in range(count)])  19.9 us
    ppermute x5, waiting for transfers between devices, spread_sum(): lax.ppermute(send, scatter_axis, [(i, i ^ step) for i in range(count)])  16.5 us
    ppermute x6, starting transfers between devices, from_behind(): return lax.ppermute(block, axis, route)  14 us
    add x1, other arithmetic, shards(): spread + short_taps[:, tap_index][:, None, None, :] * padded[:, :, tap_in...  14 us
    ppermute x5, starting transfers between devices, spread_sum(): lax.ppermute(blocks, scatter_axis, [(i, i ^ step) for i in range(count)])  12.8 us
  transfers between devices with their start and end apart: 31, of which 21 were waited for; matrix products, arithmetic and copies ran while one was open for 21% of the time, Pallas kernels for 0%

profile of v5, /device:TPU:2, one launch (start us, length us, event | category | flops | bytes accessed | tf_op | source)
XLA Modules:
  0.0 385.5 jit_solution(12845095175314548137)
XLA Ops:
  1.6 3.5 collective-permute-start.2
  5.9 3.5 collective-permute-start.1
  10.3 3.2 collective-permute-start
  19.8 2.6 fusion.133
  23.5 2.1 fusion.120
  29.0 9.5 %multiply_add_fusion = f32[3,1,128,4096]{3,2,1,0:T(8,128)S(1)} fusion(f32[3,4096]{1,0:T(4,128)S(1)} %get-tuple-element.170, f32[3,4096]{1,0:T(4,128)S(1)} %get-tuple-element.171, f32[3,4096]{1,0:T(4,128)S(1)} %get-tuple-element.172, f32[3,4096]{1,0:T(4,128)S(1)} %get-tuple-element.173, f32[3,4096]{1,0:T(4,128)S(1)} %get-tuple-element.174, ...), kind=kLoop, calls=%fused_computation.47 | loop fusion | flops 42467328 | bytes 28656512 | tf_op jit(solution)/shard_map/add | solution.py:125
  38.8 1.7 copy-done.29
  40.5 1.8 broadcast_select_fusion.7
  42.3 2.7 multiply_reduce_fusion.30
  45.0 4.1 %multiply_reduce_fusion.23 = (f32[4096]{0:T(1024)}, f32[4096]{0:T(1024)}, f32[4096]{0:T(1024)}, f32[4096]{0:T(1024)}, f32[4096]{0:T(1024)}, /*index=5*/f32[4096]{0:T(1024)}) fusion(f32[1,8,16,4096]{3,2,1,0:T(8,128)S(1)} %bitcast.507, f32[1,8,16,4096]{3,2,1,0:T(8,128)S(1)} %bitcast.510, pred[8,16]{1,0:T(8,128)(4,1)S(1)} %get-tuple-element.147, ...), kind=kLoop, calls=%fused_computation.162 | loop fusion | flops 9412608 | bytes 4293376 | tf_op jit(solution)/shard_map/reduce_sum | solution.py:210
  49.2 4.5 %multiply_reduce_fusion.14 = (f32[4096]{0:T(1024)}, f32[4096]{0:T(1024)}, f32[4096]{0:T(1024)}, f32[4096]{0:T(1024)}, f32[4096]{0:T(1024)}, /*index=5*/f32[4096]...) fusion(f32[1,8,16,4096]{3,2,1,0:T(8,128)S(1)} %bitcast.508, f32[1,8,16,4096]{3,2,1,0:T(8,128)S(1)} %bitcast.511, ...), kind=kLoop, calls=%fused_computation.153 | loop fusion | flops 14118912 | bytes 4342912 | tf_op jit(solution)/shard_map/reduce_sum | solution.py:210
  53.7 3.3 stack.205
  57.1 7.9 %fusion.13 = (f32[16,16,4096]{2,1,0:T(8,128)}, f32[16,16,4096]{2,1,0:T(8,128)}, f32[16,4096]{1,0:T(8,128)}, f32[16,4096]{1,0:T(8,128)}, f32[16,16,4096]{2,1,0:T(8,128)}) fusion(f32[16,4096]{1,0:T(8,128)} %get-tuple-element.133, f32[16,4096]{1,0:T(8,128)} %get-tuple-element.134, f32[16]{0:T(128)} %iota_convert_fusion, f32[16,4096]{1,0:T(8,128)} %get-tuple-element.135, ...), kind=kLoop, calls=%fused_computation.74 | loop fusion | flops 7208960 | bytes 14155840 | tf_op jit(solution)/shard_map/mul | solution.py:136
  65.0 4.6 %rev.6 = f32[16,16,4096]{2,1,0:T(8,128)} reverse(f32[16,16,4096]{2,1,0:T(8,128)} %get-tuple-element.109), dimensions={0} | reverse | bytes 8388608 | tf_op jit(solution)/shard_map/rev | solution.py:137
  69.6 2.0 broadcast_multiply_fusion.1
  72.4 2.7 multiply_reduce_fusion.1
  75.2 5.9 %multiply_bitcast_fusion.1 = (f32[1,16,4096]{2,1,0:T(8,128)S(1)}, f32[16,4096]{1,0:T(8,128)S(1)}) fusion(f32[]{:T(128)} %bitcast.47, f32[]{:T(128)} %bitcast.31, f32[1,8,16,4096]{3,2,1,0:T(8,128)S(1)} %bitcast.514, f32[]{:T(128)} %bitcast.33, f32[]{:T(128)} %bitcast.35, f32[]{:T(128)} %bitcast.37, f32[]{:T(128)} %bitcast.39, f32[]{:T(128)} %bitcast.41, ...), kind=kLoop, calls=%fused_computation.299 | loop fusion | flops 1769472 | bytes 2883620 | tf_op jit(solution)/shard_map/mul | solution.py:31
  83.9 1.9 copy-done.17
  85.8 2.7 multiply_reduce_fusion.3
  88.6 5.1 %fusion.72 = f32[1,16,4096]{2,1,0:T(8,128)S(1)} fusion(f32[1,8,16,4096]{3,2,1,0:T(8,128)S(1)} %bitcast.521, f32[]{:T(128)} %bitcast.45, f32[]{:T(128)} %bitcast.43, f32[]{:T(128)} %bitcast.41, f32[]{:T(128)} %bitcast.39, f32[]{:T(128)} %bitcast.37, f32[]{:T(128)} %bitcast.35, f32[]{:T(128)} %bitcast.33, f32[]{:T(128)} %bitcast.31, f32[16,4096]{1,0:T(8,128)S(1)} %copy-done.2), kind=kLoop, calls=%fused_computation.205 | loop fusion | flops 1703936 | bytes 2621472 | tf_op jit(solution)/shard_map/add | solution.py:166
  93.7 6.8 %collective-permute-start.4 = (f32[1,16,4096]{2,1,0:T(8,128)S(1)}, f32[1,16,4096]{2,1,0:T(8,128)S(1)}, u32[]{:S(2)}, u32[]{:S(2)}) collective-permute-start(f32[1,16,4096]{2,1,0:T(8,128)S(1)} %fusion.72), channel_id=1, source_target_pairs={{0,2},{1,3},{2,4},{3,5},{4,6},{5,7},{6,8},{7,9},{8,10},{9,11},{10,... | collective-permute-start | bytes 786440 | tf_op jit(solution)/shard_map/ppermute | solution.py:20
  100.6 4.2 %collective-permute-start.3 = (f32[1,16,4096]{2,1,0:T(8,128)S(1)}, f32[1,16,4096]{2,1,0:T(8,128)S(1)}, u32[]{:S(2)}, u32[]{:S(2)}) collective-permute-start(f32[1,16,4096]{2,1,0:T(8,128)S(1)} %fusion.72), channel_id=1, source_target_pairs={{0,1},{1,2},{2,3},{3,4},{4,5},{5,6},{6,7},{7,8},{8,9},{9,10},{10,1... | collective-permute-start | bytes 786440 | tf_op jit(solution)/shard_map/ppermute | solution.py:20
  107.2 3.4 collective-permute-done.3
  111.5 7.0 %collective-permute-start.5 = (f32[1,16,4096]{2,1,0:T(8,128)}, f32[1,16,4096]{2,1,0:T(8,128)}, u32[]{:S(2)}, u32[]{:S(2)}) collective-permute-start(f32[1,16,4096]{2,1,0:T(8,128)} %get-tuple-element.116), channel_id=1, source_target_pairs={{0,2},{1,3},{2,4},{3,5},{4,6},{5,7},{6,8},{7,9},{8,10},{9,11},{10,... | collective-permute-start | bytes 786440 | tf_op jit(solution)/shard_map/ppermute | solution.py:20
  124.2 8.0 %collective-permute-start.6 = (f32[1,16,4096]{2,1,0:T(8,128)S(1)}, f32[1,16,4096]{2,1,0:T(8,128)S(1)}, u32[]{:S(2)}, u32[]{:S(2)}) collective-permute-start(f32[1,16,4096]{2,1,0:T(8,128)S(1)} %fusion.102), channel_id=1, source_target_pairs={{0,4},{1,5},{2,6},{3,7},{4,8},{5,9},{6,10},{7,11},{8,12},{9,13},{1... | collective-permute-start | bytes 786440 | tf_op jit(solution)/shard_map/ppermute | solution.py:20
  132.2 9.4 %broadcast_select_fusion.8 = (f32[1,8,16,4096]{3,2,1,0:T(8,128)S(1)}, f32[1,8,16,4096]{3,2,1,0:T(8,128)S(1)}, f32[1,8,16,4096]{3,2,1,0:T(8,128)S(1)}, f32[1,8,16...) fusion(pred[8,16]{1,0:T(8,128)(4,1)S(1)} %copy-done.83, ...), kind=kLoop, calls=%fused_computation.179 | loop fusion | flops 7340032 | bytes 31459072 | tf_op jit(solution)/shard_map/jit(_where)/select_n | solution.py:154
  141.7 5.2 %collective-permute-start.7 = (f32[1,16,4096]{2,1,0:T(8,128)S(1)}, f32[1,16,4096]{2,1,0:T(8,128)S(1)}, u32[]{:S(2)}, u32[]{:S(2)}) collective-permute-start(f32[1,16,4096]{2,1,0:T(8,128)S(1)} %fusion.101), channel_id=1, source_target_pairs={{0,8},{1,9},{2,10},{3,11},{4,12},{5,13},{6,14},{7,15},{8,16},{9,17... | collective-permute-start | bytes 786440 | tf_op jit(solution)/shard_map/ppermute | solution.py:20
  147.4 3.3 collective-permute-done.7
  150.8 17.8 %collective-permute-start.8 = (f32[1,16,4096]{2,1,0:T(8,128)S(1)}, f32[1,16,4096]{2,1,0:T(8,128)S(1)}, u32[]{:S(2)}, u32[]{:S(2)}) collective-permute-start(f32[1,16,4096]{2,1,0:T(8,128)S(1)} %fusion.100), channel_id=1, source_target_pairs={{0,16},{1,17},{2,18},{3,19},{4,20},{5,21},{6,22},{7,23},{8,24},{9,... | collective-permute-start | bytes 786440 | tf_op jit(solution)/shard_map/ppermute | solution.py:20
  170.3 2.2 collective-permute-done.8
  172.6 6.2 %collective-permute-done.11 = f32[1,16,4096]{2,1,0:T(8,128)S(1)} collective-permute-done((f32[1,16,4096]{2,1,0:T(8,128)S(1)}, f32[1,16,4096]{2,1,0:T(8,128)S(1)}, u32[]{:S(2)}, u32[]{:S(2)}) %collective-permute-start.11) | collective-permute-done | bytes 262176 | tf_op jit(solution)/shard_map/ppermute | solution.py:20
  180.8 6.9 %collective-permute-done.12 = f32[1,16,4096]{2,1,0:T(8,128)S(1)} collective-permute-done((f32[1,16,4096]{2,1,0:T(8,128)S(1)}, f32[1,16,4096]{2,1,0:T(8,128)S(1)}, u32[]{:S(2)}, u32[]{:S(2)}) %collective-permute-start.12) | collective-permute-done | bytes 262176 | tf_op jit(solution)/shard_map/ppermute | solution.py:20
  189.8 10.4 %collective-permute-done.13 = f32[1,16,4096]{2,1,0:T(8,128)S(1)} collective-permute-done((f32[1,16,4096]{2,1,0:T(8,128)S(1)}, f32[1,16,4096]{2,1,0:T(8,128)S(1)}, u32[]{:S(2)}, u32[]{:S(2)}) %collective-permute-start.13) | collective-permute-done | bytes 262176 | tf_op jit(solution)/shard_map/ppermute | solution.py:20
  207.7 8.5 %multiply_reduce_fusion.2 = f32[8,16,4096]{2,1,0:T(8,128)S(1)} fusion(f32[8,16,4096]{2,1,0:T(8,128)S(1)} %bitcast.529, f32[16,16,4096]{2,1,0:T(8,128)S(1)} %copy-done.18), kind=kLoop, calls=%fused_computation.2 | loop fusion | flops 16252928 | bytes 8388608 | tf_op jit(solution)/shard_map/reduce_sum | solution.py:182
  216.6 7.0 %fusion.69 = f32[1,8,16,4096]{3,2,1,0:T(8,128)} fusion(f32[8,16,4096]{2,1,0:T(8,128)S(1)} %multiply_reduce_fusion.2, f32[1,8,16,4096]{3,2,1,0:T(8,128)S(1)} %bitcast.513, f32[8,16]{1,0:T(8,128)S(1)} %copy-done.81, f32[4096]{0:T(1024)S(1)} %bitcast.537, f32[4096]{0:T(1024)S(1)} %bitcast.539, f32[4096]{0:T(1024)S(1)} %bitcast.541, f32[4096]{0:T(1024)S(1)} %bitcast.543, ...), kind=kLoop, calls=%fused_computation.151 | loop fusion | flops 25690112 | bytes 6556160 | tf_op jit(solution)/shard_map/add | solution.py:185
  225.5 5.1 %bitcast_dynamic-update-slice_fusion.7 = (f32[8,1,16,4096]{3,2,1,0:T(8,128)S(1)}, f32[1,16,4096]{2,1,0:T(8,128)S(1)}, f32[1,16,4096]{2,1,0:T(8,128)S(1)}, f32[1,16,4096]{2,1,0:T(8,128)S(1)}) fusion(f32[1,8,16,4096]{3,2,1,0:T(8,128)S(1)} %bitcast.515, f32[]{:T(128)} %bitcast.43, f32[]{:T(128)} %bitcast.41, f32[16,4096]{1,0:T(8,128)S(1)} %copy-done.3, ...), kind=kLoop, calls=%fused_computation.213 | loop fusion | flops 1703935 | bytes 3670044
  233.3 8.4 %multiply_reduce_fusion = f32[8,16,4096]{2,1,0:T(8,128)S(1)} fusion(f32[8,16,4096]{2,1,0:T(8,128)S(1)} %bitcast.530, f32[16,16,4096]{2,1,0:T(8,128)S(1)} %reverse_multiply_fusion), kind=kLoop, calls=%fused_computation | loop fusion | flops 16252928 | bytes 8388608 | tf_op jit(solution)/shard_map/reduce_sum | solution.py:199
  241.9 7.0 %fusion.31 = f32[1,8,16,4096]{3,2,1,0:T(8,128)} fusion(f32[1,8,16,4096]{3,2,1,0:T(8,128)} %get-tuple-element.95, f32[1,8,16,4096]{3,2,1,0:T(8,128)S(1)} %get-tuple-element.83, f32[1,8,16,4096]{3,2,1,0:T(8,128)S(1)} %get-tuple-element.84, f32[1,8,16,4096]{3,2,1,0:T(8,128)S(1)} %copy-done.20, f32[1,8,16,4096]{3,2,1,0:T(8,128)S(1)} %copy-done.21, ...), kind=kLoop, calls=%fused_computation.102 | loop fusion | flops 17825792 | bytes 38011520 | tf_op jit(solution)/shard_map/add | solution.py:202
  248.9 8.2 %fusion.67 = (f32[1,1,128,4096]{3,2,1,0:T(8,128)S(1)}, f32[1,1,128,4096]{3,2,1,0:T(8,128)S(1)}, bf16[1,128,4096]{2,1,0:T(8,128)(2,1)}, f32[1,1,128,4096]{3,2,1,0:T(8,128)}) fusion(f32[3,1,128,4096]{3,2,1,0:T(8,128)} %copy-done.4, f32[1,128,4096]{2,1,0:T(8,128)S(1)} %copy-done.1, f32[4096]{0:T(1024)} %param.16, f32[1,8,16,4096]{3,2,1,0:T(8,128)} %fusion.31, ...), kind=kLoop, calls=%fused_computation.146 | loop fusion | flops 5242880 | bytes 23085056 | tf_op jit(solution)/shard_map/stack | solution.py:228
  257.2 11.8 %multiply_reduce_fusion.4 = (f32[3,4096]{1,0:T(4,128)S(1)}, f32[3,4096]{1,0:T(4,128)S(1)}, f32[3,4096]{1,0:T(4,128)S(1)}, f32[3,4096]{1,0:T(4,128)S(1)}, f32[3,4096]{1,0:T(4,128)S(1)}, /*index=5*/f32[3,4096]{1,0:T(4,128)S(1)}) fusion(pred[128]{0:T(512)(128)(4,1)S(1)} %copy-done.122, bf16[3,1,134,4096]{3,2,1,0:T(8,128)(2,1)S(1)} %pad_maximum_fusion.1, ...), kind=kLoop, calls=%fused_computation.40 | loop fusion | flops 40820736 | bytes 25461504 | tf_op jit(solution)/shard_map/reduce_sum | solution.py:239
  269.0 8.2 %multiply_reduce_fusion.10 = (f32[3,4096]{1,0:T(4,128)S(1)}, f32[3,1,128,4096]{3,2,1,0:T(8,128)}, f32[3,1,128,4096]{3,2,1,0:T(8,128)}, f32[3,1,128,4096]{3,2,1,0:T(8,128)}) fusion(pred[128]{0:T(512)(128)(4,1)S(1)} %copy-done.120, bf16[3,1,134,4096]{3,2,1,0:T(8,128)(2,1)S(1)} %pad_maximum_fusion.1, f32[1,1,128,4096]{3,2,1,0:T(8,128)S(1)} %get-tuple-element.62, ...), kind=kLoop, calls=%fused_computation.46 | loop fusion | flops 14143488 | bytes 28361088 | tf_op jit(solution)/shard_map/reduce_sum | solution.py:239
  279.9 5.8 %collective-permute-done.18 = f32[16,38,128]{2,1,0:T(8,128)} collective-permute-done((f32[16,38,128]{2,1,0:T(8,128)S(1)}, f32[16,38,128]{2,1,0:T(8,128)}, u32[]{:S(2)}, u32[]{:S(2)}) %collective-permute-start.18) | collective-permute-done | bytes 311328 | tf_op jit(solution)/shard_map/ppermute | solution.py:69
  286.7 3.1 collective-permute-start.19
  289.8 3.3 collective-permute-done.19
  293.2 7.3 %collective-permute-start.20 = (f32[4,38,128]{2,1,0:T(8,128)S(1)}, f32[4,38,128]{2,1,0:T(8,128)S(1)}, u32[]{:S(2)}, u32[]{:S(2)}) collective-permute-start(f32[4,38,128]{2,1,0:T(8,128)S(1)} %slice_select_fusion.3), channel_id=1, source_target_pairs={{0,2},{1,3},{2,0},{3,1},{4,6},{5,7},{6,4},{7,5},{8,10},{9,11},{10,... | collective-permute-start | bytes 233480 | tf_op jit(solution)/shard_map/ppermute | solution.py:69
  300.4 2.4 collective-permute-done.20
  302.9 1.8 collective-permute-start.21
  304.6 3.2 collective-permute-done.21
  307.9 6.4 %collective-permute-start.22 = (f32[1,38,128]{2,1,0:T(8,128)S(1)}, f32[1,38,128]{2,1,0:T(8,128)S(1)}, u32[]{:S(2)}, u32[]{:S(2)}) collective-permute-start(f32[1,38,128]{2,1,0:T(8,128)S(1)} %slice_select_fusion.5), channel_id=1, source_target_pairs={{0,16},{1,17},{2,18},{3,19},{4,20},{5,21},{6,22},{7,23},{8,24},{9,... | collective-permute-start | bytes 58376 | tf_op jit(solution)/shard_map/ppermute | solution.py:69
  314.2 1.8 collective-permute-done.22
  317.7 3.2 collective-permute-done.24
  321.0 2.1 collective-permute-start.25
  323.1 3.2 collective-permute-done.25
  326.3 5.9 %collective-permute-start.26 = (f32[1,38,128]{2,1,0:T(8,128)S(1)}, f32[1,38,128]{2,1,0:T(8,128)S(1)}, u32[]{:S(2)}, u32[]{:S(2)}) collective-permute-start(f32[1,38,128]{2,1,0:T(8,128)S(1)} %add.508), channel_id=1, source_target_pairs={{0,16},{1,17},{2,18},{3,19},{4,20},{5,21},{6,22},{7,23},{8,24},{9,... | collective-permute-start | bytes 58376 | tf_op jit(solution)/shard_map/ppermute | solution.py:72
  332.2 1.8 collective-permute-done.26
  334.0 1.8 collective-permute-start.27
  335.8 11.5 %broadcast_select_fusion.2 = (f32[3,1,128,4096]{3,2,1,0:T(8,128)}, f32[3,1,128,4096]{3,2,1,0:T(8,128)}, f32[3,1,128,4096]{3,2,1,0:T(8,128)}, f32[3,1,128,4096]{3,2,1,0:T(8,128)}) fusion(pred[128]{0:T(512)(128)(4,1)S(1)} %copy-done.126, f32[1,1,128,4096]{3,2,1,0:T(8,128)} %copy-done.13, f32[1,1,128,4096]{3,2,1,0:T(8,128)S(1)} %copy-done.12, ...), kind=kLoop, calls=%fused_computation.78 | loop fusion | flops 9437184 | bytes 31457792 | tf_op jit(solution)/shard_map/jit(_where)/select_n | solution.py:232
  347.4 3.6 collective-permute-start.28
  351.0 14.0 %fusion.6 = f32[3,1,134,4096]{3,2,1,0:T(8,128)S(1)} fusion(f32[3,1,128,4096]{3,2,1,0:T(8,128)S(1)} %bitcast.520, f32[3,1,128,4096]{3,2,1,0:T(8,128)} %get-tuple-element.80, f32[3,1,128,4096]{3,2,1,0:T(8,128)} %get-tuple-element.79, f32[3,1,128,4096]{3,2,1,0:T(8,128)} %get-tuple-element.78, f32[3,1,128,4096]{3,2,1,0:T(8,128)} %get-tuple-element.77, ...), kind=kLoop, calls=%fused_computation.32 | loop fusion | flops 21405696 | bytes 50970624 | tf_op jit(solution)/shard_map/add | solution.py:235
  369.1 2.7 collective-permute-done.29
  373.5 2.8 collective-permute-done.16
  376.3 2.8 collective-permute-done.15
  379.1 2.0 fusion.62
  381.1 1.8 collective-permute-done.30
  (388 shorter events, 51.9 us)
Async XLA Ops:
  0.6 26.2 %copy-start.34 = (bf16[1,128,4096]{2,1,0:T(8,128)(2,1)S(1)}, bf16[1,128,4096]{2,1,0:T(8,128)(2,1)}, u32[]{:S(2)}) copy-start(bf16[1,128,4096]{2,1,0:T(8,128)(2,1)} %param.9) | copy-start | bytes 3145732
  1.6 25.9 %collective-permute-start.2 = (bf16[1,6,4096]{2,1,0:T(8,128)(2,1)S(1)}, bf16[1,6,4096]{2,1,0:T(8,128)(2,1)S(1)}, u32[]{:S(2)}, u32[]{:S(2)}) collective-permute-start(bf16[1,6,4096]{2,1,0:T(8,128)(2,1)S(1)} %slice.492), channel_id=1, source_target_pairs={{0,1},{1,2},{2,3},{3,4},{4,5},{5,6},{6,7},{7,8},{8,9},{9,10},{10,1... | collective-permute-start | bytes 147464 | tf_op jit(solution)/shard_map/ppermute | solution.py:12
  5.9 21.2 %collective-permute-start.1 = (bf16[1,6,4096]{2,1,0:T(8,128)(2,1)S(1)}, bf16[1,6,4096]{2,1,0:T(8,128)(2,1)S(1)}, u32[]{:S(2)}, u32[]{:S(2)}) collective-permute-start(bf16[1,6,4096]{2,1,0:T(8,128)(2,1)S(1)} %slice.491), channel_id=1, source_target_pairs={{0,1},{1,2},{2,3},{3,4},{4,5},{5,6},{6,7},{7,8},{8,9},{9,10},{10,1... | collective-permute-start | bytes 147464 | tf_op jit(solution)/shard_map/ppermute | solution.py:12
  10.3 16.5 %collective-permute-start = (bf16[1,6,4096]{2,1,0:T(8,128)(2,1)S(1)}, bf16[1,6,4096]{2,1,0:T(8,128)(2,1)S(1)}, u32[]{:S(2)}, u32[]{:S(2)}) collective-permute-start(bf16[1,6,4096]{2,1,0:T(8,128)(2,1)S(1)} %slice.490), channel_id=1, source_target_pairs={{0,1},{1,2},{2,3},{3,4},{4,5},{5,6},{6,7},{7,8},{8,9},{9,10},{10,1... | collective-permute-start | bytes 147464 | tf_op jit(solution)/shard_map/ppermute | solution.py:12
  23.1 26.0 %copy-start.82 = (pred[8,16]{1,0:T(8,128)(4,1)}, pred[8,16]{1,0:T(8,128)(4,1)S(1)}, u32[]{:S(2)}) copy-start(pred[8,16]{1,0:T(8,128)(4,1)S(1)} %get-tuple-element.139) | copy-start | bytes 388
  23.1 26.0 %copy-start.85 = (pred[8,16]{1,0:T(8,128)(4,1)}, pred[8,16]{1,0:T(8,128)(4,1)S(1)}, u32[]{:S(2)}) copy-start(pred[8,16]{1,0:T(8,128)(4,1)S(1)} %get-tuple-element.140) | copy-start | bytes 388
  23.1 26.0 %copy-start.88 = (pred[8,16]{1,0:T(8,128)(4,1)}, pred[8,16]{1,0:T(8,128)(4,1)S(1)}, u32[]{:S(2)}) copy-start(pred[8,16]{1,0:T(8,128)(4,1)S(1)} %get-tuple-element.141) | copy-start | bytes 388
  23.2 26.0 %copy-start.91 = (pred[8,16]{1,0:T(8,128)(4,1)}, pred[8,16]{1,0:T(8,128)(4,1)S(1)}, u32[]{:S(2)}) copy-start(pred[8,16]{1,0:T(8,128)(4,1)S(1)} %get-tuple-element.142) | copy-start | bytes 388
  23.2 26.0 %copy-start.94 = (pred[8,16]{1,0:T(8,128)(4,1)}, pred[8,16]{1,0:T(8,128)(4,1)S(1)}, u32[]{:S(2)}) copy-start(pred[8,16]{1,0:T(8,128)(4,1)S(1)} %get-tuple-element.143) | copy-start | bytes 388
  23.2 26.0 %copy-start.96 = (pred[8,16]{1,0:T(8,128)(4,1)}, pred[8,16]{1,0:T(8,128)(4,1)S(1)}, u32[]{:S(2)}) copy-start(pred[8,16]{1,0:T(8,128)(4,1)S(1)} %get-tuple-element.144) | copy-start | bytes 388
  23.2 26.0 %copy-start.98 = (pred[8,16]{1,0:T(8,128)(4,1)}, pred[8,16]{1,0:T(8,128)(4,1)S(1)}, u32[]{:S(2)}) copy-start(pred[8,16]{1,0:T(8,128)(4,1)S(1)} %get-tuple-element.145) | copy-start | bytes 388
  23.2 26.0 %copy-start.100 = (pred[8,16]{1,0:T(8,128)(4,1)}, pred[8,16]{1,0:T(8,128)(4,1)S(1)}, u32[]{:S(2)}) copy-start(pred[8,16]{1,0:T(8,128)(4,1)S(1)} %get-tuple-element.146) | copy-start | bytes 388
  23.2 26.0 %copy-start.114 = (pred[8,16]{1,0:T(8,128)(4,1)}, pred[8,16]{1,0:T(8,128)(4,1)S(1)}, u32[]{:S(2)}) copy-start(pred[8,16]{1,0:T(8,128)(4,1)S(1)} %get-tuple-element.138) | copy-start | bytes 388
  81.0 24.4 %collective-permute-start.9 = (f32[1,16,4096]{2,1,0:T(8,128)S(1)}, f32[1,16,4096]{2,1,0:T(8,128)S(1)}, u32[]{:S(2)}, u32[]{:S(2)}) collective-permute-start(f32[1,16,4096]{2,1,0:T(8,128)S(1)} %bitcast.534), channel_id=1, source_target_pairs={{1,0},{2,1},{3,2},{4,3},{5,4},{6,5},{7,6},{8,7},{9,8},{10,9},{11,1... | collective-permute-start | bytes 786440 | tf_op jit(solution)/shard_map/ppermute | solution.py:20
  82.3 23.2 %collective-permute-start.10 = (f32[1,16,4096]{2,1,0:T(8,128)S(1)}, f32[1,16,4096]{2,1,0:T(8,128)S(1)}, u32[]{:S(2)}, u32[]{:S(2)}) collective-permute-start(f32[1,16,4096]{2,1,0:T(8,128)S(1)} %get-tuple-element.56), channel_id=1, source_target_pairs={{2,0},{3,1},{4,2},{5,3},{6,4},{7,5},{8,6},{9,7},{10,8},{11,9},{12,... | collective-permute-start | bytes 786440 | tf_op jit(solution)/shard_map/ppermute | solution.py:20
  88.6 22.9 %copy-start.15 = (f32[8,16,4096]{2,1,0:T(8,128)}, f32[8,16,4096]{2,1,0:T(8,128)S(1)}, u32[]{:S(2)}) copy-start(f32[8,16,4096]{2,1,0:T(8,128)S(1)} %multiply_reduce_fusion.3) | copy-start | bytes 6291460
  93.7 38.5 %copy-start.83 = (pred[8,16]{1,0:T(8,128)(4,1)S(1)}, pred[8,16]{1,0:T(8,128)(4,1)}, u32[]{:S(2)}) copy-start(pred[8,16]{1,0:T(8,128)(4,1)} %copy-done.82) | copy-start | bytes 388
  93.7 38.5 %copy-start.86 = (pred[8,16]{1,0:T(8,128)(4,1)S(1)}, pred[8,16]{1,0:T(8,128)(4,1)}, u32[]{:S(2)}) copy-start(pred[8,16]{1,0:T(8,128)(4,1)} %copy-done.85) | copy-start | bytes 388
  93.7 38.5 %copy-start.89 = (pred[8,16]{1,0:T(8,128)(4,1)S(1)}, pred[8,16]{1,0:T(8,128)(4,1)}, u32[]{:S(2)}) copy-start(pred[8,16]{1,0:T(8,128)(4,1)} %copy-done.88) | copy-start | bytes 388
  93.7 38.5 %copy-start.92 = (pred[8,16]{1,0:T(8,128)(4,1)S(1)}, pred[8,16]{1,0:T(8,128)(4,1)}, u32[]{:S(2)}) copy-start(pred[8,16]{1,0:T(8,128)(4,1)} %copy-done.91) | copy-start | bytes 388
  93.7 13.5 %collective-permute-start.4 = (f32[1,16,4096]{2,1,0:T(8,128)S(1)}, f32[1,16,4096]{2,1,0:T(8,128)S(1)}, u32[]{:S(2)}, u32[]{:S(2)}) collective-permute-start(f32[1,16,4096]{2,1,0:T(8,128)S(1)} %fusion.72), channel_id=1, source_target_pairs={{0,2},{1,3},{2,4},{3,5},{4,6},{5,7},{6,8},{7,9},{8,10},{9,11},{10,... | collective-permute-start | bytes 786440 | tf_op jit(solution)/shard_map/ppermute | solution.py:20
  100.6 10.0 %collective-permute-start.3 = (f32[1,16,4096]{2,1,0:T(8,128)S(1)}, f32[1,16,4096]{2,1,0:T(8,128)S(1)}, u32[]{:S(2)}, u32[]{:S(2)}) collective-permute-start(f32[1,16,4096]{2,1,0:T(8,128)S(1)} %fusion.72), channel_id=1, source_target_pairs={{0,1},{1,2},{2,3},{3,4},{4,5},{5,6},{6,7},{7,8},{8,9},{9,10},{10,1... | collective-permute-start | bytes 786440 | tf_op jit(solution)/shard_map/ppermute | solution.py:20
  111.5 11.5 %collective-permute-start.5 = (f32[1,16,4096]{2,1,0:T(8,128)}, f32[1,16,4096]{2,1,0:T(8,128)}, u32[]{:S(2)}, u32[]{:S(2)}) collective-permute-start(f32[1,16,4096]{2,1,0:T(8,128)} %get-tuple-element.116), channel_id=1, source_target_pairs={{0,2},{1,3},{2,4},{3,5},{4,6},{5,7},{6,8},{7,9},{8,10},{9,11},{10,... | collective-permute-start | bytes 786440 | tf_op jit(solution)/shard_map/ppermute | solution.py:20
  124.2 22.7 %copy-start.33 = (f32[16,4096]{1,0:T(8,128)S(1)}, f32[16,4096]{1,0:T(8,128)}, u32[]{:S(2)}) copy-start(f32[16,4096]{1,0:T(8,128)} %get-tuple-element.135) | copy-start | bytes 786436
  124.2 17.4 %collective-permute-start.6 = (f32[1,16,4096]{2,1,0:T(8,128)S(1)}, f32[1,16,4096]{2,1,0:T(8,128)S(1)}, u32[]{:S(2)}, u32[]{:S(2)}) collective-permute-start(f32[1,16,4096]{2,1,0:T(8,128)S(1)} %fusion.102), channel_id=1, source_target_pairs={{0,4},{1,5},{2,6},{3,7},{4,8},{5,9},{6,10},{7,11},{8,12},{9,13},{1... | collective-permute-start | bytes 786440 | tf_op jit(solution)/shard_map/ppermute | solution.py:20
  141.7 9.0 %collective-permute-start.7 = (f32[1,16,4096]{2,1,0:T(8,128)S(1)}, f32[1,16,4096]{2,1,0:T(8,128)S(1)}, u32[]{:S(2)}, u32[]{:S(2)}) collective-permute-start(f32[1,16,4096]{2,1,0:T(8,128)S(1)} %fusion.101), channel_id=1, source_target_pairs={{0,8},{1,9},{2,10},{3,11},{4,12},{5,13},{6,14},{7,15},{8,16},{9,17... | collective-permute-start | bytes 786440 | tf_op jit(solution)/shard_map/ppermute | solution.py:20
  146.9 22.0 %copy-start.52 = (f32[1,16,4096]{2,1,0:T(8,128)S(1)}, f32[1,16,4096]{2,1,0:T(8,128)}, u32[]{:S(2)}) copy-start(f32[1,16,4096]{2,1,0:T(8,128)} %get-tuple-element.115) | copy-start | bytes 786436
  147.4 31.3 %copy-start.16 = (f32[8,16,4096]{2,1,0:T(8,128)S(1)}, f32[8,16,4096]{2,1,0:T(8,128)}, u32[]{:S(2)}) copy-start(f32[8,16,4096]{2,1,0:T(8,128)} %copy-done.15) | copy-start | bytes 6291460
  147.4 31.3 %copy-start.38 = (f32[1,16,4096]{2,1,0:T(8,128)S(1)}, f32[1,16,4096]{2,1,0:T(8,128)}, u32[]{:S(2)}) copy-start(f32[1,16,4096]{2,1,0:T(8,128)} %copy-done.37) | copy-start | bytes 786436
  147.4 31.3 %copy-start.40 = (f32[1,16,4096]{2,1,0:T(8,128)S(1)}, f32[1,16,4096]{2,1,0:T(8,128)}, u32[]{:S(2)}) copy-start(f32[1,16,4096]{2,1,0:T(8,128)} %copy-done.39) | copy-start | bytes 786436
  150.8 21.7 %collective-permute-start.8 = (f32[1,16,4096]{2,1,0:T(8,128)S(1)}, f32[1,16,4096]{2,1,0:T(8,128)S(1)}, u32[]{:S(2)}, u32[]{:S(2)}) collective-permute-start(f32[1,16,4096]{2,1,0:T(8,128)S(1)} %fusion.100), channel_id=1, source_target_pairs={{0,16},{1,17},{2,18},{3,19},{4,20},{5,21},{6,22},{7,23},{8,24},{9,... | collective-permute-start | bytes 786440 | tf_op jit(solution)/shard_map/ppermute | solution.py:20
  168.8 47.5 %copy-start.53 = (f32[1,4096]{1,0:T(1,128)}, f32[1,4096]{1,0:T(1,128)S(1)}, u32[]{:S(2)}) copy-start(f32[1,4096]{1,0:T(1,128)S(1)} %get-tuple-element.121) | copy-start | bytes 49156
  168.8 47.5 %copy-start.55 = (f32[1,4096]{1,0:T(1,128)}, f32[1,4096]{1,0:T(1,128)S(1)}, u32[]{:S(2)}) copy-start(f32[1,4096]{1,0:T(1,128)S(1)} %get-tuple-element.122) | copy-start | bytes 49156
  168.8 47.5 %copy-start.57 = (f32[1,4096]{1,0:T(1,128)}, f32[1,4096]{1,0:T(1,128)S(1)}, u32[]{:S(2)}) copy-start(f32[1,4096]{1,0:T(1,128)S(1)} %get-tuple-element.123) | copy-start | bytes 49156
  168.9 47.5 %copy-start.59 = (f32[1,4096]{1,0:T(1,128)}, f32[1,4096]{1,0:T(1,128)S(1)}, u32[]{:S(2)}) copy-start(f32[1,4096]{1,0:T(1,128)S(1)} %get-tuple-element.124) | copy-start | bytes 49156
  168.9 47.5 %copy-start.61 = (f32[1,4096]{1,0:T(1,128)}, f32[1,4096]{1,0:T(1,128)S(1)}, u32[]{:S(2)}) copy-start(f32[1,4096]{1,0:T(1,128)S(1)} %get-tuple-element.125) | copy-start | bytes 49156
  168.9 47.5 %copy-start.63 = (f32[1,4096]{1,0:T(1,128)}, f32[1,4096]{1,0:T(1,128)S(1)}, u32[]{:S(2)}) copy-start(f32[1,4096]{1,0:T(1,128)S(1)} %get-tuple-element.126) | copy-start | bytes 49156
  168.9 47.5 %copy-start.65 = (f32[1,4096]{1,0:T(1,128)}, f32[1,4096]{1,0:T(1,128)S(1)}, u32[]{:S(2)}) copy-start(f32[1,4096]{1,0:T(1,128)S(1)} %get-tuple-element.127) | copy-start | bytes 49156
  168.9 47.5 %copy-start.67 = (f32[1,4096]{1,0:T(1,128)}, f32[1,4096]{1,0:T(1,128)S(1)}, u32[]{:S(2)}) copy-start(f32[1,4096]{1,0:T(1,128)S(1)} %get-tuple-element.128) | copy-start | bytes 49156
  168.9 47.5 %copy-start.69 = (f32[1,4096]{1,0:T(1,128)}, f32[1,4096]{1,0:T(1,128)S(1)}, u32[]{:S(2)}) copy-start(f32[1,4096]{1,0:T(1,128)S(1)} %get-tuple-element.129) | copy-start | bytes 49156
  168.9 47.5 %copy-start.71 = (f32[1,4096]{1,0:T(1,128)}, f32[1,4096]{1,0:T(1,128)S(1)}, u32[]{:S(2)}) copy-start(f32[1,4096]{1,0:T(1,128)S(1)} %get-tuple-element.130) | copy-start | bytes 49156
  168.9 47.5 %copy-start.73 = (f32[1,4096]{1,0:T(1,128)}, f32[1,4096]{1,0:T(1,128)S(1)}, u32[]{:S(2)}) copy-start(f32[1,4096]{1,0:T(1,128)S(1)} %get-tuple-element.131) | copy-start | bytes 49156
  168.9 47.5 %copy-start.75 = (f32[1,4096]{1,0:T(1,128)}, f32[1,4096]{1,0:T(1,128)S(1)}, u32[]{:S(2)}) copy-start(f32[1,4096]{1,0:T(1,128)S(1)} %get-tuple-element.132) | copy-start | bytes 49156
  169.0 9.8 %collective-permute-start.11 = (f32[1,16,4096]{2,1,0:T(8,128)S(1)}, f32[1,16,4096]{2,1,0:T(8,128)S(1)}, u32[]{:S(2)}, u32[]{:S(2)}) collective-permute-start(f32[1,16,4096]{2,1,0:T(8,128)S(1)} %copy-done.52), channel_id=1, source_target_pairs={{2,0},{3,1},{4,2},{5,3},{6,4},{7,5},{8,6},{9,7},{10,8},{11,9},{12,... | collective-permute-start | bytes 786440 | tf_op jit(solution)/shard_map/ppermute | solution.py:20
  179.5 8.3 %collective-permute-start.12 = (f32[1,16,4096]{2,1,0:T(8,128)S(1)}, f32[1,16,4096]{2,1,0:T(8,128)S(1)}, u32[]{:S(2)}, u32[]{:S(2)}) collective-permute-start(f32[1,16,4096]{2,1,0:T(8,128)S(1)} %get-tuple-element.54), channel_id=1, source_target_pairs={{4,0},{5,1},{6,2},{7,3},{8,4},{9,5},{10,6},{11,7},{12,8},{13,9},{1... | collective-permute-start | bytes 786440 | tf_op jit(solution)/shard_map/ppermute | solution.py:20
  188.5 11.7 %collective-permute-start.13 = (f32[1,16,4096]{2,1,0:T(8,128)S(1)}, f32[1,16,4096]{2,1,0:T(8,128)S(1)}, u32[]{:S(2)}, u32[]{:S(2)}) collective-permute-start(f32[1,16,4096]{2,1,0:T(8,128)S(1)} %get-tuple-element.112), channel_id=1, source_target_pairs={{8,0},{9,1},{10,2},{11,3},{12,4},{13,5},{14,6},{15,7},{16,8},{17,9... | collective-permute-start | bytes 786440 | tf_op jit(solution)/shard_map/ppermute | solution.py:20
  201.6 23.8 %collective-permute-start.14 = (f32[1,16,4096]{2,1,0:T(8,128)}, f32[1,16,4096]{2,1,0:T(8,128)S(1)}, u32[]{:S(2)}, u32[]{:S(2)}) collective-permute-start(f32[1,16,4096]{2,1,0:T(8,128)} %get-tuple-element.52), channel_id=1, source_target_pairs={{16,0},{17,1},{18,2},{19,3},{20,4},{21,5},{22,6},{23,7},{24,8},{25... | collective-permute-start | bytes 786440 | tf_op jit(solution)/shard_map/ppermute | solution.py:20
  278.4 7.3 %collective-permute-start.18 = (f32[16,38,128]{2,1,0:T(8,128)S(1)}, f32[16,38,128]{2,1,0:T(8,128)}, u32[]{:S(2)}, u32[]{:S(2)}) collective-permute-start(f32[16,38,128]{2,1,0:T(8,128)S(1)} %select_n.592), channel_id=1, source_target_pairs={{0,1},{1,0},{2,3},{3,2},{4,5},{5,4},{6,7},{7,6},{8,9},{9,8},{10,11... | collective-permute-start | bytes 933896 | tf_op jit(solution)/shard_map/ppermute | solution.py:69
  279.8 56.0 %copy-start.12 = (f32[1,1,128,4096]{3,2,1,0:T(8,128)S(1)}, f32[1,1,128,4096]{3,2,1,0:T(8,128)}, u32[]{:S(2)}) copy-start(f32[1,1,128,4096]{3,2,1,0:T(8,128)} %copy-done.11) | copy-start | bytes 6291460
  286.7 6.4 %collective-permute-start.19 = (f32[8,38,128]{2,1,0:T(8,128)S(1)}, f32[8,38,128]{2,1,0:T(8,128)S(1)}, u32[]{:S(2)}, u32[]{:S(2)}) collective-permute-start(f32[8,38,128]{2,1,0:T(8,128)S(1)} %slice_select_fusion.2), channel_id=1, source_target_pairs={{0,4},{1,5},{2,6},{3,7},{4,0},{5,1},{6,2},{7,3},{8,12},{9,13},{10,... | collective-permute-start | bytes 466952 | tf_op jit(solution)/shard_map/ppermute | solution.py:69
  293.2 9.7 %collective-permute-start.20 = (f32[4,38,128]{2,1,0:T(8,128)S(1)}, f32[4,38,128]{2,1,0:T(8,128)S(1)}, u32[]{:S(2)}, u32[]{:S(2)}) collective-permute-start(f32[4,38,128]{2,1,0:T(8,128)S(1)} %slice_select_fusion.3), channel_id=1, source_target_pairs={{0,2},{1,3},{2,0},{3,1},{4,6},{5,7},{6,4},{7,5},{8,10},{9,11},{10,... | collective-permute-start | bytes 233480 | tf_op jit(solution)/shard_map/ppermute | solution.py:69
  302.9 5.0 %collective-permute-start.21 = (f32[2,38,128]{2,1,0:T(8,128)S(1)}, f32[2,38,128]{2,1,0:T(8,128)S(1)}, u32[]{:S(2)}, u32[]{:S(2)}) collective-permute-start(f32[2,38,128]{2,1,0:T(8,128)S(1)} %slice_select_fusion.4), channel_id=1, source_target_pairs={{0,8},{1,9},{2,10},{3,11},{4,12},{5,13},{6,14},{7,15},{8,0},{9,1},... | collective-permute-start | bytes 116744 | tf_op jit(solution)/shard_map/ppermute | solution.py:69
  307.9 8.1 %collective-permute-start.22 = (f32[1,38,128]{2,1,0:T(8,128)S(1)}, f32[1,38,128]{2,1,0:T(8,128)S(1)}, u32[]{:S(2)}, u32[]{:S(2)}) collective-permute-start(f32[1,38,128]{2,1,0:T(8,128)S(1)} %slice_select_fusion.5), channel_id=1, source_target_pairs={{0,16},{1,17},{2,18},{3,19},{4,20},{5,21},{6,22},{7,23},{8,24},{9,... | collective-permute-start | bytes 58376 | tf_op jit(solution)/shard_map/ppermute | solution.py:69
  316.0 1.2 collective-permute-start.23
  317.2 3.8 collective-permute-start.24
  321.0 5.3 %collective-permute-start.25 = (f32[1,38,128]{2,1,0:T(8,128)S(1)}, f32[1,38,128]{2,1,0:T(8,128)S(1)}, u32[]{:S(2)}, u32[]{:S(2)}) collective-permute-start(f32[1,38,128]{2,1,0:T(8,128)S(1)} %add.507), channel_id=1, source_target_pairs={{0,128},{32,160},{64,192},{96,224},{128,0},{160,32},{192,64},{224,... | collective-permute-start | bytes 58376 | tf_op jit(solution)/shard_map/ppermute | solution.py:50
  326.3 7.7 %collective-permute-start.26 = (f32[1,38,128]{2,1,0:T(8,128)S(1)}, f32[1,38,128]{2,1,0:T(8,128)S(1)}, u32[]{:S(2)}, u32[]{:S(2)}) collective-permute-start(f32[1,38,128]{2,1,0:T(8,128)S(1)} %add.508), channel_id=1, source_target_pairs={{0,16},{1,17},{2,18},{3,19},{4,20},{5,21},{6,22},{7,23},{8,24},{9,... | collective-permute-start | bytes 58376 | tf_op jit(solution)/shard_map/ppermute | solution.py:72
  334.0 13.3 %collective-permute-start.27 = (f32[2,38,128]{2,1,0:T(8,128)S(1)}, f32[2,38,128]{2,1,0:T(8,128)S(1)}, u32[]{:S(2)}, u32[]{:S(2)}) collective-permute-start(f32[2,38,128]{2,1,0:T(8,128)S(1)} %maximum_select_fusion.4), channel_id=1, source_target_pairs={{0,8},{1,9},{2,10},{3,11},{4,12},{5,13},{6,14},{7,15},{8,0},{9,1},... | collective-permute-start | bytes 116744 | tf_op jit(solution)/shard_map/ppermute | solution.py:72
  347.4 17.6 %collective-permute-start.28 = (f32[4,38,128]{2,1,0:T(8,128)S(1)}, f32[4,38,128]{2,1,0:T(8,128)S(1)}, u32[]{:S(2)}, u32[]{:S(2)}) collective-permute-start(f32[4,38,128]{2,1,0:T(8,128)S(1)} %maximum_select_fusion.3), channel_id=1, source_target_pairs={{0,2},{1,3},{2,0},{3,1},{4,6},{5,7},{6,4},{7,5},{8,10},{9,11},{10,... | collective-permute-start | bytes 233480 | tf_op jit(solution)/shard_map/ppermute | solution.py:72
  365.1 6.7 %collective-permute-start.29 = (f32[8,38,128]{2,1,0:T(8,128)S(1)}, f32[8,38,128]{2,1,0:T(8,128)S(1)}, u32[]{:S(2)}, u32[]{:S(2)}) collective-permute-start(f32[8,38,128]{2,1,0:T(8,128)S(1)} %maximum_select_fusion.2), channel_id=1, source_target_pairs={{0,4},{1,5},{2,6},{3,7},{4,0},{5,1},{6,2},{7,3},{8,12},{9,13},{10,... | collective-permute-start | bytes 466952 | tf_op jit(solution)/shard_map/ppermute | solution.py:72
  365.2 8.3 %collective-permute-start.17 = (f32[1,6,4096]{2,1,0:T(8,128)S(1)}, f32[1,6,4096]{2,1,0:T(8,128)S(1)}, u32[]{:S(2)}, u32[]{:S(2)}) collective-permute-start(f32[1,6,4096]{2,1,0:T(8,128)S(1)} %get-tuple-element.69), channel_id=1, source_target_pairs={{1,0},{2,1},{3,2},{4,3},{5,4},{6,5},{7,6},{8,7},{9,8},{10,9},{11,1... | collective-permute-start | bytes 294920 | tf_op jit(solution)/shard_map/ppermute | solution.py:12
  366.5 9.8 %collective-permute-start.16 = (f32[1,6,4096]{2,1,0:T(8,128)S(1)}, f32[1,6,4096]{2,1,0:T(8,128)S(1)}, u32[]{:S(2)}, u32[]{:S(2)}) collective-permute-start(f32[1,6,4096]{2,1,0:T(8,128)S(1)} %get-tuple-element.70), channel_id=1, source_target_pairs={{1,0},{2,1},{3,2},{4,3},{5,4},{6,5},{7,6},{8,7},{9,8},{10,9},{11,1... | collective-permute-start | bytes 294920 | tf_op jit(solution)/shard_map/ppermute | solution.py:12
  367.8 11.3 %collective-permute-start.15 = (f32[1,6,4096]{2,1,0:T(8,128)S(1)}, f32[1,6,4096]{2,1,0:T(8,128)S(1)}, u32[]{:S(2)}, u32[]{:S(2)}) collective-permute-start(f32[1,6,4096]{2,1,0:T(8,128)S(1)} %get-tuple-element.71), channel_id=1, source_target_pairs={{1,0},{2,1},{3,2},{4,3},{5,4},{6,5},{7,6},{8,7},{9,8},{10,9},{11,1... | collective-permute-start | bytes 294920 | tf_op jit(solution)/shard_map/ppermute | solution.py:12
  371.8 11.1 %collective-permute-start.30 = (f32[16,38,128]{2,1,0:T(8,128)S(1)}, f32[16,38,128]{2,1,0:T(8,128)S(1)}, u32[]{:S(2)}, u32[]{:S(2)}) collective-permute-start(f32[16,38,128]{2,1,0:T(8,128)S(1)} %maximum_select_fusion.1), channel_id=1, source_target_pairs={{0,1},{1,0},{2,3},{3,2},{4,5},{5,4},{6,7},{7,6},{8,9},{9,8},{10,11... | collective-permute-start | bytes 933896 | tf_op jit(solution)/shard_map/ppermute | solution.py:72
  (102 other events, 993.2 us)

commit v6 on v5

--- a/solution.py
+++ b/solution.py
@@ -52,6 +52,46 @@
     return value
 
 
+def _digit(index, steps):
+    return sum(((index // step) % 2) * (1 << pos) for pos, step in enumerate(steps))
+
+
+def _mask(offset, steps):
+    return sum(step for pos, step in enumerate(steps) if (offset >> pos) & 1)
+
+
+def _exchange(block, axis, mask):
+    return lax.ppermute(block, axis, [(i, i ^ mask) for i in range(lax.axis_size(axis))])
+
+
+def scatter_stage(blocks, axis, steps, index):
+    radix = 1 << len(steps)
+    part = blocks.shape[0] // radix
+    digit = _digit(index, steps)
+    total = lax.dynamic_slice_in_dim(blocks, digit * part, part, axis=0)
+    for offset in range(1, radix):
+        piece = lax.dynamic_slice_in_dim(blocks, (digit ^ offset) * part, part, axis=0)
+        total = total + _exchange(piece, axis, _mask(offset, steps))
+    return total
+
+
+def gather_stage(blocks, axis, steps, index):
+    radix = 1 << len(steps)
+    digit = _digit(index, steps)
+    got = jnp.stack([blocks] + [_exchange(blocks, axis, _mask(o, steps)) for o in range(1, radix)])
+    return jnp.concatenate([lax.dynamic_index_in_dim(got, slot ^ digit, keepdims=False) for slot in range(radix)])
+
+
+def full_sum(value, axis):
+    count = lax.axis_size(axis)
+    index = lax.axis_index(axis)
+    got = jnp.stack([value] + [_exchange(value, axis, o) for o in range(1, count)])
+    total = lax.dynamic_index_in_dim(got, index, keepdims=False)
+    for member in range(1, count):
+        total = total + lax.dynamic_index_in_dim(got, member ^ index, keepdims=False)
+    return total
+
+
 def spread_sum(value, scatter_axis, other_axes):
     count = lax.axis_size(scatter_axis)
     if count & (count - 1) or value.shape[0] % count:
@@ -59,19 +99,16 @@
     index = lax.axis_index(scatter_axis)
     lanes = 128 if (value.shape[0] // count) % 128 == 0 else 1
     blocks = value.reshape(count, -1, lanes)
-    steps = [1 << bit for bit in range(count.bit_length() - 1)]
-    steps = [s for s in steps if s in (1, 4)] + [s for s in steps if s not in (1, 4)]
-    for step in steps:
-        half = blocks.shape[0] // 2
-        low = (index // step) % 2 == 0
-        keep = jnp.where(low, blocks[:half], blocks[half:])
-        send = jnp.where(low, blocks[half:], blocks[:half])
-        blocks = keep + lax.ppermute(send, scatter_axis, [(i, i ^ step) for i in range(count)])
-    blocks = butterfly_sum(blocks, other_axes)
-    for step in reversed(steps):
-        got = lax.ppermute(blocks, scatter_axis, [(i, i ^ step) for i in range(count)])
-        low = (index // step) % 2 == 0
-        blocks = jnp.where(low, jnp.concatenate([blocks, got]), jnp.concatenate([got, blocks]))
+    stages = [tuple(s for s in group if s < count) for group in ((1, 2), (4,), (8, 16))]
+    stages = [group for group in stages if group]
+    stages += [(1 << bit,) for bit in range(5, count.bit_length() - 1)]
+    for steps in stages:
+        blocks = scatter_stage(blocks, scatter_axis, steps, index)
+    for axis in other_axes:
+        size = lax.axis_size(axis)
+        blocks = full_sum(blocks, axis) if size & (size - 1) == 0 else lax.psum(blocks, axis)
+    for steps in reversed(stages):
+        blocks = gather_stage(blocks, scatter_axis, steps, index)
     return blocks.reshape(-1)
 
 

time: 390 us -> 388 us (level)
  waiting for transfers between devices: 70.4 us -> 62.5 us
    ppermute x6, waiting for transfers between devices: 5.96 us -> 1.01 us  [from_behind(): return lax.ppermute(block, axis, route)]
    ppermute x13 -> x21, waiting for transfers between devices: 30.3 us -> 27.1 us  [_exchange(): lax.ppermute(block, axis, [(i, i ^ mask) for i in range(lax.axis_size(axi...]
    ppermute x13 -> x21, starting transfers between devices: 35.3 us -> 37.4 us  [_exchange(): lax.ppermute(block, axis, [(i, i ^ mask) for i in range(lax.axis_size(axi...]
    unnamed x286 -> x298, local copies, waits for them, and re-layouts: 9.43 us -> 9.29 us
    unnamed x12 -> x13, other arithmetic: 12 us -> 11.8 us
  transfers between devices with their start and end apart: 31 -> 39, of which waited for: 21 -> 17; matrix products, arithmetic and copies ran while one was open for 21% -> 21% of each run, Pallas kernels for 0% -> 0%
where the time goes in v6:
time: 388 us; the launch traced here: 381 us
  other arithmetic  172 us (44%)
  starting transfers between devices  109 us (28%)
  waiting for transfers between devices  62.5 us (16%)
  local copies, waits for them, and re-layouts  28.6 us (7%)
  between operations  9.44 us (2%)
    ppermute x12, starting transfers between devices, moved(): return lax.ppermute(block, 'ctx', route)  57.1 us
    ppermute x21, starting transfers between devices, _exchange(): lax.ppermute(block, axis, [(i, i ^ mask) for i in range(lax.axis_size(axi...  37.4 us
    ppermute x12, waiting for transfers between devices, moved(): return lax.ppermute(block, 'ctx', route)  34.3 us
    ppermute x21, waiting for transfers between devices, _exchange(): lax.ppermute(block, axis, [(i, i ^ mask) for i in range(lax.axis_size(axi...  27.1 us
    reduce_sum x2, other arithmetic, shards(): tap_terms.append(jnp.sum(window(tap_index) * short_grads, axis=(1, 2)))  19.9 us
    ppermute x6, starting transfers between devices, from_behind(): return lax.ppermute(block, axis, route)  14 us
    add x1, other arithmetic, shards(): spread + short_taps[:, tap_index][:, None, None, :] * padded[:, :, tap_in...  14 us
    unnamed x13, other arithmetic  11.8 us
  transfers between devices with their start and end apart: 39, of which 17 were waited for; matrix products, arithmetic and copies ran while one was open for 21% of the time, Pallas kernels for 0%

profile of v6, /device:TPU:2, one launch (start us, length us, event | category | flops | bytes accessed | tf_op | source)
XLA Modules:
  0.0 381.0 jit_solution(848862969036337641)
XLA Ops:
  1.6 3.5 collective-permute-start.2
  5.9 3.5 collective-permute-start.1
  10.3 3.2 collective-permute-start
  19.3 2.9 fusion.139
  23.3 2.2 fusion.125
  28.7 9.6 %multiply_add_fusion = f32[3,1,128,4096]{3,2,1,0:T(8,128)S(1)} fusion(f32[3,4096]{1,0:T(4,128)S(1)} %get-tuple-element.190, f32[3,4096]{1,0:T(4,128)S(1)} %get-tuple-element.191, f32[3,4096]{1,0:T(4,128)S(1)} %get-tuple-element.192, f32[3,4096]{1,0:T(4,128)S(1)} %get-tuple-element.193, f32[3,4096]{1,0:T(4,128)S(1)} %get-tuple-element.194, ...), kind=kLoop, calls=%fused_computation.47 | loop fusion | flops 42467328 | bytes 28656512 | tf_op jit(solution)/shard_map/add | solution.py:162
  38.6 1.7 copy-done.29
  40.3 1.8 broadcast_select_fusion.7
  42.1 2.6 multiply_reduce_fusion.30
  44.8 4.1 %multiply_reduce_fusion.23 = (f32[4096]{0:T(1024)S(1)}, f32[4096]{0:T(1024)S(1)}, f32[4096]{0:T(1024)S(1)}, f32[4096]{0:T(1024)S(1)}, f32[4096]{0:T(1024)}, /*index=5*/f32[4096]{0:T(1024)}) fusion(f32[1,8,16,4096]{3,2,1,0:T(8,128)S(1)} %bitcast.556, f32[1,8,16,4096]{3,2,1,0:T(8,128)S(1)} %bitcast.559, pred[8,16]{1,0:T(8,128)(4,1)S(1)} %get-tuple-element.167, ...), kind=kLoop, calls=%fused_computation.162 | loop fusion | flops 9412608 | bytes 4293376 | tf_op jit(solution)/shard_map/reduce_sum | solution.py:247
  49.0 4.5 %multiply_reduce_fusion.14 = (f32[4096]{0:T(1024)}, f32[4096]{0:T(1024)}, f32[4096]{0:T(1024)}, f32[4096]{0:T(1024)}, f32[4096]{0:T(1024)}, /*index=5*/f32[4096]...) fusion(f32[1,8,16,4096]{3,2,1,0:T(8,128)S(1)} %bitcast.557, f32[1,8,16,4096]{3,2,1,0:T(8,128)S(1)} %bitcast.560, ...), kind=kLoop, calls=%fused_computation.153 | loop fusion | flops 14118912 | bytes 4342912 | tf_op jit(solution)/shard_map/reduce_sum | solution.py:247
  53.5 3.3 stack.269
  56.7 7.9 %fusion.13 = (f32[16,16,4096]{2,1,0:T(8,128)}, f32[16,16,4096]{2,1,0:T(8,128)}, f32[16,4096]{1,0:T(8,128)}, f32[16,4096]{1,0:T(8,128)}, f32[16,16,4096]{2,1,0:T(8,128)}) fusion(f32[16,4096]{1,0:T(8,128)} %get-tuple-element.140, f32[16,4096]{1,0:T(8,128)} %get-tuple-element.141, f32[16]{0:T(128)} %iota_convert_fusion, f32[16,4096]{1,0:T(8,128)} %get-tuple-element.142, ...), kind=kLoop, calls=%fused_computation.74 | loop fusion | flops 7208960 | bytes 14155840 | tf_op jit(solution)/shard_map/mul | solution.py:173
  64.7 4.6 %rev.6 = f32[16,16,4096]{2,1,0:T(8,128)} reverse(f32[16,16,4096]{2,1,0:T(8,128)} %get-tuple-element.116), dimensions={0} | reverse | bytes 8388608 | tf_op jit(solution)/shard_map/rev | solution.py:174
  69.3 2.0 broadcast_multiply_fusion.1
  72.1 2.7 multiply_reduce_fusion.1
  74.9 5.9 %multiply_bitcast_fusion.1 = (f32[1,16,4096]{2,1,0:T(8,128)S(1)}, f32[16,4096]{1,0:T(8,128)S(1)}) fusion(f32[]{:T(128)} %bitcast.47, f32[]{:T(128)} %bitcast.31, f32[1,8,16,4096]{3,2,1,0:T(8,128)S(1)} %bitcast.563, f32[]{:T(128)} %bitcast.33, f32[]{:T(128)} %bitcast.35, f32[]{:T(128)} %bitcast.37, f32[]{:T(128)} %bitcast.39, f32[]{:T(128)} %bitcast.41, ...), kind=kLoop, calls=%fused_computation.296 | loop fusion | flops 1769472 | bytes 2883620 | tf_op jit(solution)/shard_map/mul | solution.py:31
  83.7 1.9 copy-done.17
  85.6 2.7 multiply_reduce_fusion.3
  88.3 5.3 %fusion.72 = f32[1,16,4096]{2,1,0:T(8,128)S(1)} fusion(f32[1,8,16,4096]{3,2,1,0:T(8,128)S(1)} %bitcast.570, f32[]{:T(128)} %bitcast.45, f32[]{:T(128)} %bitcast.43, f32[]{:T(128)} %bitcast.41, f32[]{:T(128)} %bitcast.39, f32[]{:T(128)} %bitcast.37, f32[]{:T(128)} %bitcast.35, f32[]{:T(128)} %bitcast.33, f32[]{:T(128)} %bitcast.31, f32[16,4096]{1,0:T(8,128)S(1)} %copy-done.2), kind=kLoop, calls=%fused_computation.202 | loop fusion | flops 1703936 | bytes 2621472 | tf_op jit(solution)/shard_map/add | solution.py:203
  93.7 6.8 %collective-permute-start.4 = (f32[1,16,4096]{2,1,0:T(8,128)S(1)}, f32[1,16,4096]{2,1,0:T(8,128)S(1)}, u32[]{:S(2)}, u32[]{:S(2)}) collective-permute-start(f32[1,16,4096]{2,1,0:T(8,128)S(1)} %fusion.72), channel_id=1, source_target_pairs={{0,2},{1,3},{2,4},{3,5},{4,6},{5,7},{6,8},{7,9},{8,10},{9,11},{10,... | collective-permute-start | bytes 786440 | tf_op jit(solution)/shard_map/ppermute | solution.py:20
  100.6 4.1 %collective-permute-start.3 = (f32[1,16,4096]{2,1,0:T(8,128)S(1)}, f32[1,16,4096]{2,1,0:T(8,128)S(1)}, u32[]{:S(2)}, u32[]{:S(2)}) collective-permute-start(f32[1,16,4096]{2,1,0:T(8,128)S(1)} %fusion.72), channel_id=1, source_target_pairs={{0,1},{1,2},{2,3},{3,4},{4,5},{5,6},{6,7},{7,8},{8,9},{9,10},{10,1... | collective-permute-start | bytes 786440 | tf_op jit(solution)/shard_map/ppermute | solution.py:20
  105.3 1.9 collective-permute-done.4
  107.2 3.4 collective-permute-done.3
  111.5 7.0 %collective-permute-start.5 = (f32[1,16,4096]{2,1,0:T(8,128)}, f32[1,16,4096]{2,1,0:T(8,128)}, u32[]{:S(2)}, u32[]{:S(2)}) collective-permute-start(f32[1,16,4096]{2,1,0:T(8,128)} %get-tuple-element.123), channel_id=1, source_target_pairs={{0,2},{1,3},{2,4},{3,5},{4,6},{5,7},{6,8},{7,9},{8,10},{9,11},{10,... | collective-permute-start | bytes 786440 | tf_op jit(solution)/shard_map/ppermute | solution.py:20
  124.2 8.0 %collective-permute-start.6 = (f32[1,16,4096]{2,1,0:T(8,128)S(1)}, f32[1,16,4096]{2,1,0:T(8,128)S(1)}, u32[]{:S(2)}, u32[]{:S(2)}) collective-permute-start(f32[1,16,4096]{2,1,0:T(8,128)S(1)} %fusion.102), channel_id=1, source_target_pairs={{0,4},{1,5},{2,6},{3,7},{4,8},{5,9},{6,10},{7,11},{8,12},{9,13},{1... | collective-permute-start | bytes 786440 | tf_op jit(solution)/shard_map/ppermute | solution.py:20
  132.3 9.2 %broadcast_select_fusion.8 = (f32[1,8,16,4096]{3,2,1,0:T(8,128)S(1)}, f32[1,8,16,4096]{3,2,1,0:T(8,128)S(1)}, f32[1,8,16,4096]{3,2,1,0:T(8,128)S(1)}, f32[1,8,16...) fusion(pred[8,16]{1,0:T(8,128)(4,1)S(1)} %copy-done.77, ...), kind=kLoop, calls=%fused_computation.179 | loop fusion | flops 7340032 | bytes 31459072 | tf_op jit(solution)/shard_map/jit(_where)/select_n | solution.py:191
  141.7 5.2 %collective-permute-start.7 = (f32[1,16,4096]{2,1,0:T(8,128)S(1)}, f32[1,16,4096]{2,1,0:T(8,128)S(1)}, u32[]{:S(2)}, u32[]{:S(2)}) collective-permute-start(f32[1,16,4096]{2,1,0:T(8,128)S(1)} %fusion.101), channel_id=1, source_target_pairs={{0,8},{1,9},{2,10},{3,11},{4,12},{5,13},{6,14},{7,15},{8,16},{9,17... | collective-permute-start | bytes 786440 | tf_op jit(solution)/shard_map/ppermute | solution.py:20
  147.4 3.3 collective-permute-done.7
  150.8 17.8 %collective-permute-start.8 = (f32[1,16,4096]{2,1,0:T(8,128)S(1)}, f32[1,16,4096]{2,1,0:T(8,128)S(1)}, u32[]{:S(2)}, u32[]{:S(2)}) collective-permute-start(f32[1,16,4096]{2,1,0:T(8,128)S(1)} %fusion.100), channel_id=1, source_target_pairs={{0,16},{1,17},{2,18},{3,19},{4,20},{5,21},{6,22},{7,23},{8,24},{9,... | collective-permute-start | bytes 786440 | tf_op jit(solution)/shard_map/ppermute | solution.py:20
  170.2 2.3 collective-permute-done.8
  172.5 6.1 %collective-permute-done.11 = f32[1,16,4096]{2,1,0:T(8,128)S(1)} collective-permute-done((f32[1,16,4096]{2,1,0:T(8,128)S(1)}, f32[1,16,4096]{2,1,0:T(8,128)S(1)}, u32[]{:S(2)}, u32[]{:S(2)}) %collective-permute-start.11) | collective-permute-done | bytes 262176 | tf_op jit(solution)/shard_map/ppermute | solution.py:20
  180.9 6.9 %collective-permute-done.12 = f32[1,16,4096]{2,1,0:T(8,128)S(1)} collective-permute-done((f32[1,16,4096]{2,1,0:T(8,128)S(1)}, f32[1,16,4096]{2,1,0:T(8,128)S(1)}, u32[]{:S(2)}, u32[]{:S(2)}) %collective-permute-start.12) | collective-permute-done | bytes 262176 | tf_op jit(solution)/shard_map/ppermute | solution.py:20
  189.9 10.4 %collective-permute-done.13 = f32[1,16,4096]{2,1,0:T(8,128)S(1)} collective-permute-done((f32[1,16,4096]{2,1,0:T(8,128)S(1)}, f32[1,16,4096]{2,1,0:T(8,128)S(1)}, u32[]{:S(2)}, u32[]{:S(2)}) %collective-permute-start.13) | collective-permute-done | bytes 262176 | tf_op jit(solution)/shard_map/ppermute | solution.py:20
  200.3 1.5 broadcast_multiply_fusion.3
  201.8 1.7 collective-permute-start.14
  208.1 8.5 %multiply_reduce_fusion.2 = f32[8,16,4096]{2,1,0:T(8,128)S(1)} fusion(f32[8,16,4096]{2,1,0:T(8,128)S(1)} %bitcast.578, f32[16,16,4096]{2,1,0:T(8,128)S(1)} %copy-done.18), kind=kLoop, calls=%fused_computation.2 | loop fusion | flops 16252928 | bytes 8388608 | tf_op jit(solution)/shard_map/reduce_sum | solution.py:219
  217.0 6.9 %fusion.69 = f32[1,8,16,4096]{3,2,1,0:T(8,128)} fusion(f32[8,16,4096]{2,1,0:T(8,128)S(1)} %multiply_reduce_fusion.2, f32[1,8,16,4096]{3,2,1,0:T(8,128)S(1)} %bitcast.562, f32[8,16]{1,0:T(8,128)S(1)} %copy-done.75, f32[4096]{0:T(1024)S(1)} %bitcast.589, f32[4096]{0:T(1024)S(1)} %bitcast.591, f32[4096]{0:T(1024)S(1)} %bitcast.593, f32[4096]{0:T(1024)S(1)} %bitcast.595, ...), kind=kLoop, calls=%fused_computation.151 | loop fusion | flops 25690112 | bytes 6556160 | tf_op jit(solution)/shard_map/add | solution.py:222
  225.8 5.1 %bitcast_dynamic-update-slice_fusion.7 = (f32[8,1,16,4096]{3,2,1,0:T(8,128)S(1)}, f32[1,16,4096]{2,1,0:T(8,128)S(1)}, f32[1,16,4096]{2,1,0:T(8,128)S(1)}, f32[1,16,4096]{2,1,0:T(8,128)S(1)}) fusion(f32[1,8,16,4096]{3,2,1,0:T(8,128)S(1)} %bitcast.564, f32[]{:T(128)} %bitcast.43, f32[]{:T(128)} %bitcast.41, f32[16,4096]{1,0:T(8,128)S(1)} %copy-done.3, ...), kind=kLoop, calls=%fused_computation.210 | loop fusion | flops 1703935 | bytes 3670044
  233.5 8.4 %multiply_reduce_fusion = f32[8,16,4096]{2,1,0:T(8,128)S(1)} fusion(f32[8,16,4096]{2,1,0:T(8,128)S(1)} %bitcast.579, f32[16,16,4096]{2,1,0:T(8,128)S(1)} %reverse_multiply_fusion), kind=kLoop, calls=%fused_computation | loop fusion | flops 16252928 | bytes 8388608 | tf_op jit(solution)/shard_map/reduce_sum | solution.py:236
  242.1 7.0 %fusion.31 = f32[1,8,16,4096]{3,2,1,0:T(8,128)} fusion(f32[1,8,16,4096]{3,2,1,0:T(8,128)} %get-tuple-element.97, f32[1,8,16,4096]{3,2,1,0:T(8,128)S(1)} %get-tuple-element.85, f32[1,8,16,4096]{3,2,1,0:T(8,128)S(1)} %get-tuple-element.86, f32[1,8,16,4096]{3,2,1,0:T(8,128)S(1)} %copy-done.20, f32[1,8,16,4096]{3,2,1,0:T(8,128)S(1)} %copy-done.21, ...), kind=kLoop, calls=%fused_computation.102 | loop fusion | flops 17825792 | bytes 38011520 | tf_op jit(solution)/shard_map/add | solution.py:239
  249.1 8.3 %fusion.67 = (f32[1,1,128,4096]{3,2,1,0:T(8,128)S(1)}, f32[1,1,128,4096]{3,2,1,0:T(8,128)S(1)}, bf16[1,128,4096]{2,1,0:T(8,128)(2,1)}, f32[1,1,128,4096]{3,2,1,0:T(8,128)}) fusion(f32[3,1,128,4096]{3,2,1,0:T(8,128)} %copy-done.4, f32[1,128,4096]{2,1,0:T(8,128)S(1)} %copy-done.1, f32[4096]{0:T(1024)} %param.16, f32[1,8,16,4096]{3,2,1,0:T(8,128)} %fusion.31, ...), kind=kLoop, calls=%fused_computation.146 | loop fusion | flops 5242880 | bytes 23085056 | tf_op jit(solution)/shard_map/stack | solution.py:265
  257.5 11.8 %multiply_reduce_fusion.4 = (f32[3,4096]{1,0:T(4,128)S(1)}, f32[3,4096]{1,0:T(4,128)S(1)}, f32[3,4096]{1,0:T(4,128)S(1)}, f32[3,4096]{1,0:T(4,128)S(1)}, f32[3,4096]{1,0:T(4,128)S(1)}, /*index=5*/f32[3,4096]{1,0:T(4,128)S(1)}) fusion(pred[128]{0:T(512)(128)(4,1)S(1)} %copy-done.125, bf16[3,1,134,4096]{3,2,1,0:T(8,128)(2,1)S(1)} %pad_maximum_fusion.1, ...), kind=kLoop, calls=%fused_computation.40 | loop fusion | flops 40820736 | bytes 25461504 | tf_op jit(solution)/shard_map/reduce_sum | solution.py:276
  269.3 8.1 %multiply_reduce_fusion.10 = (f32[3,4096]{1,0:T(4,128)S(1)}, f32[3,1,128,4096]{3,2,1,0:T(8,128)}, f32[3,1,128,4096]{3,2,1,0:T(8,128)}, f32[3,1,128,4096]{3,2,1,0:T(8,128)}) fusion(pred[128]{0:T(512)(128)(4,1)S(1)} %copy-done.123, bf16[3,1,134,4096]{3,2,1,0:T(8,128)(2,1)S(1)} %pad_maximum_fusion.1, f32[1,1,128,4096]{3,2,1,0:T(8,128)S(1)} %get-tuple-element.64, ...), kind=kLoop, calls=%fused_computation.46 | loop fusion | flops 14143488 | bytes 28361088 | tf_op jit(solution)/shard_map/reduce_sum | solution.py:276
  279.3 1.7 collective-permute-start.18
  281.0 5.1 %collective-permute-start.20 = (f32[8,38,128]{2,1,0:T(8,128)S(1)}, f32[8,38,128]{2,1,0:T(8,128)}, u32[]{:S(2)}, u32[]{:S(2)}) collective-permute-start(f32[8,38,128]{2,1,0:T(8,128)S(1)} %get-tuple-element.103), channel_id=1, source_target_pairs={{0,3},{1,2},{2,1},{3,0},{4,7},{5,6},{6,5},{7,4},{8,11},{9,10},{10,... | collective-permute-start | bytes 466952 | tf_op jit(solution)/shard_map/ppermute | solution.py:64
  286.1 1.5 collective-permute-start.19
  287.6 4.7 %collective-permute-done.20 = f32[8,38,128]{2,1,0:T(8,128)} collective-permute-done((f32[8,38,128]{2,1,0:T(8,128)S(1)}, f32[8,38,128]{2,1,0:T(8,128)}, u32[]{:S(2)}, u32[]{:S(2)}) %collective-permute-start.20) | collective-permute-done | bytes 155680 | tf_op jit(solution)/shard_map/ppermute | solution.py:64
  292.3 2.2 collective-permute-done.19
  295.9 4.3 %collective-permute-done.21 = f32[4,38,128]{2,1,0:T(8,128)S(1)} collective-permute-done((f32[4,38,128]{2,1,0:T(8,128)S(1)}, f32[4,38,128]{2,1,0:T(8,128)S(1)}, u32[]{:S(2)}, u32[]{:S(2)}) %collective-permute-start.21) | collective-permute-done | bytes 77856 | tf_op jit(solution)/shard_map/ppermute | solution.py:64
  300.8 6.3 %collective-permute-start.24 = (f32[1,38,128]{2,1,0:T(8,128)S(1)}, f32[1,38,128]{2,1,0:T(8,128)S(1)}, u32[]{:S(2)}, u32[]{:S(2)}) collective-permute-start(f32[1,38,128]{2,1,0:T(8,128)S(1)} %get-tuple-element.154), channel_id=1, source_target_pairs={{0,24},{1,25},{2,26},{3,27},{4,28},{5,29},{6,30},{7,31},{8,16},{9,... | collective-permute-start | bytes 58376 | tf_op jit(solution)/shard_map/ppermute | solution.py:64
  307.7 11.7 %broadcast_select_fusion.2 = (f32[3,1,128,4096]{3,2,1,0:T(8,128)}, f32[3,1,128,4096]{3,2,1,0:T(8,128)}, f32[3,1,128,4096]{3,2,1,0:T(8,128)}, f32[3,1,128,4096]{3,2,1,0:T(8,128)}) fusion(pred[128]{0:T(512)(128)(4,1)S(1)} %copy-done.129, f32[1,1,128,4096]{3,2,1,0:T(8,128)} %copy-done.13, f32[1,1,128,4096]{3,2,1,0:T(8,128)S(1)} %copy-done.12, ...), kind=kLoop, calls=%fused_computation.78 | loop fusion | flops 9437184 | bytes 31457792 | tf_op jit(solution)/shard_map/jit(_where)/select_n | solution.py:269
  319.6 14.0 %fusion.6 = f32[3,1,134,4096]{3,2,1,0:T(8,128)S(1)} fusion(f32[3,1,128,4096]{3,2,1,0:T(8,128)S(1)} %bitcast.569, f32[3,1,128,4096]{3,2,1,0:T(8,128)} %get-tuple-element.82, f32[3,1,128,4096]{3,2,1,0:T(8,128)} %get-tuple-element.81, f32[3,1,128,4096]{3,2,1,0:T(8,128)} %get-tuple-element.80, f32[3,1,128,4096]{3,2,1,0:T(8,128)} %get-tuple-element.79, ...), kind=kLoop, calls=%fused_computation.32 | loop fusion | flops 21405696 | bytes 50970624 | tf_op jit(solution)/shard_map/add | solution.py:272
  333.6 1.6 collective-permute-start.30
  336.1 2.4 collective-permute-start.28
  338.5 1.6 collective-permute-start.27
  340.6 3.3 collective-permute-done.26
  344.0 3.1 collective-permute-done.31
  347.1 3.9 %collective-permute-start.34 = (f32[1,38,128]{2,1,0:T(8,128)S(1)}, f32[1,38,128]{2,1,0:T(8,128)S(1)}, u32[]{:S(2)}, u32[]{:S(2)}) collective-permute-start(f32[1,38,128]{2,1,0:T(8,128)S(1)} %fusion.143), channel_id=1, source_target_pairs={{0,24},{1,25},{2,26},{3,27},{4,28},{5,29},{6,30},{7,31},{8,16},{9,... | collective-permute-start | bytes 58376 | tf_op jit(solution)/shard_map/ppermute | solution.py:64
  351.1 1.8 collective-permute-start.33
  353.7 5.1 %collective-permute-done.33 = f32[1,38,128]{2,1,0:T(8,128)S(1)} collective-permute-done((f32[1,38,128]{2,1,0:T(8,128)S(1)}, f32[1,38,128]{2,1,0:T(8,128)S(1)}, u32[]{:S(2)}, u32[]{:S(2)}) %collective-permute-start.33) | collective-permute-done | bytes 19488 | tf_op jit(solution)/shard_map/ppermute | solution.py:64
  363.7 5.4 %collective-permute-start.37 = (f32[8,38,128]{2,1,0:T(8,128)S(1)}, f32[8,38,128]{2,1,0:T(8,128)S(1)}, u32[]{:S(2)}, u32[]{:S(2)}) collective-permute-start(f32[8,38,128]{2,1,0:T(8,128)S(1)} %get-tuple-element.144), channel_id=1, source_target_pairs={{0,2},{1,3},{2,0},{3,1},{4,6},{5,7},{6,4},{7,5},{8,10},{9,11},{10,... | collective-permute-start | bytes 466952 | tf_op jit(solution)/shard_map/ppermute | solution.py:64
  372.6 2.0 fusion.62
  374.6 2.9 collective-permute-done.36
  (415 shorter events, 51.2 us)
Async XLA Ops:
  1.6 25.7 %collective-permute-start.2 = (bf16[1,6,4096]{2,1,0:T(8,128)(2,1)S(1)}, bf16[1,6,4096]{2,1,0:T(8,128)(2,1)S(1)}, u32[]{:S(2)}, u32[]{:S(2)}) collective-permute-start(bf16[1,6,4096]{2,1,0:T(8,128)(2,1)S(1)} %slice.443), channel_id=1, source_target_pairs={{0,1},{1,2},{2,3},{3,4},{4,5},{5,6},{6,7},{7,8},{8,9},{9,10},{10,1... | collective-permute-start | bytes 147464 | tf_op jit(solution)/shard_map/ppermute | solution.py:12
  5.9 21.1 %collective-permute-start.1 = (bf16[1,6,4096]{2,1,0:T(8,128)(2,1)S(1)}, bf16[1,6,4096]{2,1,0:T(8,128)(2,1)S(1)}, u32[]{:S(2)}, u32[]{:S(2)}) collective-permute-start(bf16[1,6,4096]{2,1,0:T(8,128)(2,1)S(1)} %slice.442), channel_id=1, source_target_pairs={{0,1},{1,2},{2,3},{3,4},{4,5},{5,6},{6,7},{7,8},{8,9},{9,10},{10,1... | collective-permute-start | bytes 147464 | tf_op jit(solution)/shard_map/ppermute | solution.py:12
  10.3 16.4 %collective-permute-start = (bf16[1,6,4096]{2,1,0:T(8,128)(2,1)S(1)}, bf16[1,6,4096]{2,1,0:T(8,128)(2,1)S(1)}, u32[]{:S(2)}, u32[]{:S(2)}) collective-permute-start(bf16[1,6,4096]{2,1,0:T(8,128)(2,1)S(1)} %slice.441), channel_id=1, source_target_pairs={{0,1},{1,2},{2,3},{3,4},{4,5},{5,6},{6,7},{7,8},{8,9},{9,10},{10,1... | collective-permute-start | bytes 147464 | tf_op jit(solution)/shard_map/ppermute | solution.py:12
  80.8 24.5 %collective-permute-start.9 = (f32[1,16,4096]{2,1,0:T(8,128)S(1)}, f32[1,16,4096]{2,1,0:T(8,128)S(1)}, u32[]{:S(2)}, u32[]{:S(2)}) collective-permute-start(f32[1,16,4096]{2,1,0:T(8,128)S(1)} %bitcast.583), channel_id=1, source_target_pairs={{1,0},{2,1},{3,2},{4,3},{5,4},{6,5},{7,6},{8,7},{9,8},{10,9},{11,1... | collective-permute-start | bytes 786440 | tf_op jit(solution)/shard_map/ppermute | solution.py:20
  82.1 23.2 %collective-permute-start.10 = (f32[1,16,4096]{2,1,0:T(8,128)S(1)}, f32[1,16,4096]{2,1,0:T(8,128)S(1)}, u32[]{:S(2)}, u32[]{:S(2)}) collective-permute-start(f32[1,16,4096]{2,1,0:T(8,128)S(1)} %get-tuple-element.58), channel_id=1, source_target_pairs={{2,0},{3,1},{4,2},{5,3},{6,4},{7,5},{8,6},{9,7},{10,8},{11,9},{12,... | collective-permute-start | bytes 786440 | tf_op jit(solution)/shard_map/ppermute | solution.py:20
  93.6 38.6 %copy-start.77 = (pred[8,16]{1,0:T(8,128)(4,1)S(1)}, pred[8,16]{1,0:T(8,128)(4,1)}, u32[]{:S(2)}) copy-start(pred[8,16]{1,0:T(8,128)(4,1)} %copy-done.76) | copy-start | bytes 388
  93.6 38.6 %copy-start.80 = (pred[8,16]{1,0:T(8,128)(4,1)S(1)}, pred[8,16]{1,0:T(8,128)(4,1)}, u32[]{:S(2)}) copy-start(pred[8,16]{1,0:T(8,128)(4,1)} %copy-done.79) | copy-start | bytes 388
  93.6 38.6 %copy-start.83 = (pred[8,16]{1,0:T(8,128)(4,1)S(1)}, pred[8,16]{1,0:T(8,128)(4,1)}, u32[]{:S(2)}) copy-start(pred[8,16]{1,0:T(8,128)(4,1)} %copy-done.82) | copy-start | bytes 388
  93.6 38.6 %copy-start.86 = (pred[8,16]{1,0:T(8,128)(4,1)S(1)}, pred[8,16]{1,0:T(8,128)(4,1)}, u32[]{:S(2)}) copy-start(pred[8,16]{1,0:T(8,128)(4,1)} %copy-done.85) | copy-start | bytes 388
  93.6 38.6 %copy-start.89 = (pred[8,16]{1,0:T(8,128)(4,1)S(1)}, pred[8,16]{1,0:T(8,128)(4,1)}, u32[]{:S(2)}) copy-start(pred[8,16]{1,0:T(8,128)(4,1)} %copy-done.88) | copy-start | bytes 388
  93.7 38.6 %copy-start.92 = (pred[8,16]{1,0:T(8,128)(4,1)S(1)}, pred[8,16]{1,0:T(8,128)(4,1)}, u32[]{:S(2)}) copy-start(pred[8,16]{1,0:T(8,128)(4,1)} %copy-done.91) | copy-start | bytes 388
  93.7 38.6 %copy-start.95 = (pred[8,16]{1,0:T(8,128)(4,1)S(1)}, pred[8,16]{1,0:T(8,128)(4,1)}, u32[]{:S(2)}) copy-start(pred[8,16]{1,0:T(8,128)(4,1)} %copy-done.94) | copy-start | bytes 388
  93.7 38.6 %copy-start.98 = (pred[8,16]{1,0:T(8,128)(4,1)S(1)}, pred[8,16]{1,0:T(8,128)(4,1)}, u32[]{:S(2)}) copy-start(pred[8,16]{1,0:T(8,128)(4,1)} %copy-done.97) | copy-start | bytes 388
  93.7 38.6 %copy-start.101 = (pred[8,16]{1,0:T(8,128)(4,1)S(1)}, pred[8,16]{1,0:T(8,128)(4,1)}, u32[]{:S(2)}) copy-start(pred[8,16]{1,0:T(8,128)(4,1)} %copy-done.100) | copy-start | bytes 388
  93.7 38.6 %copy-start.104 = (pred[8,16]{1,0:T(8,128)(4,1)S(1)}, pred[8,16]{1,0:T(8,128)(4,1)}, u32[]{:S(2)}) copy-start(pred[8,16]{1,0:T(8,128)(4,1)} %copy-done.103) | copy-start | bytes 388
  93.7 38.6 %copy-start.107 = (pred[8,16]{1,0:T(8,128)(4,1)S(1)}, pred[8,16]{1,0:T(8,128)(4,1)}, u32[]{:S(2)}) copy-start(pred[8,16]{1,0:T(8,128)(4,1)} %copy-done.106) | copy-start | bytes 388
  93.7 38.6 %copy-start.110 = (pred[8,16]{1,0:T(8,128)(4,1)S(1)}, pred[8,16]{1,0:T(8,128)(4,1)}, u32[]{:S(2)}) copy-start(pred[8,16]{1,0:T(8,128)(4,1)} %copy-done.109) | copy-start | bytes 388
  93.7 38.6 %copy-start.113 = (pred[8,16]{1,0:T(8,128)(4,1)S(1)}, pred[8,16]{1,0:T(8,128)(4,1)}, u32[]{:S(2)}) copy-start(pred[8,16]{1,0:T(8,128)(4,1)} %copy-done.112) | copy-start | bytes 388
  93.7 38.6 %copy-start.116 = (pred[8,16]{1,0:T(8,128)(4,1)S(1)}, pred[8,16]{1,0:T(8,128)(4,1)}, u32[]{:S(2)}) copy-start(pred[8,16]{1,0:T(8,128)(4,1)} %copy-done.115) | copy-start | bytes 388
  93.7 13.5 %collective-permute-start.4 = (f32[1,16,4096]{2,1,0:T(8,128)S(1)}, f32[1,16,4096]{2,1,0:T(8,128)S(1)}, u32[]{:S(2)}, u32[]{:S(2)}) collective-permute-start(f32[1,16,4096]{2,1,0:T(8,128)S(1)} %fusion.72), channel_id=1, source_target_pairs={{0,2},{1,3},{2,4},{3,5},{4,6},{5,7},{6,8},{7,9},{8,10},{9,11},{10,... | collective-permute-start | bytes 786440 | tf_op jit(solution)/shard_map/ppermute | solution.py:20
  100.6 10.0 %collective-permute-start.3 = (f32[1,16,4096]{2,1,0:T(8,128)S(1)}, f32[1,16,4096]{2,1,0:T(8,128)S(1)}, u32[]{:S(2)}, u32[]{:S(2)}) collective-permute-start(f32[1,16,4096]{2,1,0:T(8,128)S(1)} %fusion.72), channel_id=1, source_target_pairs={{0,1},{1,2},{2,3},{3,4},{4,5},{5,6},{6,7},{7,8},{8,9},{9,10},{10,1... | collective-permute-start | bytes 786440 | tf_op jit(solution)/shard_map/ppermute | solution.py:20
  111.5 11.5 %collective-permute-start.5 = (f32[1,16,4096]{2,1,0:T(8,128)}, f32[1,16,4096]{2,1,0:T(8,128)}, u32[]{:S(2)}, u32[]{:S(2)}) collective-permute-start(f32[1,16,4096]{2,1,0:T(8,128)} %get-tuple-element.123), channel_id=1, source_target_pairs={{0,2},{1,3},{2,4},{3,5},{4,6},{5,7},{6,8},{7,9},{8,10},{9,11},{10,... | collective-permute-start | bytes 786440 | tf_op jit(solution)/shard_map/ppermute | solution.py:20
  124.2 17.4 %collective-permute-start.6 = (f32[1,16,4096]{2,1,0:T(8,128)S(1)}, f32[1,16,4096]{2,1,0:T(8,128)S(1)}, u32[]{:S(2)}, u32[]{:S(2)}) collective-permute-start(f32[1,16,4096]{2,1,0:T(8,128)S(1)} %fusion.102), channel_id=1, source_target_pairs={{0,4},{1,5},{2,6},{3,7},{4,8},{5,9},{6,10},{7,11},{8,12},{9,13},{1... | collective-permute-start | bytes 786440 | tf_op jit(solution)/shard_map/ppermute | solution.py:20
  141.7 9.0 %collective-permute-start.7 = (f32[1,16,4096]{2,1,0:T(8,128)S(1)}, f32[1,16,4096]{2,1,0:T(8,128)S(1)}, u32[]{:S(2)}, u32[]{:S(2)}) collective-permute-start(f32[1,16,4096]{2,1,0:T(8,128)S(1)} %fusion.101), channel_id=1, source_target_pairs={{0,8},{1,9},{2,10},{3,11},{4,12},{5,13},{6,14},{7,15},{8,16},{9,17... | collective-permute-start | bytes 786440 | tf_op jit(solution)/shard_map/ppermute | solution.py:20
  147.4 31.3 %copy-start.16 = (f32[8,16,4096]{2,1,0:T(8,128)S(1)}, f32[8,16,4096]{2,1,0:T(8,128)}, u32[]{:S(2)}) copy-start(f32[8,16,4096]{2,1,0:T(8,128)} %copy-done.15) | copy-start | bytes 6291460
  147.4 31.3 %copy-start.38 = (f32[1,16,4096]{2,1,0:T(8,128)S(1)}, f32[1,16,4096]{2,1,0:T(8,128)}, u32[]{:S(2)}) copy-start(f32[1,16,4096]{2,1,0:T(8,128)} %copy-done.37) | copy-start | bytes 786436
  147.4 31.3 %copy-start.40 = (f32[1,16,4096]{2,1,0:T(8,128)S(1)}, f32[1,16,4096]{2,1,0:T(8,128)}, u32[]{:S(2)}) copy-start(f32[1,16,4096]{2,1,0:T(8,128)} %copy-done.39) | copy-start | bytes 786436
  150.8 21.7 %collective-permute-start.8 = (f32[1,16,4096]{2,1,0:T(8,128)S(1)}, f32[1,16,4096]{2,1,0:T(8,128)S(1)}, u32[]{:S(2)}, u32[]{:S(2)}) collective-permute-start(f32[1,16,4096]{2,1,0:T(8,128)S(1)} %fusion.100), channel_id=1, source_target_pairs={{0,16},{1,17},{2,18},{3,19},{4,20},{5,21},{6,22},{7,23},{8,24},{9,... | collective-permute-start | bytes 786440 | tf_op jit(solution)/shard_map/ppermute | solution.py:20
  168.8 47.9 %copy-start.55 = (f32[1,4096]{1,0:T(1,128)}, f32[1,4096]{1,0:T(1,128)S(1)}, u32[]{:S(2)}) copy-start(f32[1,4096]{1,0:T(1,128)S(1)} %get-tuple-element.132) | copy-start | bytes 49156
  168.8 47.9 %copy-start.57 = (f32[1,4096]{1,0:T(1,128)}, f32[1,4096]{1,0:T(1,128)S(1)}, u32[]{:S(2)}) copy-start(f32[1,4096]{1,0:T(1,128)S(1)} %get-tuple-element.133) | copy-start | bytes 49156
  168.8 47.9 %copy-start.59 = (f32[1,4096]{1,0:T(1,128)}, f32[1,4096]{1,0:T(1,128)S(1)}, u32[]{:S(2)}) copy-start(f32[1,4096]{1,0:T(1,128)S(1)} %get-tuple-element.134) | copy-start | bytes 49156
  168.8 47.9 %copy-start.61 = (f32[1,4096]{1,0:T(1,128)}, f32[1,4096]{1,0:T(1,128)S(1)}, u32[]{:S(2)}) copy-start(f32[1,4096]{1,0:T(1,128)S(1)} %get-tuple-element.135) | copy-start | bytes 49156
  168.8 47.9 %copy-start.63 = (f32[1,4096]{1,0:T(1,128)}, f32[1,4096]{1,0:T(1,128)S(1)}, u32[]{:S(2)}) copy-start(f32[1,4096]{1,0:T(1,128)S(1)} %get-tuple-element.136) | copy-start | bytes 49156
  168.9 47.9 %copy-start.65 = (f32[1,4096]{1,0:T(1,128)}, f32[1,4096]{1,0:T(1,128)S(1)}, u32[]{:S(2)}) copy-start(f32[1,4096]{1,0:T(1,128)S(1)} %get-tuple-element.137) | copy-start | bytes 49156
  168.9 47.9 %copy-start.67 = (f32[1,4096]{1,0:T(1,128)}, f32[1,4096]{1,0:T(1,128)S(1)}, u32[]{:S(2)}) copy-start(f32[1,4096]{1,0:T(1,128)S(1)} %get-tuple-element.138) | copy-start | bytes 49156
  168.9 47.9 %copy-start.69 = (f32[1,4096]{1,0:T(1,128)}, f32[1,4096]{1,0:T(1,128)S(1)}, u32[]{:S(2)}) copy-start(f32[1,4096]{1,0:T(1,128)S(1)} %get-tuple-element.139) | copy-start | bytes 49156
  168.9 9.8 %collective-permute-start.11 = (f32[1,16,4096]{2,1,0:T(8,128)S(1)}, f32[1,16,4096]{2,1,0:T(8,128)S(1)}, u32[]{:S(2)}, u32[]{:S(2)}) collective-permute-start(f32[1,16,4096]{2,1,0:T(8,128)S(1)} %copy-done.54), channel_id=1, source_target_pairs={{2,0},{3,1},{4,2},{5,3},{6,4},{7,5},{8,6},{9,7},{10,8},{11,9},{12,... | collective-permute-start | bytes 786440 | tf_op jit(solution)/shard_map/ppermute | solution.py:20
  179.5 8.3 %collective-permute-start.12 = (f32[1,16,4096]{2,1,0:T(8,128)S(1)}, f32[1,16,4096]{2,1,0:T(8,128)S(1)}, u32[]{:S(2)}, u32[]{:S(2)}) collective-permute-start(f32[1,16,4096]{2,1,0:T(8,128)S(1)} %get-tuple-element.56), channel_id=1, source_target_pairs={{4,0},{5,1},{6,2},{7,3},{8,4},{9,5},{10,6},{11,7},{12,8},{13,9},{1... | collective-permute-start | bytes 786440 | tf_op jit(solution)/shard_map/ppermute | solution.py:20
  188.6 11.7 %collective-permute-start.13 = (f32[1,16,4096]{2,1,0:T(8,128)S(1)}, f32[1,16,4096]{2,1,0:T(8,128)S(1)}, u32[]{:S(2)}, u32[]{:S(2)}) collective-permute-start(f32[1,16,4096]{2,1,0:T(8,128)S(1)} %get-tuple-element.119), channel_id=1, source_target_pairs={{8,0},{9,1},{10,2},{11,3},{12,4},{13,5},{14,6},{15,7},{16,8},{17,9... | collective-permute-start | bytes 786440 | tf_op jit(solution)/shard_map/ppermute | solution.py:20
  201.8 24.1 %collective-permute-start.14 = (f32[1,16,4096]{2,1,0:T(8,128)}, f32[1,16,4096]{2,1,0:T(8,128)S(1)}, u32[]{:S(2)}, u32[]{:S(2)}) collective-permute-start(f32[1,16,4096]{2,1,0:T(8,128)} %get-tuple-element.54), channel_id=1, source_target_pairs={{16,0},{17,1},{18,2},{19,3},{20,4},{21,5},{22,6},{23,7},{24,8},{25... | collective-permute-start | bytes 786440 | tf_op jit(solution)/shard_map/ppermute | solution.py:20
  279.3 8.2 %collective-permute-start.18 = (f32[8,38,128]{2,1,0:T(8,128)}, f32[8,38,128]{2,1,0:T(8,128)S(1)}, u32[]{:S(2)}, u32[]{:S(2)}) collective-permute-start(f32[8,38,128]{2,1,0:T(8,128)} %get-tuple-element.102), channel_id=1, source_target_pairs={{0,1},{1,0},{2,3},{3,2},{4,5},{5,4},{6,7},{7,6},{8,9},{9,8},{10,11... | collective-permute-start | bytes 466952 | tf_op jit(solution)/shard_map/ppermute | solution.py:64
  281.0 11.3 %collective-permute-start.20 = (f32[8,38,128]{2,1,0:T(8,128)S(1)}, f32[8,38,128]{2,1,0:T(8,128)}, u32[]{:S(2)}, u32[]{:S(2)}) collective-permute-start(f32[8,38,128]{2,1,0:T(8,128)S(1)} %get-tuple-element.103), channel_id=1, source_target_pairs={{0,3},{1,2},{2,1},{3,0},{4,7},{5,6},{6,5},{7,4},{8,11},{9,10},{10,... | collective-permute-start | bytes 466952 | tf_op jit(solution)/shard_map/ppermute | solution.py:64
  286.1 8.4 %collective-permute-start.19 = (f32[8,38,128]{2,1,0:T(8,128)S(1)}, f32[8,38,128]{2,1,0:T(8,128)}, u32[]{:S(2)}, u32[]{:S(2)}) collective-permute-start(f32[8,38,128]{2,1,0:T(8,128)S(1)} %get-tuple-element.104), channel_id=1, source_target_pairs={{0,2},{1,3},{2,0},{3,1},{4,6},{5,7},{6,4},{7,5},{8,10},{9,11},{10,... | collective-permute-start | bytes 466952 | tf_op jit(solution)/shard_map/ppermute | solution.py:64
  295.6 4.5 %collective-permute-start.21 = (f32[4,38,128]{2,1,0:T(8,128)S(1)}, f32[4,38,128]{2,1,0:T(8,128)S(1)}, u32[]{:S(2)}, u32[]{:S(2)}) collective-permute-start(f32[4,38,128]{2,1,0:T(8,128)S(1)} %constant_dynamic-slice_fusion.3), channel_id=1, source_target_pairs={{0,4},{1,5},{2,6},{3,7},{4,0},{5,1},{6,2},{7,3},{8,12},{9,13},{10,... | collective-permute-start | bytes 233480 | tf_op jit(solution)/shard_map/ppermute | solution.py:64
  300.2 19.2 %collective-permute-start.22 = (f32[1,38,128]{2,1,0:T(8,128)S(1)}, f32[1,38,128]{2,1,0:T(8,128)S(1)}, u32[]{:S(2)}, u32[]{:S(2)}) collective-permute-start(f32[1,38,128]{2,1,0:T(8,128)S(1)} %get-tuple-element.153), channel_id=1, source_target_pairs={{0,8},{1,9},{2,10},{3,11},{4,12},{5,13},{6,14},{7,15},{8,0},{9,1},... | collective-permute-start | bytes 58376 | tf_op jit(solution)/shard_map/ppermute | solution.py:64
  300.8 18.6 %collective-permute-start.24 = (f32[1,38,128]{2,1,0:T(8,128)S(1)}, f32[1,38,128]{2,1,0:T(8,128)S(1)}, u32[]{:S(2)}, u32[]{:S(2)}) collective-permute-start(f32[1,38,128]{2,1,0:T(8,128)S(1)} %get-tuple-element.154), channel_id=1, source_target_pairs={{0,24},{1,25},{2,26},{3,27},{4,28},{5,29},{6,30},{7,31},{8,16},{9,... | collective-permute-start | bytes 58376 | tf_op jit(solution)/shard_map/ppermute | solution.py:64
  307.2 12.2 %collective-permute-start.23 = (f32[1,38,128]{2,1,0:T(8,128)S(1)}, f32[1,38,128]{2,1,0:T(8,128)S(1)}, u32[]{:S(2)}, u32[]{:S(2)}) collective-permute-start(f32[1,38,128]{2,1,0:T(8,128)S(1)} %get-tuple-element.155), channel_id=1, source_target_pairs={{0,16},{1,17},{2,18},{3,19},{4,20},{5,21},{6,22},{7,23},{8,24},{9,... | collective-permute-start | bytes 58376 | tf_op jit(solution)/shard_map/ppermute | solution.py:64
  319.4 20.7 %collective-permute-start.25 = (f32[1,38,128]{2,1,0:T(8,128)S(1)}, f32[1,38,128]{2,1,0:T(8,128)S(1)}, u32[]{:S(2)}, u32[]{:S(2)}) collective-permute-start(f32[1,38,128]{2,1,0:T(8,128)S(1)} %get-tuple-element.33), channel_id=1, source_target_pairs={{0,32},{32,0},{64,96},{96,64},{128,160},{160,128},{192,224},{224,1... | collective-permute-start | bytes 58376 | tf_op jit(solution)/shard_map/ppermute | solution.py:64
  333.6 10.4 %collective-permute-start.30 = (f32[1,38,128]{2,1,0:T(8,128)S(1)}, f32[1,38,128]{2,1,0:T(8,128)S(1)}, u32[]{:S(2)}, u32[]{:S(2)}) collective-permute-start(f32[1,38,128]{2,1,0:T(8,128)S(1)} %get-tuple-element.33), channel_id=1, source_target_pairs={{0,192},{32,224},{64,128},{96,160},{128,64},{160,96},{192,0},{224,... | collective-permute-start | bytes 58376 | tf_op jit(solution)/shard_map/ppermute | solution.py:64
  335.2 8.8 %collective-permute-start.29 = (f32[1,38,128]{2,1,0:T(8,128)S(1)}, f32[1,38,128]{2,1,0:T(8,128)S(1)}, u32[]{:S(2)}, u32[]{:S(2)}) collective-permute-start(f32[1,38,128]{2,1,0:T(8,128)S(1)} %get-tuple-element.33), channel_id=1, source_target_pairs={{0,160},{32,128},{64,224},{96,192},{128,32},{160,0},{192,96},{224,... | collective-permute-start | bytes 58376 | tf_op jit(solution)/shard_map/ppermute | solution.py:64
  336.1 7.9 %collective-permute-start.28 = (f32[1,38,128]{2,1,0:T(8,128)S(1)}, f32[1,38,128]{2,1,0:T(8,128)S(1)}, u32[]{:S(2)}, u32[]{:S(2)}) collective-permute-start(f32[1,38,128]{2,1,0:T(8,128)S(1)} %get-tuple-element.33), channel_id=1, source_target_pairs={{0,128},{32,160},{64,192},{96,224},{128,0},{160,32},{192,64},{224,... | collective-permute-start | bytes 58376 | tf_op jit(solution)/shard_map/ppermute | solution.py:64
  338.5 5.4 %collective-permute-start.27 = (f32[1,38,128]{2,1,0:T(8,128)S(1)}, f32[1,38,128]{2,1,0:T(8,128)S(1)}, u32[]{:S(2)}, u32[]{:S(2)}) collective-permute-start(f32[1,38,128]{2,1,0:T(8,128)S(1)} %get-tuple-element.33), channel_id=1, source_target_pairs={{0,96},{32,64},{64,32},{96,0},{128,224},{160,192},{192,160},{224,1... | collective-permute-start | bytes 58376 | tf_op jit(solution)/shard_map/ppermute | solution.py:64
  340.1 3.8 collective-permute-start.26
  343.9 3.2 collective-permute-start.31
  347.1 6.6 %collective-permute-start.34 = (f32[1,38,128]{2,1,0:T(8,128)S(1)}, f32[1,38,128]{2,1,0:T(8,128)S(1)}, u32[]{:S(2)}, u32[]{:S(2)}) collective-permute-start(f32[1,38,128]{2,1,0:T(8,128)S(1)} %fusion.143), channel_id=1, source_target_pairs={{0,24},{1,25},{2,26},{3,27},{4,28},{5,29},{6,30},{7,31},{8,16},{9,... | collective-permute-start | bytes 58376 | tf_op jit(solution)/shard_map/ppermute | solution.py:64
  351.1 7.8 %collective-permute-start.33 = (f32[1,38,128]{2,1,0:T(8,128)S(1)}, f32[1,38,128]{2,1,0:T(8,128)S(1)}, u32[]{:S(2)}, u32[]{:S(2)}) collective-permute-start(f32[1,38,128]{2,1,0:T(8,128)S(1)} %fusion.143), channel_id=1, source_target_pairs={{0,16},{1,17},{2,18},{3,19},{4,20},{5,21},{6,22},{7,23},{8,24},{9,... | collective-permute-start | bytes 58376 | tf_op jit(solution)/shard_map/ppermute | solution.py:64
  352.9 6.0 %collective-permute-start.32 = (f32[1,38,128]{2,1,0:T(8,128)S(1)}, f32[1,38,128]{2,1,0:T(8,128)S(1)}, u32[]{:S(2)}, u32[]{:S(2)}) collective-permute-start(f32[1,38,128]{2,1,0:T(8,128)S(1)} %fusion.143), channel_id=1, source_target_pairs={{0,8},{1,9},{2,10},{3,11},{4,12},{5,13},{6,14},{7,15},{8,0},{9,1},... | collective-permute-start | bytes 58376 | tf_op jit(solution)/shard_map/ppermute | solution.py:64
  358.9 4.7 %collective-permute-start.35 = (f32[4,38,128]{2,1,0:T(8,128)S(1)}, f32[4,38,128]{2,1,0:T(8,128)S(1)}, u32[]{:S(2)}, u32[]{:S(2)}) collective-permute-start(f32[4,38,128]{2,1,0:T(8,128)S(1)} %get-tuple-element.147), channel_id=1, source_target_pairs={{0,4},{1,5},{2,6},{3,7},{4,0},{5,1},{6,2},{7,3},{8,12},{9,13},{10,... | collective-permute-start | bytes 233480 | tf_op jit(solution)/shard_map/ppermute | solution.py:64
  359.1 11.5 %collective-permute-start.17 = (f32[1,6,4096]{2,1,0:T(8,128)S(1)}, f32[1,6,4096]{2,1,0:T(8,128)S(1)}, u32[]{:S(2)}, u32[]{:S(2)}) collective-permute-start(f32[1,6,4096]{2,1,0:T(8,128)S(1)} %get-tuple-element.71), channel_id=1, source_target_pairs={{1,0},{2,1},{3,2},{4,3},{5,4},{6,5},{7,6},{8,7},{9,8},{10,9},{11,1... | collective-permute-start | bytes 294920 | tf_op jit(solution)/shard_map/ppermute | solution.py:12
  360.4 11.2 %collective-permute-start.16 = (f32[1,6,4096]{2,1,0:T(8,128)S(1)}, f32[1,6,4096]{2,1,0:T(8,128)S(1)}, u32[]{:S(2)}, u32[]{:S(2)}) collective-permute-start(f32[1,6,4096]{2,1,0:T(8,128)S(1)} %get-tuple-element.72), channel_id=1, source_target_pairs={{1,0},{2,1},{3,2},{4,3},{5,4},{6,5},{7,6},{8,7},{9,8},{10,9},{11,1... | collective-permute-start | bytes 294920 | tf_op jit(solution)/shard_map/ppermute | solution.py:12
  361.7 10.9 %collective-permute-start.15 = (f32[1,6,4096]{2,1,0:T(8,128)S(1)}, f32[1,6,4096]{2,1,0:T(8,128)S(1)}, u32[]{:S(2)}, u32[]{:S(2)}) collective-permute-start(f32[1,6,4096]{2,1,0:T(8,128)S(1)} %get-tuple-element.73), channel_id=1, source_target_pairs={{1,0},{2,1},{3,2},{4,3},{5,4},{6,5},{7,6},{8,7},{9,8},{10,9},{11,1... | collective-permute-start | bytes 294920 | tf_op jit(solution)/shard_map/ppermute | solution.py:12
  363.7 10.9 %collective-permute-start.37 = (f32[8,38,128]{2,1,0:T(8,128)S(1)}, f32[8,38,128]{2,1,0:T(8,128)S(1)}, u32[]{:S(2)}, u32[]{:S(2)}) collective-permute-start(f32[8,38,128]{2,1,0:T(8,128)S(1)} %get-tuple-element.144), channel_id=1, source_target_pairs={{0,2},{1,3},{2,0},{3,1},{4,6},{5,7},{6,4},{7,5},{8,10},{9,11},{10,... | collective-permute-start | bytes 466952 | tf_op jit(solution)/shard_map/ppermute | solution.py:64
  369.1 8.4 %collective-permute-start.36 = (f32[8,38,128]{2,1,0:T(8,128)S(1)}, f32[8,38,128]{2,1,0:T(8,128)S(1)}, u32[]{:S(2)}, u32[]{:S(2)}) collective-permute-start(f32[8,38,128]{2,1,0:T(8,128)S(1)} %get-tuple-element.144), channel_id=1, source_target_pairs={{0,1},{1,0},{2,3},{3,2},{4,5},{5,4},{6,7},{7,6},{8,9},{9,8},{10,11... | collective-permute-start | bytes 466952 | tf_op jit(solution)/shard_map/ppermute | solution.py:64
  370.5 7.7 %collective-permute-start.38 = (f32[8,38,128]{2,1,0:T(8,128)S(1)}, f32[8,38,128]{2,1,0:T(8,128)S(1)}, u32[]{:S(2)}, u32[]{:S(2)}) collective-permute-start(f32[8,38,128]{2,1,0:T(8,128)S(1)} %get-tuple-element.144), channel_id=1, source_target_pairs={{0,3},{1,2},{2,1},{3,0},{4,7},{5,6},{6,5},{7,4},{8,11},{9,10},{10,... | collective-permute-start | bytes 466952 | tf_op jit(solution)/shard_map/ppermute | solution.py:64
  (113 other events, 1347.4 us)

commit v7 on v6

--- a/solution.py
+++ b/solution.py
@@ -23,19 +23,23 @@
         return condition.astype(jnp.float32)[:, None, None]
 
     sums = moved(values, 1)
-    if count <= 2:
-        return sums
-    if direction > 0:
-        sums = sums + gate(firsts > tok_len) * jnp.exp(step_log) * moved(values, 2)
-    else:
-        sums = sums + jnp.exp(step_log) * moved(gate(firsts > tok_len) * values, 2)
-    distance = 2
-    while distance < count:
+    for lag in range(2, min(4, count - 1) + 1):
         if direction > 0:
-            sums = sums + gate(firsts > distance * tok_len) * jnp.exp(distance * step_log) * moved(sums, distance)
+            sums = sums + gate(firsts > (lag - 1) * tok_len) * jnp.exp((lag - 1) * step_log) * moved(values, lag)
         else:
-            sums = sums + jnp.exp(distance * step_log) * moved(gate(lasts >= distance * tok_len) * sums, distance)
-        distance *= 2
+            sums = sums + jnp.exp((lag - 1) * step_log) * moved(gate(firsts > (lag - 1) * tok_len) * values, lag)
+    span = 4
+    while span < count:
+        radix = min(4, count // span)
+        total = sums
+        for part in range(1, radix):
+            reach = part * span
+            if direction > 0:
+                total = total + gate(firsts > reach * tok_len) * jnp.exp(reach * step_log) * moved(sums, reach)
+            else:
+                total = total + jnp.exp(reach * step_log) * moved(gate(lasts >= reach * tok_len) * sums, reach)
+        sums = total
+        span *= radix
     return sums
 
 

time: 388 us -> 424 us (1.093)
  waiting for transfers between devices: 62.5 us -> 104 us
  starting transfers between devices: 109 us -> 104 us
    ppermute x12 -> x16, waiting for transfers between devices: 34.3 us -> 74.9 us  [moved(): return lax.ppermute(block, 'ctx', route)]
    ppermute x21, starting transfers between devices: 37.4 us -> 31.2 us  [_exchange(): lax.ppermute(block, axis, [(i, i ^ mask) for i in range(lax.axis_size(axi...]
    mul x4 -> x5, other arithmetic: 9.13 us -> 6.55 us  [the longest x2 4.92 us: device_scan(): gate(firsts > (lag - 1) * tok_len) * values]
    unnamed x298 -> x238, local copies, waits for them, and re-layouts: 9.29 us -> 11.6 us
    ppermute x12 -> x16, starting transfers between devices: 57.1 us -> 58.7 us  [moved(): return lax.ppermute(block, 'ctx', route)]
  transfers between devices with their start and end apart: 39 -> 43, of which waited for: 17 -> 19; matrix products, arithmetic and copies ran while one was open for 21% -> 20% of each run, Pallas kernels for 0% -> 0%
where the time goes in v7:
time: 424 us; the launch traced here: 417 us
  other arithmetic  168 us (40%)
  starting transfers between devices  104 us (25%)
  waiting for transfers between devices  104 us (25%)
  local copies, waits for them, and re-layouts  30.5 us (7%)
  between operations  10.4 us (2%)
    ppermute x16, waiting for transfers between devices, moved(): return lax.ppermute(block, 'ctx', route)  74.9 us
    ppermute x16, starting transfers between devices, moved(): return lax.ppermute(block, 'ctx', route)  58.7 us
    ppermute x21, starting transfers between devices, _exchange(): lax.ppermute(block, axis, [(i, i ^ mask) for i in range(lax.axis_size(axi...  31.2 us
    ppermute x21, waiting for transfers between devices, _exchange(): lax.ppermute(block, axis, [(i, i ^ mask) for i in range(lax.axis_size(axi...  27 us
    reduce_sum x2, other arithmetic, shards(): tap_terms.append(jnp.sum(window(tap_index) * short_grads, axis=(1, 2)))  19.9 us
    ppermute x6, starting transfers between devices, from_behind(): return lax.ppermute(block, axis, route)  14 us
    add x1, other arithmetic, shards(): spread + short_taps[:, tap_index][:, None, None, :] * padded[:, :, tap_in...  14 us
    unnamed x238, local copies, waits for them, and re-layouts  11.6 us
  transfers between devices with their start and end apart: 43, of which 19 were waited for; matrix products, arithmetic and copies ran while one was open for 20% of the time, Pallas kernels for 0%

profile of v7, /device:TPU:2, one launch (start us, length us, event | category | flops | bytes accessed | tf_op | source)
XLA Modules:
  0.0 416.8 jit_solution(10574505999407423417)
XLA Ops:
  1.6 3.5 collective-permute-start.2
  5.9 3.5 collective-permute-start.1
  10.3 3.2 collective-permute-start
  19.2 2.6 fusion.143
  24.0 2.0 fusion.129
  36.8 9.5 %multiply_add_fusion = f32[3,1,128,4096]{3,2,1,0:T(8,128)S(1)} fusion(f32[3,4096]{1,0:T(4,128)S(1)} %copy-done.39, f32[3,4096]{1,0:T(4,128)S(1)} %copy-done.41, f32[3,4096]{1,0:T(4,128)S(1)} %get-tuple-element.193, f32[3,4096]{1,0:T(4,128)S(1)} %get-tuple-element.194, f32[3,4096]{1,0:T(4,128)S(1)} %copy-done.35, f32[3,4096]{1,0:T(4,128)S(1)} %copy-done.37, ...), kind=kLoop, calls=%fused_computation.47 | loop fusion | flops 42467328 | bytes 28656512 | tf_op jit(solution)/shard_map/add | solution.py:166
  46.6 1.7 copy-done.24
  48.3 1.9 broadcast_select_fusion.7
  50.3 2.1 multiply_reduce_fusion.30
  52.5 4.1 multiply_reduce_fusion.23
  56.7 4.5 %multiply_reduce_fusion.14 = (f32[4096]{0:T(1024)}, f32[4096]{0:T(1024)}, f32[4096]{0:T(1024)}, f32[4096]{0:T(1024)}, f32[4096]{0:T(1024)}, /*index=5*/f32[4096]...) fusion(f32[1,8,16,4096]{3,2,1,0:T(8,128)S(1)} %bitcast.589, f32[1,8,16,4096]{3,2,1,0:T(8,128)S(1)} %bitcast.592, ...), kind=kLoop, calls=%fused_computation.153 | loop fusion | flops 14118912 | bytes 4342912 | tf_op jit(solution)/shard_map/reduce_sum | solution.py:251
  61.2 3.3 stack.269
  64.5 7.9 %fusion.13 = (f32[16,16,4096]{2,1,0:T(8,128)}, f32[16,16,4096]{2,1,0:T(8,128)}, f32[16,4096]{1,0:T(8,128)}, f32[16,4096]{1,0:T(8,128)}, f32[16,16,4096]{2,1,0:T(8,128)}) fusion(f32[16,4096]{1,0:T(8,128)} %get-tuple-element.141, f32[16,4096]{1,0:T(8,128)} %get-tuple-element.142, f32[16]{0:T(128)} %iota_convert_fusion, f32[16,4096]{1,0:T(8,128)} %get-tuple-element.143, ...), kind=kLoop, calls=%fused_computation.74 | loop fusion | flops 7208960 | bytes 14155840 | tf_op jit(solution)/shard_map/mul | solution.py:177
  72.4 4.6 %rev.6 = f32[16,16,4096]{2,1,0:T(8,128)} reverse(f32[16,16,4096]{2,1,0:T(8,128)} %get-tuple-element.116), dimensions={0} | reverse | bytes 8388608 | tf_op jit(solution)/shard_map/rev | solution.py:178
  77.0 2.0 broadcast_multiply_fusion.2
  79.9 2.7 multiply_reduce_fusion.3
  82.7 5.0 %fusion.72 = f32[1,16,4096]{2,1,0:T(8,128)S(1)} fusion(f32[1,8,16,4096]{3,2,1,0:T(8,128)S(1)} %bitcast.602, f32[]{:T(128)} %bitcast.45, f32[]{:T(128)} %bitcast.43, f32[]{:T(128)} %bitcast.41, f32[]{:T(128)} %bitcast.39, f32[]{:T(128)} %bitcast.37, f32[]{:T(128)} %bitcast.35, f32[]{:T(128)} %bitcast.33, f32[]{:T(128)} %bitcast.31, f32[16,4096]{1,0:T(8,128)S(1)} %copy-done.2), kind=kLoop, calls=%fused_computation.202 | loop fusion | flops 1703936 | bytes 2621472 | tf_op jit(solution)/shard_map/add | solution.py:207
  87.7 3.8 collective-permute-start.6
  91.6 5.2 %collective-permute-start.5 = (f32[1,16,4096]{2,1,0:T(8,128)S(1)}, f32[1,16,4096]{2,1,0:T(8,128)S(1)}, u32[]{:S(2)}, u32[]{:S(2)}) collective-permute-start(f32[1,16,4096]{2,1,0:T(8,128)S(1)} %fusion.72), channel_id=1, source_target_pairs={{0,3},{1,4},{2,5},{3,6},{4,7},{5,8},{6,9},{7,10},{8,11},{9,12},{10... | collective-permute-start | bytes 786440 | tf_op jit(solution)/shard_map/ppermute | solution.py:20
  96.8 3.6 collective-permute-start.4
  100.4 2.9 collective-permute-start.3
  103.5 8.5 %broadcast_select_fusion.8 = (f32[1,8,16,4096]{3,2,1,0:T(8,128)S(1)}, f32[1,8,16,4096]{3,2,1,0:T(8,128)S(1)}, f32[1,8,16,4096]{3,2,1,0:T(8,128)S(1)}, f32[1,8,16...) fusion(pred[8,16]{1,0:T(8,128)(4,1)S(1)} %copy-done.49, ...), kind=kLoop, calls=%fused_computation.179 | loop fusion | flops 7340032 | bytes 31459072 | tf_op jit(solution)/shard_map/jit(_where)/select_n | solution.py:195
  112.3 1.9 copy-done.6
  114.2 2.7 multiply_reduce_fusion.1
  117.2 4.9 %multiply_bitcast_fusion.3 = (f32[1,16,4096]{2,1,0:T(8,128)S(1)}, f32[16,4096]{1,0:T(8,128)S(1)}) fusion(f32[]{:T(128)} %bitcast.47, f32[]{:T(128)} %bitcast.31, f32[1,8,16,4096]{3,2,1,0:T(8,128)S(1)} %bitcast.595, f32[]{:T(128)} %bitcast.33, f32[]{:T(128)} %bitcast.35, f32[]{:T(128)} %bitcast.37, f32[]{:T(128)} %bitcast.39, f32[]{:T(128)} %bitcast.41, ...), kind=kLoop, calls=%fused_computation.306 | loop fusion | flops 1769472 | bytes 2883620 | tf_op jit(solution)/shard_map/mul | solution.py:30
  122.4 5.9 %collective-permute-start.9 = (f32[1,16,4096]{2,1,0:T(8,128)S(1)}, f32[1,16,4096]{2,1,0:T(8,128)S(1)}, u32[]{:S(2)}, u32[]{:S(2)}) collective-permute-start(f32[1,16,4096]{2,1,0:T(8,128)S(1)} %fusion.105), channel_id=1, source_target_pairs={{0,12},{1,13},{2,14},{3,15},{4,16},{5,17},{6,18},{7,19},{8,20},{9,... | collective-permute-start | bytes 786440 | tf_op jit(solution)/shard_map/ppermute | solution.py:20
  128.3 2.5 collective-permute-start.8
  130.8 1.9 collective-permute-start.7
  132.8 2.2 collective-permute-done.9
  135.0 5.4 %collective-permute-done.8 = f32[1,16,4096]{2,1,0:T(8,128)S(1)} collective-permute-done((f32[1,16,4096]{2,1,0:T(8,128)S(1)}, f32[1,16,4096]{2,1,0:T(8,128)S(1)}, u32[]{:S(2)}, u32[]{:S(2)}) %collective-permute-start.8) | collective-permute-done | bytes 262176 | tf_op jit(solution)/shard_map/ppermute | solution.py:20
  140.4 2.8 collective-permute-done.7
  143.4 22.4 %collective-permute-start.10 = (f32[1,16,4096]{2,1,0:T(8,128)S(1)}, f32[1,16,4096]{2,1,0:T(8,128)S(1)}, u32[]{:S(2)}, u32[]{:S(2)}) collective-permute-start(f32[1,16,4096]{2,1,0:T(8,128)S(1)} %fusion.102), channel_id=1, source_target_pairs={{0,16},{1,17},{2,18},{3,19},{4,20},{5,21},{6,22},{7,23},{8,24},{9,... | collective-permute-start | bytes 786440 | tf_op jit(solution)/shard_map/ppermute | solution.py:20
  172.0 2.7 collective-permute-done.11
  174.7 7.4 %collective-permute-done.12 = f32[1,16,4096]{2,1,0:T(8,128)S(1)} collective-permute-done((f32[1,16,4096]{2,1,0:T(8,128)S(1)}, f32[1,16,4096]{2,1,0:T(8,128)S(1)}, u32[]{:S(2)}, u32[]{:S(2)}) %collective-permute-start.12) | collective-permute-done | bytes 262176 | tf_op jit(solution)/shard_map/ppermute | solution.py:20
  182.1 1.9 collective-permute-done.13
  184.0 20.1 %collective-permute-done.14 = f32[1,16,4096]{2,1,0:T(8,128)S(1)} collective-permute-done((f32[1,16,4096]{2,1,0:T(8,128)S(1)}, f32[1,16,4096]{2,1,0:T(8,128)S(1)}, u32[]{:S(2)}, u32[]{:S(2)}) %collective-permute-start.14) | collective-permute-done | bytes 262176 | tf_op jit(solution)/shard_map/ppermute | solution.py:20
  208.9 11.0 %collective-permute-done.15 = f32[1,16,4096]{2,1,0:T(8,128)S(1)} collective-permute-done((f32[1,16,4096]{2,1,0:T(8,128)S(1)}, f32[1,16,4096]{2,1,0:T(8,128)S(1)}, u32[]{:S(2)}, u32[]{:S(2)}) %collective-permute-start.15) | collective-permute-done | bytes 262176 | tf_op jit(solution)/shard_map/ppermute | solution.py:20
  220.9 20.4 %collective-permute-done.17 = f32[1,16,4096]{2,1,0:T(8,128)S(1)} collective-permute-done((f32[1,16,4096]{2,1,0:T(8,128)S(1)}, f32[1,16,4096]{2,1,0:T(8,128)S(1)}, u32[]{:S(2)}, u32[]{:S(2)}) %collective-permute-start.17) | collective-permute-done | bytes 262176 | tf_op jit(solution)/shard_map/ppermute | solution.py:20
  247.9 9.6 %multiply_reduce_fusion.2 = f32[8,16,4096]{2,1,0:T(8,128)} fusion(f32[8,16,4096]{2,1,0:T(8,128)S(1)} %bitcast.610, f32[16,16,4096]{2,1,0:T(8,128)S(1)} %copy-done.12), kind=kLoop, calls=%fused_computation.2 | loop fusion | flops 16252928 | bytes 8388608 | tf_op jit(solution)/shard_map/reduce_sum | solution.py:223
  257.6 8.1 %fusion.69 = f32[1,8,16,4096]{3,2,1,0:T(8,128)} fusion(f32[8,16,4096]{2,1,0:T(8,128)} %multiply_reduce_fusion.2, f32[1,8,16,4096]{3,2,1,0:T(8,128)S(1)} %bitcast.594, f32[8,16]{1,0:T(8,128)S(1)} %copy-done.47, f32[4096]{0:T(1024)S(1)} %bitcast.621, f32[4096]{0:T(1024)S(1)} %bitcast.623, f32[4096]{0:T(1024)S(1)} %bitcast.625, f32[4096]{0:T(1024)S(1)} %bitcast.627, ...), kind=kLoop, calls=%fused_computation.151 | loop fusion | flops 25690112 | bytes 6556160 | tf_op jit(solution)/shard_map/add | solution.py:226
  267.6 4.8 %bitcast_dynamic-update-slice_fusion.7 = (f32[8,1,16,4096]{3,2,1,0:T(8,128)S(1)}, f32[1,16,4096]{2,1,0:T(8,128)S(1)}, f32[1,16,4096]{2,1,0:T(8,128)S(1)}, f32[1,16,4096]{2,1,0:T(8,128)S(1)}) fusion(f32[1,8,16,4096]{3,2,1,0:T(8,128)S(1)} %bitcast.596, f32[]{:T(128)} %bitcast.43, f32[]{:T(128)} %bitcast.41, f32[16,4096]{1,0:T(8,128)S(1)} %copy-done.2, ...), kind=kLoop, calls=%fused_computation.210 | loop fusion | flops 1703935 | bytes 3670044
  274.9 8.3 %multiply_reduce_fusion = f32[8,16,4096]{2,1,0:T(8,128)S(1)} fusion(f32[8,16,4096]{2,1,0:T(8,128)S(1)} %bitcast.611, f32[16,16,4096]{2,1,0:T(8,128)S(1)} %reverse_multiply_fusion), kind=kLoop, calls=%fused_computation | loop fusion | flops 16252928 | bytes 8388608 | tf_op jit(solution)/shard_map/reduce_sum | solution.py:240
  283.3 6.7 %fusion.31 = f32[1,8,16,4096]{3,2,1,0:T(8,128)} fusion(f32[1,8,16,4096]{3,2,1,0:T(8,128)} %get-tuple-element.97, f32[1,8,16,4096]{3,2,1,0:T(8,128)S(1)} %get-tuple-element.85, f32[1,8,16,4096]{3,2,1,0:T(8,128)S(1)} %get-tuple-element.86, f32[1,8,16,4096]{3,2,1,0:T(8,128)S(1)} %copy-done.14, f32[1,8,16,4096]{3,2,1,0:T(8,128)S(1)} %copy-done.15, ...), kind=kLoop, calls=%fused_computation.102 | loop fusion | flops 17825792 | bytes 38011520 | tf_op jit(solution)/shard_map/add | solution.py:243
  290.1 8.3 %fusion.67 = (f32[1,1,128,4096]{3,2,1,0:T(8,128)S(1)}, f32[1,1,128,4096]{3,2,1,0:T(8,128)S(1)}, bf16[1,128,4096]{2,1,0:T(8,128)(2,1)}, f32[1,1,128,4096]{3,2,1,0:T(8,128)}) fusion(f32[3,1,128,4096]{3,2,1,0:T(8,128)} %copy-done.3, f32[1,128,4096]{2,1,0:T(8,128)S(1)} %copy-done.1, f32[4096]{0:T(1024)} %param.16, f32[1,8,16,4096]{3,2,1,0:T(8,128)} %fusion.31, ...), kind=kLoop, calls=%fused_computation.146 | loop fusion | flops 5242880 | bytes 23085056 | tf_op jit(solution)/shard_map/stack | solution.py:269
  298.5 11.8 %multiply_reduce_fusion.4 = (f32[3,4096]{1,0:T(4,128)S(1)}, f32[3,4096]{1,0:T(4,128)S(1)}, f32[3,4096]{1,0:T(4,128)S(1)}, f32[3,4096]{1,0:T(4,128)S(1)}, f32[3,4096]{1,0:T(4,128)S(1)}, /*index=5*/f32[3,4096]{1,0:T(4,128)S(1)}) fusion(pred[128]{0:T(512)(128)(4,1)S(1)} %copy-done.95, bf16[3,1,134,4096]{3,2,1,0:T(8,128)(2,1)S(1)} %pad_maximum_fusion.1, ...), kind=kLoop, calls=%fused_computation.40 | loop fusion | flops 40820736 | bytes 25461504 | tf_op jit(solution)/shard_map/reduce_sum | solution.py:280
  310.3 8.2 %multiply_reduce_fusion.10 = (f32[3,4096]{1,0:T(4,128)S(1)}, f32[3,1,128,4096]{3,2,1,0:T(8,128)}, f32[3,1,128,4096]{3,2,1,0:T(8,128)}, f32[3,1,128,4096]{3,2,1,0:T(8,128)}) fusion(pred[128]{0:T(512)(128)(4,1)S(1)} %copy-done.93, bf16[3,1,134,4096]{3,2,1,0:T(8,128)(2,1)S(1)} %pad_maximum_fusion.1, f32[1,1,128,4096]{3,2,1,0:T(8,128)S(1)} %get-tuple-element.64, ...), kind=kLoop, calls=%fused_computation.46 | loop fusion | flops 14143488 | bytes 28361088 | tf_op jit(solution)/shard_map/reduce_sum | solution.py:280
  321.7 2.8 collective-permute-start.23
  324.5 3.0 collective-permute-done.22
  327.5 4.6 %collective-permute-done.24 = f32[8,38,128]{2,1,0:T(8,128)} collective-permute-done((f32[8,38,128]{2,1,0:T(8,128)S(1)}, f32[8,38,128]{2,1,0:T(8,128)}, u32[]{:S(2)}, u32[]{:S(2)}) %collective-permute-start.24) | collective-permute-done | bytes 155680 | tf_op jit(solution)/shard_map/ppermute | solution.py:68
  333.5 4.3 %collective-permute-done.25 = f32[4,38,128]{2,1,0:T(8,128)S(1)} collective-permute-done((f32[4,38,128]{2,1,0:T(8,128)S(1)}, f32[4,38,128]{2,1,0:T(8,128)S(1)}, u32[]{:S(2)}, u32[]{:S(2)}) %collective-permute-start.25) | collective-permute-done | bytes 77856 | tf_op jit(solution)/shard_map/ppermute | solution.py:68
  337.9 6.9 %collective-permute-start.28 = (f32[1,38,128]{2,1,0:T(8,128)S(1)}, f32[1,38,128]{2,1,0:T(8,128)S(1)}, u32[]{:S(2)}, u32[]{:S(2)}) collective-permute-start(f32[1,38,128]{2,1,0:T(8,128)S(1)} %get-tuple-element.155), channel_id=1, source_target_pairs={{0,24},{1,25},{2,26},{3,27},{4,28},{5,29},{6,30},{7,31},{8,16},{9,... | collective-permute-start | bytes 58376 | tf_op jit(solution)/shard_map/ppermute | solution.py:68
  344.9 11.5 %broadcast_select_fusion.2 = (f32[3,1,128,4096]{3,2,1,0:T(8,128)}, f32[3,1,128,4096]{3,2,1,0:T(8,128)}, f32[3,1,128,4096]{3,2,1,0:T(8,128)}, f32[3,1,128,4096]{3,2,1,0:T(8,128)}) fusion(pred[128]{0:T(512)(128)(4,1)S(1)} %copy-done.99, f32[1,1,128,4096]{3,2,1,0:T(8,128)} %copy-done.9, f32[1,1,128,4096]{3,2,1,0:T(8,128)S(1)} %copy-done.8, ...), kind=kLoop, calls=%fused_computation.78 | loop fusion | flops 9437184 | bytes 31457792 | tf_op jit(solution)/shard_map/jit(_where)/select_n | solution.py:273
  356.7 14.0 %fusion.6 = f32[3,1,134,4096]{3,2,1,0:T(8,128)S(1)} fusion(f32[3,1,128,4096]{3,2,1,0:T(8,128)S(1)} %bitcast.601, f32[3,1,128,4096]{3,2,1,0:T(8,128)} %get-tuple-element.82, f32[3,1,128,4096]{3,2,1,0:T(8,128)} %get-tuple-element.81, f32[3,1,128,4096]{3,2,1,0:T(8,128)} %get-tuple-element.80, f32[3,1,128,4096]{3,2,1,0:T(8,128)} %get-tuple-element.79, ...), kind=kLoop, calls=%fused_computation.32 | loop fusion | flops 21405696 | bytes 50970624 | tf_op jit(solution)/shard_map/add | solution.py:276
  373.1 2.4 collective-permute-start.32
  375.6 1.6 collective-permute-start.31
  377.7 3.3 collective-permute-done.30
  381.1 3.1 collective-permute-done.35
  384.2 3.6 collective-permute-start.38
  387.8 2.4 collective-permute-start.37
  390.8 4.7 %collective-permute-done.37 = f32[1,38,128]{2,1,0:T(8,128)S(1)} collective-permute-done((f32[1,38,128]{2,1,0:T(8,128)S(1)}, f32[1,38,128]{2,1,0:T(8,128)S(1)}, u32[]{:S(2)}, u32[]{:S(2)}) %collective-permute-start.37) | collective-permute-done | bytes 19488 | tf_op jit(solution)/shard_map/ppermute | solution.py:68
  401.0 4.8 %collective-permute-start.41 = (f32[8,38,128]{2,1,0:T(8,128)S(1)}, f32[8,38,128]{2,1,0:T(8,128)S(1)}, u32[]{:S(2)}, u32[]{:S(2)}) collective-permute-start(f32[8,38,128]{2,1,0:T(8,128)S(1)} %get-tuple-element.145), channel_id=1, source_target_pairs={{0,2},{1,3},{2,0},{3,1},{4,6},{5,7},{6,4},{7,5},{8,10},{9,11},{10,... | collective-permute-start | bytes 466952 | tf_op jit(solution)/shard_map/ppermute | solution.py:68
  407.2 2.1 collective-permute-done.19
  409.3 2.0 fusion.62
  411.3 2.7 collective-permute-done.40
  (363 shorter events, 56.4 us)
Async XLA Ops:
  0.6 33.7 %copy-start.29 = (bf16[1,128,4096]{2,1,0:T(8,128)(2,1)S(1)}, bf16[1,128,4096]{2,1,0:T(8,128)(2,1)}, u32[]{:S(2)}) copy-start(bf16[1,128,4096]{2,1,0:T(8,128)(2,1)} %param.9) | copy-start | bytes 3145732
  1.6 33.3 %collective-permute-start.2 = (bf16[1,6,4096]{2,1,0:T(8,128)(2,1)S(1)}, bf16[1,6,4096]{2,1,0:T(8,128)(2,1)S(1)}, u32[]{:S(2)}, u32[]{:S(2)}) collective-permute-start(bf16[1,6,4096]{2,1,0:T(8,128)(2,1)S(1)} %slice.443), channel_id=1, source_target_pairs={{0,1},{1,2},{2,3},{3,4},{4,5},{5,6},{6,7},{7,8},{8,9},{9,10},{10,1... | collective-permute-start | bytes 147464 | tf_op jit(solution)/shard_map/ppermute | solution.py:12
  5.9 28.6 %collective-permute-start.1 = (bf16[1,6,4096]{2,1,0:T(8,128)(2,1)S(1)}, bf16[1,6,4096]{2,1,0:T(8,128)(2,1)S(1)}, u32[]{:S(2)}, u32[]{:S(2)}) collective-permute-start(bf16[1,6,4096]{2,1,0:T(8,128)(2,1)S(1)} %slice.442), channel_id=1, source_target_pairs={{0,1},{1,2},{2,3},{3,4},{4,5},{5,6},{6,7},{7,8},{8,9},{9,10},{10,1... | collective-permute-start | bytes 147464 | tf_op jit(solution)/shard_map/ppermute | solution.py:12
  10.3 24.0 %collective-permute-start = (bf16[1,6,4096]{2,1,0:T(8,128)(2,1)S(1)}, bf16[1,6,4096]{2,1,0:T(8,128)(2,1)S(1)}, u32[]{:S(2)}, u32[]{:S(2)}) collective-permute-start(bf16[1,6,4096]{2,1,0:T(8,128)(2,1)S(1)} %slice.441), channel_id=1, source_target_pairs={{0,1},{1,2},{2,3},{3,4},{4,5},{5,6},{6,7},{7,8},{8,9},{9,10},{10,1... | collective-permute-start | bytes 147464 | tf_op jit(solution)/shard_map/ppermute | solution.py:12
  15.5 20.8 %copy-start.94 = (pred[128]{0:T(512)(128)(4,1)}, pred[128]{0:T(512)(128)(4,1)S(1)}, u32[]{:S(2)}) copy-start(pred[128]{0:T(512)(128)(4,1)S(1)} %get-tuple-element.185) | copy-start | bytes 388
  15.5 20.8 %copy-start.96 = (pred[128]{0:T(512)(128)(4,1)}, pred[128]{0:T(512)(128)(4,1)S(1)}, u32[]{:S(2)}) copy-start(pred[128]{0:T(512)(128)(4,1)S(1)} %get-tuple-element.186) | copy-start | bytes 388
  15.5 20.8 %copy-start.98 = (pred[128]{0:T(512)(128)(4,1)}, pred[128]{0:T(512)(128)(4,1)S(1)}, u32[]{:S(2)}) copy-start(pred[128]{0:T(512)(128)(4,1)S(1)} %get-tuple-element.187) | copy-start | bytes 388
  15.5 20.8 %copy-start.100 = (pred[128]{0:T(512)(128)(4,1)}, pred[128]{0:T(512)(128)(4,1)S(1)}, u32[]{:S(2)}) copy-start(pred[128]{0:T(512)(128)(4,1)S(1)} %get-tuple-element.188) | copy-start | bytes 388
  15.5 20.8 %copy-start.102 = (pred[128]{0:T(512)(128)(4,1)}, pred[128]{0:T(512)(128)(4,1)S(1)}, u32[]{:S(2)}) copy-start(pred[128]{0:T(512)(128)(4,1)S(1)} %get-tuple-element.189) | copy-start | bytes 388
  15.5 20.8 %copy-start.104 = (pred[128]{0:T(512)(128)(4,1)}, pred[128]{0:T(512)(128)(4,1)S(1)}, u32[]{:S(2)}) copy-start(pred[128]{0:T(512)(128)(4,1)S(1)} %get-tuple-element.190) | copy-start | bytes 388
  15.5 34.7 %copy-start.92 = (pred[128]{0:T(512)(128)(4,1)}, pred[128]{0:T(512)(128)(4,1)S(1)}, u32[]{:S(2)}) copy-start(pred[128]{0:T(512)(128)(4,1)S(1)} %get-tuple-element.184) | copy-start | bytes 388
  22.4 24.2 %copy-start.87 = (pred[8,16]{1,0:T(8,128)(4,1)}, pred[8,16]{1,0:T(8,128)(4,1)S(1)}, u32[]{:S(2)}) copy-start(pred[8,16]{1,0:T(8,128)(4,1)S(1)} %get-tuple-element.159) | copy-start | bytes 388
  82.6 20.7 %copy-start.1 = (f32[1,128,4096]{2,1,0:T(8,128)S(1)}, f32[1,128,4096]{2,1,0:T(8,128)}, u32[]{:S(2)}) copy-start(f32[1,128,4096]{2,1,0:T(8,128)} %copy-done) | copy-start | bytes 6291460
  82.6 20.7 %copy-start.49 = (pred[8,16]{1,0:T(8,128)(4,1)S(1)}, pred[8,16]{1,0:T(8,128)(4,1)}, u32[]{:S(2)}) copy-start(pred[8,16]{1,0:T(8,128)(4,1)} %get-tuple-element.160) | copy-start | bytes 388
  82.6 20.7 %copy-start.51 = (pred[8,16]{1,0:T(8,128)(4,1)S(1)}, pred[8,16]{1,0:T(8,128)(4,1)}, u32[]{:S(2)}) copy-start(pred[8,16]{1,0:T(8,128)(4,1)} %get-tuple-element.161) | copy-start | bytes 388
  82.6 20.7 %copy-start.53 = (pred[8,16]{1,0:T(8,128)(4,1)S(1)}, pred[8,16]{1,0:T(8,128)(4,1)}, u32[]{:S(2)}) copy-start(pred[8,16]{1,0:T(8,128)(4,1)} %get-tuple-element.162) | copy-start | bytes 388
  82.6 20.7 %copy-start.55 = (pred[8,16]{1,0:T(8,128)(4,1)S(1)}, pred[8,16]{1,0:T(8,128)(4,1)}, u32[]{:S(2)}) copy-start(pred[8,16]{1,0:T(8,128)(4,1)} %get-tuple-element.163) | copy-start | bytes 388
  82.6 20.7 %copy-start.58 = (pred[8,16]{1,0:T(8,128)(4,1)S(1)}, pred[8,16]{1,0:T(8,128)(4,1)}, u32[]{:S(2)}) copy-start(pred[8,16]{1,0:T(8,128)(4,1)} %get-tuple-element.164) | copy-start | bytes 388
  82.6 20.7 %copy-start.61 = (pred[8,16]{1,0:T(8,128)(4,1)S(1)}, pred[8,16]{1,0:T(8,128)(4,1)}, u32[]{:S(2)}) copy-start(pred[8,16]{1,0:T(8,128)(4,1)} %get-tuple-element.165) | copy-start | bytes 388
  82.7 20.7 %copy-start.64 = (pred[8,16]{1,0:T(8,128)(4,1)S(1)}, pred[8,16]{1,0:T(8,128)(4,1)}, u32[]{:S(2)}) copy-start(pred[8,16]{1,0:T(8,128)(4,1)} %get-tuple-element.166) | copy-start | bytes 388
  82.7 20.7 %copy-start.67 = (pred[8,16]{1,0:T(8,128)(4,1)S(1)}, pred[8,16]{1,0:T(8,128)(4,1)}, u32[]{:S(2)}) copy-start(pred[8,16]{1,0:T(8,128)(4,1)} %get-tuple-element.167) | copy-start | bytes 388
  87.7 24.3 %copy-start.47 = (f32[8,16]{1,0:T(8,128)S(1)}, f32[8,16]{1,0:T(8,128)}, u32[]{:S(2)}) copy-start(f32[8,16]{1,0:T(8,128)} %get-tuple-element.158) | copy-start | bytes 1540
  87.7 34.4 %collective-permute-start.6 = (f32[1,16,4096]{2,1,0:T(8,128)S(1)}, f32[1,16,4096]{2,1,0:T(8,128)S(1)}, u32[]{:S(2)}, u32[]{:S(2)}) collective-permute-start(f32[1,16,4096]{2,1,0:T(8,128)S(1)} %fusion.72), channel_id=1, source_target_pairs={{0,4},{1,5},{2,6},{3,7},{4,8},{5,9},{6,10},{7,11},{8,12},{9,13},{1... | collective-permute-start | bytes 786440 | tf_op jit(solution)/shard_map/ppermute | solution.py:20
  91.6 30.6 %collective-permute-start.5 = (f32[1,16,4096]{2,1,0:T(8,128)S(1)}, f32[1,16,4096]{2,1,0:T(8,128)S(1)}, u32[]{:S(2)}, u32[]{:S(2)}) collective-permute-start(f32[1,16,4096]{2,1,0:T(8,128)S(1)} %fusion.72), channel_id=1, source_target_pairs={{0,3},{1,4},{2,5},{3,6},{4,7},{5,8},{6,9},{7,10},{8,11},{9,12},{10... | collective-permute-start | bytes 786440 | tf_op jit(solution)/shard_map/ppermute | solution.py:20
  96.8 25.3 %collective-permute-start.4 = (f32[1,16,4096]{2,1,0:T(8,128)S(1)}, f32[1,16,4096]{2,1,0:T(8,128)S(1)}, u32[]{:S(2)}, u32[]{:S(2)}) collective-permute-start(f32[1,16,4096]{2,1,0:T(8,128)S(1)} %fusion.72), channel_id=1, source_target_pairs={{0,2},{1,3},{2,4},{3,5},{4,6},{5,7},{6,8},{7,9},{8,10},{9,11},{10,... | collective-permute-start | bytes 786440 | tf_op jit(solution)/shard_map/ppermute | solution.py:20
  100.4 21.7 %collective-permute-start.3 = (f32[1,16,4096]{2,1,0:T(8,128)S(1)}, f32[1,16,4096]{2,1,0:T(8,128)S(1)}, u32[]{:S(2)}, u32[]{:S(2)}) collective-permute-start(f32[1,16,4096]{2,1,0:T(8,128)S(1)} %fusion.72), channel_id=1, source_target_pairs={{0,1},{1,2},{2,3},{3,4},{4,5},{5,6},{6,7},{7,8},{8,9},{9,10},{10,1... | collective-permute-start | bytes 786440 | tf_op jit(solution)/shard_map/ppermute | solution.py:20
  122.1 43.7 %copy-start.33 = (f32[16,4096]{1,0:T(8,128)S(1)}, f32[16,4096]{1,0:T(8,128)}, u32[]{:S(2)}) copy-start(f32[16,4096]{1,0:T(8,128)} %get-tuple-element.107) | copy-start | bytes 786436
  122.4 12.6 %collective-permute-start.9 = (f32[1,16,4096]{2,1,0:T(8,128)S(1)}, f32[1,16,4096]{2,1,0:T(8,128)S(1)}, u32[]{:S(2)}, u32[]{:S(2)}) collective-permute-start(f32[1,16,4096]{2,1,0:T(8,128)S(1)} %fusion.105), channel_id=1, source_target_pairs={{0,12},{1,13},{2,14},{3,15},{4,16},{5,17},{6,18},{7,19},{8,20},{9,... | collective-permute-start | bytes 786440 | tf_op jit(solution)/shard_map/ppermute | solution.py:20
  128.3 12.1 %collective-permute-start.8 = (f32[1,16,4096]{2,1,0:T(8,128)S(1)}, f32[1,16,4096]{2,1,0:T(8,128)S(1)}, u32[]{:S(2)}, u32[]{:S(2)}) collective-permute-start(f32[1,16,4096]{2,1,0:T(8,128)S(1)} %fusion.105), channel_id=1, source_target_pairs={{0,8},{1,9},{2,10},{3,11},{4,12},{5,13},{6,14},{7,15},{8,16},{9,17... | collective-permute-start | bytes 786440 | tf_op jit(solution)/shard_map/ppermute | solution.py:20
  130.8 12.4 %collective-permute-start.7 = (f32[1,16,4096]{2,1,0:T(8,128)S(1)}, f32[1,16,4096]{2,1,0:T(8,128)S(1)}, u32[]{:S(2)}, u32[]{:S(2)}) collective-permute-start(f32[1,16,4096]{2,1,0:T(8,128)S(1)} %fusion.105), channel_id=1, source_target_pairs={{0,4},{1,5},{2,6},{3,7},{4,8},{5,9},{6,10},{7,11},{8,12},{9,13},{1... | collective-permute-start | bytes 786440 | tf_op jit(solution)/shard_map/ppermute | solution.py:20
  143.4 27.9 %collective-permute-start.10 = (f32[1,16,4096]{2,1,0:T(8,128)S(1)}, f32[1,16,4096]{2,1,0:T(8,128)S(1)}, u32[]{:S(2)}, u32[]{:S(2)}) collective-permute-start(f32[1,16,4096]{2,1,0:T(8,128)S(1)} %fusion.102), channel_id=1, source_target_pairs={{0,16},{1,17},{2,18},{3,19},{4,20},{5,21},{6,22},{7,23},{8,24},{9,... | collective-permute-start | bytes 786440 | tf_op jit(solution)/shard_map/ppermute | solution.py:20
  166.0 8.7 %collective-permute-start.11 = (f32[1,16,4096]{2,1,0:T(8,128)S(1)}, f32[1,16,4096]{2,1,0:T(8,128)S(1)}, u32[]{:S(2)}, u32[]{:S(2)}) collective-permute-start(f32[1,16,4096]{2,1,0:T(8,128)S(1)} %bitcast.613), channel_id=1, source_target_pairs={{1,0},{2,1},{3,2},{4,3},{5,4},{6,5},{7,6},{8,7},{9,8},{10,9},{11,1... | collective-permute-start | bytes 786440 | tf_op jit(solution)/shard_map/ppermute | solution.py:20
  167.3 14.8 %collective-permute-start.12 = (f32[1,16,4096]{2,1,0:T(8,128)S(1)}, f32[1,16,4096]{2,1,0:T(8,128)S(1)}, u32[]{:S(2)}, u32[]{:S(2)}) collective-permute-start(f32[1,16,4096]{2,1,0:T(8,128)S(1)} %get-tuple-element.58), channel_id=1, source_target_pairs={{2,0},{3,1},{4,2},{5,3},{6,4},{7,5},{8,6},{9,7},{10,8},{11,9},{12,... | collective-permute-start | bytes 786440 | tf_op jit(solution)/shard_map/ppermute | solution.py:20
  168.6 15.4 %collective-permute-start.13 = (f32[1,16,4096]{2,1,0:T(8,128)S(1)}, f32[1,16,4096]{2,1,0:T(8,128)S(1)}, u32[]{:S(2)}, u32[]{:S(2)}) collective-permute-start(f32[1,16,4096]{2,1,0:T(8,128)S(1)} %get-tuple-element.123), channel_id=1, source_target_pairs={{3,0},{4,1},{5,2},{6,3},{7,4},{8,5},{9,6},{10,7},{11,8},{12,9},{13... | collective-permute-start | bytes 786440 | tf_op jit(solution)/shard_map/ppermute | solution.py:20
  169.9 34.2 %collective-permute-start.14 = (f32[1,16,4096]{2,1,0:T(8,128)S(1)}, f32[1,16,4096]{2,1,0:T(8,128)S(1)}, u32[]{:S(2)}, u32[]{:S(2)}) collective-permute-start(f32[1,16,4096]{2,1,0:T(8,128)S(1)} %get-tuple-element.124), channel_id=1, source_target_pairs={{4,0},{5,1},{6,2},{7,3},{8,4},{9,5},{10,6},{11,7},{12,8},{13,9},{1... | collective-permute-start | bytes 786440 | tf_op jit(solution)/shard_map/ppermute | solution.py:20
  204.9 15.0 %collective-permute-start.15 = (f32[1,16,4096]{2,1,0:T(8,128)S(1)}, f32[1,16,4096]{2,1,0:T(8,128)S(1)}, u32[]{:S(2)}, u32[]{:S(2)}) collective-permute-start(f32[1,16,4096]{2,1,0:T(8,128)S(1)} %get-tuple-element.56), channel_id=1, source_target_pairs={{4,0},{5,1},{6,2},{7,3},{8,4},{9,5},{10,6},{11,7},{12,8},{13,9},{1... | collective-permute-start | bytes 786440 | tf_op jit(solution)/shard_map/ppermute | solution.py:20
  206.2 14.7 %collective-permute-start.16 = (f32[1,16,4096]{2,1,0:T(8,128)S(1)}, f32[1,16,4096]{2,1,0:T(8,128)S(1)}, u32[]{:S(2)}, u32[]{:S(2)}) collective-permute-start(f32[1,16,4096]{2,1,0:T(8,128)S(1)} %get-tuple-element.119), channel_id=1, source_target_pairs={{8,0},{9,1},{10,2},{11,3},{12,4},{13,5},{14,6},{15,7},{16,8},{17,9... | collective-permute-start | bytes 786440 | tf_op jit(solution)/shard_map/ppermute | solution.py:20
  207.5 33.8 %collective-permute-start.17 = (f32[1,16,4096]{2,1,0:T(8,128)S(1)}, f32[1,16,4096]{2,1,0:T(8,128)S(1)}, u32[]{:S(2)}, u32[]{:S(2)}) collective-permute-start(f32[1,16,4096]{2,1,0:T(8,128)S(1)} %get-tuple-element.120), channel_id=1, source_target_pairs={{12,0},{13,1},{14,2},{15,3},{16,4},{17,5},{18,6},{19,7},{20,8},{21... | collective-permute-start | bytes 786440 | tf_op jit(solution)/shard_map/ppermute | solution.py:20
  242.2 25.5 %collective-permute-start.18 = (f32[1,16,4096]{2,1,0:T(8,128)S(1)}, f32[1,16,4096]{2,1,0:T(8,128)S(1)}, u32[]{:S(2)}, u32[]{:S(2)}) collective-permute-start(f32[1,16,4096]{2,1,0:T(8,128)S(1)} %get-tuple-element.54), channel_id=1, source_target_pairs={{16,0},{17,1},{18,2},{19,3},{20,4},{21,5},{22,6},{23,7},{24,8},{25... | collective-permute-start | bytes 786440 | tf_op jit(solution)/shard_map/ppermute | solution.py:20
  319.7 25.3 %copy-start.8 = (f32[1,1,128,4096]{3,2,1,0:T(8,128)S(1)}, f32[1,1,128,4096]{3,2,1,0:T(8,128)}, u32[]{:S(2)}) copy-start(f32[1,1,128,4096]{3,2,1,0:T(8,128)} %copy-done.7) | copy-start | bytes 6291460
  320.4 7.1 %collective-permute-start.22 = (f32[8,38,128]{2,1,0:T(8,128)}, f32[8,38,128]{2,1,0:T(8,128)S(1)}, u32[]{:S(2)}, u32[]{:S(2)}) collective-permute-start(f32[8,38,128]{2,1,0:T(8,128)} %get-tuple-element.102), channel_id=1, source_target_pairs={{0,1},{1,0},{2,3},{3,2},{4,5},{5,4},{6,7},{7,6},{8,9},{9,8},{10,11... | collective-permute-start | bytes 466952 | tf_op jit(solution)/shard_map/ppermute | solution.py:68
  321.7 10.5 %collective-permute-start.24 = (f32[8,38,128]{2,1,0:T(8,128)S(1)}, f32[8,38,128]{2,1,0:T(8,128)}, u32[]{:S(2)}, u32[]{:S(2)}) collective-permute-start(f32[8,38,128]{2,1,0:T(8,128)S(1)} %get-tuple-element.103), channel_id=1, source_target_pairs={{0,3},{1,2},{2,1},{3,0},{4,7},{5,6},{6,5},{7,4},{8,11},{9,10},{10,... | collective-permute-start | bytes 466952 | tf_op jit(solution)/shard_map/ppermute | solution.py:68
  321.7 10.5 %collective-permute-start.23 = (f32[8,38,128]{2,1,0:T(8,128)S(1)}, f32[8,38,128]{2,1,0:T(8,128)}, u32[]{:S(2)}, u32[]{:S(2)}) collective-permute-start(f32[8,38,128]{2,1,0:T(8,128)S(1)} %get-tuple-element.104), channel_id=1, source_target_pairs={{0,2},{1,3},{2,0},{3,1},{4,6},{5,7},{6,4},{7,5},{8,10},{9,11},{10,... | collective-permute-start | bytes 466952 | tf_op jit(solution)/shard_map/ppermute | solution.py:68
  333.2 4.5 %collective-permute-start.25 = (f32[4,38,128]{2,1,0:T(8,128)S(1)}, f32[4,38,128]{2,1,0:T(8,128)S(1)}, u32[]{:S(2)}, u32[]{:S(2)}) collective-permute-start(f32[4,38,128]{2,1,0:T(8,128)S(1)} %constant_dynamic-slice_fusion.3), channel_id=1, source_target_pairs={{0,4},{1,5},{2,6},{3,7},{4,0},{5,1},{6,2},{7,3},{8,12},{9,13},{10,... | collective-permute-start | bytes 233480 | tf_op jit(solution)/shard_map/ppermute | solution.py:68
  337.8 18.7 %collective-permute-start.26 = (f32[1,38,128]{2,1,0:T(8,128)S(1)}, f32[1,38,128]{2,1,0:T(8,128)S(1)}, u32[]{:S(2)}, u32[]{:S(2)}) collective-permute-start(f32[1,38,128]{2,1,0:T(8,128)S(1)} %get-tuple-element.154), channel_id=1, source_target_pairs={{0,8},{1,9},{2,10},{3,11},{4,12},{5,13},{6,14},{7,15},{8,0},{9,1},... | collective-permute-start | bytes 58376 | tf_op jit(solution)/shard_map/ppermute | solution.py:68
  337.9 18.6 %collective-permute-start.28 = (f32[1,38,128]{2,1,0:T(8,128)S(1)}, f32[1,38,128]{2,1,0:T(8,128)S(1)}, u32[]{:S(2)}, u32[]{:S(2)}) collective-permute-start(f32[1,38,128]{2,1,0:T(8,128)S(1)} %get-tuple-element.155), channel_id=1, source_target_pairs={{0,24},{1,25},{2,26},{3,27},{4,28},{5,29},{6,30},{7,31},{8,16},{9,... | collective-permute-start | bytes 58376 | tf_op jit(solution)/shard_map/ppermute | solution.py:68
  344.8 11.7 %collective-permute-start.27 = (f32[1,38,128]{2,1,0:T(8,128)S(1)}, f32[1,38,128]{2,1,0:T(8,128)S(1)}, u32[]{:S(2)}, u32[]{:S(2)}) collective-permute-start(f32[1,38,128]{2,1,0:T(8,128)S(1)} %get-tuple-element.156), channel_id=1, source_target_pairs={{0,16},{1,17},{2,18},{3,19},{4,20},{5,21},{6,22},{7,23},{8,24},{9,... | collective-permute-start | bytes 58376 | tf_op jit(solution)/shard_map/ppermute | solution.py:68
  356.5 20.7 %collective-permute-start.29 = (f32[1,38,128]{2,1,0:T(8,128)S(1)}, f32[1,38,128]{2,1,0:T(8,128)S(1)}, u32[]{:S(2)}, u32[]{:S(2)}) collective-permute-start(f32[1,38,128]{2,1,0:T(8,128)S(1)} %get-tuple-element.33), channel_id=1, source_target_pairs={{0,32},{32,0},{64,96},{96,64},{128,160},{160,128},{192,224},{224,1... | collective-permute-start | bytes 58376 | tf_op jit(solution)/shard_map/ppermute | solution.py:68
  370.7 10.4 %collective-permute-start.34 = (f32[1,38,128]{2,1,0:T(8,128)S(1)}, f32[1,38,128]{2,1,0:T(8,128)S(1)}, u32[]{:S(2)}, u32[]{:S(2)}) collective-permute-start(f32[1,38,128]{2,1,0:T(8,128)S(1)} %get-tuple-element.33), channel_id=1, source_target_pairs={{0,192},{32,224},{64,128},{96,160},{128,64},{160,96},{192,0},{224,... | collective-permute-start | bytes 58376 | tf_op jit(solution)/shard_map/ppermute | solution.py:68
  372.2 8.8 %collective-permute-start.33 = (f32[1,38,128]{2,1,0:T(8,128)S(1)}, f32[1,38,128]{2,1,0:T(8,128)S(1)}, u32[]{:S(2)}, u32[]{:S(2)}) collective-permute-start(f32[1,38,128]{2,1,0:T(8,128)S(1)} %get-tuple-element.33), channel_id=1, source_target_pairs={{0,160},{32,128},{64,224},{96,192},{128,32},{160,0},{192,96},{224,... | collective-permute-start | bytes 58376 | tf_op jit(solution)/shard_map/ppermute | solution.py:68
  373.1 7.9 %collective-permute-start.32 = (f32[1,38,128]{2,1,0:T(8,128)S(1)}, f32[1,38,128]{2,1,0:T(8,128)S(1)}, u32[]{:S(2)}, u32[]{:S(2)}) collective-permute-start(f32[1,38,128]{2,1,0:T(8,128)S(1)} %get-tuple-element.33), channel_id=1, source_target_pairs={{0,128},{32,160},{64,192},{96,224},{128,0},{160,32},{192,64},{224,... | collective-permute-start | bytes 58376 | tf_op jit(solution)/shard_map/ppermute | solution.py:68
  375.6 5.4 %collective-permute-start.31 = (f32[1,38,128]{2,1,0:T(8,128)S(1)}, f32[1,38,128]{2,1,0:T(8,128)S(1)}, u32[]{:S(2)}, u32[]{:S(2)}) collective-permute-start(f32[1,38,128]{2,1,0:T(8,128)S(1)} %get-tuple-element.33), channel_id=1, source_target_pairs={{0,96},{32,64},{64,32},{96,0},{128,224},{160,192},{192,160},{224,1... | collective-permute-start | bytes 58376 | tf_op jit(solution)/shard_map/ppermute | solution.py:68
  377.2 3.8 collective-permute-start.30
  381.0 3.2 collective-permute-start.35
  384.2 6.6 %collective-permute-start.38 = (f32[1,38,128]{2,1,0:T(8,128)S(1)}, f32[1,38,128]{2,1,0:T(8,128)S(1)}, u32[]{:S(2)}, u32[]{:S(2)}) collective-permute-start(f32[1,38,128]{2,1,0:T(8,128)S(1)} %fusion.147), channel_id=1, source_target_pairs={{0,24},{1,25},{2,26},{3,27},{4,28},{5,29},{6,30},{7,31},{8,16},{9,... | collective-permute-start | bytes 58376 | tf_op jit(solution)/shard_map/ppermute | solution.py:68
  387.8 7.7 %collective-permute-start.37 = (f32[1,38,128]{2,1,0:T(8,128)S(1)}, f32[1,38,128]{2,1,0:T(8,128)S(1)}, u32[]{:S(2)}, u32[]{:S(2)}) collective-permute-start(f32[1,38,128]{2,1,0:T(8,128)S(1)} %fusion.147), channel_id=1, source_target_pairs={{0,16},{1,17},{2,18},{3,19},{4,20},{5,21},{6,22},{7,23},{8,24},{9,... | collective-permute-start | bytes 58376 | tf_op jit(solution)/shard_map/ppermute | solution.py:68
  390.2 5.3 %collective-permute-start.36 = (f32[1,38,128]{2,1,0:T(8,128)S(1)}, f32[1,38,128]{2,1,0:T(8,128)S(1)}, u32[]{:S(2)}, u32[]{:S(2)}) collective-permute-start(f32[1,38,128]{2,1,0:T(8,128)S(1)} %fusion.147), channel_id=1, source_target_pairs={{0,8},{1,9},{2,10},{3,11},{4,12},{5,13},{6,14},{7,15},{8,0},{9,1},... | collective-permute-start | bytes 58376 | tf_op jit(solution)/shard_map/ppermute | solution.py:68
  395.6 5.3 %collective-permute-start.39 = (f32[4,38,128]{2,1,0:T(8,128)S(1)}, f32[4,38,128]{2,1,0:T(8,128)S(1)}, u32[]{:S(2)}, u32[]{:S(2)}) collective-permute-start(f32[4,38,128]{2,1,0:T(8,128)S(1)} %get-tuple-element.148), channel_id=1, source_target_pairs={{0,4},{1,5},{2,6},{3,7},{4,0},{5,1},{6,2},{7,3},{8,12},{9,13},{10,... | collective-permute-start | bytes 233480 | tf_op jit(solution)/shard_map/ppermute | solution.py:68
  395.7 11.5 %collective-permute-start.21 = (f32[1,6,4096]{2,1,0:T(8,128)S(1)}, f32[1,6,4096]{2,1,0:T(8,128)S(1)}, u32[]{:S(2)}, u32[]{:S(2)}) collective-permute-start(f32[1,6,4096]{2,1,0:T(8,128)S(1)} %get-tuple-element.71), channel_id=1, source_target_pairs={{1,0},{2,1},{3,2},{4,3},{5,4},{6,5},{7,6},{8,7},{9,8},{10,9},{11,1... | collective-permute-start | bytes 294920 | tf_op jit(solution)/shard_map/ppermute | solution.py:12
  397.0 10.2 %collective-permute-start.20 = (f32[1,6,4096]{2,1,0:T(8,128)S(1)}, f32[1,6,4096]{2,1,0:T(8,128)S(1)}, u32[]{:S(2)}, u32[]{:S(2)}) collective-permute-start(f32[1,6,4096]{2,1,0:T(8,128)S(1)} %get-tuple-element.72), channel_id=1, source_target_pairs={{1,0},{2,1},{3,2},{4,3},{5,4},{6,5},{7,6},{8,7},{9,8},{10,9},{11,1... | collective-permute-start | bytes 294920 | tf_op jit(solution)/shard_map/ppermute | solution.py:12
  398.3 11.0 %collective-permute-start.19 = (f32[1,6,4096]{2,1,0:T(8,128)S(1)}, f32[1,6,4096]{2,1,0:T(8,128)S(1)}, u32[]{:S(2)}, u32[]{:S(2)}) collective-permute-start(f32[1,6,4096]{2,1,0:T(8,128)S(1)} %get-tuple-element.73), channel_id=1, source_target_pairs={{1,0},{2,1},{3,2},{4,3},{5,4},{6,5},{7,6},{8,7},{9,8},{10,9},{11,1... | collective-permute-start | bytes 294920 | tf_op jit(solution)/shard_map/ppermute | solution.py:12
  401.0 10.3 %collective-permute-start.41 = (f32[8,38,128]{2,1,0:T(8,128)S(1)}, f32[8,38,128]{2,1,0:T(8,128)S(1)}, u32[]{:S(2)}, u32[]{:S(2)}) collective-permute-start(f32[8,38,128]{2,1,0:T(8,128)S(1)} %get-tuple-element.145), channel_id=1, source_target_pairs={{0,2},{1,3},{2,0},{3,1},{4,6},{5,7},{6,4},{7,5},{8,10},{9,11},{10,... | collective-permute-start | bytes 466952 | tf_op jit(solution)/shard_map/ppermute | solution.py:68
  405.7 8.3 %collective-permute-start.40 = (f32[8,38,128]{2,1,0:T(8,128)S(1)}, f32[8,38,128]{2,1,0:T(8,128)S(1)}, u32[]{:S(2)}, u32[]{:S(2)}) collective-permute-start(f32[8,38,128]{2,1,0:T(8,128)S(1)} %get-tuple-element.145), channel_id=1, source_target_pairs={{0,1},{1,0},{2,3},{3,2},{4,5},{5,4},{6,7},{7,6},{8,9},{9,8},{10,11... | collective-permute-start | bytes 466952 | tf_op jit(solution)/shard_map/ppermute | solution.py:68
  407.2 6.9 %collective-permute-start.42 = (f32[8,38,128]{2,1,0:T(8,128)S(1)}, f32[8,38,128]{2,1,0:T(8,128)S(1)}, u32[]{:S(2)}, u32[]{:S(2)}) collective-permute-start(f32[8,38,128]{2,1,0:T(8,128)S(1)} %get-tuple-element.145), channel_id=1, source_target_pairs={{0,3},{1,2},{2,1},{3,0},{4,7},{5,6},{6,5},{7,4},{8,11},{9,10},{10,... | collective-permute-start | bytes 466952 | tf_op jit(solution)/shard_map/ppermute | solution.py:68
  (87 other events, 707.8 us)
